TPU v7x, 512 devices: a whole 4x4x16 slice. The times are simulated.
512 devices in a mesh: gx: 32 (over y, x, core), gy: 16 (over z).
Axes of the slice: x: 4, y: 4, z: 16, core: 2. Of those that a mesh axis runs over, the one named last changes fastest.
Arguments:
- rhs_field: float32 [256, 512, 256], P('gx', 'gy'), may hold values from -50 to 50
- alpha_coef: float32 [256, 512, 256], P('gx', 'gy'), may hold values from 0.2 to 5
- beta_coef: float32 [256, 512, 256], P('gx', 'gy'), may hold values from 0.3 to 27
Outputs:
- solution: float32 [256, 512, 256], P('gx', 'gy')
All inputs are finite; a program needn't handle non-finite values.
Results may differ from a plain program's by a relative error of at most 0.0001.
Values sent between devices are 32-bit elements; how exact they have to be, the bound alone decides.
No kernel may reach another device: no remote copies, remote signals or barrier semaphores. Data moves between devices by JAX's collectives and lax.ppermute only.
A program may use at most 128 MiB of HBM per device.

v0:
```python
import jax
import jax.numpy as jnp
from jax import lax
from jax.sharding import PartitionSpec as P

LEVELS = 4
PRE_STEPS = 3
POST_STEPS = 3
COARSE_STEPS = 8


HELM_SHIFT = 0.05
LOW_FRACTION = 0.1


def with_halo(x, sides, width):
    for axis, dim in sides:
        peers, length = (lax.axis_size(axis), x.shape[dim])
        up = [(i, (i + 1) % peers) for i in range(peers - 1)]
        down = [(j, i) for i, j in up]
        last = lax.slice_in_dim(x, length - width, length, axis=dim)
        initial = lax.slice_in_dim(x, 0, width, axis=dim)
        before = lax.ppermute(last, axis, up)
        after = lax.ppermute(initial, axis, down)
        x = jnp.concatenate([before, x, after], axis=dim)
    return x


def restrict(values):
    first, second, third = values.shape
    return values.reshape(first // 2, 2, second // 2, 2, third // 2, 2).mean(axis=(1, 3, 5))


def prolong(values):
    return jnp.repeat(jnp.repeat(jnp.repeat(values, 2, 0), 2, 1), 2, 2)


def depth_pad(values):
    return jnp.pad(values, ((0, 0), (0, 0), (1, 1)))


def face_pad(field):
    padded = with_halo(field, (("gx", 0), ("gy", 1)), 1)
    return depth_pad(padded)


def coef_pad(beta_level):
    padded = with_halo(beta_level, (("gx", 0), ("gy", 1)), 1)
    return depth_pad(padded)


def neighbours(padded):
    return [
        padded[2:, 1:-1, 1:-1],
        padded[:-2, 1:-1, 1:-1],
        padded[1:-1, 2:, 1:-1],
        padded[1:-1, :-2, 1:-1],
        padded[1:-1, 1:-1, 2:],
        padded[1:-1, 1:-1, :-2],
    ]


def apply_op(u_padded, b_padded, alpha_level, inv_spacing):
    field = u_padded[1:-1, 1:-1, 1:-1]
    interior = b_padded[1:-1, 1:-1, 1:-1]
    summed = jnp.zeros_like(field)
    for near_u, near_b in zip(neighbours(u_padded), neighbours(b_padded)):
        summed = summed + (interior + near_b) * (field - near_u)
    return HELM_SHIFT * alpha_level * field + 0.5 * inv_spacing * summed


def smooth(field, source, alpha_level, b_padded, inv_spacing, upper, sweeps, start_zero, padder):
    lower = LOW_FRACTION * upper
    middle = 0.5 * (upper + lower)
    half_width = 0.5 * (upper - lower)
    scaled = middle / half_width
    factor = 1.0 / scaled
    if start_zero:
        residual = source
    else:
        residual = source - apply_op(padder(field), b_padded, alpha_level, inv_spacing)
    direction = residual / middle
    field = direction if start_zero else field + direction
    for k in range(1, sweeps):
        residual = source - apply_op(padder(field), b_padded, alpha_level, inv_spacing)
        factor_new = 1.0 / (2.0 * scaled - factor)
        direction = factor_new * factor * direction + 2.0 * factor_new / half_width * residual
        field = field + direction
        factor = factor_new
    return field


def descend(level_idx, sources, fields, alphas, b_pads, uppers, padder):
    inv_spacing = 1.0 / 4.0**level_idx
    smoothed = smooth(
        jnp.zeros_like(sources[level_idx]),
        sources[level_idx],
        alphas[level_idx],
        b_pads[level_idx],
        inv_spacing,
        uppers[level_idx],
        PRE_STEPS,
        True,
        padder,
    )
    residual = sources[level_idx] - apply_op(
        padder(smoothed), b_pads[level_idx], alphas[level_idx], inv_spacing
    )
    sources.append(restrict(residual))
    fields.append(smoothed)


def local(rhs_field, alpha_coef, beta_coef):
    alphas = [alpha_coef]
    betas = [beta_coef]
    for level_idx in range(1, LEVELS):
        alphas.append(restrict(alphas[-1]))
        betas.append(restrict(betas[-1]))
    maxima = jnp.stack([jnp.stack([jnp.max(alphas[i]), jnp.max(betas[i])]) for i in range(LEVELS)])
    maxima = lax.pmax(maxima, ("gx", "gy"))
    uppers = [HELM_SHIFT * maxima[i, 0] + 12.0 * maxima[i, 1] / 4.0**i for i in range(LEVELS)]
    b_pads = [coef_pad(betas[i]) for i in range(LEVELS - 2)]
    sources = [rhs_field]
    fields = []
    for level_idx in range(LEVELS - 2):
        descend(level_idx, sources, fields, alphas, b_pads, uppers, face_pad)
    second = LEVELS - 2
    last = LEVELS - 1
    coarse_inv = 1.0 / 4.0**last
    second_inv = 1.0 / 4.0**second
    b_pads.append(coef_pad(betas[second]))
    descend(second, sources, fields, alphas, b_pads, uppers, face_pad)
    coarse_beta = with_halo(betas[last], (("gx", 0), ("gy", 1)), 1)
    coarse = smooth(
        jnp.zeros_like(sources[last]),
        sources[last],
        alphas[last],
        depth_pad(coarse_beta),
        coarse_inv,
        uppers[last],
        COARSE_STEPS,
        True,
        face_pad,
    )
    smoothed = fields[second] + prolong(coarse)
    coarse = smooth(
        smoothed,
        sources[second],
        alphas[second],
        b_pads[second],
        second_inv,
        uppers[second],
        POST_STEPS,
        False,
        face_pad,
    )
    for level_idx in range(LEVELS - 3, -1, -1):
        smoothed = fields[level_idx] + prolong(coarse)
        coarse = smooth(
            smoothed,
            sources[level_idx],
            alphas[level_idx],
            b_pads[level_idx],
            1.0 / 4.0**level_idx,
            uppers[level_idx],
            POST_STEPS,
            False,
            face_pad,
        )
    return coarse


def solution(mesh):
    placed = (P("gx", "gy", None), P("gx", "gy", None), P("gx", "gy", None))
    return jax.shard_map(
        local, mesh=mesh, in_specs=placed, out_specs=P("gx", "gy", None), check_vma=False
    )
```

profile of v0, /device:TPU:136, one launch (start us, length us, event | category | flops | bytes accessed | tf_op | source)
XLA Modules:
  0.0 704.4 jit_solution(6474126762915922463)
XLA Ops:
  2.8 18.9 %reshape.134 = f32[4,2,16,2,128,2]{5,4,3,2,1,0:T(8,128)} reshape(f32[8,32,256]{2,1,0:T(8,128)} %param.5) | data formatting | bytes 524288 | tf_op jit(solution)/shard_map/reshape | solution.py:31
  21.7 7.0 reduce_sum.103
  32.2 18.1 %reshape.133 = f32[4,2,16,2,128,2]{5,4,3,2,1,0:T(8,128)} reshape(f32[8,32,256]{2,1,0:T(8,128)S(1)} %copy-done.1) | data formatting | bytes 524288 | tf_op jit(solution)/shard_map/reshape | solution.py:31
  50.3 7.0 reduce_sum.102
  69.0 5.8 collective-permute-start
  74.7 101.1 %pmax.7 = f32[4,2]{1,0:T(4,128)S(1)} all-reduce(f32[4,2]{1,0:T(4,128)S(1)} %pad_maximum_fusion.272), channel_id=1, replica_groups=mesh['gx'=32,'gy'=16] {'gx','gy'}, use_global_device_ids=true, to_apply=%region_16.17 | all-reduce | flops 8 | bytes 64 | tf_op jit(solution)/shard_map/pmax | solution.py:120
  177.7 4.1 collective-permute-start.1
  189.9 4.1 collective-permute-start.5
  196.3 4.5 collective-permute-done.7
  207.4 5.4 collective-permute-done.9
  214.7 4.1 collective-permute-start.11
  226.6 4.9 collective-permute-done.13
  233.4 3.9 collective-permute-start.15
  239.3 5.8 collective-permute-start.16
  246.9 18.1 %reshape.135 = f32[4,2,16,2,128,2]{5,4,3,2,1,0:T(8,128)} reshape(f32[8,32,256]{2,1,0:T(8,128)S(1)} %fusion.65) | data formatting | bytes 524288 | tf_op jit(solution)/shard_map/reshape | solution.py:31
  265.0 7.0 reduce_sum.112
  282.3 4.3 collective-permute-start.21
  288.9 4.4 collective-permute-done.23
  298.8 5.1 collective-permute-done.25
  317.2 4.7 collective-permute-done.29
  323.8 3.9 collective-permute-start.31
  338.8 5.3 collective-permute-start.33
  352.0 4.3 collective-permute-start.37
  358.6 4.5 collective-permute-done.39
  368.9 5.1 collective-permute-done.41
  387.2 5.3 collective-permute-start.48
  407.9 4.6 collective-permute-start.49
  414.7 4.9 collective-permute-done.51
  419.6 4.6 collective-permute-start.53
  426.2 4.7 collective-permute-done.55
  435.4 4.6 collective-permute-done.57
  453.1 4.6 collective-permute-done.61
  470.8 4.6 collective-permute-done.65
  488.5 4.6 collective-permute-done.69
  506.2 4.6 collective-permute-done.73
  523.9 4.6 collective-permute-done.77
  541.8 4.6 collective-permute-done.81
  548.4 3.9 collective-permute-start.83
  559.6 4.6 collective-permute-done.85
  566.1 3.9 collective-permute-start.87
  577.6 4.6 collective-permute-done.89
  584.1 3.9 collective-permute-start.91
  595.7 4.7 collective-permute-done.93
  613.6 4.7 collective-permute-done.97
  631.4 4.7 collective-permute-done.101
  651.9 4.9 collective-permute-done.105
  670.6 4.9 collective-permute-done.109
  689.4 4.9 collective-permute-done.113
  (349 shorter events, 328.7 us)
Async XLA Ops:
  0.8 64.9 %collective-permute-start.2 = (f32[1,32,256]{2,1,0:T(8,128)S(1)}, f32[1,32,256]{2,1,0:T(8,128)S(1)}, u32[]{:S(2)}, u32[]{:S(2)}) collective-permute-start(f32[1,32,256]{2,1,0:T(8,128)S(1)} %get-tuple-element.86), channel_id=1, source_target_pairs={{0,16},{16,32},{32,48},{48,64},{64,80},{80,96},{96,112},{112,128},... | collective-permute-start | bytes 98312 | tf_op jit(solution)/shard_map/ppermute | solution.py:23
  69.0 114.8 %collective-permute-start = (f32[1,32,256]{2,1,0:T(8,128)S(1)}, f32[1,32,256]{2,1,0:T(8,128)S(1)}, u32[]{:S(2)}, u32[]{:S(2)}) collective-permute-start(f32[1,32,256]{2,1,0:T(8,128)S(1)} %get-tuple-element.85), channel_id=1, source_target_pairs={{16,0},{32,16},{48,32},{64,48},{80,64},{96,80},{112,96},{128,112},... | collective-permute-start | bytes 98312 | tf_op jit(solution)/shard_map/ppermute | solution.py:24
  177.7 12.1 %collective-permute-start.1 = (f32[1,32,256]{2,1,0:T(8,128)S(1)}, f32[1,32,256]{2,1,0:T(8,128)S(1)}, u32[]{:S(2)}, u32[]{:S(2)}) collective-permute-start(f32[1,32,256]{2,1,0:T(8,128)S(1)} %get-tuple-element.88), channel_id=1, source_target_pairs={{16,0},{32,16},{48,32},{64,48},{80,64},{96,80},{112,96},{128,112},... | collective-permute-start | bytes 98312 | tf_op jit(solution)/shard_map/ppermute | solution.py:24
  181.8 8.0 %collective-permute-start.3 = (f32[1,32,256]{2,1,0:T(8,128)S(1)}, f32[1,32,256]{2,1,0:T(8,128)S(1)}, u32[]{:S(2)}, u32[]{:S(2)}) collective-permute-start(f32[1,32,256]{2,1,0:T(8,128)S(1)} %get-tuple-element.87), channel_id=1, source_target_pairs={{0,16},{16,32},{32,48},{48,64},{64,80},{80,96},{96,112},{112,128},... | collective-permute-start | bytes 98312 | tf_op jit(solution)/shard_map/ppermute | solution.py:23
  184.0 12.0 %collective-permute-start.4 = (f32[10,1,256]{2,1,0:T(1,128)S(1)}, f32[10,1,256]{2,1,0:T(1,128)S(1)}, u32[]{:S(2)}, u32[]{:S(2)}) collective-permute-start(f32[10,1,256]{2,1,0:T(1,128)S(1)} %get-tuple-element.70), channel_id=1, source_target_pairs={{1,0},{2,1},{3,2},{4,3},{5,4},{6,5},{7,6},{8,7},{9,8},{10,9},{11,1... | collective-permute-start | bytes 30728 | tf_op jit(solution)/shard_map/ppermute | solution.py:24
  186.9 9.1 %collective-permute-start.6 = (f32[10,1,256]{2,1,0:T(1,128)S(1)}, f32[10,1,256]{2,1,0:T(1,128)S(1)}, u32[]{:S(2)}, u32[]{:S(2)}) collective-permute-start(f32[10,1,256]{2,1,0:T(1,128)S(1)} %get-tuple-element.69), channel_id=1, source_target_pairs={{0,1},{1,2},{2,3},{3,4},{4,5},{5,6},{6,7},{7,8},{8,9},{9,10},{10,1... | collective-permute-start | bytes 30728 | tf_op jit(solution)/shard_map/ppermute | solution.py:23
  205.4 7.3 %collective-permute-start.9 = (f32[1,32,256]{2,1,0:T(8,128)S(1)}, f32[1,32,256]{2,1,0:T(8,128)S(1)}, u32[]{:S(2)}, u32[]{:S(2)}) collective-permute-start(f32[1,32,256]{2,1,0:T(8,128)S(1)} %get-tuple-element.81), channel_id=1, source_target_pairs={{0,16},{16,32},{32,48},{48,64},{64,80},{80,96},{96,112},{112,128},... | collective-permute-start | bytes 98312 | tf_op jit(solution)/shard_map/ppermute | solution.py:23
  224.2 7.3 %collective-permute-start.13 = (f32[1,32,256]{2,1,0:T(8,128)S(1)}, f32[1,32,256]{2,1,0:T(8,128)S(1)}, u32[]{:S(2)}, u32[]{:S(2)}) collective-permute-start(f32[1,32,256]{2,1,0:T(8,128)S(1)} %get-tuple-element.79), channel_id=1, source_target_pairs={{0,16},{16,32},{32,48},{48,64},{64,80},{80,96},{96,112},{112,128},... | collective-permute-start | bytes 98312 | tf_op jit(solution)/shard_map/ppermute | solution.py:23
  231.5 14.7 %collective-permute-start.14 = (f32[10,1,256]{2,1,0:T(1,128)S(1)}, f32[10,1,256]{2,1,0:T(1,128)S(1)}, u32[]{:S(2)}, u32[]{:S(2)}) collective-permute-start(f32[10,1,256]{2,1,0:T(1,128)S(1)} %get-tuple-element.66), channel_id=1, source_target_pairs={{1,0},{2,1},{3,2},{4,3},{5,4},{6,5},{7,6},{8,7},{9,8},{10,9},{11,1... | collective-permute-start | bytes 30728 | tf_op jit(solution)/shard_map/ppermute | solution.py:24
  233.4 12.8 %collective-permute-start.15 = (f32[10,1,256]{2,1,0:T(1,128)S(1)}, f32[10,1,256]{2,1,0:T(1,128)S(1)}, u32[]{:S(2)}, u32[]{:S(2)}) collective-permute-start(f32[10,1,256]{2,1,0:T(1,128)S(1)} %get-tuple-element.65), channel_id=1, source_target_pairs={{0,1},{1,2},{2,3},{3,4},{4,5},{5,6},{6,7},{7,8},{8,9},{9,10},{10,1... | collective-permute-start | bytes 30728 | tf_op jit(solution)/shard_map/ppermute | solution.py:23
  237.4 39.0 %collective-permute-start.18 = (f32[1,16,128]{2,1,0:T(8,128)S(1)}, f32[1,16,128]{2,1,0:T(8,128)S(1)}, u32[]{:S(2)}, u32[]{:S(2)}) collective-permute-start(f32[1,16,128]{2,1,0:T(8,128)S(1)} %get-tuple-element.114), channel_id=1, source_target_pairs={{0,16},{16,32},{32,48},{48,64},{64,80},{80,96},{96,112},{112,128},... | collective-permute-start | bytes 24584 | tf_op jit(solution)/shard_map/ppermute | solution.py:23
  239.3 37.1 %collective-permute-start.16 = (f32[1,16,128]{2,1,0:T(8,128)S(1)}, f32[1,16,128]{2,1,0:T(8,128)S(1)}, u32[]{:S(2)}, u32[]{:S(2)}) collective-permute-start(f32[1,16,128]{2,1,0:T(8,128)S(1)} %get-tuple-element.113), channel_id=1, source_target_pairs={{16,0},{32,16},{48,32},{64,48},{80,64},{96,80},{112,96},{128,112},... | collective-permute-start | bytes 24584 | tf_op jit(solution)/shard_map/ppermute | solution.py:24
  272.0 10.2 %collective-permute-start.17 = (f32[1,16,128]{2,1,0:T(8,128)S(1)}, f32[1,16,128]{2,1,0:T(8,128)S(1)}, u32[]{:S(2)}, u32[]{:S(2)}) collective-permute-start(f32[1,16,128]{2,1,0:T(8,128)S(1)} %get-tuple-element.116), channel_id=1, source_target_pairs={{16,0},{32,16},{48,32},{64,48},{80,64},{96,80},{112,96},{128,112},... | collective-permute-start | bytes 24584 | tf_op jit(solution)/shard_map/ppermute | solution.py:24
  273.9 8.3 %collective-permute-start.19 = (f32[1,16,128]{2,1,0:T(8,128)S(1)}, f32[1,16,128]{2,1,0:T(8,128)S(1)}, u32[]{:S(2)}, u32[]{:S(2)}) collective-permute-start(f32[1,16,128]{2,1,0:T(8,128)S(1)} %get-tuple-element.115), channel_id=1, source_target_pairs={{0,16},{16,32},{32,48},{48,64},{64,80},{80,96},{96,112},{112,128},... | collective-permute-start | bytes 24584 | tf_op jit(solution)/shard_map/ppermute | solution.py:23
  276.4 12.2 %collective-permute-start.20 = (f32[6,1,128]{2,1,0:T(1,128)S(1)}, f32[6,1,128]{2,1,0:T(1,128)S(1)}, u32[]{:S(2)}, u32[]{:S(2)}) collective-permute-start(f32[6,1,128]{2,1,0:T(1,128)S(1)} %get-tuple-element.100), channel_id=1, source_target_pairs={{1,0},{2,1},{3,2},{4,3},{5,4},{6,5},{7,6},{8,7},{9,8},{10,9},{11,1... | collective-permute-start | bytes 9224 | tf_op jit(solution)/shard_map/ppermute | solution.py:24
  279.5 9.0 %collective-permute-start.22 = (f32[6,1,128]{2,1,0:T(1,128)S(1)}, f32[6,1,128]{2,1,0:T(1,128)S(1)}, u32[]{:S(2)}, u32[]{:S(2)}) collective-permute-start(f32[6,1,128]{2,1,0:T(1,128)S(1)} %get-tuple-element.99), channel_id=1, source_target_pairs={{0,1},{1,2},{2,3},{3,4},{4,5},{5,6},{6,7},{7,8},{8,9},{9,10},{10,1... | collective-permute-start | bytes 9224 | tf_op jit(solution)/shard_map/ppermute | solution.py:23
  296.9 7.1 %collective-permute-start.25 = (f32[1,16,128]{2,1,0:T(8,128)S(1)}, f32[1,16,128]{2,1,0:T(8,128)S(1)}, u32[]{:S(2)}, u32[]{:S(2)}) collective-permute-start(f32[1,16,128]{2,1,0:T(8,128)S(1)} %get-tuple-element.111), channel_id=1, source_target_pairs={{0,16},{16,32},{32,48},{48,64},{64,80},{80,96},{96,112},{112,128},... | collective-permute-start | bytes 24584 | tf_op jit(solution)/shard_map/ppermute | solution.py:23
  314.8 7.1 %collective-permute-start.29 = (f32[1,16,128]{2,1,0:T(8,128)S(1)}, f32[1,16,128]{2,1,0:T(8,128)S(1)}, u32[]{:S(2)}, u32[]{:S(2)}) collective-permute-start(f32[1,16,128]{2,1,0:T(8,128)S(1)} %get-tuple-element.109), channel_id=1, source_target_pairs={{0,16},{16,32},{32,48},{48,64},{64,80},{80,96},{96,112},{112,128},... | collective-permute-start | bytes 24584 | tf_op jit(solution)/shard_map/ppermute | solution.py:23
  321.9 11.5 %collective-permute-start.30 = (f32[6,1,128]{2,1,0:T(1,128)S(1)}, f32[6,1,128]{2,1,0:T(1,128)S(1)}, u32[]{:S(2)}, u32[]{:S(2)}) collective-permute-start(f32[6,1,128]{2,1,0:T(1,128)S(1)} %get-tuple-element.96), channel_id=1, source_target_pairs={{1,0},{2,1},{3,2},{4,3},{5,4},{6,5},{7,6},{8,7},{9,8},{10,9},{11,1... | collective-permute-start | bytes 9224 | tf_op jit(solution)/shard_map/ppermute | solution.py:24
  323.8 9.6 %collective-permute-start.31 = (f32[6,1,128]{2,1,0:T(1,128)S(1)}, f32[6,1,128]{2,1,0:T(1,128)S(1)}, u32[]{:S(2)}, u32[]{:S(2)}) collective-permute-start(f32[6,1,128]{2,1,0:T(1,128)S(1)} %get-tuple-element.95), channel_id=1, source_target_pairs={{0,1},{1,2},{2,3},{3,4},{4,5},{5,6},{6,7},{7,8},{8,9},{9,10},{10,1... | collective-permute-start | bytes 9224 | tf_op jit(solution)/shard_map/ppermute | solution.py:23
  327.7 18.3 %collective-permute-start.32 = (f32[1,8,64]{2,1,0:T(8,128)S(1)}, f32[1,8,64]{2,1,0:T(8,128)S(1)}, u32[]{:S(2)}, u32[]{:S(2)}) collective-permute-start(f32[1,8,64]{2,1,0:T(8,128)S(1)} %get-tuple-element.146), channel_id=1, source_target_pairs={{16,0},{32,16},{48,32},{64,48},{80,64},{96,80},{112,96},{128,112},... | collective-permute-start | bytes 6152 | tf_op jit(solution)/shard_map/ppermute | solution.py:24
  329.7 16.4 %collective-permute-start.34 = (f32[1,8,64]{2,1,0:T(8,128)S(1)}, f32[1,8,64]{2,1,0:T(8,128)S(1)}, u32[]{:S(2)}, u32[]{:S(2)}) collective-permute-start(f32[1,8,64]{2,1,0:T(8,128)S(1)} %get-tuple-element.145), channel_id=1, source_target_pairs={{0,16},{16,32},{32,48},{48,64},{64,80},{80,96},{96,112},{112,128},... | collective-permute-start | bytes 6152 | tf_op jit(solution)/shard_map/ppermute | solution.py:23
  338.8 13.1 %collective-permute-start.33 = (f32[1,8,64]{2,1,0:T(8,128)S(1)}, f32[1,8,64]{2,1,0:T(8,128)S(1)}, u32[]{:S(2)}, u32[]{:S(2)}) collective-permute-start(f32[1,8,64]{2,1,0:T(8,128)S(1)} %get-tuple-element.149), channel_id=1, source_target_pairs={{16,0},{32,16},{48,32},{64,48},{80,64},{96,80},{112,96},{128,112},... | collective-permute-start | bytes 6152 | tf_op jit(solution)/shard_map/ppermute | solution.py:24
  344.1 7.8 %collective-permute-start.35 = (f32[1,8,64]{2,1,0:T(8,128)S(1)}, f32[1,8,64]{2,1,0:T(8,128)S(1)}, u32[]{:S(2)}, u32[]{:S(2)}) collective-permute-start(f32[1,8,64]{2,1,0:T(8,128)S(1)} %get-tuple-element.148), channel_id=1, source_target_pairs={{0,16},{16,32},{32,48},{48,64},{64,80},{80,96},{96,112},{112,128},... | collective-permute-start | bytes 6152 | tf_op jit(solution)/shard_map/ppermute | solution.py:23
  346.1 12.2 %collective-permute-start.36 = (f32[4,1,64]{2,1,0:T(1,128)S(1)}, f32[4,1,64]{2,1,0:T(1,128)S(1)}, u32[]{:S(2)}, u32[]{:S(2)}) collective-permute-start(f32[4,1,64]{2,1,0:T(1,128)S(1)} %get-tuple-element.132), channel_id=1, source_target_pairs={{1,0},{2,1},{3,2},{4,3},{5,4},{6,5},{7,6},{8,7},{9,8},{10,9},{11,1... | collective-permute-start | bytes 3080 | tf_op jit(solution)/shard_map/ppermute | solution.py:24
  349.2 9.0 %collective-permute-start.38 = (f32[4,1,64]{2,1,0:T(1,128)S(1)}, f32[4,1,64]{2,1,0:T(1,128)S(1)}, u32[]{:S(2)}, u32[]{:S(2)}) collective-permute-start(f32[4,1,64]{2,1,0:T(1,128)S(1)} %get-tuple-element.131), channel_id=1, source_target_pairs={{0,1},{1,2},{2,3},{3,4},{4,5},{5,6},{6,7},{7,8},{8,9},{9,10},{10,1... | collective-permute-start | bytes 3080 | tf_op jit(solution)/shard_map/ppermute | solution.py:23
  367.0 7.0 collective-permute-start.41
  382.8 11.5 %collective-permute-start.44 = (f32[1,8,64]{2,1,0:T(8,128)S(1)}, f32[1,8,64]{2,1,0:T(8,128)S(1)}, u32[]{:S(2)}, u32[]{:S(2)}) collective-permute-start(f32[1,8,64]{2,1,0:T(8,128)S(1)} %get-tuple-element.142), channel_id=1, source_target_pairs={{16,0},{32,16},{48,32},{64,48},{80,64},{96,80},{112,96},{128,112},... | collective-permute-start | bytes 6152 | tf_op jit(solution)/shard_map/ppermute | solution.py:24
  384.8 9.6 %collective-permute-start.45 = (f32[1,8,64]{2,1,0:T(8,128)S(1)}, f32[1,8,64]{2,1,0:T(8,128)S(1)}, u32[]{:S(2)}, u32[]{:S(2)}) collective-permute-start(f32[1,8,64]{2,1,0:T(8,128)S(1)} %get-tuple-element.141), channel_id=1, source_target_pairs={{0,16},{16,32},{32,48},{48,64},{64,80},{80,96},{96,112},{112,128},... | collective-permute-start | bytes 6152 | tf_op jit(solution)/shard_map/ppermute | solution.py:23
  387.2 13.1 %collective-permute-start.48 = (f32[1,4,32]{2,1,0:T(4,128)S(1)}, f32[1,4,32]{2,1,0:T(4,128)S(1)}, u32[]{:S(2)}, u32[]{:S(2)}) collective-permute-start(f32[1,4,32]{2,1,0:T(4,128)S(1)} %get-tuple-element.166), channel_id=1, source_target_pairs={{16,0},{32,16},{48,32},{64,48},{80,64},{96,80},{112,96},{128,112},... | collective-permute-start | bytes 1544 | tf_op jit(solution)/shard_map/ppermute | solution.py:24
  392.5 7.8 %collective-permute-start.50 = (f32[1,4,32]{2,1,0:T(4,128)S(1)}, f32[1,4,32]{2,1,0:T(4,128)S(1)}, u32[]{:S(2)}, u32[]{:S(2)}) collective-permute-start(f32[1,4,32]{2,1,0:T(4,128)S(1)} %get-tuple-element.166), channel_id=1, source_target_pairs={{0,16},{16,32},{32,48},{48,64},{64,80},{80,96},{96,112},{112,128},... | collective-permute-start | bytes 1544 | tf_op jit(solution)/shard_map/ppermute | solution.py:23
  394.4 13.0 %collective-permute-start.46 = (f32[4,1,64]{2,1,0:T(1,128)S(1)}, f32[4,1,64]{2,1,0:T(1,128)S(1)}, u32[]{:S(2)}, u32[]{:S(2)}) collective-permute-start(f32[4,1,64]{2,1,0:T(1,128)S(1)} %get-tuple-element.128), channel_id=1, source_target_pairs={{1,0},{2,1},{3,2},{4,3},{5,4},{6,5},{7,6},{8,7},{9,8},{10,9},{11,1... | collective-permute-start | bytes 3080 | tf_op jit(solution)/shard_map/ppermute | solution.py:24
  396.4 11.1 %collective-permute-start.47 = (f32[4,1,64]{2,1,0:T(1,128)S(1)}, f32[4,1,64]{2,1,0:T(1,128)S(1)}, u32[]{:S(2)}, u32[]{:S(2)}) collective-permute-start(f32[4,1,64]{2,1,0:T(1,128)S(1)} %get-tuple-element.127), channel_id=1, source_target_pairs={{0,1},{1,2},{2,3},{3,4},{4,5},{5,6},{6,7},{7,8},{8,9},{9,10},{10,1... | collective-permute-start | bytes 3080 | tf_op jit(solution)/shard_map/ppermute | solution.py:23
  400.3 14.1 %collective-permute-start.52 = (f32[3,1,32]{2,1,0:T(1,128)S(1)}, f32[3,1,32]{2,1,0:T(1,128)S(1)}, u32[]{:S(2)}, u32[]{:S(2)}) collective-permute-start(f32[3,1,32]{2,1,0:T(1,128)S(1)} %get-tuple-element.163), channel_id=1, source_target_pairs={{1,0},{2,1},{3,2},{4,3},{5,4},{6,5},{7,6},{8,7},{9,8},{10,9},{11,1... | collective-permute-start | bytes 1160 | tf_op jit(solution)/shard_map/ppermute | solution.py:24
  403.5 11.0 %collective-permute-start.54 = (f32[3,1,32]{2,1,0:T(1,128)S(1)}, f32[3,1,32]{2,1,0:T(1,128)S(1)}, u32[]{:S(2)}, u32[]{:S(2)}) collective-permute-start(f32[3,1,32]{2,1,0:T(1,128)S(1)} %get-tuple-element.162), channel_id=1, source_target_pairs={{0,1},{1,2},{2,3},{3,4},{4,5},{5,6},{6,7},{7,8},{8,9},{9,10},{10,1... | collective-permute-start | bytes 1160 | tf_op jit(solution)/shard_map/ppermute | solution.py:23
  412.5 7.0 collective-permute-start.51
  432.9 7.0 collective-permute-start.57
  450.7 7.0 collective-permute-start.61
  468.4 7.0 collective-permute-start.65
  539.4 7.0 collective-permute-start.81
  557.2 7.0 collective-permute-start.85
  575.1 7.0 collective-permute-start.89
  593.3 7.1 %collective-permute-start.93 = (f32[1,16,128]{2,1,0:T(8,128)S(1)}, f32[1,16,128]{2,1,0:T(8,128)S(1)}, u32[]{:S(2)}, u32[]{:S(2)}) collective-permute-start(f32[1,16,128]{2,1,0:T(8,128)S(1)} %get-tuple-element.107), channel_id=1, source_target_pairs={{0,16},{16,32},{32,48},{48,64},{64,80},{80,96},{96,112},{112,128},... | collective-permute-start | bytes 24584 | tf_op jit(solution)/shard_map/ppermute | solution.py:23
  611.1 7.1 %collective-permute-start.97 = (f32[1,16,128]{2,1,0:T(8,128)S(1)}, f32[1,16,128]{2,1,0:T(8,128)S(1)}, u32[]{:S(2)}, u32[]{:S(2)}) collective-permute-start(f32[1,16,128]{2,1,0:T(8,128)S(1)} %get-tuple-element.105), channel_id=1, source_target_pairs={{0,16},{16,32},{32,48},{48,64},{64,80},{80,96},{96,112},{112,128},... | collective-permute-start | bytes 24584 | tf_op jit(solution)/shard_map/ppermute | solution.py:23
  629.0 7.1 %collective-permute-start.101 = (f32[1,16,128]{2,1,0:T(8,128)S(1)}, f32[1,16,128]{2,1,0:T(8,128)S(1)}, u32[]{:S(2)}, u32[]{:S(2)}) collective-permute-start(f32[1,16,128]{2,1,0:T(8,128)S(1)} %get-tuple-element.103), channel_id=1, source_target_pairs={{0,16},{16,32},{32,48},{48,64},{64,80},{80,96},{96,112},{112,128},... | collective-permute-start | bytes 24584 | tf_op jit(solution)/shard_map/ppermute | solution.py:23
  649.5 7.3 %collective-permute-start.105 = (f32[1,32,256]{2,1,0:T(8,128)S(1)}, f32[1,32,256]{2,1,0:T(8,128)S(1)}, u32[]{:S(2)}, u32[]{:S(2)}) collective-permute-start(f32[1,32,256]{2,1,0:T(8,128)S(1)} %get-tuple-element.77), channel_id=1, source_target_pairs={{0,16},{16,32},{32,48},{48,64},{64,80},{80,96},{96,112},{112,128},... | collective-permute-start | bytes 98312 | tf_op jit(solution)/shard_map/ppermute | solution.py:23
  668.2 7.3 %collective-permute-start.109 = (f32[1,32,256]{2,1,0:T(8,128)S(1)}, f32[1,32,256]{2,1,0:T(8,128)S(1)}, u32[]{:S(2)}, u32[]{:S(2)}) collective-permute-start(f32[1,32,256]{2,1,0:T(8,128)S(1)} %get-tuple-element.75), channel_id=1, source_target_pairs={{0,16},{16,32},{32,48},{48,64},{64,80},{80,96},{96,112},{112,128},... | collective-permute-start | bytes 98312 | tf_op jit(solution)/shard_map/ppermute | solution.py:23
  686.9 7.3 %collective-permute-start.113 = (f32[1,32,256]{2,1,0:T(8,128)S(1)}, f32[1,32,256]{2,1,0:T(8,128)S(1)}, u32[]{:S(2)}, u32[]{:S(2)}) collective-permute-start(f32[1,32,256]{2,1,0:T(8,128)S(1)} %get-tuple-element.73), channel_id=1, source_target_pairs={{0,16},{16,32},{32,48},{48,64},{64,80},{80,96},{96,112},{112,128},... | collective-permute-start | bytes 98312 | tf_op jit(solution)/shard_map/ppermute | solution.py:23
  (71 other events, 609.0 us)
where the time goes:
time: 708 us; the launch traced here: 704 us
  starting transfers between devices  317 us (45%)
  waiting for transfers between devices  167 us (24%)
  blocking collectives  101 us (14%)
  local copies, waits for them, and re-layouts  67.5 us (10%)
  other arithmetic  43.1 us (6%)
  between operations  8.48 us (1%)
    ppermute x58, waiting for transfers between devices, with_halo(): before = lax.ppermute(last, axis, up)  167 us
    ppermute x58, starting transfers between devices, with_halo(): before = lax.ppermute(last, axis, up)  167 us
    ppermute x58, starting transfers between devices, with_halo(): after = lax.ppermute(initial, axis, down)  150 us
    pmax x1, blocking collectives, local(): maxima = lax.pmax(maxima, ('gx', 'gy'))  101 us
    reshape x4, local copies, waits for them, and re-layouts, restrict(): values.reshape(first // 2, 2, second // 2, 2, third // 2, 2)  58.5 us
    reduce_sum x10, other arithmetic, restrict(): values.reshape(first // 2, 2, second // 2, 2, third // 2, 2)  23.6 us
  transfers between devices with their start and end apart: 116, of which 43 were waited for; matrix products, arithmetic and copies ran while one was open for 14% of the time, Pallas kernels for 0%

commit v1 on v0

v1 whole, which is shorter than its diff:
```python
import jax
import jax.numpy as jnp
from jax import lax
from jax.sharding import PartitionSpec as P

LEVELS = 4
PRE_STEPS = 3
POST_STEPS = 3
COARSE_STEPS = 8


HELM_SHIFT = 0.05
LOW_FRACTION = 0.1


def exchange(x):
    halos = []
    for axis, dim in (("gx", 0), ("gy", 1)):
        peers = lax.axis_size(axis)
        length = x.shape[dim]
        up = [(i, i + 1) for i in range(peers - 1)]
        down = [(i + 1, i) for i in range(peers - 1)]
        last = lax.slice_in_dim(x, length - 1, length, axis=dim)
        first = lax.slice_in_dim(x, 0, 1, axis=dim)
        before = lax.ppermute(last, axis, up)
        after = lax.ppermute(first, axis, down)
        halos.append((before, after))
    return halos


def shifted(x, halos):
    (lo0, hi0), (lo1, hi1) = halos
    zero2 = jnp.zeros_like(x[:, :, :1])
    return [
        jnp.concatenate([x[1:], hi0], axis=0),
        jnp.concatenate([lo0, x[:-1]], axis=0),
        jnp.concatenate([x[:, 1:], hi1], axis=1),
        jnp.concatenate([lo1, x[:, :-1]], axis=1),
        jnp.concatenate([x[:, :, 1:], zero2], axis=2),
        jnp.concatenate([zero2, x[:, :, :-1]], axis=2),
    ]


def coef_sums(beta_level):
    near = shifted(beta_level, exchange(beta_level))
    return [beta_level + b for b in near]


def pool_matrix(n, dtype):
    rows = jnp.arange(n)[:, None] // 2
    cols = jnp.arange(n // 2)[None, :]
    return (rows == cols).astype(dtype)


def restrict(values):
    first, second, third = values.shape
    pairs = values.reshape(first // 2, 2, second, third)
    summed = pairs[:, 0] + pairs[:, 1]
    pool1 = pool_matrix(second, values.dtype)
    pool2 = pool_matrix(third, values.dtype)
    summed = jnp.einsum("ajk,jb->abk", summed, pool1, precision=lax.Precision.HIGHEST)
    summed = jnp.einsum("abk,kc->abc", summed, pool2, precision=lax.Precision.HIGHEST)
    return summed * 0.125


def prolong(values):
    return jnp.repeat(jnp.repeat(jnp.repeat(values, 2, 0), 2, 1), 2, 2)


def apply_op(field, sums, alpha_level, inv_spacing):
    summed = jnp.zeros_like(field)
    for near_u, near_b in zip(shifted(field, exchange(field)), sums):
        summed = summed + near_b * (field - near_u)
    return HELM_SHIFT * alpha_level * field + 0.5 * inv_spacing * summed


def smooth(field, source, alpha_level, sums, inv_spacing, upper, sweeps, start_zero):
    lower = LOW_FRACTION * upper
    middle = 0.5 * (upper + lower)
    half_width = 0.5 * (upper - lower)
    scaled = middle / half_width
    factor = 1.0 / scaled
    if start_zero:
        residual = source
    else:
        residual = source - apply_op(field, sums, alpha_level, inv_spacing)
    direction = residual / middle
    field = direction if start_zero else field + direction
    for k in range(1, sweeps):
        residual = source - apply_op(field, sums, alpha_level, inv_spacing)
        factor_new = 1.0 / (2.0 * scaled - factor)
        direction = factor_new * factor * direction + 2.0 * factor_new / half_width * residual
        field = field + direction
        factor = factor_new
    return field


def all_max(values):
    for axis in ("gx", "gy"):
        peers = lax.axis_size(axis)
        if peers & (peers - 1):
            values = lax.pmax(values, axis)
            continue
        step = 1
        while step < peers:
            pairs = [(i, i ^ step) for i in range(peers)]
            values = jnp.maximum(values, lax.ppermute(values, axis, pairs))
            step *= 2
    return values


def local(rhs_field, alpha_coef, beta_coef):
    alphas = [alpha_coef]
    betas = [beta_coef]
    for level_idx in range(1, LEVELS):
        alphas.append(restrict(alphas[-1]))
        betas.append(restrict(betas[-1]))
    maxima = jnp.stack([jnp.stack([jnp.max(alphas[i]), jnp.max(betas[i])]) for i in range(LEVELS)])
    maxima = all_max(maxima)
    uppers = [HELM_SHIFT * maxima[i, 0] + 12.0 * maxima[i, 1] / 4.0**i for i in range(LEVELS)]
    sums = [coef_sums(betas[i]) for i in range(LEVELS)]
    sources = [rhs_field]
    fields = []
    for level_idx in range(LEVELS - 1):
        inv_spacing = 1.0 / 4.0**level_idx
        smoothed = smooth(
            jnp.zeros_like(sources[level_idx]),
            sources[level_idx],
            alphas[level_idx],
            sums[level_idx],
            inv_spacing,
            uppers[level_idx],
            PRE_STEPS,
            True,
        )
        residual = sources[level_idx] - apply_op(
            smoothed, sums[level_idx], alphas[level_idx], inv_spacing
        )
        sources.append(restrict(residual))
        fields.append(smoothed)
    last = LEVELS - 1
    coarse = smooth(
        jnp.zeros_like(sources[last]),
        sources[last],
        alphas[last],
        sums[last],
        1.0 / 4.0**last,
        uppers[last],
        COARSE_STEPS,
        True,
    )
    for level_idx in range(LEVELS - 2, -1, -1):
        smoothed = fields[level_idx] + prolong(coarse)
        coarse = smooth(
            smoothed,
            sources[level_idx],
            alphas[level_idx],
            sums[level_idx],
            1.0 / 4.0**level_idx,
            uppers[level_idx],
            POST_STEPS,
            False,
        )
    return coarse


def solution(mesh):
    placed = (P("gx", "gy", None), P("gx", "gy", None), P("gx", "gy", None))
    return jax.shard_map(
        local, mesh=mesh, in_specs=placed, out_specs=P("gx", "gy", None), check_vma=False
    )
```

time: 708 us -> 567 us (0.80)
  the two profiles are of different devices: /device:TPU:136 before, /device:TPU:143 now
where the time goes in v1:
time: 567 us; the launch traced here: 563 us
  starting transfers between devices  421 us (74%)
  waiting for transfers between devices  84.7 us (15%)
  local copies, waits for them, and re-layouts  24.4 us (4%)
  other arithmetic  16.1 us (3%)
  between operations  9.26 us (2%)
  matrix products  7.17 us (1%)
    ppermute x58, starting transfers between devices, exchange(): before = lax.ppermute(last, axis, up)  241 us
    ppermute x58, starting transfers between devices, exchange(): after = lax.ppermute(first, axis, down)  148 us
    ppermute x58, waiting for transfers between devices, exchange(): after = lax.ppermute(first, axis, down)  47 us
    ppermute x9, starting transfers between devices, all_max(): values = jnp.maximum(values, lax.ppermute(values, axis, pairs))  31.8 us
    ppermute x9, waiting for transfers between devices, all_max(): values = jnp.maximum(values, lax.ppermute(values, axis, pairs))  22.6 us
    ppermute x58, waiting for transfers between devices, exchange(): before = lax.ppermute(last, axis, up)  15.1 us
  transfers between devices with their start and end apart: 125, of which 29 were waited for; matrix products, arithmetic and copies ran while one was open for 3% of the time, Pallas kernels for 0%

profile of v1, /device:TPU:143, one launch (start us, length us, event | category | flops | bytes accessed | tf_op | source)
XLA Modules:
  0.0 562.8 jit_solution(7834558358645116314)
XLA Ops:
  62.6 4.7 collective-permute-start.6
  70.1 6.3 %collective-permute-done.7 = f32[4,2]{1,0:T(4,128)S(1)} collective-permute-done((f32[4,2]{1,0:T(4,128)S(1)}, f32[4,2]{1,0:T(4,128)S(1)}, u32[]{:S(2)}, u32[]{:S(2)}) %collective-permute-start.7) | collective-permute-done | bytes 64 | tf_op jit(solution)/shard_map/ppermute | solution.py:107
  76.4 10.2 %collective-permute-start.8 = (f32[4,2]{1,0:T(4,128)S(1)}, f32[4,2]{1,0:T(4,128)S(1)}, u32[]{:S(2)}, u32[]{:S(2)}) collective-permute-start(f32[4,2]{1,0:T(4,128)S(1)} %max.34), channel_id=1, source_target_pairs={{0,8},{1,9},{2,10},{3,11},{4,12},{5,13},{6,14},{7,15},{8,0},{9,1},... | collective-permute-start | bytes 104 | tf_op jit(solution)/shard_map/ppermute | solution.py:107
  93.2 3.6 collective-permute-start.16
  99.8 14.9 %collective-permute-start.12 = (f32[1,32,256]{2,1,0:T(8,128)S(1)}, f32[1,32,256]{2,1,0:T(8,128)S(1)}, u32[]{:S(2)}, u32[]{:S(2)}) collective-permute-start(f32[1,32,256]{2,1,0:T(8,128)S(1)} %get-tuple-element.122), channel_id=1, source_target_pairs={{0,16},{16,32},{32,48},{48,64},{64,80},{80,96},{96,112},{112,128},... | collective-permute-start | bytes 98312 | tf_op jit(solution)/shard_map/ppermute | solution.py:25
  129.4 6.0 %collective-permute-start.18 = (f32[1,32,256]{2,1,0:T(8,128)S(1)}, f32[1,32,256]{2,1,0:T(8,128)S(1)}, u32[]{:S(2)}, u32[]{:S(2)}) collective-permute-start(f32[1,32,256]{2,1,0:T(8,128)S(1)} %get-tuple-element.105), channel_id=1, source_target_pairs={{0,16},{16,32},{32,48},{48,64},{64,80},{80,96},{96,112},{112,128},... | collective-permute-start | bytes 98312 | tf_op jit(solution)/shard_map/ppermute | solution.py:25
  135.4 4.1 collective-permute-start.19
  141.5 3.6 collective-permute-done.20
  147.8 5.8 %collective-permute-start.22 = (f32[1,32,256]{2,1,0:T(8,128)S(1)}, f32[1,32,256]{2,1,0:T(8,128)S(1)}, u32[]{:S(2)}, u32[]{:S(2)}) collective-permute-start(f32[1,32,256]{2,1,0:T(8,128)S(1)} %get-tuple-element.95), channel_id=1, source_target_pairs={{0,16},{16,32},{32,48},{48,64},{64,80},{80,96},{96,112},{112,128},... | collective-permute-start | bytes 98312 | tf_op jit(solution)/shard_map/ppermute | solution.py:25
  171.2 4.1 collective-permute-start.30
  175.3 6.3 %collective-permute-start.28 = (f32[1,16,128]{2,1,0:T(8,128)S(1)}, f32[1,16,128]{2,1,0:T(8,128)S(1)}, u32[]{:S(2)}, u32[]{:S(2)}) collective-permute-start(f32[1,16,128]{2,1,0:T(8,128)S(1)} %get-tuple-element.192), channel_id=1, source_target_pairs={{0,16},{16,32},{32,48},{48,64},{64,80},{80,96},{96,112},{112,128},... | collective-permute-start | bytes 24584 | tf_op jit(solution)/shard_map/ppermute | solution.py:25
  190.9 5.8 %collective-permute-start.34 = (f32[1,16,128]{2,1,0:T(8,128)S(1)}, f32[1,16,128]{2,1,0:T(8,128)S(1)}, u32[]{:S(2)}, u32[]{:S(2)}) collective-permute-start(f32[1,16,128]{2,1,0:T(8,128)S(1)} %get-tuple-element.175), channel_id=1, source_target_pairs={{0,16},{16,32},{32,48},{48,64},{64,80},{80,96},{96,112},{112,128},... | collective-permute-start | bytes 24584 | tf_op jit(solution)/shard_map/ppermute | solution.py:25
  206.7 5.8 %collective-permute-start.38 = (f32[1,16,128]{2,1,0:T(8,128)S(1)}, f32[1,16,128]{2,1,0:T(8,128)S(1)}, u32[]{:S(2)}, u32[]{:S(2)}) collective-permute-start(f32[1,16,128]{2,1,0:T(8,128)S(1)} %get-tuple-element.165), channel_id=1, source_target_pairs={{0,16},{16,32},{32,48},{48,64},{64,80},{80,96},{96,112},{112,128},... | collective-permute-start | bytes 24584 | tf_op jit(solution)/shard_map/ppermute | solution.py:25
  230.2 4.1 collective-permute-start.46
  234.3 6.3 %collective-permute-start.44 = (f32[1,8,64]{2,1,0:T(8,128)S(1)}, f32[1,8,64]{2,1,0:T(8,128)S(1)}, u32[]{:S(2)}, u32[]{:S(2)}) collective-permute-start(f32[1,8,64]{2,1,0:T(8,128)S(1)} %get-tuple-element.249), channel_id=1, source_target_pairs={{0,16},{16,32},{32,48},{48,64},{64,80},{80,96},{96,112},{112,128},... | collective-permute-start | bytes 6152 | tf_op jit(solution)/shard_map/ppermute | solution.py:25
  250.4 5.8 %collective-permute-start.50 = (f32[1,8,64]{2,1,0:T(8,128)S(1)}, f32[1,8,64]{2,1,0:T(8,128)S(1)}, u32[]{:S(2)}, u32[]{:S(2)}) collective-permute-start(f32[1,8,64]{2,1,0:T(8,128)S(1)} %get-tuple-element.239), channel_id=1, source_target_pairs={{0,16},{16,32},{32,48},{48,64},{64,80},{80,96},{96,112},{112,128},... | collective-permute-start | bytes 6152 | tf_op jit(solution)/shard_map/ppermute | solution.py:25
  265.7 5.8 %collective-permute-start.54 = (f32[1,8,64]{2,1,0:T(8,128)S(1)}, f32[1,8,64]{2,1,0:T(8,128)S(1)}, u32[]{:S(2)}, u32[]{:S(2)}) collective-permute-start(f32[1,8,64]{2,1,0:T(8,128)S(1)} %get-tuple-element.231), channel_id=1, source_target_pairs={{0,16},{16,32},{32,48},{48,64},{64,80},{80,96},{96,112},{112,128},... | collective-permute-start | bytes 6152 | tf_op jit(solution)/shard_map/ppermute | solution.py:25
  294.0 4.1 collective-permute-start.62
  300.6 6.7 %collective-permute-start.66 = (f32[1,4,32]{2,1,0:T(4,128)S(1)}, f32[1,4,32]{2,1,0:T(4,128)S(1)}, u32[]{:S(2)}, u32[]{:S(2)}) collective-permute-start(f32[1,4,32]{2,1,0:T(4,128)S(1)} %get-tuple-element.27), channel_id=1, source_target_pairs={{0,16},{16,32},{32,48},{48,64},{64,80},{80,96},{96,112},{112,128},... | collective-permute-start | bytes 1544 | tf_op jit(solution)/shard_map/ppermute | solution.py:25
  309.2 4.9 collective-permute-start.68
  318.9 6.9 %collective-permute-start.70 = (f32[1,4,32]{2,1,0:T(4,128)S(1)}, f32[1,4,32]{2,1,0:T(4,128)S(1)}, u32[]{:S(2)}, u32[]{:S(2)}) collective-permute-start(f32[1,4,32]{2,1,0:T(4,128)S(1)} %get-tuple-element.25), channel_id=1, source_target_pairs={{0,16},{16,32},{32,48},{48,64},{64,80},{80,96},{96,112},{112,128},... | collective-permute-start | bytes 1544 | tf_op jit(solution)/shard_map/ppermute | solution.py:25
  327.7 4.5 collective-permute-start.72
  337.0 6.9 %collective-permute-start.74 = (f32[1,4,32]{2,1,0:T(4,128)S(1)}, f32[1,4,32]{2,1,0:T(4,128)S(1)}, u32[]{:S(2)}, u32[]{:S(2)}) collective-permute-start(f32[1,4,32]{2,1,0:T(4,128)S(1)} %get-tuple-element.23), channel_id=1, source_target_pairs={{0,16},{16,32},{32,48},{48,64},{64,80},{80,96},{96,112},{112,128},... | collective-permute-start | bytes 1544 | tf_op jit(solution)/shard_map/ppermute | solution.py:25
  345.8 3.6 collective-permute-start.76
  353.9 7.2 %collective-permute-start.78 = (f32[1,4,32]{2,1,0:T(4,128)S(1)}, f32[1,4,32]{2,1,0:T(4,128)S(1)}, u32[]{:S(2)}, u32[]{:S(2)}) collective-permute-start(f32[1,4,32]{2,1,0:T(4,128)S(1)} %get-tuple-element.21), channel_id=1, source_target_pairs={{0,16},{16,32},{32,48},{48,64},{64,80},{80,96},{96,112},{112,128},... | collective-permute-start | bytes 1544 | tf_op jit(solution)/shard_map/ppermute | solution.py:25
  365.9 3.6 collective-permute-start.79
  370.4 7.1 %collective-permute-start.82 = (f32[1,4,32]{2,1,0:T(4,128)S(1)}, f32[1,4,32]{2,1,0:T(4,128)S(1)}, u32[]{:S(2)}, u32[]{:S(2)}) collective-permute-start(f32[1,4,32]{2,1,0:T(4,128)S(1)} %get-tuple-element.19), channel_id=1, source_target_pairs={{0,16},{16,32},{32,48},{48,64},{64,80},{80,96},{96,112},{112,128},... | collective-permute-start | bytes 1544 | tf_op jit(solution)/shard_map/ppermute | solution.py:25
  382.3 3.9 collective-permute-start.83
  387.1 6.9 %collective-permute-start.86 = (f32[1,4,32]{2,1,0:T(4,128)S(1)}, f32[1,4,32]{2,1,0:T(4,128)S(1)}, u32[]{:S(2)}, u32[]{:S(2)}) collective-permute-start(f32[1,4,32]{2,1,0:T(4,128)S(1)} %get-tuple-element.17), channel_id=1, source_target_pairs={{0,16},{16,32},{32,48},{48,64},{64,80},{80,96},{96,112},{112,128},... | collective-permute-start | bytes 1544 | tf_op jit(solution)/shard_map/ppermute | solution.py:25
  398.7 3.9 collective-permute-start.87
  406.6 3.8 collective-permute-start.91
  410.5 7.2 %collective-permute-start.90 = (f32[1,8,64]{2,1,0:T(8,128)S(1)}, f32[1,8,64]{2,1,0:T(8,128)S(1)}, u32[]{:S(2)}, u32[]{:S(2)}) collective-permute-start(f32[1,8,64]{2,1,0:T(8,128)S(1)} %get-tuple-element.217), channel_id=1, source_target_pairs={{0,16},{16,32},{32,48},{48,64},{64,80},{80,96},{96,112},{112,128},... | collective-permute-start | bytes 6152 | tf_op jit(solution)/shard_map/ppermute | solution.py:25
  419.6 5.1 collective-permute-done.89
  426.9 4.5 collective-permute-start.95
  435.8 5.1 collective-permute-done.93
  442.9 5.8 %collective-permute-start.98 = (f32[1,8,64]{2,1,0:T(8,128)S(1)}, f32[1,8,64]{2,1,0:T(8,128)S(1)}, u32[]{:S(2)}, u32[]{:S(2)}) collective-permute-start(f32[1,8,64]{2,1,0:T(8,128)S(1)} %get-tuple-element.207), channel_id=1, source_target_pairs={{0,16},{16,32},{32,48},{48,64},{64,80},{80,96},{96,112},{112,128},... | collective-permute-start | bytes 6152 | tf_op jit(solution)/shard_map/ppermute | solution.py:25
  459.1 4.6 collective-permute-start.103
  463.7 3.9 collective-permute-start.102
  469.6 5.1 collective-permute-done.101
  476.8 4.6 collective-permute-start.107
  485.9 5.1 collective-permute-done.105
  493.1 5.8 %collective-permute-start.110 = (f32[1,16,128]{2,1,0:T(8,128)S(1)}, f32[1,16,128]{2,1,0:T(8,128)S(1)}, u32[]{:S(2)}, u32[]{:S(2)}) collective-permute-start(f32[1,16,128]{2,1,0:T(8,128)S(1)} %get-tuple-element.135), channel_id=1, source_target_pairs={{0,16},{16,32},{32,48},{48,64},{64,80},{80,96},{96,112},{112,128},... | collective-permute-start | bytes 24584 | tf_op jit(solution)/shard_map/ppermute | solution.py:25
  513.2 4.3 collective-permute-start.115
  517.5 3.6 collective-permute-start.114
  523.2 5.3 collective-permute-done.113
  531.1 4.6 collective-permute-start.119
  540.2 5.3 collective-permute-done.117
  548.2 5.8 %collective-permute-start.122 = (f32[1,32,256]{2,1,0:T(8,128)S(1)}, f32[1,32,256]{2,1,0:T(8,128)S(1)}, u32[]{:S(2)}, u32[]{:S(2)}) collective-permute-start(f32[1,32,256]{2,1,0:T(8,128)S(1)} %get-tuple-element.65), channel_id=1, source_target_pairs={{0,16},{16,32},{32,48},{48,64},{64,80},{80,96},{96,112},{112,128},... | collective-permute-start | bytes 98312 | tf_op jit(solution)/shard_map/ppermute | solution.py:25
  (513 shorter events, 291.0 us)
Async XLA Ops:
  14.4 23.2 %collective-permute-start = (f32[4,2]{1,0:T(4,128)S(1)}, f32[4,2]{1,0:T(4,128)S(1)}, u32[]{:S(2)}, u32[]{:S(2)}) collective-permute-start(f32[4,2]{1,0:T(4,128)S(1)} %pad_maximum_fusion), channel_id=1, source_target_pairs={{0,16},{16,0},{32,48},{48,32},{64,80},{80,64},{96,112},{112,96},{1... | collective-permute-start | bytes 104 | tf_op jit(solution)/shard_map/ppermute | solution.py:107
  17.1 79.8 %collective-permute-start.15 = (f32[8,1,256]{2,0,1:T(8,128)S(1)}, f32[8,1,256]{2,0,1:T(8,128)S(1)}, u32[]{:S(2)}, u32[]{:S(2)}) collective-permute-start(f32[8,1,256]{2,0,1:T(8,128)S(1)} %copy.327), channel_id=1, source_target_pairs={{0,1},{1,2},{2,3},{3,4},{4,5},{5,6},{6,7},{7,8},{8,9},{9,10},{10,1... | collective-permute-start | bytes 24584 | tf_op jit(solution)/shard_map/ppermute | solution.py:25
  20.6 79.1 %collective-permute-start.13 = (f32[8,1,256]{2,0,1:T(8,128)S(1)}, f32[8,1,256]{2,0,1:T(8,128)S(1)}, u32[]{:S(2)}, u32[]{:S(2)}) collective-permute-start(f32[8,1,256]{2,0,1:T(8,128)S(1)} %copy.326), channel_id=1, source_target_pairs={{1,0},{2,1},{3,2},{4,3},{5,4},{6,5},{7,6},{8,7},{9,8},{10,9},{11,1... | collective-permute-start | bytes 24584 | tf_op jit(solution)/shard_map/ppermute | solution.py:26
  23.6 101.6 %collective-permute-start.11 = (f32[1,32,256]{2,1,0:T(8,128)S(1)}, f32[1,32,256]{2,1,0:T(8,128)S(1)}, u32[]{:S(2)}, u32[]{:S(2)}) collective-permute-start(f32[1,32,256]{2,1,0:T(8,128)S(1)} %get-tuple-element.112), channel_id=1, source_target_pairs={{0,16},{16,32},{32,48},{48,64},{64,80},{80,96},{96,112},{112,128},... | collective-permute-start | bytes 98312 | tf_op jit(solution)/shard_map/ppermute | solution.py:25
  27.2 98.0 %collective-permute-start.9 = (f32[1,32,256]{2,1,0:T(8,128)S(1)}, f32[1,32,256]{2,1,0:T(8,128)S(1)}, u32[]{:S(2)}, u32[]{:S(2)}) collective-permute-start(f32[1,32,256]{2,1,0:T(8,128)S(1)} %get-tuple-element.111), channel_id=1, source_target_pairs={{16,0},{32,16},{48,32},{64,48},{80,64},{96,80},{112,96},{128,112},... | collective-permute-start | bytes 98312 | tf_op jit(solution)/shard_map/ppermute | solution.py:26
  93.2 21.5 %collective-permute-start.16 = (f32[8,1,256]{2,0,1:T(8,128)S(1)}, f32[8,1,256]{2,0,1:T(8,128)S(1)}, u32[]{:S(2)}, u32[]{:S(2)}) collective-permute-start(f32[8,1,256]{2,0,1:T(8,128)S(1)} %copy.285), channel_id=1, source_target_pairs={{0,1},{1,2},{2,3},{3,4},{4,5},{5,6},{6,7},{7,8},{8,9},{9,10},{10,1... | collective-permute-start | bytes 24584 | tf_op jit(solution)/shard_map/ppermute | solution.py:25
  96.9 25.8 %collective-permute-start.14 = (f32[8,1,256]{2,0,1:T(8,128)S(1)}, f32[8,1,256]{2,0,1:T(8,128)S(1)}, u32[]{:S(2)}, u32[]{:S(2)}) collective-permute-start(f32[8,1,256]{2,0,1:T(8,128)S(1)} %copy.281), channel_id=1, source_target_pairs={{1,0},{2,1},{3,2},{4,3},{5,4},{6,5},{7,6},{8,7},{9,8},{10,9},{11,1... | collective-permute-start | bytes 24584 | tf_op jit(solution)/shard_map/ppermute | solution.py:26
  99.8 25.4 %collective-permute-start.12 = (f32[1,32,256]{2,1,0:T(8,128)S(1)}, f32[1,32,256]{2,1,0:T(8,128)S(1)}, u32[]{:S(2)}, u32[]{:S(2)}) collective-permute-start(f32[1,32,256]{2,1,0:T(8,128)S(1)} %get-tuple-element.122), channel_id=1, source_target_pairs={{0,16},{16,32},{32,48},{48,64},{64,80},{80,96},{96,112},{112,128},... | collective-permute-start | bytes 98312 | tf_op jit(solution)/shard_map/ppermute | solution.py:25
  122.7 48.5 %collective-permute-start.31 = (f32[4,1,128]{2,1,0:T(1,128)}, f32[4,1,128]{2,1,0:T(1,128)S(1)}, u32[]{:S(2)}, u32[]{:S(2)}) collective-permute-start(f32[4,1,128]{2,1,0:T(1,128)} %get-tuple-element.186), channel_id=1, source_target_pairs={{0,1},{1,2},{2,3},{3,4},{4,5},{5,6},{6,7},{7,8},{8,9},{9,10},{10,1... | collective-permute-start | bytes 6152 | tf_op jit(solution)/shard_map/ppermute | solution.py:25
  127.4 17.7 %collective-permute-start.17 = (f32[1,32,256]{2,1,0:T(8,128)S(1)}, f32[1,32,256]{2,1,0:T(8,128)S(1)}, u32[]{:S(2)}, u32[]{:S(2)}) collective-permute-start(f32[1,32,256]{2,1,0:T(8,128)S(1)} %get-tuple-element.106), channel_id=1, source_target_pairs={{16,0},{32,16},{48,32},{64,48},{80,64},{96,80},{112,96},{128,112},... | collective-permute-start | bytes 98312 | tf_op jit(solution)/shard_map/ppermute | solution.py:26
  129.4 15.8 %collective-permute-start.18 = (f32[1,32,256]{2,1,0:T(8,128)S(1)}, f32[1,32,256]{2,1,0:T(8,128)S(1)}, u32[]{:S(2)}, u32[]{:S(2)}) collective-permute-start(f32[1,32,256]{2,1,0:T(8,128)S(1)} %get-tuple-element.105), channel_id=1, source_target_pairs={{0,16},{16,32},{32,48},{48,64},{64,80},{80,96},{96,112},{112,128},... | collective-permute-start | bytes 98312 | tf_op jit(solution)/shard_map/ppermute | solution.py:25
  145.9 18.8 %collective-permute-start.21 = (f32[1,32,256]{2,1,0:T(8,128)S(1)}, f32[1,32,256]{2,1,0:T(8,128)S(1)}, u32[]{:S(2)}, u32[]{:S(2)}) collective-permute-start(f32[1,32,256]{2,1,0:T(8,128)S(1)} %get-tuple-element.96), channel_id=1, source_target_pairs={{16,0},{32,16},{48,32},{64,48},{80,64},{96,80},{112,96},{128,112},... | collective-permute-start | bytes 98312 | tf_op jit(solution)/shard_map/ppermute | solution.py:26
  147.8 18.8 %collective-permute-start.22 = (f32[1,32,256]{2,1,0:T(8,128)S(1)}, f32[1,32,256]{2,1,0:T(8,128)S(1)}, u32[]{:S(2)}, u32[]{:S(2)}) collective-permute-start(f32[1,32,256]{2,1,0:T(8,128)S(1)} %get-tuple-element.95), channel_id=1, source_target_pairs={{0,16},{16,32},{32,48},{48,64},{64,80},{80,96},{96,112},{112,128},... | collective-permute-start | bytes 98312 | tf_op jit(solution)/shard_map/ppermute | solution.py:25
  159.0 16.4 %collective-permute-start.29 = (f32[4,1,128]{2,1,0:T(1,128)S(1)}, f32[4,1,128]{2,1,0:T(1,128)S(1)}, u32[]{:S(2)}, u32[]{:S(2)}) collective-permute-start(f32[4,1,128]{2,1,0:T(1,128)S(1)} %copy-done.29), channel_id=1, source_target_pairs={{1,0},{2,1},{3,2},{4,3},{5,4},{6,5},{7,6},{8,7},{9,8},{10,9},{11,1... | collective-permute-start | bytes 6152 | tf_op jit(solution)/shard_map/ppermute | solution.py:26
  162.1 19.5 %collective-permute-start.27 = (f32[1,16,128]{2,1,0:T(8,128)S(1)}, f32[1,16,128]{2,1,0:T(8,128)S(1)}, u32[]{:S(2)}, u32[]{:S(2)}) collective-permute-start(f32[1,16,128]{2,1,0:T(8,128)S(1)} %copy-done.20), channel_id=1, source_target_pairs={{0,16},{16,32},{32,48},{48,64},{64,80},{80,96},{96,112},{112,128},... | collective-permute-start | bytes 24584 | tf_op jit(solution)/shard_map/ppermute | solution.py:25
  164.7 19.0 %collective-permute-start.25 = (f32[1,16,128]{2,1,0:T(8,128)S(1)}, f32[1,16,128]{2,1,0:T(8,128)S(1)}, u32[]{:S(2)}, u32[]{:S(2)}) collective-permute-start(f32[1,16,128]{2,1,0:T(8,128)S(1)} %copy-done.19), channel_id=1, source_target_pairs={{16,0},{32,16},{48,32},{64,48},{80,64},{96,80},{112,96},{128,112},... | collective-permute-start | bytes 24584 | tf_op jit(solution)/shard_map/ppermute | solution.py:26
  168.8 17.4 %collective-permute-start.32 = (f32[4,1,128]{2,1,0:T(1,128)S(1)}, f32[4,1,128]{2,1,0:T(1,128)S(1)}, u32[]{:S(2)}, u32[]{:S(2)}) collective-permute-start(f32[4,1,128]{2,1,0:T(1,128)S(1)} %get-tuple-element.196), channel_id=1, source_target_pairs={{0,1},{1,2},{2,3},{3,4},{4,5},{5,6},{6,7},{7,8},{8,9},{9,10},{10,1... | collective-permute-start | bytes 6152 | tf_op jit(solution)/shard_map/ppermute | solution.py:25
  171.2 15.0 %collective-permute-start.30 = (f32[4,1,128]{2,1,0:T(1,128)S(1)}, f32[4,1,128]{2,1,0:T(1,128)S(1)}, u32[]{:S(2)}, u32[]{:S(2)}) collective-permute-start(f32[4,1,128]{2,1,0:T(1,128)S(1)} %get-tuple-element.195), channel_id=1, source_target_pairs={{1,0},{2,1},{3,2},{4,3},{5,4},{6,5},{7,6},{8,7},{9,8},{10,9},{11,1... | collective-permute-start | bytes 6152 | tf_op jit(solution)/shard_map/ppermute | solution.py:26
  184.3 45.9 %collective-permute-start.47 = (f32[2,1,64]{2,1,0:T(1,128)S(1)}, f32[2,1,64]{2,1,0:T(1,128)S(1)}, u32[]{:S(2)}, u32[]{:S(2)}) collective-permute-start(f32[2,1,64]{2,1,0:T(1,128)S(1)} %copy-done.31), channel_id=1, source_target_pairs={{0,1},{1,2},{2,3},{3,4},{4,5},{5,6},{6,7},{7,8},{8,9},{9,10},{10,1... | collective-permute-start | bytes 1544 | tf_op jit(solution)/shard_map/ppermute | solution.py:25
  189.0 15.6 %collective-permute-start.33 = (f32[1,16,128]{2,1,0:T(8,128)S(1)}, f32[1,16,128]{2,1,0:T(8,128)S(1)}, u32[]{:S(2)}, u32[]{:S(2)}) collective-permute-start(f32[1,16,128]{2,1,0:T(8,128)S(1)} %get-tuple-element.176), channel_id=1, source_target_pairs={{16,0},{32,16},{48,32},{64,48},{80,64},{96,80},{112,96},{128,112},... | collective-permute-start | bytes 24584 | tf_op jit(solution)/shard_map/ppermute | solution.py:26
  190.9 13.7 %collective-permute-start.34 = (f32[1,16,128]{2,1,0:T(8,128)S(1)}, f32[1,16,128]{2,1,0:T(8,128)S(1)}, u32[]{:S(2)}, u32[]{:S(2)}) collective-permute-start(f32[1,16,128]{2,1,0:T(8,128)S(1)} %get-tuple-element.175), channel_id=1, source_target_pairs={{0,16},{16,32},{32,48},{48,64},{64,80},{80,96},{96,112},{112,128},... | collective-permute-start | bytes 24584 | tf_op jit(solution)/shard_map/ppermute | solution.py:25
  204.8 19.3 %collective-permute-start.37 = (f32[1,16,128]{2,1,0:T(8,128)S(1)}, f32[1,16,128]{2,1,0:T(8,128)S(1)}, u32[]{:S(2)}, u32[]{:S(2)}) collective-permute-start(f32[1,16,128]{2,1,0:T(8,128)S(1)} %get-tuple-element.166), channel_id=1, source_target_pairs={{16,0},{32,16},{48,32},{64,48},{80,64},{96,80},{112,96},{128,112},... | collective-permute-start | bytes 24584 | tf_op jit(solution)/shard_map/ppermute | solution.py:26
  206.7 19.4 %collective-permute-start.38 = (f32[1,16,128]{2,1,0:T(8,128)S(1)}, f32[1,16,128]{2,1,0:T(8,128)S(1)}, u32[]{:S(2)}, u32[]{:S(2)}) collective-permute-start(f32[1,16,128]{2,1,0:T(8,128)S(1)} %get-tuple-element.165), channel_id=1, source_target_pairs={{0,16},{16,32},{32,48},{48,64},{64,80},{80,96},{96,112},{112,128},... | collective-permute-start | bytes 24584 | tf_op jit(solution)/shard_map/ppermute | solution.py:25
  218.4 15.9 %collective-permute-start.45 = (f32[2,1,64]{2,1,0:T(1,128)S(1)}, f32[2,1,64]{2,1,0:T(1,128)S(1)}, u32[]{:S(2)}, u32[]{:S(2)}) collective-permute-start(f32[2,1,64]{2,1,0:T(1,128)S(1)} %copy-done.30), channel_id=1, source_target_pairs={{1,0},{2,1},{3,2},{4,3},{5,4},{6,5},{7,6},{8,7},{9,8},{10,9},{11,1... | collective-permute-start | bytes 1544 | tf_op jit(solution)/shard_map/ppermute | solution.py:26
  221.6 19.0 %collective-permute-start.43 = (f32[1,8,64]{2,1,0:T(8,128)S(1)}, f32[1,8,64]{2,1,0:T(8,128)S(1)}, u32[]{:S(2)}, u32[]{:S(2)}) collective-permute-start(f32[1,8,64]{2,1,0:T(8,128)S(1)} %copy-done.13), channel_id=1, source_target_pairs={{0,16},{16,32},{32,48},{48,64},{64,80},{80,96},{96,112},{112,128},... | collective-permute-start | bytes 6152 | tf_op jit(solution)/shard_map/ppermute | solution.py:25
  224.1 18.5 %collective-permute-start.41 = (f32[1,8,64]{2,1,0:T(8,128)S(1)}, f32[1,8,64]{2,1,0:T(8,128)S(1)}, u32[]{:S(2)}, u32[]{:S(2)}) collective-permute-start(f32[1,8,64]{2,1,0:T(8,128)S(1)} %copy-done.14), channel_id=1, source_target_pairs={{16,0},{32,16},{48,32},{64,48},{80,64},{96,80},{112,96},{128,112},... | collective-permute-start | bytes 6152 | tf_op jit(solution)/shard_map/ppermute | solution.py:26
  227.8 16.8 %collective-permute-start.48 = (f32[2,1,64]{2,1,0:T(1,128)S(1)}, f32[2,1,64]{2,1,0:T(1,128)S(1)}, u32[]{:S(2)}, u32[]{:S(2)}) collective-permute-start(f32[2,1,64]{2,1,0:T(1,128)S(1)} %get-tuple-element.254), channel_id=1, source_target_pairs={{0,1},{1,2},{2,3},{3,4},{4,5},{5,6},{6,7},{7,8},{8,9},{9,10},{10,1... | collective-permute-start | bytes 1544 | tf_op jit(solution)/shard_map/ppermute | solution.py:25
  230.2 14.4 %collective-permute-start.46 = (f32[2,1,64]{2,1,0:T(1,128)S(1)}, f32[2,1,64]{2,1,0:T(1,128)S(1)}, u32[]{:S(2)}, u32[]{:S(2)}) collective-permute-start(f32[2,1,64]{2,1,0:T(1,128)S(1)} %get-tuple-element.253), channel_id=1, source_target_pairs={{1,0},{2,1},{3,2},{4,3},{5,4},{6,5},{7,6},{8,7},{9,8},{10,9},{11,1... | collective-permute-start | bytes 1544 | tf_op jit(solution)/shard_map/ppermute | solution.py:26
  242.6 51.3 %collective-permute-start.57 = (f32[1,4,32]{2,1,0:T(4,128)S(1)}, f32[1,4,32]{2,1,0:T(4,128)S(1)}, u32[]{:S(2)}, u32[]{:S(2)}) collective-permute-start(f32[1,4,32]{2,1,0:T(4,128)S(1)} %bitcast.376), channel_id=1, source_target_pairs={{16,0},{32,16},{48,32},{64,48},{80,64},{96,80},{112,96},{128,112},... | collective-permute-start | bytes 1544 | tf_op jit(solution)/shard_map/ppermute | solution.py:26
  248.5 15.1 %collective-permute-start.49 = (f32[1,8,64]{2,1,0:T(8,128)S(1)}, f32[1,8,64]{2,1,0:T(8,128)S(1)}, u32[]{:S(2)}, u32[]{:S(2)}) collective-permute-start(f32[1,8,64]{2,1,0:T(8,128)S(1)} %get-tuple-element.240), channel_id=1, source_target_pairs={{16,0},{32,16},{48,32},{64,48},{80,64},{96,80},{112,96},{128,112},... | collective-permute-start | bytes 6152 | tf_op jit(solution)/shard_map/ppermute | solution.py:26
  250.4 13.2 %collective-permute-start.50 = (f32[1,8,64]{2,1,0:T(8,128)S(1)}, f32[1,8,64]{2,1,0:T(8,128)S(1)}, u32[]{:S(2)}, u32[]{:S(2)}) collective-permute-start(f32[1,8,64]{2,1,0:T(8,128)S(1)} %get-tuple-element.239), channel_id=1, source_target_pairs={{0,16},{16,32},{32,48},{48,64},{64,80},{80,96},{96,112},{112,128},... | collective-permute-start | bytes 6152 | tf_op jit(solution)/shard_map/ppermute | solution.py:25
  263.8 18.5 %collective-permute-start.53 = (f32[1,8,64]{2,1,0:T(8,128)S(1)}, f32[1,8,64]{2,1,0:T(8,128)S(1)}, u32[]{:S(2)}, u32[]{:S(2)}) collective-permute-start(f32[1,8,64]{2,1,0:T(8,128)S(1)} %get-tuple-element.232), channel_id=1, source_target_pairs={{16,0},{32,16},{48,32},{64,48},{80,64},{96,80},{112,96},{128,112},... | collective-permute-start | bytes 6152 | tf_op jit(solution)/shard_map/ppermute | solution.py:26
  265.7 19.0 %collective-permute-start.54 = (f32[1,8,64]{2,1,0:T(8,128)S(1)}, f32[1,8,64]{2,1,0:T(8,128)S(1)}, u32[]{:S(2)}, u32[]{:S(2)}) collective-permute-start(f32[1,8,64]{2,1,0:T(8,128)S(1)} %get-tuple-element.231), channel_id=1, source_target_pairs={{0,16},{16,32},{32,48},{48,64},{64,80},{80,96},{96,112},{112,128},... | collective-permute-start | bytes 6152 | tf_op jit(solution)/shard_map/ppermute | solution.py:25
  276.8 21.2 %collective-permute-start.59 = (f32[1,4,32]{2,1,0:T(4,128)S(1)}, f32[1,4,32]{2,1,0:T(4,128)S(1)}, u32[]{:S(2)}, u32[]{:S(2)}) collective-permute-start(f32[1,4,32]{2,1,0:T(4,128)S(1)} %bitcast.377), channel_id=1, source_target_pairs={{0,16},{16,32},{32,48},{48,64},{64,80},{80,96},{96,112},{112,128},... | collective-permute-start | bytes 1544 | tf_op jit(solution)/shard_map/ppermute | solution.py:25
  286.2 13.6 %collective-permute-start.60 = (f32[1,4,32]{2,1,0:T(4,128)S(1)}, f32[1,4,32]{2,1,0:T(4,128)S(1)}, u32[]{:S(2)}, u32[]{:S(2)}) collective-permute-start(f32[1,4,32]{2,1,0:T(4,128)S(1)} %fusion.384), channel_id=1, source_target_pairs={{0,16},{16,32},{32,48},{48,64},{64,80},{80,96},{96,112},{112,128},... | collective-permute-start | bytes 1544 | tf_op jit(solution)/shard_map/ppermute | solution.py:25
  300.6 18.1 %collective-permute-start.66 = (f32[1,4,32]{2,1,0:T(4,128)S(1)}, f32[1,4,32]{2,1,0:T(4,128)S(1)}, u32[]{:S(2)}, u32[]{:S(2)}) collective-permute-start(f32[1,4,32]{2,1,0:T(4,128)S(1)} %get-tuple-element.27), channel_id=1, source_target_pairs={{0,16},{16,32},{32,48},{48,64},{64,80},{80,96},{96,112},{112,128},... | collective-permute-start | bytes 1544 | tf_op jit(solution)/shard_map/ppermute | solution.py:25
  318.9 17.9 %collective-permute-start.70 = (f32[1,4,32]{2,1,0:T(4,128)S(1)}, f32[1,4,32]{2,1,0:T(4,128)S(1)}, u32[]{:S(2)}, u32[]{:S(2)}) collective-permute-start(f32[1,4,32]{2,1,0:T(4,128)S(1)} %get-tuple-element.25), channel_id=1, source_target_pairs={{0,16},{16,32},{32,48},{48,64},{64,80},{80,96},{96,112},{112,128},... | collective-permute-start | bytes 1544 | tf_op jit(solution)/shard_map/ppermute | solution.py:25
  337.0 16.8 %collective-permute-start.74 = (f32[1,4,32]{2,1,0:T(4,128)S(1)}, f32[1,4,32]{2,1,0:T(4,128)S(1)}, u32[]{:S(2)}, u32[]{:S(2)}) collective-permute-start(f32[1,4,32]{2,1,0:T(4,128)S(1)} %get-tuple-element.23), channel_id=1, source_target_pairs={{0,16},{16,32},{32,48},{48,64},{64,80},{80,96},{96,112},{112,128},... | collective-permute-start | bytes 1544 | tf_op jit(solution)/shard_map/ppermute | solution.py:25
  353.9 16.3 %collective-permute-start.78 = (f32[1,4,32]{2,1,0:T(4,128)S(1)}, f32[1,4,32]{2,1,0:T(4,128)S(1)}, u32[]{:S(2)}, u32[]{:S(2)}) collective-permute-start(f32[1,4,32]{2,1,0:T(4,128)S(1)} %get-tuple-element.21), channel_id=1, source_target_pairs={{0,16},{16,32},{32,48},{48,64},{64,80},{80,96},{96,112},{112,128},... | collective-permute-start | bytes 1544 | tf_op jit(solution)/shard_map/ppermute | solution.py:25
  370.4 16.6 %collective-permute-start.82 = (f32[1,4,32]{2,1,0:T(4,128)S(1)}, f32[1,4,32]{2,1,0:T(4,128)S(1)}, u32[]{:S(2)}, u32[]{:S(2)}) collective-permute-start(f32[1,4,32]{2,1,0:T(4,128)S(1)} %get-tuple-element.19), channel_id=1, source_target_pairs={{0,16},{16,32},{32,48},{48,64},{64,80},{80,96},{96,112},{112,128},... | collective-permute-start | bytes 1544 | tf_op jit(solution)/shard_map/ppermute | solution.py:25
  387.1 16.3 %collective-permute-start.86 = (f32[1,4,32]{2,1,0:T(4,128)S(1)}, f32[1,4,32]{2,1,0:T(4,128)S(1)}, u32[]{:S(2)}, u32[]{:S(2)}) collective-permute-start(f32[1,4,32]{2,1,0:T(4,128)S(1)} %get-tuple-element.17), channel_id=1, source_target_pairs={{0,16},{16,32},{32,48},{48,64},{64,80},{80,96},{96,112},{112,128},... | collective-permute-start | bytes 1544 | tf_op jit(solution)/shard_map/ppermute | solution.py:25
  403.7 15.9 %collective-permute-start.92 = (f32[2,1,64]{2,1,0:T(1,128)S(1)}, f32[2,1,64]{2,1,0:T(1,128)S(1)}, u32[]{:S(2)}, u32[]{:S(2)}) collective-permute-start(f32[2,1,64]{2,1,0:T(1,128)S(1)} %get-tuple-element.222), channel_id=1, source_target_pairs={{0,1},{1,2},{2,3},{3,4},{4,5},{5,6},{6,7},{7,8},{8,9},{9,10},{10,1... | collective-permute-start | bytes 1544 | tf_op jit(solution)/shard_map/ppermute | solution.py:25
  441.0 15.7 %collective-permute-start.97 = (f32[1,8,64]{2,1,0:T(8,128)S(1)}, f32[1,8,64]{2,1,0:T(8,128)S(1)}, u32[]{:S(2)}, u32[]{:S(2)}) collective-permute-start(f32[1,8,64]{2,1,0:T(8,128)S(1)} %get-tuple-element.208), channel_id=1, source_target_pairs={{16,0},{32,16},{48,32},{64,48},{80,64},{96,80},{112,96},{128,112},... | collective-permute-start | bytes 6152 | tf_op jit(solution)/shard_map/ppermute | solution.py:26
  442.9 13.7 %collective-permute-start.98 = (f32[1,8,64]{2,1,0:T(8,128)S(1)}, f32[1,8,64]{2,1,0:T(8,128)S(1)}, u32[]{:S(2)}, u32[]{:S(2)}) collective-permute-start(f32[1,8,64]{2,1,0:T(8,128)S(1)} %get-tuple-element.207), channel_id=1, source_target_pairs={{0,16},{16,32},{32,48},{48,64},{64,80},{80,96},{96,112},{112,128},... | collective-permute-start | bytes 6152 | tf_op jit(solution)/shard_map/ppermute | solution.py:25
  491.2 15.2 %collective-permute-start.109 = (f32[1,16,128]{2,1,0:T(8,128)S(1)}, f32[1,16,128]{2,1,0:T(8,128)S(1)}, u32[]{:S(2)}, u32[]{:S(2)}) collective-permute-start(f32[1,16,128]{2,1,0:T(8,128)S(1)} %get-tuple-element.136), channel_id=1, source_target_pairs={{16,0},{32,16},{48,32},{64,48},{80,64},{96,80},{112,96},{128,112},... | collective-permute-start | bytes 24584 | tf_op jit(solution)/shard_map/ppermute | solution.py:26
  493.1 13.2 %collective-permute-start.110 = (f32[1,16,128]{2,1,0:T(8,128)S(1)}, f32[1,16,128]{2,1,0:T(8,128)S(1)}, u32[]{:S(2)}, u32[]{:S(2)}) collective-permute-start(f32[1,16,128]{2,1,0:T(8,128)S(1)} %get-tuple-element.135), channel_id=1, source_target_pairs={{0,16},{16,32},{32,48},{48,64},{64,80},{80,96},{96,112},{112,128},... | collective-permute-start | bytes 24584 | tf_op jit(solution)/shard_map/ppermute | solution.py:25
  546.3 15.3 %collective-permute-start.121 = (f32[1,32,256]{2,1,0:T(8,128)S(1)}, f32[1,32,256]{2,1,0:T(8,128)S(1)}, u32[]{:S(2)}, u32[]{:S(2)}) collective-permute-start(f32[1,32,256]{2,1,0:T(8,128)S(1)} %get-tuple-element.66), channel_id=1, source_target_pairs={{16,0},{32,16},{48,32},{64,48},{80,64},{96,80},{112,96},{128,112},... | collective-permute-start | bytes 98312 | tf_op jit(solution)/shard_map/ppermute | solution.py:26
  548.2 13.3 %collective-permute-start.122 = (f32[1,32,256]{2,1,0:T(8,128)S(1)}, f32[1,32,256]{2,1,0:T(8,128)S(1)}, u32[]{:S(2)}, u32[]{:S(2)}) collective-permute-start(f32[1,32,256]{2,1,0:T(8,128)S(1)} %get-tuple-element.65), channel_id=1, source_target_pairs={{0,16},{16,32},{32,48},{48,64},{64,80},{80,96},{96,112},{112,128},... | collective-permute-start | bytes 98312 | tf_op jit(solution)/shard_map/ppermute | solution.py:25
  (115 other events, 831.5 us)

commit v2 on v1

v2 whole, which is shorter than its diff:
```python
import jax
import jax.numpy as jnp
from jax import lax
from jax.sharding import PartitionSpec as P

LEVELS = 4
PRE_STEPS = 3
POST_STEPS = 3
COARSE_STEPS = 8


HELM_SHIFT = 0.05
LOW_FRACTION = 0.1
HALO_DEPTH = 3


def extend(x, depth):
    dim0 = x.ndim - 3
    for axis, dim in (("gx", dim0), ("gy", dim0 + 1)):
        peers = lax.axis_size(axis)
        length = x.shape[dim]
        up = [(i, i + 1) for i in range(peers - 1)]
        down = [(i + 1, i) for i in range(peers - 1)]
        last = lax.slice_in_dim(x, length - depth, length, axis=dim)
        first = lax.slice_in_dim(x, 0, depth, axis=dim)
        before = lax.ppermute(last, axis, up)
        after = lax.ppermute(first, axis, down)
        x = jnp.concatenate([before, x, after], axis=dim)
    return x


def crop(x, k):
    if k == 0:
        return x
    return x[..., k:-k, k:-k, :]


def neighbours(u):
    centre = u[1:-1, 1:-1]
    zero = jnp.zeros_like(centre[:, :, :1])
    return centre, [
        u[2:, 1:-1],
        u[:-2, 1:-1],
        u[1:-1, 2:],
        u[1:-1, :-2],
        jnp.concatenate([centre[:, :, 1:], zero], axis=2),
        jnp.concatenate([zero, centre[:, :, :-1]], axis=2),
    ]


def pool_matrix(n, dtype):
    rows = jnp.arange(n)[:, None] // 2
    cols = jnp.arange(n // 2)[None, :]
    return (rows == cols).astype(dtype)


def restrict(values):
    first, second, third = values.shape
    pairs = values.reshape(first // 2, 2, second, third)
    summed = pairs[:, 0] + pairs[:, 1]
    pool1 = pool_matrix(second, values.dtype)
    pool2 = pool_matrix(third, values.dtype)
    summed = jnp.einsum("ajk,jb->abk", summed, pool1, precision=lax.Precision.HIGHEST)
    summed = jnp.einsum("abk,kc->abc", summed, pool2, precision=lax.Precision.HIGHEST)
    return summed * 0.125


def prolong(values):
    return jnp.repeat(jnp.repeat(jnp.repeat(values, 2, 0), 2, 1), 2, 2)


def inside_mask(shape, depth):
    n0, n1 = shape[0], shape[1]
    rows = lax.axis_index("gx") * n0 + jnp.arange(n0 + 2 * depth) - depth
    cols = lax.axis_index("gy") * n1 + jnp.arange(n1 + 2 * depth) - depth
    ok0 = (rows >= 0) & (rows < n0 * lax.axis_size("gx"))
    ok1 = (cols >= 0) & (cols < n1 * lax.axis_size("gy"))
    return ok0[:, None, None] & ok1[None, :, None]


class Level:
    def __init__(self, source, alpha, beta, inv_spacing, upper):
        n0, n1 = source.shape[0], source.shape[1]
        self.depth = min(HALO_DEPTH, n0, n1)
        stacked = extend(jnp.stack([source, beta, alpha]), self.depth)
        self.source = stacked[0]
        beta_ext = stacked[1]
        self.alpha = stacked[2]
        centre, near = neighbours(beta_ext)
        self.sums = [centre + b for b in near]
        self.mask = inside_mask(source.shape, self.depth)
        self.inv_spacing = inv_spacing
        self.upper = upper

    def apply(self, u, e):
        centre, near = neighbours(u)
        sums = [crop(s, self.depth - e) for s in self.sums]
        alpha = crop(self.alpha, self.depth - e + 1)
        summed = jnp.zeros_like(centre)
        for near_u, near_b in zip(near, sums):
            summed = summed + near_b * (centre - near_u)
        return HELM_SHIFT * alpha * centre + 0.5 * self.inv_spacing * summed

    def residual(self, u, e):
        out = e - 1
        r = crop(self.source, self.depth - out) - self.apply(u, e)
        if out > 0:
            r = jnp.where(crop(self.mask, self.depth - out), r, 0.0)
        return r


def smooth(level, field, sweeps, start_zero, tail):
    upper = level.upper
    lower = LOW_FRACTION * upper
    middle = 0.5 * (upper + lower)
    half_width = 0.5 * (upper - lower)
    scaled = middle / half_width
    factor = 1.0 / scaled
    remaining = sweeps - 1 + tail if start_zero else sweeps + tail
    if start_zero:
        e = level.depth
        direction = level.source / middle
        field = direction
    else:
        e = min(level.depth, remaining)
        field = extend(field, e)
        residual = level.residual(field, e)
        remaining -= 1
        e -= 1
        direction = residual / middle
        field = crop(field, 1) + direction
    for k in range(1, sweeps):
        if e == 0:
            e = min(level.depth, remaining)
            both = extend(jnp.stack([field, direction]), e)
            field, direction = both[0], both[1]
        residual = level.residual(field, e)
        remaining -= 1
        e -= 1
        factor_new = 1.0 / (2.0 * scaled - factor)
        direction = (
            factor_new * factor * crop(direction, 1) + 2.0 * factor_new / half_width * residual
        )
        field = crop(field, 1) + direction
        factor = factor_new
    return field, e


def to_depth_zero(field, e):
    return crop(field, e)


def all_max(values):
    for axis in ("gx", "gy"):
        peers = lax.axis_size(axis)
        if peers & (peers - 1):
            values = lax.pmax(values, axis)
            continue
        step = 1
        while step < peers:
            pairs = [(i, i ^ step) for i in range(peers)]
            values = jnp.maximum(values, lax.ppermute(values, axis, pairs))
            step *= 2
    return values


def local(rhs_field, alpha_coef, beta_coef):
    alphas = [alpha_coef]
    betas = [beta_coef]
    for level_idx in range(1, LEVELS):
        alphas.append(restrict(alphas[-1]))
        betas.append(restrict(betas[-1]))
    maxima = jnp.stack([jnp.stack([jnp.max(alphas[i]), jnp.max(betas[i])]) for i in range(LEVELS)])
    maxima = all_max(maxima)
    uppers = [HELM_SHIFT * maxima[i, 0] + 12.0 * maxima[i, 1] / 4.0**i for i in range(LEVELS)]
    levels = []
    fields = []
    source = rhs_field
    for level_idx in range(LEVELS - 1):
        level = Level(source, alphas[level_idx], betas[level_idx], 1.0 / 4.0**level_idx, uppers[level_idx])
        levels.append(level)
        smoothed, e = smooth(level, None, PRE_STEPS, True, 1)
        if e == 0:
            e = 1
            smoothed_ext = extend(smoothed, 1)
        else:
            smoothed_ext = smoothed
        residual = level.residual(smoothed_ext, e)
        source = restrict(to_depth_zero(residual, e - 1))
        fields.append(to_depth_zero(smoothed_ext, e))
    last = LEVELS - 1
    level = Level(source, alphas[last], betas[last], 1.0 / 4.0**last, uppers[last])
    coarse, e = smooth(level, None, COARSE_STEPS, True, 0)
    coarse = to_depth_zero(coarse, e)
    for level_idx in range(LEVELS - 2, -1, -1):
        smoothed = fields[level_idx] + prolong(coarse)
        coarse, e = smooth(levels[level_idx], smoothed, POST_STEPS, False, 0)
        coarse = to_depth_zero(coarse, e)
    return coarse


def solution(mesh):
    placed = (P("gx", "gy", None), P("gx", "gy", None), P("gx", "gy", None))
    return jax.shard_map(
        local, mesh=mesh, in_specs=placed, out_specs=P("gx", "gy", None), check_vma=False
    )
```

time: 567 us -> 413 us (0.73)
  the two profiles are of different devices: /device:TPU:143 before, /device:TPU:408 now
where the time goes in v2:
time: 413 us; the launch traced here: 409 us
  starting transfers between devices  186 us (45%)
  waiting for transfers between devices  141 us (34%)
  other arithmetic  41.7 us (10%)
  local copies, waits for them, and re-layouts  19.9 us (5%)
  matrix products  11.7 us (3%)
  between operations  8.73 us (2%)
    ppermute x30, waiting for transfers between devices, extend(): before = lax.ppermute(last, axis, up)  108 us
    ppermute x30, starting transfers between devices, extend(): before = lax.ppermute(last, axis, up)  87.2 us
    ppermute x30, starting transfers between devices, extend(): after = lax.ppermute(first, axis, down)  72.1 us
    ppermute x9, waiting for transfers between devices, all_max(): values = jnp.maximum(values, lax.ppermute(values, axis, pairs))  31.6 us
    ppermute x9, starting transfers between devices, all_max(): values = jnp.maximum(values, lax.ppermute(values, axis, pairs))  27 us
    add x15, other arithmetic, smooth(): field = crop(field, 1) + direction  10.2 us
  transfers between devices with their start and end apart: 69, of which 37 were waited for; matrix products, arithmetic and copies ran while one was open for 2% of the time, Pallas kernels for 0%

profile of v2, /device:TPU:408, one launch (start us, length us, event | category | flops | bytes accessed | tf_op | source)
XLA Modules:
  0.0 409.5 jit_solution(10340816962457242701)
XLA Ops:
  20.9 4.9 %collective-permute-start.1 = (f32[3,3,32,256]{3,2,1,0:T(8,128)S(1)}, f32[3,3,32,256]{3,2,1,0:T(8,128)S(1)}, u32[]{:S(2)}, u32[]{:S(2)}) collective-permute-start(f32[3,3,32,256]{3,2,1,0:T(8,128)S(1)} %get-tuple-element.65), channel_id=1, source_target_pairs={{16,0},{32,16},{48,32},{64,48},{80,64},{96,80},{112,96},{128,112},... | collective-permute-start | bytes 884744 | tf_op jit(solution)/shard_map/ppermute | solution.py:27
  32.0 4.0 collective-permute-done
  36.2 4.1 %collective-permute-start.3 = (f32[3,14,3,256]{3,1,2,0:T(8,128)S(1)}, f32[3,14,3,256]{3,1,2,0:T(8,128)S(1)}, u32[]{:S(2)}, u32[]{:S(2)}) collective-permute-start(f32[3,14,3,256]{3,1,2,0:T(8,128)S(1)} %copy.131), channel_id=1, source_target_pairs={{1,0},{2,1},{3,2},{4,3},{5,4},{6,5},{7,6},{8,7},{9,8},{10,9},{11,1... | collective-permute-start | bytes 387080 | tf_op jit(solution)/shard_map/ppermute | solution.py:27
  44.2 5.1 %collective-permute-done.6 = f32[4,2]{1,0:T(4,128)S(1)} collective-permute-done((f32[4,2]{1,0:T(4,128)S(1)}, f32[4,2]{1,0:T(4,128)S(1)}, u32[]{:S(2)}, u32[]{:S(2)}) %collective-permute-start.6) | collective-permute-done | bytes 64 | tf_op jit(solution)/shard_map/ppermute | solution.py:162
  51.6 3.1 collective-permute-done.7
  57.6 4.1 %collective-permute-done.8 = f32[4,2]{1,0:T(4,128)S(1)} collective-permute-done((f32[4,2]{1,0:T(4,128)S(1)}, f32[4,2]{1,0:T(4,128)S(1)}, u32[]{:S(2)}, u32[]{:S(2)}) %collective-permute-start.8) | collective-permute-done | bytes 64 | tf_op jit(solution)/shard_map/ppermute | solution.py:162
  67.2 3.2 collective-permute-start.10
  70.4 3.2 collective-permute-done.10
  73.6 5.2 %collective-permute-start.11 = (f32[4,2]{1,0:T(4,128)S(1)}, f32[4,2]{1,0:T(4,128)S(1)}, u32[]{:S(2)}, u32[]{:S(2)}) collective-permute-start(f32[4,2]{1,0:T(4,128)S(1)} %max.33), channel_id=1, source_target_pairs={{0,4},{1,5},{2,6},{3,7},{4,0},{5,1},{6,2},{7,3},{8,12},{9,13},{10,... | collective-permute-start | bytes 104 | tf_op jit(solution)/shard_map/ppermute | solution.py:162
  78.8 4.1 %collective-permute-done.11 = f32[4,2]{1,0:T(4,128)S(1)} collective-permute-done((f32[4,2]{1,0:T(4,128)S(1)}, f32[4,2]{1,0:T(4,128)S(1)}, u32[]{:S(2)}, u32[]{:S(2)}) %collective-permute-start.11) | collective-permute-done | bytes 64 | tf_op jit(solution)/shard_map/ppermute | solution.py:162
  83.0 4.9 %collective-permute-start.12 = (f32[4,2]{1,0:T(4,128)S(1)}, f32[4,2]{1,0:T(4,128)S(1)}, u32[]{:S(2)}, u32[]{:S(2)}) collective-permute-start(f32[4,2]{1,0:T(4,128)S(1)} %max.34), channel_id=1, source_target_pairs={{0,8},{1,9},{2,10},{3,11},{4,12},{5,13},{6,14},{7,15},{8,0},{9,1},... | collective-permute-start | bytes 104 | tf_op jit(solution)/shard_map/ppermute | solution.py:162
  87.9 9.3 %collective-permute-done.12 = f32[4,2]{1,0:T(4,128)S(1)} collective-permute-done((f32[4,2]{1,0:T(4,128)S(1)}, f32[4,2]{1,0:T(4,128)S(1)}, u32[]{:S(2)}, u32[]{:S(2)}) %collective-permute-start.12) | collective-permute-done | bytes 64 | tf_op jit(solution)/shard_map/ppermute | solution.py:162
  108.9 4.8 %collective-permute-done.13 = f32[3,3,16,128]{3,2,1,0:T(8,128)S(1)} collective-permute-done((f32[3,3,16,128]{3,2,1,0:T(8,128)S(1)}, f32[3,3,16,128]{3,2,1,0:T(8,128)S(1)}, u32[]{:S(2)}, u32[]{:S(2)}) %collective-permute-start.13) | collective-permute-done | bytes 73760 | tf_op jit(solution)/shard_map/ppermute | solution.py:26
  114.4 5.1 %collective-permute-start.16 = (f32[3,10,3,128]{3,2,1,0:T(4,128)}, f32[3,10,3,128]{3,2,1,0:T(4,128)}, u32[]{:S(2)}, u32[]{:S(2)}) collective-permute-start(f32[3,10,3,128]{3,2,1,0:T(4,128)} %get-tuple-element.88), channel_id=1, source_target_pairs={{1,0},{2,1},{3,2},{4,3},{5,4},{6,5},{7,6},{8,7},{9,8},{10,9},{11,1... | collective-permute-start | bytes 138248 | tf_op jit(solution)/shard_map/ppermute | solution.py:27
  123.5 3.7 collective-permute-done.15
  134.2 4.7 %collective-permute-done.17 = f32[3,2,8,64]{3,2,1,0:T(8,128)S(1)} collective-permute-done((f32[3,2,8,64]{3,2,1,0:T(8,128)S(1)}, f32[3,2,8,64]{3,2,1,0:T(8,128)S(1)}, u32[]{:S(2)}, u32[]{:S(2)}) %collective-permute-start.17) | collective-permute-done | bytes 12320 | tf_op jit(solution)/shard_map/ppermute | solution.py:26
  141.5 3.9 collective-permute-start.19
  155.0 4.6 %collective-permute-done.22 = f32[1,8,64]{2,1,0:T(8,128)S(1)} collective-permute-done((f32[1,8,64]{2,1,0:T(8,128)S(1)}, f32[1,8,64]{2,1,0:T(8,128)S(1)}, u32[]{:S(2)}, u32[]{:S(2)}) %collective-permute-start.22) | collective-permute-done | bytes 2080 | tf_op jit(solution)/shard_map/ppermute | solution.py:26
  162.3 4.3 %collective-permute-start.23 = (f32[4,1,64]{2,1,0:T(1,128)S(1)}, f32[4,1,64]{2,1,0:T(1,128)S(1)}, u32[]{:S(2)}, u32[]{:S(2)}) collective-permute-start(f32[4,1,64]{2,1,0:T(1,128)S(1)} %get-tuple-element.151), channel_id=1, source_target_pairs={{1,0},{2,1},{3,2},{4,3},{5,4},{6,5},{7,6},{8,7},{9,8},{10,9},{11,1... | collective-permute-start | bytes 3080 | tf_op jit(solution)/shard_map/ppermute | solution.py:27
  174.2 4.6 %collective-permute-done.25 = f32[3,1,4,32]{3,2,1,0:T(4,128)S(1)} collective-permute-done((f32[3,1,4,32]{3,2,1,0:T(4,128)S(1)}, f32[3,1,4,32]{3,2,1,0:T(4,128)S(1)}, u32[]{:S(2)}, u32[]{:S(2)}) %collective-permute-start.25) | collective-permute-done | bytes 1568 | tf_op jit(solution)/shard_map/ppermute | solution.py:26
  179.4 5.4 %collective-permute-start.28 = (f32[3,3,1,32]{3,2,1,0:T(1,128)}, f32[3,3,1,32]{3,2,1,0:T(1,128)}, u32[]{:S(2)}, u32[]{:S(2)}) collective-permute-start(f32[3,3,1,32]{3,2,1,0:T(1,128)} %get-tuple-element.148), channel_id=1, source_target_pairs={{1,0},{2,1},{3,2},{4,3},{5,4},{6,5},{7,6},{8,7},{9,8},{10,9},{11,1... | collective-permute-start | bytes 3464 | tf_op jit(solution)/shard_map/ppermute | solution.py:27
  188.1 3.7 collective-permute-done.27
  197.7 4.6 %collective-permute-done.29 = f32[2,1,4,32]{3,2,1,0:T(4,128)S(1)} collective-permute-done((f32[2,1,4,32]{3,2,1,0:T(4,128)S(1)}, f32[2,1,4,32]{3,2,1,0:T(4,128)S(1)}, u32[]{:S(2)}, u32[]{:S(2)}) %collective-permute-start.29) | collective-permute-done | bytes 1056 | tf_op jit(solution)/shard_map/ppermute | solution.py:26
  204.8 3.9 collective-permute-start.31
  208.9 3.0 collective-permute-done.31
  217.8 4.6 %collective-permute-done.33 = f32[2,1,4,32]{3,2,1,0:T(4,128)S(1)} collective-permute-done((f32[2,1,4,32]{3,2,1,0:T(4,128)S(1)}, f32[2,1,4,32]{3,2,1,0:T(4,128)S(1)}, u32[]{:S(2)}, u32[]{:S(2)}) %collective-permute-start.33) | collective-permute-done | bytes 1056 | tf_op jit(solution)/shard_map/ppermute | solution.py:26
  225.0 3.9 collective-permute-start.35
  229.0 3.0 collective-permute-done.35
  237.9 4.6 %collective-permute-done.37 = f32[2,1,4,32]{3,2,1,0:T(4,128)S(1)} collective-permute-done((f32[2,1,4,32]{3,2,1,0:T(4,128)S(1)}, f32[2,1,4,32]{3,2,1,0:T(4,128)S(1)}, u32[]{:S(2)}, u32[]{:S(2)}) %collective-permute-start.37) | collective-permute-done | bytes 1056 | tf_op jit(solution)/shard_map/ppermute | solution.py:26
  245.1 3.9 collective-permute-start.39
  249.1 3.0 collective-permute-done.39
  258.1 4.6 %collective-permute-done.41 = f32[2,1,4,32]{3,2,1,0:T(4,128)S(1)} collective-permute-done((f32[2,1,4,32]{3,2,1,0:T(4,128)S(1)}, f32[2,1,4,32]{3,2,1,0:T(4,128)S(1)}, u32[]{:S(2)}, u32[]{:S(2)}) %collective-permute-start.41) | collective-permute-done | bytes 1056 | tf_op jit(solution)/shard_map/ppermute | solution.py:26
  265.2 3.9 collective-permute-start.43
  269.2 3.0 collective-permute-done.43
  278.2 4.6 %collective-permute-done.45 = f32[2,1,4,32]{3,2,1,0:T(4,128)S(1)} collective-permute-done((f32[2,1,4,32]{3,2,1,0:T(4,128)S(1)}, f32[2,1,4,32]{3,2,1,0:T(4,128)S(1)}, u32[]{:S(2)}, u32[]{:S(2)}) %collective-permute-start.45) | collective-permute-done | bytes 1056 | tf_op jit(solution)/shard_map/ppermute | solution.py:26
  285.3 3.9 collective-permute-start.47
  298.3 4.6 %collective-permute-done.49 = f32[2,1,4,32]{3,2,1,0:T(4,128)S(1)} collective-permute-done((f32[2,1,4,32]{3,2,1,0:T(4,128)S(1)}, f32[2,1,4,32]{3,2,1,0:T(4,128)S(1)}, u32[]{:S(2)}, u32[]{:S(2)}) %collective-permute-start.49) | collective-permute-done | bytes 1056 | tf_op jit(solution)/shard_map/ppermute | solution.py:26
  305.5 3.9 collective-permute-start.51
  309.5 3.0 collective-permute-done.51
  320.1 4.7 %collective-permute-done.53 = f32[2,8,64]{2,1,0:T(8,128)S(1)} collective-permute-done((f32[2,8,64]{2,1,0:T(8,128)S(1)}, f32[2,8,64]{2,1,0:T(8,128)S(1)}, u32[]{:S(2)}, u32[]{:S(2)}) %collective-permute-start.53) | collective-permute-done | bytes 4128 | tf_op jit(solution)/shard_map/ppermute | solution.py:26
  326.7 3.9 collective-permute-start.55
  339.8 4.7 %collective-permute-done.57 = f32[2,1,8,64]{3,2,1,0:T(8,128)S(1)} collective-permute-done((f32[2,1,8,64]{3,2,1,0:T(8,128)S(1)}, f32[2,1,8,64]{3,2,1,0:T(8,128)S(1)}, u32[]{:S(2)}, u32[]{:S(2)}) %collective-permute-start.57) | collective-permute-done | bytes 4128 | tf_op jit(solution)/shard_map/ppermute | solution.py:26
  346.4 3.9 collective-permute-start.59
  363.1 4.8 %collective-permute-done.61 = f32[3,16,128]{2,1,0:T(8,128)S(1)} collective-permute-done((f32[3,16,128]{2,1,0:T(8,128)S(1)}, f32[3,16,128]{2,1,0:T(8,128)S(1)}, u32[]{:S(2)}, u32[]{:S(2)}) %collective-permute-start.61) | collective-permute-done | bytes 24608 | tf_op jit(solution)/shard_map/ppermute | solution.py:26
  369.8 3.9 collective-permute-start.63
  391.0 5.6 %collective-permute-done.65 = f32[3,32,256]{2,1,0:T(8,128)S(1)} collective-permute-done((f32[3,32,256]{2,1,0:T(8,128)S(1)}, f32[3,32,256]{2,1,0:T(8,128)S(1)}, u32[]{:S(2)}, u32[]{:S(2)}) %collective-permute-start.65) | collective-permute-done | bytes 98336 | tf_op jit(solution)/shard_map/ppermute | solution.py:26
  398.8 3.9 collective-permute-start.67
  402.9 3.1 collective-permute-done.67
  (464 shorter events, 195.9 us)
Async XLA Ops:
  17.8 12.3 %collective-permute-start.4 = (f32[4,2]{1,0:T(4,128)S(1)}, f32[4,2]{1,0:T(4,128)S(1)}, u32[]{:S(2)}, u32[]{:S(2)}) collective-permute-start(f32[4,2]{1,0:T(4,128)S(1)} %pad_maximum_fusion.101), channel_id=1, source_target_pairs={{0,16},{16,0},{32,48},{48,32},{64,80},{80,64},{96,112},{112,96},{1... | collective-permute-start | bytes 104 | tf_op jit(solution)/shard_map/ppermute | solution.py:162
  20.9 11.1 %collective-permute-start.1 = (f32[3,3,32,256]{3,2,1,0:T(8,128)S(1)}, f32[3,3,32,256]{3,2,1,0:T(8,128)S(1)}, u32[]{:S(2)}, u32[]{:S(2)}) collective-permute-start(f32[3,3,32,256]{3,2,1,0:T(8,128)S(1)} %get-tuple-element.65), channel_id=1, source_target_pairs={{16,0},{32,16},{48,32},{64,48},{80,64},{96,80},{112,96},{128,112},... | collective-permute-start | bytes 884744 | tf_op jit(solution)/shard_map/ppermute | solution.py:27
  25.9 10.2 %collective-permute-start = (f32[3,3,32,256]{3,2,1,0:T(8,128)S(1)}, f32[3,3,32,256]{3,2,1,0:T(8,128)S(1)}, u32[]{:S(2)}, u32[]{:S(2)}) collective-permute-start(f32[3,3,32,256]{3,2,1,0:T(8,128)S(1)} %get-tuple-element.64), channel_id=1, source_target_pairs={{0,16},{16,32},{32,48},{48,64},{64,80},{80,96},{96,112},{112,128},... | collective-permute-start | bytes 884744 | tf_op jit(solution)/shard_map/ppermute | solution.py:26
  30.1 12.2 %collective-permute-start.5 = (f32[4,2]{1,0:T(4,128)S(1)}, f32[4,2]{1,0:T(4,128)S(1)}, u32[]{:S(2)}, u32[]{:S(2)}) collective-permute-start(f32[4,2]{1,0:T(4,128)S(1)} %fusion.426), channel_id=1, source_target_pairs={{0,32},{16,48},{32,0},{48,16},{64,96},{80,112},{96,64},{112,80},{1... | collective-permute-start | bytes 104 | tf_op jit(solution)/shard_map/ppermute | solution.py:162
  36.2 63.1 %collective-permute-start.3 = (f32[3,14,3,256]{3,1,2,0:T(8,128)S(1)}, f32[3,14,3,256]{3,1,2,0:T(8,128)S(1)}, u32[]{:S(2)}, u32[]{:S(2)}) collective-permute-start(f32[3,14,3,256]{3,1,2,0:T(8,128)S(1)} %copy.131), channel_id=1, source_target_pairs={{1,0},{2,1},{3,2},{4,3},{5,4},{6,5},{7,6},{8,7},{9,8},{10,9},{11,1... | collective-permute-start | bytes 387080 | tf_op jit(solution)/shard_map/ppermute | solution.py:27
  40.3 59.0 %collective-permute-start.2 = (f32[3,14,3,256]{3,1,2,0:T(8,128)S(1)}, f32[3,14,3,256]{3,1,2,0:T(8,128)S(1)}, u32[]{:S(2)}, u32[]{:S(2)}) collective-permute-start(f32[3,14,3,256]{3,1,2,0:T(8,128)S(1)} %copy.130), channel_id=1, source_target_pairs={{0,1},{1,2},{2,3},{3,4},{4,5},{5,6},{6,7},{7,8},{8,9},{9,10},{10,1... | collective-permute-start | bytes 387080 | tf_op jit(solution)/shard_map/ppermute | solution.py:26
  42.3 7.0 %collective-permute-start.6 = (f32[4,2]{1,0:T(4,128)S(1)}, f32[4,2]{1,0:T(4,128)S(1)}, u32[]{:S(2)}, u32[]{:S(2)}) collective-permute-start(f32[4,2]{1,0:T(4,128)S(1)} %fusion.490), channel_id=1, source_target_pairs={{0,64},{16,80},{32,96},{48,112},{64,0},{80,16},{96,32},{112,48},{1... | collective-permute-start | bytes 104 | tf_op jit(solution)/shard_map/ppermute | solution.py:162
  54.8 7.0 %collective-permute-start.8 = (f32[4,2]{1,0:T(4,128)S(1)}, f32[4,2]{1,0:T(4,128)S(1)}, u32[]{:S(2)}, u32[]{:S(2)}) collective-permute-start(f32[4,2]{1,0:T(4,128)S(1)} %max.30), channel_id=1, source_target_pairs={{0,256},{16,272},{32,288},{48,304},{64,320},{80,336},{96,352},{112... | collective-permute-start | bytes 104 | tf_op jit(solution)/shard_map/ppermute | solution.py:162
  67.2 6.4 %collective-permute-start.10 = (f32[4,2]{1,0:T(4,128)S(1)}, f32[4,2]{1,0:T(4,128)S(1)}, u32[]{:S(2)}, u32[]{:S(2)}) collective-permute-start(f32[4,2]{1,0:T(4,128)S(1)} %max.32), channel_id=1, source_target_pairs={{0,2},{1,3},{2,0},{3,1},{4,6},{5,7},{6,4},{7,5},{8,10},{9,11},{10,... | collective-permute-start | bytes 104 | tf_op jit(solution)/shard_map/ppermute | solution.py:162
  73.6 9.4 %collective-permute-start.11 = (f32[4,2]{1,0:T(4,128)S(1)}, f32[4,2]{1,0:T(4,128)S(1)}, u32[]{:S(2)}, u32[]{:S(2)}) collective-permute-start(f32[4,2]{1,0:T(4,128)S(1)} %max.33), channel_id=1, source_target_pairs={{0,4},{1,5},{2,6},{3,7},{4,0},{5,1},{6,2},{7,3},{8,12},{9,13},{10,... | collective-permute-start | bytes 104 | tf_op jit(solution)/shard_map/ppermute | solution.py:162
  83.0 14.2 %collective-permute-start.12 = (f32[4,2]{1,0:T(4,128)S(1)}, f32[4,2]{1,0:T(4,128)S(1)}, u32[]{:S(2)}, u32[]{:S(2)}) collective-permute-start(f32[4,2]{1,0:T(4,128)S(1)} %max.34), channel_id=1, source_target_pairs={{0,8},{1,9},{2,10},{3,11},{4,12},{5,13},{6,14},{7,15},{8,0},{9,1},... | collective-permute-start | bytes 104 | tf_op jit(solution)/shard_map/ppermute | solution.py:162
  105.9 7.8 %collective-permute-start.13 = (f32[3,3,16,128]{3,2,1,0:T(8,128)S(1)}, f32[3,3,16,128]{3,2,1,0:T(8,128)S(1)}, u32[]{:S(2)}, u32[]{:S(2)}) collective-permute-start(f32[3,3,16,128]{3,2,1,0:T(8,128)S(1)} %get-tuple-element.102), channel_id=1, source_target_pairs={{0,16},{16,32},{32,48},{48,64},{64,80},{80,96},{96,112},{112,128},... | collective-permute-start | bytes 221192 | tf_op jit(solution)/shard_map/ppermute | solution.py:26
  114.4 9.1 %collective-permute-start.16 = (f32[3,10,3,128]{3,2,1,0:T(4,128)}, f32[3,10,3,128]{3,2,1,0:T(4,128)}, u32[]{:S(2)}, u32[]{:S(2)}) collective-permute-start(f32[3,10,3,128]{3,2,1,0:T(4,128)} %get-tuple-element.88), channel_id=1, source_target_pairs={{1,0},{2,1},{3,2},{4,3},{5,4},{6,5},{7,6},{8,7},{9,8},{10,9},{11,1... | collective-permute-start | bytes 138248 | tf_op jit(solution)/shard_map/ppermute | solution.py:27
  119.5 7.6 %collective-permute-start.15 = (f32[3,10,3,128]{3,2,1,0:T(4,128)}, f32[3,10,3,128]{3,2,1,0:T(4,128)}, u32[]{:S(2)}, u32[]{:S(2)}) collective-permute-start(f32[3,10,3,128]{3,2,1,0:T(4,128)} %get-tuple-element.87), channel_id=1, source_target_pairs={{0,1},{1,2},{2,3},{3,4},{4,5},{5,6},{6,7},{7,8},{8,9},{9,10},{10,1... | collective-permute-start | bytes 138248 | tf_op jit(solution)/shard_map/ppermute | solution.py:26
  131.7 7.3 %collective-permute-start.17 = (f32[3,2,8,64]{3,2,1,0:T(8,128)S(1)}, f32[3,2,8,64]{3,2,1,0:T(8,128)S(1)}, u32[]{:S(2)}, u32[]{:S(2)}) collective-permute-start(f32[3,2,8,64]{3,2,1,0:T(8,128)S(1)} %pad_maximum_fusion.31), channel_id=1, source_target_pairs={{0,16},{16,32},{32,48},{48,64},{64,80},{80,96},{96,112},{112,128},... | collective-permute-start | bytes 36872 | tf_op jit(solution)/shard_map/ppermute | solution.py:26
  139.6 8.0 %collective-permute-start.20 = (f32[3,6,2,64]{3,2,1,0:T(2,128)}, f32[3,6,2,64]{3,2,1,0:T(2,128)}, u32[]{:S(2)}, u32[]{:S(2)}) collective-permute-start(f32[3,6,2,64]{3,2,1,0:T(2,128)} %get-tuple-element.109), channel_id=1, source_target_pairs={{1,0},{2,1},{3,2},{4,3},{5,4},{6,5},{7,6},{8,7},{9,8},{10,9},{11,1... | collective-permute-start | bytes 27656 | tf_op jit(solution)/shard_map/ppermute | solution.py:27
  141.5 7.2 %collective-permute-start.19 = (f32[3,6,2,64]{3,2,1,0:T(2,128)}, f32[3,6,2,64]{3,2,1,0:T(2,128)}, u32[]{:S(2)}, u32[]{:S(2)}) collective-permute-start(f32[3,6,2,64]{3,2,1,0:T(2,128)} %get-tuple-element.108), channel_id=1, source_target_pairs={{0,1},{1,2},{2,3},{3,4},{4,5},{5,6},{6,7},{7,8},{8,9},{9,10},{10,1... | collective-permute-start | bytes 27656 | tf_op jit(solution)/shard_map/ppermute | solution.py:26
  152.5 7.0 %collective-permute-start.22 = (f32[1,8,64]{2,1,0:T(8,128)S(1)}, f32[1,8,64]{2,1,0:T(8,128)S(1)}, u32[]{:S(2)}, u32[]{:S(2)}) collective-permute-start(f32[1,8,64]{2,1,0:T(8,128)S(1)} %get-tuple-element.183), channel_id=1, source_target_pairs={{0,16},{16,32},{32,48},{48,64},{64,80},{80,96},{96,112},{112,128},... | collective-permute-start | bytes 6152 | tf_op jit(solution)/shard_map/ppermute | solution.py:26
  159.6 7.1 %collective-permute-start.24 = (f32[4,1,64]{2,1,0:T(1,128)S(1)}, f32[4,1,64]{2,1,0:T(1,128)S(1)}, u32[]{:S(2)}, u32[]{:S(2)}) collective-permute-start(f32[4,1,64]{2,1,0:T(1,128)S(1)} %get-tuple-element.152), channel_id=1, source_target_pairs={{0,1},{1,2},{2,3},{3,4},{4,5},{5,6},{6,7},{7,8},{8,9},{9,10},{10,1... | collective-permute-start | bytes 3080 | tf_op jit(solution)/shard_map/ppermute | solution.py:26
  171.7 7.1 %collective-permute-start.25 = (f32[3,1,4,32]{3,2,1,0:T(4,128)S(1)}, f32[3,1,4,32]{3,2,1,0:T(4,128)S(1)}, u32[]{:S(2)}, u32[]{:S(2)}) collective-permute-start(f32[3,1,4,32]{3,2,1,0:T(4,128)S(1)} %pad_maximum_fusion.58), channel_id=1, source_target_pairs={{0,16},{16,32},{32,48},{48,64},{64,80},{80,96},{96,112},{112,128},... | collective-permute-start | bytes 4616 | tf_op jit(solution)/shard_map/ppermute | solution.py:26
  179.4 8.7 %collective-permute-start.28 = (f32[3,3,1,32]{3,2,1,0:T(1,128)}, f32[3,3,1,32]{3,2,1,0:T(1,128)}, u32[]{:S(2)}, u32[]{:S(2)}) collective-permute-start(f32[3,3,1,32]{3,2,1,0:T(1,128)} %get-tuple-element.148), channel_id=1, source_target_pairs={{1,0},{2,1},{3,2},{4,3},{5,4},{6,5},{7,6},{8,7},{9,8},{10,9},{11,1... | collective-permute-start | bytes 3464 | tf_op jit(solution)/shard_map/ppermute | solution.py:27
  184.8 7.0 %collective-permute-start.27 = (f32[3,3,1,32]{3,2,1,0:T(1,128)}, f32[3,3,1,32]{3,2,1,0:T(1,128)}, u32[]{:S(2)}, u32[]{:S(2)}) collective-permute-start(f32[3,3,1,32]{3,2,1,0:T(1,128)} %get-tuple-element.147), channel_id=1, source_target_pairs={{0,1},{1,2},{2,3},{3,4},{4,5},{5,6},{6,7},{7,8},{8,9},{9,10},{10,1... | collective-permute-start | bytes 3464 | tf_op jit(solution)/shard_map/ppermute | solution.py:26
  195.3 7.0 %collective-permute-start.29 = (f32[2,1,4,32]{3,2,1,0:T(4,128)S(1)}, f32[2,1,4,32]{3,2,1,0:T(4,128)S(1)}, u32[]{:S(2)}, u32[]{:S(2)}) collective-permute-start(f32[2,1,4,32]{3,2,1,0:T(4,128)S(1)} %pad_maximum_fusion.68), channel_id=1, source_target_pairs={{0,16},{16,32},{32,48},{48,64},{64,80},{80,96},{96,112},{112,128},... | collective-permute-start | bytes 3080 | tf_op jit(solution)/shard_map/ppermute | solution.py:26
  202.9 5.9 %collective-permute-start.32 = (f32[2,3,1,32]{3,2,1,0:T(1,128)}, f32[2,3,1,32]{3,2,1,0:T(1,128)}, u32[]{:S(2)}, u32[]{:S(2)}) collective-permute-start(f32[2,3,1,32]{3,2,1,0:T(1,128)} %get-tuple-element.176), channel_id=1, source_target_pairs={{1,0},{2,1},{3,2},{4,3},{5,4},{6,5},{7,6},{8,7},{9,8},{10,9},{11,1... | collective-permute-start | bytes 2312 | tf_op jit(solution)/shard_map/ppermute | solution.py:27
  204.8 7.0 %collective-permute-start.31 = (f32[2,3,1,32]{3,2,1,0:T(1,128)}, f32[2,3,1,32]{3,2,1,0:T(1,128)}, u32[]{:S(2)}, u32[]{:S(2)}) collective-permute-start(f32[2,3,1,32]{3,2,1,0:T(1,128)} %get-tuple-element.175), channel_id=1, source_target_pairs={{0,1},{1,2},{2,3},{3,4},{4,5},{5,6},{6,7},{7,8},{8,9},{9,10},{10,1... | collective-permute-start | bytes 2312 | tf_op jit(solution)/shard_map/ppermute | solution.py:26
  215.4 7.0 %collective-permute-start.33 = (f32[2,1,4,32]{3,2,1,0:T(4,128)S(1)}, f32[2,1,4,32]{3,2,1,0:T(4,128)S(1)}, u32[]{:S(2)}, u32[]{:S(2)}) collective-permute-start(f32[2,1,4,32]{3,2,1,0:T(4,128)S(1)} %pad_maximum_fusion.69), channel_id=1, source_target_pairs={{0,16},{16,32},{32,48},{48,64},{64,80},{80,96},{96,112},{112,128},... | collective-permute-start | bytes 3080 | tf_op jit(solution)/shard_map/ppermute | solution.py:26
  223.0 5.9 %collective-permute-start.36 = (f32[2,3,1,32]{3,2,1,0:T(1,128)}, f32[2,3,1,32]{3,2,1,0:T(1,128)}, u32[]{:S(2)}, u32[]{:S(2)}) collective-permute-start(f32[2,3,1,32]{3,2,1,0:T(1,128)} %get-tuple-element.172), channel_id=1, source_target_pairs={{1,0},{2,1},{3,2},{4,3},{5,4},{6,5},{7,6},{8,7},{9,8},{10,9},{11,1... | collective-permute-start | bytes 2312 | tf_op jit(solution)/shard_map/ppermute | solution.py:27
  225.0 7.0 %collective-permute-start.35 = (f32[2,3,1,32]{3,2,1,0:T(1,128)}, f32[2,3,1,32]{3,2,1,0:T(1,128)}, u32[]{:S(2)}, u32[]{:S(2)}) collective-permute-start(f32[2,3,1,32]{3,2,1,0:T(1,128)} %get-tuple-element.171), channel_id=1, source_target_pairs={{0,1},{1,2},{2,3},{3,4},{4,5},{5,6},{6,7},{7,8},{8,9},{9,10},{10,1... | collective-permute-start | bytes 2312 | tf_op jit(solution)/shard_map/ppermute | solution.py:26
  235.5 7.0 %collective-permute-start.37 = (f32[2,1,4,32]{3,2,1,0:T(4,128)S(1)}, f32[2,1,4,32]{3,2,1,0:T(4,128)S(1)}, u32[]{:S(2)}, u32[]{:S(2)}) collective-permute-start(f32[2,1,4,32]{3,2,1,0:T(4,128)S(1)} %pad_maximum_fusion.70), channel_id=1, source_target_pairs={{0,16},{16,32},{32,48},{48,64},{64,80},{80,96},{96,112},{112,128},... | collective-permute-start | bytes 3080 | tf_op jit(solution)/shard_map/ppermute | solution.py:26
  243.2 5.9 %collective-permute-start.40 = (f32[2,3,1,32]{3,2,1,0:T(1,128)}, f32[2,3,1,32]{3,2,1,0:T(1,128)}, u32[]{:S(2)}, u32[]{:S(2)}) collective-permute-start(f32[2,3,1,32]{3,2,1,0:T(1,128)} %get-tuple-element.168), channel_id=1, source_target_pairs={{1,0},{2,1},{3,2},{4,3},{5,4},{6,5},{7,6},{8,7},{9,8},{10,9},{11,1... | collective-permute-start | bytes 2312 | tf_op jit(solution)/shard_map/ppermute | solution.py:27
  245.1 7.0 %collective-permute-start.39 = (f32[2,3,1,32]{3,2,1,0:T(1,128)}, f32[2,3,1,32]{3,2,1,0:T(1,128)}, u32[]{:S(2)}, u32[]{:S(2)}) collective-permute-start(f32[2,3,1,32]{3,2,1,0:T(1,128)} %get-tuple-element.167), channel_id=1, source_target_pairs={{0,1},{1,2},{2,3},{3,4},{4,5},{5,6},{6,7},{7,8},{8,9},{9,10},{10,1... | collective-permute-start | bytes 2312 | tf_op jit(solution)/shard_map/ppermute | solution.py:26
  255.6 7.0 %collective-permute-start.41 = (f32[2,1,4,32]{3,2,1,0:T(4,128)S(1)}, f32[2,1,4,32]{3,2,1,0:T(4,128)S(1)}, u32[]{:S(2)}, u32[]{:S(2)}) collective-permute-start(f32[2,1,4,32]{3,2,1,0:T(4,128)S(1)} %pad_maximum_fusion.71), channel_id=1, source_target_pairs={{0,16},{16,32},{32,48},{48,64},{64,80},{80,96},{96,112},{112,128},... | collective-permute-start | bytes 3080 | tf_op jit(solution)/shard_map/ppermute | solution.py:26
  265.2 7.0 %collective-permute-start.43 = (f32[2,3,1,32]{3,2,1,0:T(1,128)}, f32[2,3,1,32]{3,2,1,0:T(1,128)}, u32[]{:S(2)}, u32[]{:S(2)}) collective-permute-start(f32[2,3,1,32]{3,2,1,0:T(1,128)} %get-tuple-element.163), channel_id=1, source_target_pairs={{0,1},{1,2},{2,3},{3,4},{4,5},{5,6},{6,7},{7,8},{8,9},{9,10},{10,1... | collective-permute-start | bytes 2312 | tf_op jit(solution)/shard_map/ppermute | solution.py:26
  275.8 7.0 %collective-permute-start.45 = (f32[2,1,4,32]{3,2,1,0:T(4,128)S(1)}, f32[2,1,4,32]{3,2,1,0:T(4,128)S(1)}, u32[]{:S(2)}, u32[]{:S(2)}) collective-permute-start(f32[2,1,4,32]{3,2,1,0:T(4,128)S(1)} %pad_maximum_fusion.72), channel_id=1, source_target_pairs={{0,16},{16,32},{32,48},{48,64},{64,80},{80,96},{96,112},{112,128},... | collective-permute-start | bytes 3080 | tf_op jit(solution)/shard_map/ppermute | solution.py:26
  283.4 5.9 %collective-permute-start.48 = (f32[2,3,1,32]{3,2,1,0:T(1,128)}, f32[2,3,1,32]{3,2,1,0:T(1,128)}, u32[]{:S(2)}, u32[]{:S(2)}) collective-permute-start(f32[2,3,1,32]{3,2,1,0:T(1,128)} %get-tuple-element.160), channel_id=1, source_target_pairs={{1,0},{2,1},{3,2},{4,3},{5,4},{6,5},{7,6},{8,7},{9,8},{10,9},{11,1... | collective-permute-start | bytes 2312 | tf_op jit(solution)/shard_map/ppermute | solution.py:27
  285.3 7.0 %collective-permute-start.47 = (f32[2,3,1,32]{3,2,1,0:T(1,128)}, f32[2,3,1,32]{3,2,1,0:T(1,128)}, u32[]{:S(2)}, u32[]{:S(2)}) collective-permute-start(f32[2,3,1,32]{3,2,1,0:T(1,128)} %get-tuple-element.159), channel_id=1, source_target_pairs={{0,1},{1,2},{2,3},{3,4},{4,5},{5,6},{6,7},{7,8},{8,9},{9,10},{10,1... | collective-permute-start | bytes 2312 | tf_op jit(solution)/shard_map/ppermute | solution.py:26
  295.9 7.0 %collective-permute-start.49 = (f32[2,1,4,32]{3,2,1,0:T(4,128)S(1)}, f32[2,1,4,32]{3,2,1,0:T(4,128)S(1)}, u32[]{:S(2)}, u32[]{:S(2)}) collective-permute-start(f32[2,1,4,32]{3,2,1,0:T(4,128)S(1)} %pad_maximum_fusion.73), channel_id=1, source_target_pairs={{0,16},{16,32},{32,48},{48,64},{64,80},{80,96},{96,112},{112,128},... | collective-permute-start | bytes 3080 | tf_op jit(solution)/shard_map/ppermute | solution.py:26
  303.5 5.9 %collective-permute-start.52 = (f32[2,3,1,32]{3,2,1,0:T(1,128)}, f32[2,3,1,32]{3,2,1,0:T(1,128)}, u32[]{:S(2)}, u32[]{:S(2)}) collective-permute-start(f32[2,3,1,32]{3,2,1,0:T(1,128)} %get-tuple-element.156), channel_id=1, source_target_pairs={{1,0},{2,1},{3,2},{4,3},{5,4},{6,5},{7,6},{8,7},{9,8},{10,9},{11,1... | collective-permute-start | bytes 2312 | tf_op jit(solution)/shard_map/ppermute | solution.py:27
  305.5 7.0 %collective-permute-start.51 = (f32[2,3,1,32]{3,2,1,0:T(1,128)}, f32[2,3,1,32]{3,2,1,0:T(1,128)}, u32[]{:S(2)}, u32[]{:S(2)}) collective-permute-start(f32[2,3,1,32]{3,2,1,0:T(1,128)} %get-tuple-element.155), channel_id=1, source_target_pairs={{0,1},{1,2},{2,3},{3,4},{4,5},{5,6},{6,7},{7,8},{8,9},{9,10},{10,1... | collective-permute-start | bytes 2312 | tf_op jit(solution)/shard_map/ppermute | solution.py:26
  317.7 7.1 %collective-permute-start.53 = (f32[2,8,64]{2,1,0:T(8,128)S(1)}, f32[2,8,64]{2,1,0:T(8,128)S(1)}, u32[]{:S(2)}, u32[]{:S(2)}) collective-permute-start(f32[2,8,64]{2,1,0:T(8,128)S(1)} %broadcast_add_fusion), channel_id=1, source_target_pairs={{0,16},{16,32},{32,48},{48,64},{64,80},{80,96},{96,112},{112,128},... | collective-permute-start | bytes 12296 | tf_op jit(solution)/shard_map/ppermute | solution.py:26
  326.7 6.7 %collective-permute-start.55 = (f32[6,2,64]{2,1,0:T(2,128)S(1)}, f32[6,2,64]{2,1,0:T(2,128)S(1)}, u32[]{:S(2)}, u32[]{:S(2)}) collective-permute-start(f32[6,2,64]{2,1,0:T(2,128)S(1)} %get-tuple-element.133), channel_id=1, source_target_pairs={{0,1},{1,2},{2,3},{3,4},{4,5},{5,6},{6,7},{7,8},{8,9},{9,10},{10,1... | collective-permute-start | bytes 9224 | tf_op jit(solution)/shard_map/ppermute | solution.py:26
  337.4 7.1 %collective-permute-start.57 = (f32[2,1,8,64]{3,2,1,0:T(8,128)S(1)}, f32[2,1,8,64]{3,2,1,0:T(8,128)S(1)}, u32[]{:S(2)}, u32[]{:S(2)}) collective-permute-start(f32[2,1,8,64]{3,2,1,0:T(8,128)S(1)} %get-tuple-element.149), channel_id=1, source_target_pairs={{0,16},{16,32},{32,48},{48,64},{64,80},{80,96},{96,112},{112,128},... | collective-permute-start | bytes 12296 | tf_op jit(solution)/shard_map/ppermute | solution.py:26
  346.4 6.7 %collective-permute-start.59 = (f32[2,4,1,64]{3,2,1,0:T(1,128)S(1)}, f32[2,4,1,64]{3,2,1,0:T(1,128)S(1)}, u32[]{:S(2)}, u32[]{:S(2)}) collective-permute-start(f32[2,4,1,64]{3,2,1,0:T(1,128)S(1)} %get-tuple-element.127), channel_id=1, source_target_pairs={{0,1},{1,2},{2,3},{3,4},{4,5},{5,6},{6,7},{7,8},{8,9},{9,10},{10,1... | collective-permute-start | bytes 6152 | tf_op jit(solution)/shard_map/ppermute | solution.py:26
  360.6 7.3 %collective-permute-start.61 = (f32[3,16,128]{2,1,0:T(8,128)S(1)}, f32[3,16,128]{2,1,0:T(8,128)S(1)}, u32[]{:S(2)}, u32[]{:S(2)}) collective-permute-start(f32[3,16,128]{2,1,0:T(8,128)S(1)} %get-tuple-element.123), channel_id=1, source_target_pairs={{0,16},{16,32},{32,48},{48,64},{64,80},{80,96},{96,112},{112,128},... | collective-permute-start | bytes 73736 | tf_op jit(solution)/shard_map/ppermute | solution.py:26
  369.8 6.9 %collective-permute-start.63 = (f32[10,3,128]{2,1,0:T(4,128)S(1)}, f32[10,3,128]{2,1,0:T(4,128)S(1)}, u32[]{:S(2)}, u32[]{:S(2)}) collective-permute-start(f32[10,3,128]{2,1,0:T(4,128)S(1)} %get-tuple-element.104), channel_id=1, source_target_pairs={{0,1},{1,2},{2,3},{3,4},{4,5},{5,6},{6,7},{7,8},{8,9},{9,10},{10,1... | collective-permute-start | bytes 46088 | tf_op jit(solution)/shard_map/ppermute | solution.py:26
  388.6 8.0 %collective-permute-start.65 = (f32[3,32,256]{2,1,0:T(8,128)S(1)}, f32[3,32,256]{2,1,0:T(8,128)S(1)}, u32[]{:S(2)}, u32[]{:S(2)}) collective-permute-start(f32[3,32,256]{2,1,0:T(8,128)S(1)} %get-tuple-element.85), channel_id=1, source_target_pairs={{0,16},{16,32},{32,48},{48,64},{64,80},{80,96},{96,112},{112,128},... | collective-permute-start | bytes 294920 | tf_op jit(solution)/shard_map/ppermute | solution.py:26
  396.7 6.1 %collective-permute-start.68 = (f32[14,3,256]{2,0,1:T(8,128)S(1)}, f32[14,3,256]{2,0,1:T(8,128)S(1)}, u32[]{:S(2)}, u32[]{:S(2)}) collective-permute-start(f32[14,3,256]{2,0,1:T(8,128)S(1)} %copy.127), channel_id=1, source_target_pairs={{1,0},{2,1},{3,2},{4,3},{5,4},{6,5},{7,6},{8,7},{9,8},{10,9},{11,1... | collective-permute-start | bytes 129032 | tf_op jit(solution)/shard_map/ppermute | solution.py:27
  398.8 7.2 %collective-permute-start.67 = (f32[14,3,256]{2,0,1:T(8,128)S(1)}, f32[14,3,256]{2,0,1:T(8,128)S(1)}, u32[]{:S(2)}, u32[]{:S(2)}) collective-permute-start(f32[14,3,256]{2,0,1:T(8,128)S(1)} %copy.126), channel_id=1, source_target_pairs={{0,1},{1,2},{2,3},{3,4},{4,5},{5,6},{6,7},{7,8},{8,9},{9,10},{10,1... | collective-permute-start | bytes 129032 | tf_op jit(solution)/shard_map/ppermute | solution.py:26
  (112 other events, 1113.6 us)

commit v3 on v2

--- a/solution.py
+++ b/solution.py
@@ -11,21 +11,60 @@
 
 HELM_SHIFT = 0.05
 LOW_FRACTION = 0.1
-HALO_DEPTH = 3
+
+
+def halo_plan(size, depth):
+    plan, held = [], 0
+    while held < depth:
+        take = min(depth - held, (1 + (2 * held) // size) * size)
+        hop = -(-take // size)
+        plan.append((held, take, hop))
+        held += take
+    return plan
+
+
+def join(before, x, after, dim):
+    if dim < x.ndim - 2:
+        return jnp.concatenate([before, x, after], axis=dim)
+    wide = before.shape[dim] + x.shape[dim] + after.shape[dim]
+
+    def place(piece, at):
+        pads = [(0, 0, 0)] * x.ndim
+        pads[dim] = (at, wide - at - piece.shape[dim], 0)
+        return lax.pad(piece, jnp.zeros((), piece.dtype), pads)
+
+    return (
+        place(before, 0)
+        + place(x, before.shape[dim])
+        + place(after, before.shape[dim] + x.shape[dim])
+    )
 
 
 def extend(x, depth):
     dim0 = x.ndim - 3
     for axis, dim in (("gx", dim0), ("gy", dim0 + 1)):
         peers = lax.axis_size(axis)
-        length = x.shape[dim]
-        up = [(i, i + 1) for i in range(peers - 1)]
-        down = [(i + 1, i) for i in range(peers - 1)]
-        last = lax.slice_in_dim(x, length - depth, length, axis=dim)
-        first = lax.slice_in_dim(x, 0, depth, axis=dim)
-        before = lax.ppermute(last, axis, up)
-        after = lax.ppermute(first, axis, down)
-        x = jnp.concatenate([before, x, after], axis=dim)
+        size = x.shape[dim]
+        plan = halo_plan(size, depth)
+        cyclic = any(hop > 1 for _, _, hop in plan)
+        for held, take, hop in plan:
+            low = lax.slice_in_dim(x, hop * size - take, hop * size, axis=dim)
+            start = size + 2 * held - hop * size
+            high = lax.slice_in_dim(x, start, start + take, axis=dim)
+            if cyclic:
+                up = [(i, (i + hop) % peers) for i in range(peers)]
+                down = [(i, (i - hop) % peers) for i in range(peers)]
+            else:
+                up = [(i, i + hop) for i in range(peers - hop)]
+                down = [(i + hop, i) for i in range(peers - hop)]
+            before = lax.ppermute(low, axis, up)
+            after = lax.ppermute(high, axis, down)
+            x = join(before, x, after, dim)
+        if cyclic:
+            index = lax.axis_index(axis) * size + jnp.arange(size + 2 * depth) - depth
+            keep = (index >= 0) & (index < size * peers)
+            keep = keep.reshape([-1 if d == dim else 1 for d in range(x.ndim)])
+            x = jnp.where(keep, x, jnp.zeros_like(x))
     return x
 
 
@@ -66,7 +105,13 @@
 
 
 def prolong(values):
-    return jnp.repeat(jnp.repeat(jnp.repeat(values, 2, 0), 2, 1), 2, 2)
+    first, second, third = values.shape
+    doubled = jnp.broadcast_to(values[:, None], (first, 2, second, third))
+    doubled = doubled.reshape(2 * first, second, third)
+    spread1 = pool_matrix(2 * second, values.dtype).T
+    spread2 = pool_matrix(2 * third, values.dtype).T
+    doubled = jnp.einsum("ajk,jb->abk", doubled, spread1, precision=lax.Precision.HIGHEST)
+    return jnp.einsum("abk,kc->abc", doubled, spread2, precision=lax.Precision.HIGHEST)
 
 
 def inside_mask(shape, depth):
@@ -79,9 +124,8 @@
 
 
 class Level:
-    def __init__(self, source, alpha, beta, inv_spacing, upper):
-        n0, n1 = source.shape[0], source.shape[1]
-        self.depth = min(HALO_DEPTH, n0, n1)
+    def __init__(self, source, alpha, beta, inv_spacing, upper, depth):
+        self.depth = depth
         stacked = extend(jnp.stack([source, beta, alpha]), self.depth)
         self.source = stacked[0]
         beta_ext = stacked[1]
@@ -109,33 +153,24 @@
         return r
 
 
-def smooth(level, field, sweeps, start_zero, tail):
+def smooth(level, field, e, sweeps, start_zero):
     upper = level.upper
     lower = LOW_FRACTION * upper
     middle = 0.5 * (upper + lower)
     half_width = 0.5 * (upper - lower)
     scaled = middle / half_width
     factor = 1.0 / scaled
-    remaining = sweeps - 1 + tail if start_zero else sweeps + tail
     if start_zero:
         e = level.depth
         direction = level.source / middle
         field = direction
     else:
-        e = min(level.depth, remaining)
-        field = extend(field, e)
         residual = level.residual(field, e)
-        remaining -= 1
         e -= 1
         direction = residual / middle
         field = crop(field, 1) + direction
     for k in range(1, sweeps):
-        if e == 0:
-            e = min(level.depth, remaining)
-            both = extend(jnp.stack([field, direction]), e)
-            field, direction = both[0], both[1]
         residual = level.residual(field, e)
-        remaining -= 1
         e -= 1
         factor_new = 1.0 / (2.0 * scaled - factor)
         direction = (
@@ -144,10 +179,6 @@
         field = crop(field, 1) + direction
         factor = factor_new
     return field, e
-
-
-def to_depth_zero(field, e):
-    return crop(field, e)
 
 
 def all_max(values):
@@ -173,30 +204,39 @@
     maxima = jnp.stack([jnp.stack([jnp.max(alphas[i]), jnp.max(betas[i])]) for i in range(LEVELS)])
     maxima = all_max(maxima)
     uppers = [HELM_SHIFT * maxima[i, 0] + 12.0 * maxima[i, 1] / 4.0**i for i in range(LEVELS)]
+    out_depth = [0]
+    for level_idx in range(1, LEVELS):
+        out_depth.append(-(-(out_depth[-1] + POST_STEPS) // 2))
+    depths = [out_depth[i] + POST_STEPS + PRE_STEPS - 1 for i in range(LEVELS - 1)]
+    depths.append(out_depth[LEVELS - 1] + COARSE_STEPS - 1)
     levels = []
     fields = []
     source = rhs_field
     for level_idx in range(LEVELS - 1):
-        level = Level(source, alphas[level_idx], betas[level_idx], 1.0 / 4.0**level_idx, uppers[level_idx])
+        level = Level(
+            source,
+            alphas[level_idx],
+            betas[level_idx],
+            1.0 / 4.0**level_idx,
+            uppers[level_idx],
+            depths[level_idx],
+        )
         levels.append(level)
-        smoothed, e = smooth(level, None, PRE_STEPS, True, 1)
-        if e == 0:
-            e = 1
-            smoothed_ext = extend(smoothed, 1)
-        else:
-            smoothed_ext = smoothed
-        residual = level.residual(smoothed_ext, e)
-        source = restrict(to_depth_zero(residual, e - 1))
-        fields.append(to_depth_zero(smoothed_ext, e))
+        smoothed, e = smooth(level, None, 0, PRE_STEPS, True)
+        residual = level.residual(smoothed, e)
+        source = restrict(crop(residual, e - 1))
+        fields.append((smoothed, e))
     last = LEVELS - 1
-    level = Level(source, alphas[last], betas[last], 1.0 / 4.0**last, uppers[last])
-    coarse, e = smooth(level, None, COARSE_STEPS, True, 0)
-    coarse = to_depth_zero(coarse, e)
+    level = Level(source, alphas[last], betas[last], 1.0 / 4.0**last, uppers[last], depths[last])
+    coarse, e = smooth(level, None, 0, COARSE_STEPS, True)
     for level_idx in range(LEVELS - 2, -1, -1):
-        smoothed = fields[level_idx] + prolong(coarse)
-        coarse, e = smooth(levels[level_idx], smoothed, POST_STEPS, False, 0)
-        coarse = to_depth_zero(coarse, e)
-    return coarse
+        smoothed, have = fields[level_idx]
+        need = out_depth[level_idx] + POST_STEPS
+        correction = crop(prolong(coarse), 2 * e - need)
+        coarse, e = smooth(
+            levels[level_idx], crop(smoothed, have - need) + correction, need, POST_STEPS, False
+        )
+    return crop(coarse, e)
 
 
 def solution(mesh):

time: 413 us -> 273 us (0.66)
  the two profiles are of different devices: /device:TPU:408 before, /device:TPU:72 now
where the time goes in v3:
time: 273 us; the launch traced here: 271 us
  starting transfers between devices  135 us (49%)
  waiting for transfers between devices  62.1 us (23%)
  other arithmetic  29.2 us (11%)
  local copies, waits for them, and re-layouts  23.3 us (9%)
  matrix products  12.7 us (5%)
  between operations  8.52 us (3%)
    ppermute x13, starting transfers between devices, extend(): after = lax.ppermute(high, axis, down)  53.2 us
    ppermute x9, starting transfers between devices, all_max(): values = jnp.maximum(values, lax.ppermute(values, axis, pairs))  41.5 us
    ppermute x13, starting transfers between devices, extend(): before = lax.ppermute(low, axis, up)  40.6 us
    ppermute x13, waiting for transfers between devices, extend(): after = lax.ppermute(high, axis, down)  30.4 us
    ppermute x9, waiting for transfers between devices, all_max(): values = jnp.maximum(values, lax.ppermute(values, axis, pairs))  19.4 us
    ppermute x13, waiting for transfers between devices, extend(): before = lax.ppermute(low, axis, up)  12.3 us
    add x22, other arithmetic, smooth(): field = crop(field, 1) + direction  10.9 us
    broadcast_in_dim x21, local copies, waits for them, and re-layouts, residual(): r = jnp.where(crop(self.mask, self.depth - out), r, 0.0)  9.17 us
  transfers between devices with their start and end apart: 35, of which 22 were waited for; matrix products, arithmetic and copies ran while one was open for 5% of the time, Pallas kernels for 0%

profile of v3, /device:TPU:72, one launch (start us, length us, event | category | flops | bytes accessed | tf_op | source)
XLA Modules:
  0.0 271.1 jit_solution(14643501893295798948)
XLA Ops:
  13.0 2.4 maximum_bitcast_fusion.2
  15.5 2.6 maximum_bitcast_fusion
  18.1 1.9 collective-permute-start.4
  21.5 2.4 collective-permute-start
  23.9 5.3 %collective-permute-start.1 = (f32[3,5,32,256]{3,2,1,0:T(8,128)S(1)}, f32[3,5,32,256]{3,2,1,0:T(8,128)}, u32[]{:S(2)}, u32[]{:S(2)}) collective-permute-start(f32[3,5,32,256]{3,2,1,0:T(8,128)S(1)} %get-tuple-element.72), channel_id=1, source_target_pairs={{16,0},{32,16},{48,32},{64,48},{80,64},{96,80},{112,96},{128,112},... | collective-permute-start | bytes 1474568 | tf_op jit(solution)/shard_map/ppermute | solution.py:61
  37.8 1.9 collective-permute-start.5
  41.1 3.8 %collective-permute-start.2 = (f32[3,18,5,256]{3,2,1,0:T(8,128)S(1)}, f32[3,18,5,256]{3,2,1,0:T(8,128)S(1)}, u32[]{:S(2)}, u32[]{:S(2)}) collective-permute-start(f32[3,18,5,256]{3,2,1,0:T(8,128)S(1)} %get-tuple-element.62), channel_id=1, source_target_pairs={{0,1},{1,2},{2,3},{3,4},{4,5},{5,6},{6,7},{7,8},{8,9},{9,10},{10,1... | collective-permute-start | bytes 829448 | tf_op jit(solution)/shard_map/ppermute | solution.py:60
  45.0 2.0 collective-permute-start.3
  47.0 4.0 %collective-permute-start.6 = (f32[4,2]{1,0:T(4,128)S(1)}, f32[4,2]{1,0:T(4,128)S(1)}, u32[]{:S(2)}, u32[]{:S(2)}) collective-permute-start(f32[4,2]{1,0:T(4,128)S(1)} %fusion.540), channel_id=1, source_target_pairs={{0,64},{16,80},{32,96},{48,112},{64,0},{80,16},{96,32},{112,48},{1... | collective-permute-start | bytes 104 | tf_op jit(solution)/shard_map/ppermute | solution.py:193
  51.0 3.0 %collective-permute-done.6 = f32[4,2]{1,0:T(4,128)S(1)} collective-permute-done((f32[4,2]{1,0:T(4,128)S(1)}, f32[4,2]{1,0:T(4,128)S(1)}, u32[]{:S(2)}, u32[]{:S(2)}) %collective-permute-start.6) | collective-permute-done | bytes 64 | tf_op jit(solution)/shard_map/ppermute | solution.py:193
  54.0 1.9 collective-permute-start.7
  55.9 3.6 %collective-permute-done.7 = f32[4,2]{1,0:T(4,128)S(1)} collective-permute-done((f32[4,2]{1,0:T(4,128)S(1)}, f32[4,2]{1,0:T(4,128)S(1)}, u32[]{:S(2)}, u32[]{:S(2)}) %collective-permute-start.7) | collective-permute-done | bytes 64 | tf_op jit(solution)/shard_map/ppermute | solution.py:193
  59.5 4.2 %collective-permute-start.8 = (f32[4,2]{1,0:T(4,128)S(1)}, f32[4,2]{1,0:T(4,128)S(1)}, u32[]{:S(2)}, u32[]{:S(2)}) collective-permute-start(f32[4,2]{1,0:T(4,128)S(1)} %max.30), channel_id=1, source_target_pairs={{0,256},{16,272},{32,288},{48,304},{64,320},{80,336},{96,352},{112... | collective-permute-start | bytes 104 | tf_op jit(solution)/shard_map/ppermute | solution.py:193
  63.7 2.8 %collective-permute-done.8 = f32[4,2]{1,0:T(4,128)S(1)} collective-permute-done((f32[4,2]{1,0:T(4,128)S(1)}, f32[4,2]{1,0:T(4,128)S(1)}, u32[]{:S(2)}, u32[]{:S(2)}) %collective-permute-start.8) | collective-permute-done | bytes 64 | tf_op jit(solution)/shard_map/ppermute | solution.py:193
  66.5 4.9 %collective-permute-start.9 = (f32[4,2]{1,0:T(4,128)S(1)}, f32[4,2]{1,0:T(4,128)S(1)}, u32[]{:S(2)}, u32[]{:S(2)}) collective-permute-start(f32[4,2]{1,0:T(4,128)S(1)} %max.31), channel_id=1, source_target_pairs={{0,1},{1,0},{2,3},{3,2},{4,5},{5,4},{6,7},{7,6},{8,9},{9,8},{10,11... | collective-permute-start | bytes 104 | tf_op jit(solution)/shard_map/ppermute | solution.py:193
  74.9 4.4 %collective-permute-done.10 = f32[4,2]{1,0:T(4,128)S(1)} collective-permute-done((f32[4,2]{1,0:T(4,128)S(1)}, f32[4,2]{1,0:T(4,128)S(1)}, u32[]{:S(2)}, u32[]{:S(2)}) %collective-permute-start.10) | collective-permute-done | bytes 64 | tf_op jit(solution)/shard_map/ppermute | solution.py:193
  79.3 9.1 %collective-permute-start.11 = (f32[4,2]{1,0:T(4,128)S(1)}, f32[4,2]{1,0:T(4,128)S(1)}, u32[]{:S(2)}, u32[]{:S(2)}) collective-permute-start(f32[4,2]{1,0:T(4,128)S(1)} %max.33), channel_id=1, source_target_pairs={{0,4},{1,5},{2,6},{3,7},{4,0},{5,1},{6,2},{7,3},{8,12},{9,13},{10,... | collective-permute-start | bytes 104 | tf_op jit(solution)/shard_map/ppermute | solution.py:193
  90.0 11.6 %collective-permute-start.12 = (f32[4,2]{1,0:T(4,128)S(1)}, f32[4,2]{1,0:T(4,128)S(1)}, u32[]{:S(2)}, u32[]{:S(2)}) collective-permute-start(f32[4,2]{1,0:T(4,128)S(1)} %max.34), channel_id=1, source_target_pairs={{0,8},{1,9},{2,10},{3,11},{4,12},{5,13},{6,14},{7,15},{8,0},{9,1},... | collective-permute-start | bytes 104 | tf_op jit(solution)/shard_map/ppermute | solution.py:193
  101.6 2.5 collective-permute-done.12
  114.2 1.9 collective-permute-start.13
  116.8 5.7 %collective-permute-start.15 = (f32[3,4,16,128]{3,2,1,0:T(8,128)S(1)}, f32[3,4,16,128]{3,2,1,0:T(8,128)S(1)}, u32[]{:S(2)}, u32[]{:S(2)}) collective-permute-start(f32[3,4,16,128]{3,2,1,0:T(8,128)S(1)} %pad_maximum_fusion.2), channel_id=1, source_target_pairs={{16,0},{32,16},{48,32},{64,48},{80,64},{96,80},{112,96},{128,112},... | collective-permute-start | bytes 294920 | tf_op jit(solution)/shard_map/ppermute | solution.py:61
  122.6 1.9 collective-permute-start.14
  125.8 5.8 %collective-permute-start.16 = (f32[3,3,16,128]{3,2,1,0:T(8,128)S(1)}, f32[3,3,16,128]{3,2,1,0:T(8,128)S(1)}, u32[]{:S(2)}, u32[]{:S(2)}) collective-permute-start(f32[3,3,16,128]{3,2,1,0:T(8,128)S(1)} %slice.1975), channel_id=1, source_target_pairs={{16,0},{32,16},{48,32},{64,48},{80,64},{96,80},{112,96},{128,112},... | collective-permute-start | bytes 221192 | tf_op jit(solution)/shard_map/ppermute | solution.py:61
  134.3 3.9 %collective-permute-start.17 = (f32[3,18,7,128]{3,2,1,0:T(8,128)}, f32[3,18,7,128]{3,2,1,0:T(8,128)}, u32[]{:S(2)}, u32[]{:S(2)}) collective-permute-start(f32[3,18,7,128]{3,2,1,0:T(8,128)} %get-tuple-element.93), channel_id=1, source_target_pairs={{0,1},{1,2},{2,3},{3,4},{4,5},{5,6},{6,7},{7,8},{8,9},{9,10},{10,1... | collective-permute-start | bytes 580616 | tf_op jit(solution)/shard_map/ppermute | solution.py:60
  138.2 1.9 collective-permute-start.18
  142.5 4.1 %collective-permute-done.18 = f32[3,18,7,128]{3,2,1,0:T(8,128)} collective-permute-done((f32[3,18,7,128]{3,2,1,0:T(8,128)}, f32[3,18,7,128]{3,2,1,0:T(8,128)}, u32[]{:S(2)}, u32[]{:S(2)}) %collective-permute-start.18) | collective-permute-done | bytes 193568 | tf_op jit(solution)/shard_map/ppermute | solution.py:61
  151.0 1.9 collective-permute-start.19
  152.9 5.8 %collective-permute-start.20 = (f32[3,2,8,64]{3,2,1,0:T(8,128)S(1)}, f32[3,2,8,64]{3,2,1,0:T(8,128)S(1)}, u32[]{:S(2)}, u32[]{:S(2)}) collective-permute-start(f32[3,2,8,64]{3,2,1,0:T(8,128)S(1)} %pad_maximum_fusion.6), channel_id=1, source_target_pairs={{0,496},{16,0},{32,16},{48,32},{64,48},{80,64},{96,80},{112,96},{1... | collective-permute-start | bytes 36872 | tf_op jit(solution)/shard_map/ppermute | solution.py:61
  160.2 1.9 collective-permute-start.21
  162.2 6.0 %collective-permute-start.22 = (f32[3,6,8,64]{3,2,1,0:T(8,128)S(1)}, f32[3,6,8,64]{3,2,1,0:T(8,128)S(1)}, u32[]{:S(2)}, u32[]{:S(2)}) collective-permute-start(f32[3,6,8,64]{3,2,1,0:T(8,128)S(1)} %pad_maximum_fusion.3), channel_id=1, source_target_pairs={{0,464},{16,480},{32,496},{48,0},{64,16},{80,32},{96,48},{112,64},... | collective-permute-start | bytes 110600 | tf_op jit(solution)/shard_map/ppermute | solution.py:61
  170.3 5.1 %collective-permute-start.23 = (f32[3,18,8,64]{3,2,1,0:T(8,128)S(1)}, f32[3,18,8,64]{3,2,1,0:T(8,128)}, u32[]{:S(2)}, u32[]{:S(2)}) collective-permute-start(f32[3,18,8,64]{3,2,1,0:T(8,128)S(1)} %broadcast_select_fusion), channel_id=1, source_target_pairs={{0,1},{1,2},{2,3},{3,4},{4,5},{5,6},{6,7},{7,8},{8,9},{9,10},{10,1... | collective-permute-start | bytes 331784 | tf_op jit(solution)/shard_map/ppermute | solution.py:60
  175.4 2.1 collective-permute-start.24
  180.7 4.8 %collective-permute-done.24 = f32[3,18,8,64]{3,2,1,0:T(8,128)} collective-permute-done((f32[3,18,8,64]{3,2,1,0:T(8,128)S(1)}, f32[3,18,8,64]{3,2,1,0:T(8,128)}, u32[]{:S(2)}, u32[]{:S(2)}) %collective-permute-start.24) | collective-permute-done | bytes 110624 | tf_op jit(solution)/shard_map/ppermute | solution.py:61
  189.4 2.0 collective-permute-start.25
  191.4 5.6 %collective-permute-start.26 = (f32[3,1,4,32]{3,2,1,0:T(4,128)S(1)}, f32[3,1,4,32]{3,2,1,0:T(4,128)S(1)}, u32[]{:S(2)}, u32[]{:S(2)}) collective-permute-start(f32[3,1,4,32]{3,2,1,0:T(4,128)S(1)} %pad_maximum_fusion.8), channel_id=1, source_target_pairs={{0,496},{16,0},{32,16},{48,32},{64,48},{80,64},{96,80},{112,96},{1... | collective-permute-start | bytes 4616 | tf_op jit(solution)/shard_map/ppermute | solution.py:61
  198.4 2.3 collective-permute-start.27
  200.7 5.7 %collective-permute-start.29 = (f32[3,3,4,32]{3,2,1,0:T(4,128)S(1)}, f32[3,3,4,32]{3,2,1,0:T(4,128)S(1)}, u32[]{:S(2)}, u32[]{:S(2)}) collective-permute-start(f32[3,3,4,32]{3,2,1,0:T(4,128)S(1)} %pad_maximum_fusion.7), channel_id=1, source_target_pairs={{0,464},{16,480},{32,496},{48,0},{64,16},{80,32},{96,48},{112,64},... | collective-permute-start | bytes 13832 | tf_op jit(solution)/shard_map/ppermute | solution.py:61
  207.9 3.3 %collective-permute-start.28 = (f32[3,6,4,32]{3,2,1,0:T(4,128)S(1)}, f32[3,6,4,32]{3,2,1,0:T(4,128)S(1)}, u32[]{:S(2)}, u32[]{:S(2)}) collective-permute-start(f32[3,6,4,32]{3,2,1,0:T(4,128)S(1)} %get-tuple-element.150), channel_id=1, source_target_pairs={{0,96},{16,112},{32,128},{48,144},{64,160},{80,176},{96,192},{112,... | collective-permute-start | bytes 27656 | tf_op jit(solution)/shard_map/ppermute | solution.py:60
  211.2 3.4 %collective-permute-start.30 = (f32[3,6,4,32]{3,2,1,0:T(4,128)S(1)}, f32[3,6,4,32]{3,2,1,0:T(4,128)S(1)}, u32[]{:S(2)}, u32[]{:S(2)}) collective-permute-start(f32[3,6,4,32]{3,2,1,0:T(4,128)S(1)} %get-tuple-element.149), channel_id=1, source_target_pairs={{0,416},{16,432},{32,448},{48,464},{64,480},{80,496},{96,0},{112,1... | collective-permute-start | bytes 27656 | tf_op jit(solution)/shard_map/ppermute | solution.py:61
  215.0 3.3 %collective-permute-done.30 = f32[3,6,4,32]{3,2,1,0:T(4,128)S(1)} collective-permute-done((f32[3,6,4,32]{3,2,1,0:T(4,128)S(1)}, f32[3,6,4,32]{3,2,1,0:T(4,128)S(1)}, u32[]{:S(2)}, u32[]{:S(2)}) %collective-permute-start.30) | collective-permute-done | bytes 9248 | tf_op jit(solution)/shard_map/ppermute | solution.py:61
  218.4 3.9 %collective-permute-start.31 = (f32[3,21,4,32]{3,2,1,0:T(4,128)S(1)}, f32[3,21,4,32]{3,2,1,0:T(4,128)S(1)}, u32[]{:S(2)}, u32[]{:S(2)}) collective-permute-start(f32[3,21,4,32]{3,2,1,0:T(4,128)S(1)} %broadcast_select_fusion.1), channel_id=1, source_target_pairs={{0,1},{1,2},{2,3},{3,4},{4,5},{5,6},{6,7},{7,8},{8,9},{9,10},{10,1... | collective-permute-start | bytes 96776 | tf_op jit(solution)/shard_map/ppermute | solution.py:60
  222.3 1.9 collective-permute-start.32
  224.3 2.4 collective-permute-done.31
  226.6 3.9 %collective-permute-done.32 = f32[3,21,4,32]{3,2,1,0:T(4,128)S(1)} collective-permute-done((f32[3,21,4,32]{3,2,1,0:T(4,128)S(1)}, f32[3,21,4,32]{3,2,1,0:T(4,128)S(1)}, u32[]{:S(2)}, u32[]{:S(2)}) %collective-permute-start.32) | collective-permute-done | bytes 32288 | tf_op jit(solution)/shard_map/ppermute | solution.py:61
  232.3 6.1 %collective-permute-start.33 = (f32[3,21,6,32]{3,2,1,0:T(8,128)}, f32[3,21,6,32]{3,2,1,0:T(8,128)}, u32[]{:S(2)}, u32[]{:S(2)}) collective-permute-start(f32[3,21,6,32]{3,2,1,0:T(8,128)} %get-tuple-element.89), channel_id=1, source_target_pairs={{0,2},{1,3},{2,4},{3,5},{4,6},{5,7},{6,8},{7,9},{8,10},{9,11},{10,... | collective-permute-start | bytes 145160 | tf_op jit(solution)/shard_map/ppermute | solution.py:60
  238.3 1.9 collective-permute-start.34
  242.3 7.3 %collective-permute-done.33 = f32[3,21,6,32]{3,2,1,0:T(8,128)} collective-permute-done((f32[3,21,6,32]{3,2,1,0:T(8,128)}, f32[3,21,6,32]{3,2,1,0:T(8,128)}, u32[]{:S(2)}, u32[]{:S(2)}) %collective-permute-start.33) | collective-permute-done | bytes 48416 | tf_op jit(solution)/shard_map/ppermute | solution.py:60
  249.6 6.6 %collective-permute-done.34 = f32[3,21,6,32]{3,2,1,0:T(8,128)} collective-permute-done((f32[3,21,6,32]{3,2,1,0:T(8,128)}, f32[3,21,6,32]{3,2,1,0:T(8,128)}, u32[]{:S(2)}, u32[]{:S(2)}) %collective-permute-start.34) | collective-permute-done | bytes 48416 | tf_op jit(solution)/shard_map/ppermute | solution.py:61
  (411 shorter events, 75.6 us)
Async XLA Ops:
  0.0 21.5 %copy-start.60 = (s32[256]{0:T(256)}, s32[256]{0:T(256)S(1)}, u32[]{:S(2)}) copy-start(s32[256]{0:T(256)S(1)} %and_select_fusion.7) | copy-start | bytes 3076
  0.0 20.1 %copy-start.79 = (s32[32]{0:T(128)}, s32[32]{0:T(128)S(1)}, u32[]{:S(2)}) copy-start(s32[32]{0:T(128)S(1)} %and_select_fusion.8) | copy-start | bytes 388
  0.0 21.5 %copy-start.93 = (s32[16]{0:T(128)}, s32[16]{0:T(128)S(1)}, u32[]{:S(2)}) copy-start(s32[16]{0:T(128)S(1)} %and_select_fusion.6) | copy-start | bytes 196
  0.1 21.5 %copy-start.74 = (s32[128]{0:T(128)}, s32[128]{0:T(128)S(1)}, u32[]{:S(2)}) copy-start(s32[128]{0:T(128)S(1)} %and_select_fusion.5) | copy-start | bytes 1540
  0.1 21.4 %copy-start.91 = (s32[8]{0:T(128)}, s32[8]{0:T(128)S(1)}, u32[]{:S(2)}) copy-start(s32[8]{0:T(128)S(1)} %and_select_fusion.4) | copy-start | bytes 100
  0.1 21.4 %copy-start.88 = (s32[64]{0:T(128)}, s32[64]{0:T(128)S(1)}, u32[]{:S(2)}) copy-start(s32[64]{0:T(128)S(1)} %and_select_fusion.3) | copy-start | bytes 772
  18.1 19.7 %collective-permute-start.4 = (f32[4,2]{1,0:T(4,128)S(1)}, f32[4,2]{1,0:T(4,128)S(1)}, u32[]{:S(2)}, u32[]{:S(2)}) collective-permute-start(f32[4,2]{1,0:T(4,128)S(1)} %pad_maximum_fusion.9), channel_id=1, source_target_pairs={{0,16},{16,0},{32,48},{48,32},{64,80},{80,64},{96,112},{112,96},{1... | collective-permute-start | bytes 104 | tf_op jit(solution)/shard_map/ppermute | solution.py:193
  20.1 19.7 %copy-start.43 = (f32[8,32,256]{2,1,0:T(8,128)S(1)}, f32[8,32,256]{2,1,0:T(8,128)}, u32[]{:S(2)}) copy-start(f32[8,32,256]{2,1,0:T(8,128)} %param.5) | copy-start | bytes 786436
  20.1 19.7 %copy-start.44 = (f32[8,32,256]{2,1,0:T(8,128)S(1)}, f32[8,32,256]{2,1,0:T(8,128)}, u32[]{:S(2)}) copy-start(f32[8,32,256]{2,1,0:T(8,128)} %param.4) | copy-start | bytes 786436
  21.5 18.2 %collective-permute-start = (f32[3,5,32,256]{3,2,1,0:T(8,128)S(1)}, f32[3,5,32,256]{3,2,1,0:T(8,128)S(1)}, u32[]{:S(2)}, u32[]{:S(2)}) collective-permute-start(f32[3,5,32,256]{3,2,1,0:T(8,128)S(1)} %get-tuple-element.71), channel_id=1, source_target_pairs={{0,16},{16,32},{32,48},{48,64},{64,80},{80,96},{96,112},{112,128},... | collective-permute-start | bytes 1474568 | tf_op jit(solution)/shard_map/ppermute | solution.py:60
  23.9 15.8 %collective-permute-start.1 = (f32[3,5,32,256]{3,2,1,0:T(8,128)S(1)}, f32[3,5,32,256]{3,2,1,0:T(8,128)}, u32[]{:S(2)}, u32[]{:S(2)}) collective-permute-start(f32[3,5,32,256]{3,2,1,0:T(8,128)S(1)} %get-tuple-element.72), channel_id=1, source_target_pairs={{16,0},{32,16},{48,32},{64,48},{80,64},{96,80},{112,96},{128,112},... | collective-permute-start | bytes 1474568 | tf_op jit(solution)/shard_map/ppermute | solution.py:61
  37.8 9.2 %collective-permute-start.5 = (f32[4,2]{1,0:T(4,128)S(1)}, f32[4,2]{1,0:T(4,128)S(1)}, u32[]{:S(2)}, u32[]{:S(2)}) collective-permute-start(f32[4,2]{1,0:T(4,128)S(1)} %fusion.471), channel_id=1, source_target_pairs={{0,32},{16,48},{32,0},{48,16},{64,96},{80,112},{96,64},{112,80},{1... | collective-permute-start | bytes 104 | tf_op jit(solution)/shard_map/ppermute | solution.py:193
  41.1 65.2 %collective-permute-start.2 = (f32[3,18,5,256]{3,2,1,0:T(8,128)S(1)}, f32[3,18,5,256]{3,2,1,0:T(8,128)S(1)}, u32[]{:S(2)}, u32[]{:S(2)}) collective-permute-start(f32[3,18,5,256]{3,2,1,0:T(8,128)S(1)} %get-tuple-element.62), channel_id=1, source_target_pairs={{0,1},{1,2},{2,3},{3,4},{4,5},{5,6},{6,7},{7,8},{8,9},{9,10},{10,1... | collective-permute-start | bytes 829448 | tf_op jit(solution)/shard_map/ppermute | solution.py:60
  45.0 61.3 %collective-permute-start.3 = (f32[3,18,5,256]{3,2,1,0:T(8,128)S(1)}, f32[3,18,5,256]{3,2,1,0:T(8,128)}, u32[]{:S(2)}, u32[]{:S(2)}) collective-permute-start(f32[3,18,5,256]{3,2,1,0:T(8,128)S(1)} %get-tuple-element.63), channel_id=1, source_target_pairs={{1,0},{2,1},{3,2},{4,3},{5,4},{6,5},{7,6},{8,7},{9,8},{10,9},{11,1... | collective-permute-start | bytes 829448 | tf_op jit(solution)/shard_map/ppermute | solution.py:61
  47.0 7.0 %collective-permute-start.6 = (f32[4,2]{1,0:T(4,128)S(1)}, f32[4,2]{1,0:T(4,128)S(1)}, u32[]{:S(2)}, u32[]{:S(2)}) collective-permute-start(f32[4,2]{1,0:T(4,128)S(1)} %fusion.540), channel_id=1, source_target_pairs={{0,64},{16,80},{32,96},{48,112},{64,0},{80,16},{96,32},{112,48},{1... | collective-permute-start | bytes 104 | tf_op jit(solution)/shard_map/ppermute | solution.py:193
  54.0 5.5 %collective-permute-start.7 = (f32[4,2]{1,0:T(4,128)S(1)}, f32[4,2]{1,0:T(4,128)S(1)}, u32[]{:S(2)}, u32[]{:S(2)}) collective-permute-start(f32[4,2]{1,0:T(4,128)S(1)} %max.29), channel_id=1, source_target_pairs={{0,128},{16,144},{32,160},{48,176},{64,192},{80,208},{96,224},{112... | collective-permute-start | bytes 104 | tf_op jit(solution)/shard_map/ppermute | solution.py:193
  59.5 7.0 %collective-permute-start.8 = (f32[4,2]{1,0:T(4,128)S(1)}, f32[4,2]{1,0:T(4,128)S(1)}, u32[]{:S(2)}, u32[]{:S(2)}) collective-permute-start(f32[4,2]{1,0:T(4,128)S(1)} %max.30), channel_id=1, source_target_pairs={{0,256},{16,272},{32,288},{48,304},{64,320},{80,336},{96,352},{112... | collective-permute-start | bytes 104 | tf_op jit(solution)/shard_map/ppermute | solution.py:193
  66.5 6.5 %collective-permute-start.9 = (f32[4,2]{1,0:T(4,128)S(1)}, f32[4,2]{1,0:T(4,128)S(1)}, u32[]{:S(2)}, u32[]{:S(2)}) collective-permute-start(f32[4,2]{1,0:T(4,128)S(1)} %max.31), channel_id=1, source_target_pairs={{0,1},{1,0},{2,3},{3,2},{4,5},{5,4},{6,7},{7,6},{8,9},{9,8},{10,11... | collective-permute-start | bytes 104 | tf_op jit(solution)/shard_map/ppermute | solution.py:193
  73.0 6.4 %collective-permute-start.10 = (f32[4,2]{1,0:T(4,128)S(1)}, f32[4,2]{1,0:T(4,128)S(1)}, u32[]{:S(2)}, u32[]{:S(2)}) collective-permute-start(f32[4,2]{1,0:T(4,128)S(1)} %max.32), channel_id=1, source_target_pairs={{0,2},{1,3},{2,0},{3,1},{4,6},{5,7},{6,4},{7,5},{8,10},{9,11},{10,... | collective-permute-start | bytes 104 | tf_op jit(solution)/shard_map/ppermute | solution.py:193
  79.3 10.6 %collective-permute-start.11 = (f32[4,2]{1,0:T(4,128)S(1)}, f32[4,2]{1,0:T(4,128)S(1)}, u32[]{:S(2)}, u32[]{:S(2)}) collective-permute-start(f32[4,2]{1,0:T(4,128)S(1)} %max.33), channel_id=1, source_target_pairs={{0,4},{1,5},{2,6},{3,7},{4,0},{5,1},{6,2},{7,3},{8,12},{9,13},{10,... | collective-permute-start | bytes 104 | tf_op jit(solution)/shard_map/ppermute | solution.py:193
  90.0 14.2 %collective-permute-start.12 = (f32[4,2]{1,0:T(4,128)S(1)}, f32[4,2]{1,0:T(4,128)S(1)}, u32[]{:S(2)}, u32[]{:S(2)}) collective-permute-start(f32[4,2]{1,0:T(4,128)S(1)} %max.34), channel_id=1, source_target_pairs={{0,8},{1,9},{2,10},{3,11},{4,12},{5,13},{6,14},{7,15},{8,0},{9,1},... | collective-permute-start | bytes 104 | tf_op jit(solution)/shard_map/ppermute | solution.py:193
  113.3 26.8 %copy-start.55 = (pred[18,24,1]{1,0,2:T(8,128)(4,1)S(1)}, pred[18,24,1]{1,0,2:T(8,128)(4,1)}, u32[]{:S(2)}) copy-start(pred[18,24,1]{1,0,2:T(8,128)(4,1)} %copy-done.54) | copy-start | bytes 1300
  114.2 8.4 %collective-permute-start.13 = (f32[3,4,16,128]{3,2,1,0:T(8,128)S(1)}, f32[3,4,16,128]{3,2,1,0:T(8,128)S(1)}, u32[]{:S(2)}, u32[]{:S(2)}) collective-permute-start(f32[3,4,16,128]{3,2,1,0:T(8,128)S(1)} %pad_maximum_fusion.2), channel_id=1, source_target_pairs={{0,16},{16,32},{32,48},{48,64},{64,80},{80,96},{96,112},{112,128},... | collective-permute-start | bytes 294920 | tf_op jit(solution)/shard_map/ppermute | solution.py:60
  116.8 8.9 %collective-permute-start.15 = (f32[3,4,16,128]{3,2,1,0:T(8,128)S(1)}, f32[3,4,16,128]{3,2,1,0:T(8,128)S(1)}, u32[]{:S(2)}, u32[]{:S(2)}) collective-permute-start(f32[3,4,16,128]{3,2,1,0:T(8,128)S(1)} %pad_maximum_fusion.2), channel_id=1, source_target_pairs={{16,0},{32,16},{48,32},{64,48},{80,64},{96,80},{112,96},{128,112},... | collective-permute-start | bytes 294920 | tf_op jit(solution)/shard_map/ppermute | solution.py:61
  122.6 8.9 %collective-permute-start.14 = (f32[3,3,16,128]{3,2,1,0:T(8,128)S(1)}, f32[3,3,16,128]{3,2,1,0:T(8,128)S(1)}, u32[]{:S(2)}, u32[]{:S(2)}) collective-permute-start(f32[3,3,16,128]{3,2,1,0:T(8,128)S(1)} %slice.1974), channel_id=1, source_target_pairs={{0,16},{16,32},{32,48},{48,64},{64,80},{80,96},{96,112},{112,128},... | collective-permute-start | bytes 221192 | tf_op jit(solution)/shard_map/ppermute | solution.py:60
  125.8 7.7 %collective-permute-start.16 = (f32[3,3,16,128]{3,2,1,0:T(8,128)S(1)}, f32[3,3,16,128]{3,2,1,0:T(8,128)S(1)}, u32[]{:S(2)}, u32[]{:S(2)}) collective-permute-start(f32[3,3,16,128]{3,2,1,0:T(8,128)S(1)} %slice.1975), channel_id=1, source_target_pairs={{16,0},{32,16},{48,32},{64,48},{80,64},{96,80},{112,96},{128,112},... | collective-permute-start | bytes 221192 | tf_op jit(solution)/shard_map/ppermute | solution.py:61
  134.3 8.1 %collective-permute-start.17 = (f32[3,18,7,128]{3,2,1,0:T(8,128)}, f32[3,18,7,128]{3,2,1,0:T(8,128)}, u32[]{:S(2)}, u32[]{:S(2)}) collective-permute-start(f32[3,18,7,128]{3,2,1,0:T(8,128)} %get-tuple-element.93), channel_id=1, source_target_pairs={{0,1},{1,2},{2,3},{3,4},{4,5},{5,6},{6,7},{7,8},{8,9},{9,10},{10,1... | collective-permute-start | bytes 580616 | tf_op jit(solution)/shard_map/ppermute | solution.py:60
  138.2 8.3 %collective-permute-start.18 = (f32[3,18,7,128]{3,2,1,0:T(8,128)}, f32[3,18,7,128]{3,2,1,0:T(8,128)}, u32[]{:S(2)}, u32[]{:S(2)}) collective-permute-start(f32[3,18,7,128]{3,2,1,0:T(8,128)} %get-tuple-element.94), channel_id=1, source_target_pairs={{1,0},{2,1},{3,2},{4,3},{5,4},{6,5},{7,6},{8,7},{9,8},{10,9},{11,1... | collective-permute-start | bytes 580616 | tf_op jit(solution)/shard_map/ppermute | solution.py:61
  149.9 20.2 %copy-start.85 = (pred[18]{0:T(512)(128)(4,1)S(1)}, pred[18]{0:T(512)(128)(4,1)}, u32[]{:S(2)}) copy-start(pred[18]{0:T(512)(128)(4,1)} %copy-done.84) | copy-start | bytes 58
  150.2 27.4 %copy-start.68 = (pred[12,18]{1,0:T(8,128)(4,1)S(1)}, pred[12,18]{1,0:T(8,128)(4,1)}, u32[]{:S(2)}) copy-start(pred[12,18]{1,0:T(8,128)(4,1)} %slice_bitcast_fusion.21) | copy-start | bytes 652
  151.0 7.8 %collective-permute-start.19 = (f32[3,2,8,64]{3,2,1,0:T(8,128)S(1)}, f32[3,2,8,64]{3,2,1,0:T(8,128)S(1)}, u32[]{:S(2)}, u32[]{:S(2)}) collective-permute-start(f32[3,2,8,64]{3,2,1,0:T(8,128)S(1)} %pad_maximum_fusion.6), channel_id=1, source_target_pairs={{0,16},{16,32},{32,48},{48,64},{64,80},{80,96},{96,112},{112,128},... | collective-permute-start | bytes 36872 | tf_op jit(solution)/shard_map/ppermute | solution.py:60
  152.9 7.3 %collective-permute-start.20 = (f32[3,2,8,64]{3,2,1,0:T(8,128)S(1)}, f32[3,2,8,64]{3,2,1,0:T(8,128)S(1)}, u32[]{:S(2)}, u32[]{:S(2)}) collective-permute-start(f32[3,2,8,64]{3,2,1,0:T(8,128)S(1)} %pad_maximum_fusion.6), channel_id=1, source_target_pairs={{0,496},{16,0},{32,16},{48,32},{64,48},{80,64},{96,80},{112,96},{1... | collective-permute-start | bytes 36872 | tf_op jit(solution)/shard_map/ppermute | solution.py:61
  160.2 8.1 %collective-permute-start.21 = (f32[3,6,8,64]{3,2,1,0:T(8,128)S(1)}, f32[3,6,8,64]{3,2,1,0:T(8,128)S(1)}, u32[]{:S(2)}, u32[]{:S(2)}) collective-permute-start(f32[3,6,8,64]{3,2,1,0:T(8,128)S(1)} %pad_maximum_fusion.3), channel_id=1, source_target_pairs={{0,48},{16,64},{32,80},{48,96},{64,112},{80,128},{96,144},{112,160... | collective-permute-start | bytes 110600 | tf_op jit(solution)/shard_map/ppermute | solution.py:60
  162.2 8.0 %collective-permute-start.22 = (f32[3,6,8,64]{3,2,1,0:T(8,128)S(1)}, f32[3,6,8,64]{3,2,1,0:T(8,128)S(1)}, u32[]{:S(2)}, u32[]{:S(2)}) collective-permute-start(f32[3,6,8,64]{3,2,1,0:T(8,128)S(1)} %pad_maximum_fusion.3), channel_id=1, source_target_pairs={{0,464},{16,480},{32,496},{48,0},{64,16},{80,32},{96,48},{112,64},... | collective-permute-start | bytes 110600 | tf_op jit(solution)/shard_map/ppermute | solution.py:61
  170.3 10.5 %collective-permute-start.23 = (f32[3,18,8,64]{3,2,1,0:T(8,128)S(1)}, f32[3,18,8,64]{3,2,1,0:T(8,128)}, u32[]{:S(2)}, u32[]{:S(2)}) collective-permute-start(f32[3,18,8,64]{3,2,1,0:T(8,128)S(1)} %broadcast_select_fusion), channel_id=1, source_target_pairs={{0,1},{1,2},{2,3},{3,4},{4,5},{5,6},{6,7},{7,8},{8,9},{9,10},{10,1... | collective-permute-start | bytes 331784 | tf_op jit(solution)/shard_map/ppermute | solution.py:60
  175.4 10.1 %collective-permute-start.24 = (f32[3,18,8,64]{3,2,1,0:T(8,128)S(1)}, f32[3,18,8,64]{3,2,1,0:T(8,128)}, u32[]{:S(2)}, u32[]{:S(2)}) collective-permute-start(f32[3,18,8,64]{3,2,1,0:T(8,128)S(1)} %broadcast_select_fusion), channel_id=1, source_target_pairs={{1,0},{2,1},{3,2},{4,3},{5,4},{6,5},{7,6},{8,7},{9,8},{10,9},{11,1... | collective-permute-start | bytes 331784 | tf_op jit(solution)/shard_map/ppermute | solution.py:61
  188.4 29.9 %copy-start.83 = (pred[21]{0:T(512)(128)(4,1)S(1)}, pred[21]{0:T(512)(128)(4,1)}, u32[]{:S(2)}) copy-start(pred[21]{0:T(512)(128)(4,1)} %copy-done.82) | copy-start | bytes 67
  188.9 67.2 %copy-start.87 = (pred[24]{0:T(512)(128)(4,1)S(1)}, pred[24]{0:T(512)(128)(4,1)}, u32[]{:S(2)}) copy-start(pred[24]{0:T(512)(128)(4,1)} %copy-done.86) | copy-start | bytes 76
  189.4 7.8 %collective-permute-start.25 = (f32[3,1,4,32]{3,2,1,0:T(4,128)S(1)}, f32[3,1,4,32]{3,2,1,0:T(4,128)S(1)}, u32[]{:S(2)}, u32[]{:S(2)}) collective-permute-start(f32[3,1,4,32]{3,2,1,0:T(4,128)S(1)} %pad_maximum_fusion.8), channel_id=1, source_target_pairs={{0,16},{16,32},{32,48},{48,64},{64,80},{80,96},{96,112},{112,128},... | collective-permute-start | bytes 4616 | tf_op jit(solution)/shard_map/ppermute | solution.py:60
  191.4 7.0 %collective-permute-start.26 = (f32[3,1,4,32]{3,2,1,0:T(4,128)S(1)}, f32[3,1,4,32]{3,2,1,0:T(4,128)S(1)}, u32[]{:S(2)}, u32[]{:S(2)}) collective-permute-start(f32[3,1,4,32]{3,2,1,0:T(4,128)S(1)} %pad_maximum_fusion.8), channel_id=1, source_target_pairs={{0,496},{16,0},{32,16},{48,32},{64,48},{80,64},{96,80},{112,96},{1... | collective-permute-start | bytes 4616 | tf_op jit(solution)/shard_map/ppermute | solution.py:61
  198.4 8.0 %collective-permute-start.27 = (f32[3,3,4,32]{3,2,1,0:T(4,128)S(1)}, f32[3,3,4,32]{3,2,1,0:T(4,128)S(1)}, u32[]{:S(2)}, u32[]{:S(2)}) collective-permute-start(f32[3,3,4,32]{3,2,1,0:T(4,128)S(1)} %pad_maximum_fusion.7), channel_id=1, source_target_pairs={{0,48},{16,64},{32,80},{48,96},{64,112},{80,128},{96,144},{112,160... | collective-permute-start | bytes 13832 | tf_op jit(solution)/shard_map/ppermute | solution.py:60
  200.7 7.1 %collective-permute-start.29 = (f32[3,3,4,32]{3,2,1,0:T(4,128)S(1)}, f32[3,3,4,32]{3,2,1,0:T(4,128)S(1)}, u32[]{:S(2)}, u32[]{:S(2)}) collective-permute-start(f32[3,3,4,32]{3,2,1,0:T(4,128)S(1)} %pad_maximum_fusion.7), channel_id=1, source_target_pairs={{0,464},{16,480},{32,496},{48,0},{64,16},{80,32},{96,48},{112,64},... | collective-permute-start | bytes 13832 | tf_op jit(solution)/shard_map/ppermute | solution.py:61
  207.9 7.0 %collective-permute-start.28 = (f32[3,6,4,32]{3,2,1,0:T(4,128)S(1)}, f32[3,6,4,32]{3,2,1,0:T(4,128)S(1)}, u32[]{:S(2)}, u32[]{:S(2)}) collective-permute-start(f32[3,6,4,32]{3,2,1,0:T(4,128)S(1)} %get-tuple-element.150), channel_id=1, source_target_pairs={{0,96},{16,112},{32,128},{48,144},{64,160},{80,176},{96,192},{112,... | collective-permute-start | bytes 27656 | tf_op jit(solution)/shard_map/ppermute | solution.py:60
  211.2 7.1 %collective-permute-start.30 = (f32[3,6,4,32]{3,2,1,0:T(4,128)S(1)}, f32[3,6,4,32]{3,2,1,0:T(4,128)S(1)}, u32[]{:S(2)}, u32[]{:S(2)}) collective-permute-start(f32[3,6,4,32]{3,2,1,0:T(4,128)S(1)} %get-tuple-element.149), channel_id=1, source_target_pairs={{0,416},{16,432},{32,448},{48,464},{64,480},{80,496},{96,0},{112,1... | collective-permute-start | bytes 27656 | tf_op jit(solution)/shard_map/ppermute | solution.py:61
  218.4 8.2 %collective-permute-start.31 = (f32[3,21,4,32]{3,2,1,0:T(4,128)S(1)}, f32[3,21,4,32]{3,2,1,0:T(4,128)S(1)}, u32[]{:S(2)}, u32[]{:S(2)}) collective-permute-start(f32[3,21,4,32]{3,2,1,0:T(4,128)S(1)} %broadcast_select_fusion.1), channel_id=1, source_target_pairs={{0,1},{1,2},{2,3},{3,4},{4,5},{5,6},{6,7},{7,8},{8,9},{9,10},{10,1... | collective-permute-start | bytes 96776 | tf_op jit(solution)/shard_map/ppermute | solution.py:60
  222.3 8.2 %collective-permute-start.32 = (f32[3,21,4,32]{3,2,1,0:T(4,128)S(1)}, f32[3,21,4,32]{3,2,1,0:T(4,128)S(1)}, u32[]{:S(2)}, u32[]{:S(2)}) collective-permute-start(f32[3,21,4,32]{3,2,1,0:T(4,128)S(1)} %broadcast_select_fusion.1), channel_id=1, source_target_pairs={{0,15},{1,0},{2,1},{3,2},{4,3},{5,4},{6,5},{7,6},{8,7},{9,8},{10,9... | collective-permute-start | bytes 96776 | tf_op jit(solution)/shard_map/ppermute | solution.py:61
  232.3 17.3 %collective-permute-start.33 = (f32[3,21,6,32]{3,2,1,0:T(8,128)}, f32[3,21,6,32]{3,2,1,0:T(8,128)}, u32[]{:S(2)}, u32[]{:S(2)}) collective-permute-start(f32[3,21,6,32]{3,2,1,0:T(8,128)} %get-tuple-element.89), channel_id=1, source_target_pairs={{0,2},{1,3},{2,4},{3,5},{4,6},{5,7},{6,8},{7,9},{8,10},{9,11},{10,... | collective-permute-start | bytes 145160 | tf_op jit(solution)/shard_map/ppermute | solution.py:60
  238.3 17.8 %collective-permute-start.34 = (f32[3,21,6,32]{3,2,1,0:T(8,128)}, f32[3,21,6,32]{3,2,1,0:T(8,128)}, u32[]{:S(2)}, u32[]{:S(2)}) collective-permute-start(f32[3,21,6,32]{3,2,1,0:T(8,128)} %get-tuple-element.90), channel_id=1, source_target_pairs={{0,14},{1,15},{2,0},{3,1},{4,2},{5,3},{6,4},{7,5},{8,6},{9,7},{10,... | collective-permute-start | bytes 145160 | tf_op jit(solution)/shard_map/ppermute | solution.py:61
  (82 other events, 191.8 us)

commit v4 on v3

--- a/solution.py
+++ b/solution.py
@@ -46,6 +46,15 @@
         peers = lax.axis_size(axis)
         size = x.shape[dim]
         plan = halo_plan(size, depth)
+        if len(plan) > 2:
+            whole = lax.all_gather(x, axis, axis=dim, tiled=True)
+            pads = [(0, 0, 0)] * x.ndim
+            pads[dim] = (depth, depth, 0)
+            whole = lax.pad(whole, jnp.zeros((), x.dtype), pads)
+            x = lax.dynamic_slice_in_dim(
+                whole, lax.axis_index(axis) * size, size + 2 * depth, axis=dim
+            )
+            continue
         cyclic = any(hop > 1 for _, _, hop in plan)
         for held, take, hop in plan:
             low = lax.slice_in_dim(x, hop * size - take, hop * size, axis=dim)

time: 273 us -> 267 us (0.978)
  the two profiles are of different devices: /device:TPU:72 before, /device:TPU:98 now
where the time goes in v4:
time: 267 us; the launch traced here: 265 us
  starting transfers between devices  107 us (40%)
  waiting for transfers between devices  55.2 us (21%)
  local copies, waits for them, and re-layouts  28.6 us (11%)
  other arithmetic  26.9 us (10%)
  blocking collectives  26.4 us (10%)
  matrix products  12.7 us (5%)
  between operations  8.59 us (3%)
    ppermute x9, starting transfers between devices, all_max(): values = jnp.maximum(values, lax.ppermute(values, axis, pairs))  43.9 us
    ppermute x10, starting transfers between devices, extend(): before = lax.ppermute(low, axis, up)  32.2 us
    ppermute x10, starting transfers between devices, extend(): after = lax.ppermute(high, axis, down)  30.7 us
    all_gather x1, blocking collectives, extend(): whole = lax.all_gather(x, axis, axis=dim, tiled=True)  26.4 us
    ppermute x10, waiting for transfers between devices, extend(): after = lax.ppermute(high, axis, down)  26.4 us
    ppermute x9, waiting for transfers between devices, all_max(): values = jnp.maximum(values, lax.ppermute(values, axis, pairs))  18.3 us
    broadcast_in_dim x21, local copies, waits for them, and re-layouts, residual(): r = jnp.where(crop(self.mask, self.depth - out), r, 0.0)  13.4 us
    add x22, other arithmetic, smooth(): field = crop(field, 1) + direction  10.9 us
  transfers between devices with their start and end apart: 29, of which 19 were waited for; matrix products, arithmetic and copies ran while one was open for 7% of the time, Pallas kernels for 0%

profile of v4, /device:TPU:98, one launch (start us, length us, event | category | flops | bytes accessed | tf_op | source)
XLA Modules:
  0.0 265.2 jit_solution(154152377065473441)
XLA Ops:
  0.1 1.6 reduce_max.72
  1.7 1.6 reduce_max.73
  13.0 2.6 maximum_bitcast_fusion.2
  15.5 2.5 maximum_bitcast_fusion
  18.0 1.9 collective-permute-start.4
  21.4 2.4 collective-permute-start
  23.9 3.2 %collective-permute-start.1 = (f32[3,5,32,256]{3,2,1,0:T(8,128)S(1)}, f32[3,5,32,256]{3,2,1,0:T(8,128)S(1)}, u32[]{:S(2)}, u32[]{:S(2)}) collective-permute-start(f32[3,5,32,256]{3,2,1,0:T(8,128)S(1)} %get-tuple-element.72), channel_id=1, source_target_pairs={{16,0},{32,16},{48,32},{64,48},{80,64},{96,80},{112,96},{128,112},... | collective-permute-start | bytes 1474568 | tf_op jit(solution)/shard_map/ppermute | solution.py:70
  38.2 1.9 collective-permute-start.5
  40.5 5.0 %collective-permute-start.2 = (f32[3,18,5,256]{3,2,1,0:T(8,128)S(1)}, f32[3,18,5,256]{3,2,1,0:T(8,128)S(1)}, u32[]{:S(2)}, u32[]{:S(2)}) collective-permute-start(f32[3,18,5,256]{3,2,1,0:T(8,128)S(1)} %get-tuple-element.62), channel_id=1, source_target_pairs={{0,1},{1,2},{2,3},{3,4},{4,5},{5,6},{6,7},{7,8},{8,9},{9,10},{10,1... | collective-permute-start | bytes 829448 | tf_op jit(solution)/shard_map/ppermute | solution.py:69
  45.6 1.9 collective-permute-start.3
  47.6 4.8 %collective-permute-start.6 = (f32[4,2]{1,0:T(4,128)S(1)}, f32[4,2]{1,0:T(4,128)S(1)}, u32[]{:S(2)}, u32[]{:S(2)}) collective-permute-start(f32[4,2]{1,0:T(4,128)S(1)} %fusion.540), channel_id=1, source_target_pairs={{0,64},{16,80},{32,96},{48,112},{64,0},{80,16},{96,32},{112,48},{1... | collective-permute-start | bytes 104 | tf_op jit(solution)/shard_map/ppermute | solution.py:202
  52.4 2.1 collective-permute-done.6
  54.6 6.1 %collective-permute-start.7 = (f32[4,2]{1,0:T(4,128)S(1)}, f32[4,2]{1,0:T(4,128)S(1)}, u32[]{:S(2)}, u32[]{:S(2)}) collective-permute-start(f32[4,2]{1,0:T(4,128)S(1)} %max.29), channel_id=1, source_target_pairs={{0,128},{16,144},{32,160},{48,176},{64,192},{80,208},{96,224},{112... | collective-permute-start | bytes 104 | tf_op jit(solution)/shard_map/ppermute | solution.py:202
  60.7 1.5 collective-permute-done.7
  62.2 5.5 %collective-permute-start.8 = (f32[4,2]{1,0:T(4,128)S(1)}, f32[4,2]{1,0:T(4,128)S(1)}, u32[]{:S(2)}, u32[]{:S(2)}) collective-permute-start(f32[4,2]{1,0:T(4,128)S(1)} %max.30), channel_id=1, source_target_pairs={{0,256},{16,272},{32,288},{48,304},{64,320},{80,336},{96,352},{112... | collective-permute-start | bytes 104 | tf_op jit(solution)/shard_map/ppermute | solution.py:202
  69.3 1.9 collective-permute-start.9
  71.2 3.6 %collective-permute-done.9 = f32[4,2]{1,0:T(4,128)S(1)} collective-permute-done((f32[4,2]{1,0:T(4,128)S(1)}, f32[4,2]{1,0:T(4,128)S(1)}, u32[]{:S(2)}, u32[]{:S(2)}) %collective-permute-start.9) | collective-permute-done | bytes 64 | tf_op jit(solution)/shard_map/ppermute | solution.py:202
  74.8 1.9 collective-permute-start.10
  76.7 4.4 %collective-permute-done.10 = f32[4,2]{1,0:T(4,128)S(1)} collective-permute-done((f32[4,2]{1,0:T(4,128)S(1)}, f32[4,2]{1,0:T(4,128)S(1)}, u32[]{:S(2)}, u32[]{:S(2)}) %collective-permute-start.10) | collective-permute-done | bytes 64 | tf_op jit(solution)/shard_map/ppermute | solution.py:202
  81.2 9.1 %collective-permute-start.11 = (f32[4,2]{1,0:T(4,128)S(1)}, f32[4,2]{1,0:T(4,128)S(1)}, u32[]{:S(2)}, u32[]{:S(2)}) collective-permute-start(f32[4,2]{1,0:T(4,128)S(1)} %max.33), channel_id=1, source_target_pairs={{0,4},{1,5},{2,6},{3,7},{4,0},{5,1},{6,2},{7,3},{8,12},{9,13},{10,... | collective-permute-start | bytes 104 | tf_op jit(solution)/shard_map/ppermute | solution.py:202
  90.3 1.5 collective-permute-done.11
  91.8 10.6 %collective-permute-start.12 = (f32[4,2]{1,0:T(4,128)S(1)}, f32[4,2]{1,0:T(4,128)S(1)}, u32[]{:S(2)}, u32[]{:S(2)}) collective-permute-start(f32[4,2]{1,0:T(4,128)S(1)} %max.34), channel_id=1, source_target_pairs={{0,8},{1,9},{2,10},{3,11},{4,12},{5,13},{6,14},{7,15},{8,0},{9,1},... | collective-permute-start | bytes 104 | tf_op jit(solution)/shard_map/ppermute | solution.py:202
  102.5 3.5 %collective-permute-done.12 = f32[4,2]{1,0:T(4,128)S(1)} collective-permute-done((f32[4,2]{1,0:T(4,128)S(1)}, f32[4,2]{1,0:T(4,128)S(1)}, u32[]{:S(2)}, u32[]{:S(2)}) %collective-permute-start.12) | collective-permute-done | bytes 64 | tf_op jit(solution)/shard_map/ppermute | solution.py:202
  115.3 1.9 collective-permute-start.13
  117.3 3.6 %collective-permute-start.15 = (f32[3,4,16,128]{3,2,1,0:T(8,128)S(1)}, f32[3,4,16,128]{3,2,1,0:T(8,128)S(1)}, u32[]{:S(2)}, u32[]{:S(2)}) collective-permute-start(f32[3,4,16,128]{3,2,1,0:T(8,128)S(1)} %pad_maximum_fusion.2), channel_id=1, source_target_pairs={{16,0},{32,16},{48,32},{64,48},{80,64},{96,80},{112,96},{128,112},... | collective-permute-start | bytes 294920 | tf_op jit(solution)/shard_map/ppermute | solution.py:70
  121.2 1.9 collective-permute-start.14
  123.8 3.6 %collective-permute-start.16 = (f32[3,3,16,128]{3,2,1,0:T(8,128)S(1)}, f32[3,3,16,128]{3,2,1,0:T(8,128)S(1)}, u32[]{:S(2)}, u32[]{:S(2)}) collective-permute-start(f32[3,3,16,128]{3,2,1,0:T(8,128)S(1)} %slice.1971), channel_id=1, source_target_pairs={{16,0},{32,16},{48,32},{64,48},{80,64},{96,80},{112,96},{128,112},... | collective-permute-start | bytes 221192 | tf_op jit(solution)/shard_map/ppermute | solution.py:70
  127.5 1.9 collective-permute-done.16
  130.2 4.0 %collective-permute-start.17 = (f32[3,18,7,128]{3,2,1,0:T(8,128)}, f32[3,18,7,128]{3,2,1,0:T(8,128)}, u32[]{:S(2)}, u32[]{:S(2)}) collective-permute-start(f32[3,18,7,128]{3,2,1,0:T(8,128)} %get-tuple-element.93), channel_id=1, source_target_pairs={{0,1},{1,2},{2,3},{3,4},{4,5},{5,6},{6,7},{7,8},{8,9},{9,10},{10,1... | collective-permute-start | bytes 580616 | tf_op jit(solution)/shard_map/ppermute | solution.py:69
  134.3 1.9 collective-permute-start.18
  140.3 5.0 %collective-permute-done.18 = f32[3,18,7,128]{3,2,1,0:T(8,128)} collective-permute-done((f32[3,18,7,128]{3,2,1,0:T(8,128)}, f32[3,18,7,128]{3,2,1,0:T(8,128)}, u32[]{:S(2)}, u32[]{:S(2)}) %collective-permute-start.18) | collective-permute-done | bytes 193568 | tf_op jit(solution)/shard_map/ppermute | solution.py:70
  149.6 1.9 collective-permute-start.19
  151.6 3.6 %collective-permute-start.20 = (f32[3,2,8,64]{3,2,1,0:T(8,128)S(1)}, f32[3,2,8,64]{3,2,1,0:T(8,128)S(1)}, u32[]{:S(2)}, u32[]{:S(2)}) collective-permute-start(f32[3,2,8,64]{3,2,1,0:T(8,128)S(1)} %pad_maximum_fusion.4), channel_id=1, source_target_pairs={{0,496},{16,0},{32,16},{48,32},{64,48},{80,64},{96,80},{112,96},{1... | collective-permute-start | bytes 36872 | tf_op jit(solution)/shard_map/ppermute | solution.py:70
  156.7 5.2 %collective-permute-start.21 = (f32[3,6,8,64]{3,2,1,0:T(8,128)S(1)}, f32[3,6,8,64]{3,2,1,0:T(8,128)S(1)}, u32[]{:S(2)}, u32[]{:S(2)}) collective-permute-start(f32[3,6,8,64]{3,2,1,0:T(8,128)S(1)} %pad_maximum_fusion.3), channel_id=1, source_target_pairs={{0,48},{16,64},{32,80},{48,96},{64,112},{80,128},{96,144},{112,160... | collective-permute-start | bytes 110600 | tf_op jit(solution)/shard_map/ppermute | solution.py:69
  163.2 4.0 %collective-permute-start.22 = (f32[3,6,8,64]{3,2,1,0:T(8,128)S(1)}, f32[3,6,8,64]{3,2,1,0:T(8,128)S(1)}, u32[]{:S(2)}, u32[]{:S(2)}) collective-permute-start(f32[3,6,8,64]{3,2,1,0:T(8,128)S(1)} %pad_maximum_fusion.3), channel_id=1, source_target_pairs={{0,464},{16,480},{32,496},{48,0},{64,16},{80,32},{96,48},{112,64},... | collective-permute-start | bytes 110600 | tf_op jit(solution)/shard_map/ppermute | solution.py:70
  167.3 4.4 %collective-permute-done.22 = f32[3,6,8,64]{3,2,1,0:T(8,128)S(1)} collective-permute-done((f32[3,6,8,64]{3,2,1,0:T(8,128)S(1)}, f32[3,6,8,64]{3,2,1,0:T(8,128)S(1)}, u32[]{:S(2)}, u32[]{:S(2)}) %collective-permute-start.22) | collective-permute-done | bytes 36896 | tf_op jit(solution)/shard_map/ppermute | solution.py:70
  171.8 2.7 %collective-permute-start.23 = (f32[3,18,8,64]{3,2,1,0:T(8,128)S(1)}, f32[3,18,8,64]{3,2,1,0:T(8,128)}, u32[]{:S(2)}, u32[]{:S(2)}) collective-permute-start(f32[3,18,8,64]{3,2,1,0:T(8,128)S(1)} %broadcast_select_fusion), channel_id=1, source_target_pairs={{0,1},{1,2},{2,3},{3,4},{4,5},{5,6},{6,7},{7,8},{8,9},{9,10},{10,1... | collective-permute-start | bytes 331784 | tf_op jit(solution)/shard_map/ppermute | solution.py:69
  174.5 3.3 %collective-permute-start.24 = (f32[3,18,8,64]{3,2,1,0:T(8,128)S(1)}, f32[3,18,8,64]{3,2,1,0:T(8,128)}, u32[]{:S(2)}, u32[]{:S(2)}) collective-permute-start(f32[3,18,8,64]{3,2,1,0:T(8,128)S(1)} %broadcast_select_fusion), channel_id=1, source_target_pairs={{1,0},{2,1},{3,2},{4,3},{5,4},{6,5},{7,6},{8,7},{9,8},{10,9},{11,1... | collective-permute-start | bytes 331784 | tf_op jit(solution)/shard_map/ppermute | solution.py:70
  180.3 3.6 %collective-permute-done.24 = f32[3,18,8,64]{3,2,1,0:T(8,128)} collective-permute-done((f32[3,18,8,64]{3,2,1,0:T(8,128)S(1)}, f32[3,18,8,64]{3,2,1,0:T(8,128)}, u32[]{:S(2)}, u32[]{:S(2)}) %collective-permute-start.24) | collective-permute-done | bytes 110624 | tf_op jit(solution)/shard_map/ppermute | solution.py:70
  187.9 26.4 %all_gather.3 = f32[3,32,4,32]{3,2,1,0:T(4,128)S(1)} all-gather(f32[3,1,4,32]{3,2,1,0:T(4,128)S(1)} %pad_maximum_fusion.5), channel_id=1, replica_groups=mesh['gx'=32,'gy'=16] {'gx'}, dimensions={1}, use_global_device_ids=true | all-gather | bytes 50688 | tf_op jit(solution)/shard_map/all_gather | solution.py:50
  214.3 2.3 collective-permute-start.25
  216.6 3.5 %collective-permute-start.26 = (f32[3,21,4,32]{3,2,1,0:T(4,128)S(1)}, f32[3,21,4,32]{3,2,1,0:T(4,128)S(1)}, u32[]{:S(2)}, u32[]{:S(2)}) collective-permute-start(f32[3,21,4,32]{3,2,1,0:T(4,128)S(1)} %pad_dynamic-slice_fusion), channel_id=1, source_target_pairs={{0,15},{1,0},{2,1},{3,2},{4,3},{5,4},{6,5},{7,6},{8,7},{9,8},{10,9... | collective-permute-start | bytes 96776 | tf_op jit(solution)/shard_map/ppermute | solution.py:70
  220.2 1.7 collective-permute-done.25
  221.9 4.9 %collective-permute-done.26 = f32[3,21,4,32]{3,2,1,0:T(4,128)S(1)} collective-permute-done((f32[3,21,4,32]{3,2,1,0:T(4,128)S(1)}, f32[3,21,4,32]{3,2,1,0:T(4,128)S(1)}, u32[]{:S(2)}, u32[]{:S(2)}) %collective-permute-start.26) | collective-permute-done | bytes 32288 | tf_op jit(solution)/shard_map/ppermute | solution.py:70
  228.6 4.8 %collective-permute-start.27 = (f32[3,21,6,32]{3,2,1,0:T(8,128)}, f32[3,21,6,32]{3,2,1,0:T(8,128)}, u32[]{:S(2)}, u32[]{:S(2)}) collective-permute-start(f32[3,21,6,32]{3,2,1,0:T(8,128)} %get-tuple-element.89), channel_id=1, source_target_pairs={{0,2},{1,3},{2,4},{3,5},{4,6},{5,7},{6,8},{7,9},{8,10},{9,11},{10,... | collective-permute-start | bytes 145160 | tf_op jit(solution)/shard_map/ppermute | solution.py:69
  233.4 1.9 collective-permute-start.28
  237.3 6.3 %collective-permute-done.27 = f32[3,21,6,32]{3,2,1,0:T(8,128)} collective-permute-done((f32[3,21,6,32]{3,2,1,0:T(8,128)}, f32[3,21,6,32]{3,2,1,0:T(8,128)}, u32[]{:S(2)}, u32[]{:S(2)}) %collective-permute-start.27) | collective-permute-done | bytes 48416 | tf_op jit(solution)/shard_map/ppermute | solution.py:69
  243.7 6.4 %collective-permute-done.28 = f32[3,21,6,32]{3,2,1,0:T(8,128)} collective-permute-done((f32[3,21,6,32]{3,2,1,0:T(8,128)}, f32[3,21,6,32]{3,2,1,0:T(8,128)}, u32[]{:S(2)}, u32[]{:S(2)}) %collective-permute-start.28) | collective-permute-done | bytes 48416 | tf_op jit(solution)/shard_map/ppermute | solution.py:70
  (415 shorter events, 64.1 us)
Async XLA Ops:
  0.0 20.0 %copy-start.56 = (s32[256]{0:T(256)}, s32[256]{0:T(256)S(1)}, u32[]{:S(2)}) copy-start(s32[256]{0:T(256)S(1)} %and_select_fusion.7) | copy-start | bytes 3076
  0.0 20.0 %copy-start.105 = (s32[16]{0:T(128)}, s32[16]{0:T(128)S(1)}, u32[]{:S(2)}) copy-start(s32[16]{0:T(128)S(1)} %and_select_fusion.6) | copy-start | bytes 196
  0.1 20.0 %copy-start.72 = (s32[128]{0:T(128)}, s32[128]{0:T(128)S(1)}, u32[]{:S(2)}) copy-start(s32[128]{0:T(128)S(1)} %and_select_fusion.5) | copy-start | bytes 1540
  0.1 19.9 %copy-start.103 = (s32[8]{0:T(128)}, s32[8]{0:T(128)S(1)}, u32[]{:S(2)}) copy-start(s32[8]{0:T(128)S(1)} %and_select_fusion.4) | copy-start | bytes 100
  0.1 19.9 %copy-start.99 = (s32[64]{0:T(128)}, s32[64]{0:T(128)S(1)}, u32[]{:S(2)}) copy-start(s32[64]{0:T(128)S(1)} %and_select_fusion.3) | copy-start | bytes 772
  6.7 13.2 %copy-start.46 = (f32[4,16,128]{2,1,0:T(8,128)}, f32[4,16,128]{2,1,0:T(8,128)S(1)}, u32[]{:S(2)}) copy-start(f32[4,16,128]{2,1,0:T(8,128)S(1)} %get-tuple-element.168) | copy-start | bytes 98308
  7.6 12.3 %copy-start.48 = (f32[4,16,128]{2,1,0:T(8,128)}, f32[4,16,128]{2,1,0:T(8,128)S(1)}, u32[]{:S(2)}) copy-start(f32[4,16,128]{2,1,0:T(8,128)S(1)} %get-tuple-element.166) | copy-start | bytes 98308
  15.5 22.6 %copy-start.76 = (f32[1,2]{1,0:T(1,128)}, f32[1,2]{1,0:T(1,128)S(1)}, u32[]{:S(2)}) copy-start(f32[1,2]{1,0:T(1,128)S(1)} %get-tuple-element.171) | copy-start | bytes 28
  15.5 22.6 %copy-start.78 = (f32[1,2]{1,0:T(1,128)}, f32[1,2]{1,0:T(1,128)S(1)}, u32[]{:S(2)}) copy-start(f32[1,2]{1,0:T(1,128)S(1)} %get-tuple-element.172) | copy-start | bytes 28
  18.0 20.1 %copy-start.80 = (f32[1,2]{1,0:T(1,128)}, f32[1,2]{1,0:T(1,128)S(1)}, u32[]{:S(2)}) copy-start(f32[1,2]{1,0:T(1,128)S(1)} %get-tuple-element.169) | copy-start | bytes 28
  18.0 20.1 %copy-start.82 = (f32[1,2]{1,0:T(1,128)}, f32[1,2]{1,0:T(1,128)S(1)}, u32[]{:S(2)}) copy-start(f32[1,2]{1,0:T(1,128)S(1)} %get-tuple-element.170) | copy-start | bytes 28
  18.0 20.1 %collective-permute-start.4 = (f32[4,2]{1,0:T(4,128)S(1)}, f32[4,2]{1,0:T(4,128)S(1)}, u32[]{:S(2)}, u32[]{:S(2)}) collective-permute-start(f32[4,2]{1,0:T(4,128)S(1)} %pad_maximum_fusion.6), channel_id=1, source_target_pairs={{0,16},{16,0},{32,48},{48,32},{64,80},{80,64},{96,112},{112,96},{1... | collective-permute-start | bytes 104 | tf_op jit(solution)/shard_map/ppermute | solution.py:202
  20.0 20.1 %copy-start.43 = (f32[8,32,256]{2,1,0:T(8,128)S(1)}, f32[8,32,256]{2,1,0:T(8,128)}, u32[]{:S(2)}) copy-start(f32[8,32,256]{2,1,0:T(8,128)} %param.5) | copy-start | bytes 786436
  20.1 20.1 %copy-start.44 = (f32[8,32,256]{2,1,0:T(8,128)S(1)}, f32[8,32,256]{2,1,0:T(8,128)}, u32[]{:S(2)}) copy-start(f32[8,32,256]{2,1,0:T(8,128)} %param.4) | copy-start | bytes 786436
  20.1 20.1 %copy-start.45 = (f32[8,32,256]{2,1,0:T(8,128)S(1)}, f32[8,32,256]{2,1,0:T(8,128)}, u32[]{:S(2)}) copy-start(f32[8,32,256]{2,1,0:T(8,128)} %param.3) | copy-start | bytes 786436
  21.4 18.6 %collective-permute-start = (f32[3,5,32,256]{3,2,1,0:T(8,128)S(1)}, f32[3,5,32,256]{3,2,1,0:T(8,128)S(1)}, u32[]{:S(2)}, u32[]{:S(2)}) collective-permute-start(f32[3,5,32,256]{3,2,1,0:T(8,128)S(1)} %get-tuple-element.71), channel_id=1, source_target_pairs={{0,16},{16,32},{32,48},{48,64},{64,80},{80,96},{96,112},{112,128},... | collective-permute-start | bytes 1474568 | tf_op jit(solution)/shard_map/ppermute | solution.py:69
  23.9 16.3 %collective-permute-start.1 = (f32[3,5,32,256]{3,2,1,0:T(8,128)S(1)}, f32[3,5,32,256]{3,2,1,0:T(8,128)S(1)}, u32[]{:S(2)}, u32[]{:S(2)}) collective-permute-start(f32[3,5,32,256]{3,2,1,0:T(8,128)S(1)} %get-tuple-element.72), channel_id=1, source_target_pairs={{16,0},{32,16},{48,32},{64,48},{80,64},{96,80},{112,96},{128,112},... | collective-permute-start | bytes 1474568 | tf_op jit(solution)/shard_map/ppermute | solution.py:70
  28.5 11.6 %copy-start.58 = (pred[12,36]{1,0:T(8,128)(4,1)}, pred[12,36]{1,0:T(8,128)(4,1)S(1)}, u32[]{:S(2)}) copy-start(pred[12,36]{1,0:T(8,128)(4,1)S(1)} %slice_bitcast_fusion.27) | copy-start | bytes 1300
  30.6 9.5 %copy-start.95 = (pred[18]{0:T(512)(128)(4,1)}, pred[18]{0:T(512)(128)(4,1)S(1)}, u32[]{:S(2)}) copy-start(pred[18]{0:T(512)(128)(4,1)S(1)} %compare_and_fusion.3) | copy-start | bytes 58
  38.2 9.4 %collective-permute-start.5 = (f32[4,2]{1,0:T(4,128)S(1)}, f32[4,2]{1,0:T(4,128)S(1)}, u32[]{:S(2)}, u32[]{:S(2)}) collective-permute-start(f32[4,2]{1,0:T(4,128)S(1)} %fusion.471), channel_id=1, source_target_pairs={{0,32},{16,48},{32,0},{48,16},{64,96},{80,112},{96,64},{112,80},{1... | collective-permute-start | bytes 104 | tf_op jit(solution)/shard_map/ppermute | solution.py:202
  40.5 67.6 %collective-permute-start.2 = (f32[3,18,5,256]{3,2,1,0:T(8,128)S(1)}, f32[3,18,5,256]{3,2,1,0:T(8,128)S(1)}, u32[]{:S(2)}, u32[]{:S(2)}) collective-permute-start(f32[3,18,5,256]{3,2,1,0:T(8,128)S(1)} %get-tuple-element.62), channel_id=1, source_target_pairs={{0,1},{1,2},{2,3},{3,4},{4,5},{5,6},{6,7},{7,8},{8,9},{9,10},{10,1... | collective-permute-start | bytes 829448 | tf_op jit(solution)/shard_map/ppermute | solution.py:69
  45.6 62.5 %collective-permute-start.3 = (f32[3,18,5,256]{3,2,1,0:T(8,128)S(1)}, f32[3,18,5,256]{3,2,1,0:T(8,128)S(1)}, u32[]{:S(2)}, u32[]{:S(2)}) collective-permute-start(f32[3,18,5,256]{3,2,1,0:T(8,128)S(1)} %get-tuple-element.63), channel_id=1, source_target_pairs={{1,0},{2,1},{3,2},{4,3},{5,4},{6,5},{7,6},{8,7},{9,8},{10,9},{11,1... | collective-permute-start | bytes 829448 | tf_op jit(solution)/shard_map/ppermute | solution.py:70
  47.6 7.0 %collective-permute-start.6 = (f32[4,2]{1,0:T(4,128)S(1)}, f32[4,2]{1,0:T(4,128)S(1)}, u32[]{:S(2)}, u32[]{:S(2)}) collective-permute-start(f32[4,2]{1,0:T(4,128)S(1)} %fusion.540), channel_id=1, source_target_pairs={{0,64},{16,80},{32,96},{48,112},{64,0},{80,16},{96,32},{112,48},{1... | collective-permute-start | bytes 104 | tf_op jit(solution)/shard_map/ppermute | solution.py:202
  54.6 7.7 %collective-permute-start.7 = (f32[4,2]{1,0:T(4,128)S(1)}, f32[4,2]{1,0:T(4,128)S(1)}, u32[]{:S(2)}, u32[]{:S(2)}) collective-permute-start(f32[4,2]{1,0:T(4,128)S(1)} %max.29), channel_id=1, source_target_pairs={{0,128},{16,144},{32,160},{48,176},{64,192},{80,208},{96,224},{112... | collective-permute-start | bytes 104 | tf_op jit(solution)/shard_map/ppermute | solution.py:202
  62.2 7.1 %collective-permute-start.8 = (f32[4,2]{1,0:T(4,128)S(1)}, f32[4,2]{1,0:T(4,128)S(1)}, u32[]{:S(2)}, u32[]{:S(2)}) collective-permute-start(f32[4,2]{1,0:T(4,128)S(1)} %max.30), channel_id=1, source_target_pairs={{0,256},{16,272},{32,288},{48,304},{64,320},{80,336},{96,352},{112... | collective-permute-start | bytes 104 | tf_op jit(solution)/shard_map/ppermute | solution.py:202
  69.3 5.5 %collective-permute-start.9 = (f32[4,2]{1,0:T(4,128)S(1)}, f32[4,2]{1,0:T(4,128)S(1)}, u32[]{:S(2)}, u32[]{:S(2)}) collective-permute-start(f32[4,2]{1,0:T(4,128)S(1)} %max.31), channel_id=1, source_target_pairs={{0,1},{1,0},{2,3},{3,2},{4,5},{5,4},{6,7},{7,6},{8,9},{9,8},{10,11... | collective-permute-start | bytes 104 | tf_op jit(solution)/shard_map/ppermute | solution.py:202
  74.8 6.4 %collective-permute-start.10 = (f32[4,2]{1,0:T(4,128)S(1)}, f32[4,2]{1,0:T(4,128)S(1)}, u32[]{:S(2)}, u32[]{:S(2)}) collective-permute-start(f32[4,2]{1,0:T(4,128)S(1)} %max.32), channel_id=1, source_target_pairs={{0,2},{1,3},{2,0},{3,1},{4,6},{5,7},{6,4},{7,5},{8,10},{9,11},{10,... | collective-permute-start | bytes 104 | tf_op jit(solution)/shard_map/ppermute | solution.py:202
  81.2 10.6 %collective-permute-start.11 = (f32[4,2]{1,0:T(4,128)S(1)}, f32[4,2]{1,0:T(4,128)S(1)}, u32[]{:S(2)}, u32[]{:S(2)}) collective-permute-start(f32[4,2]{1,0:T(4,128)S(1)} %max.33), channel_id=1, source_target_pairs={{0,4},{1,5},{2,6},{3,7},{4,0},{5,1},{6,2},{7,3},{8,12},{9,13},{10,... | collective-permute-start | bytes 104 | tf_op jit(solution)/shard_map/ppermute | solution.py:202
  91.8 14.2 %collective-permute-start.12 = (f32[4,2]{1,0:T(4,128)S(1)}, f32[4,2]{1,0:T(4,128)S(1)}, u32[]{:S(2)}, u32[]{:S(2)}) collective-permute-start(f32[4,2]{1,0:T(4,128)S(1)} %max.34), channel_id=1, source_target_pairs={{0,8},{1,9},{2,10},{3,11},{4,12},{5,13},{6,14},{7,15},{8,0},{9,1},... | collective-permute-start | bytes 104 | tf_op jit(solution)/shard_map/ppermute | solution.py:202
  115.3 5.9 %collective-permute-start.13 = (f32[3,4,16,128]{3,2,1,0:T(8,128)S(1)}, f32[3,4,16,128]{3,2,1,0:T(8,128)S(1)}, u32[]{:S(2)}, u32[]{:S(2)}) collective-permute-start(f32[3,4,16,128]{3,2,1,0:T(8,128)S(1)} %pad_maximum_fusion.2), channel_id=1, source_target_pairs={{0,16},{16,32},{32,48},{48,64},{64,80},{80,96},{96,112},{112,128},... | collective-permute-start | bytes 294920 | tf_op jit(solution)/shard_map/ppermute | solution.py:69
  117.3 6.5 %collective-permute-start.15 = (f32[3,4,16,128]{3,2,1,0:T(8,128)S(1)}, f32[3,4,16,128]{3,2,1,0:T(8,128)S(1)}, u32[]{:S(2)}, u32[]{:S(2)}) collective-permute-start(f32[3,4,16,128]{3,2,1,0:T(8,128)S(1)} %pad_maximum_fusion.2), channel_id=1, source_target_pairs={{16,0},{32,16},{48,32},{64,48},{80,64},{96,80},{112,96},{128,112},... | collective-permute-start | bytes 294920 | tf_op jit(solution)/shard_map/ppermute | solution.py:70
  121.2 6.2 %collective-permute-start.14 = (f32[3,3,16,128]{3,2,1,0:T(8,128)S(1)}, f32[3,3,16,128]{3,2,1,0:T(8,128)S(1)}, u32[]{:S(2)}, u32[]{:S(2)}) collective-permute-start(f32[3,3,16,128]{3,2,1,0:T(8,128)S(1)} %slice.1970), channel_id=1, source_target_pairs={{0,16},{16,32},{32,48},{48,64},{64,80},{80,96},{96,112},{112,128},... | collective-permute-start | bytes 221192 | tf_op jit(solution)/shard_map/ppermute | solution.py:69
  123.8 5.6 %collective-permute-start.16 = (f32[3,3,16,128]{3,2,1,0:T(8,128)S(1)}, f32[3,3,16,128]{3,2,1,0:T(8,128)S(1)}, u32[]{:S(2)}, u32[]{:S(2)}) collective-permute-start(f32[3,3,16,128]{3,2,1,0:T(8,128)S(1)} %slice.1971), channel_id=1, source_target_pairs={{16,0},{32,16},{48,32},{64,48},{80,64},{96,80},{112,96},{128,112},... | collective-permute-start | bytes 221192 | tf_op jit(solution)/shard_map/ppermute | solution.py:70
  130.2 10.1 %collective-permute-start.17 = (f32[3,18,7,128]{3,2,1,0:T(8,128)}, f32[3,18,7,128]{3,2,1,0:T(8,128)}, u32[]{:S(2)}, u32[]{:S(2)}) collective-permute-start(f32[3,18,7,128]{3,2,1,0:T(8,128)} %get-tuple-element.93), channel_id=1, source_target_pairs={{0,1},{1,2},{2,3},{3,4},{4,5},{5,6},{6,7},{7,8},{8,9},{9,10},{10,1... | collective-permute-start | bytes 580616 | tf_op jit(solution)/shard_map/ppermute | solution.py:69
  134.3 11.0 %collective-permute-start.18 = (f32[3,18,7,128]{3,2,1,0:T(8,128)}, f32[3,18,7,128]{3,2,1,0:T(8,128)}, u32[]{:S(2)}, u32[]{:S(2)}) collective-permute-start(f32[3,18,7,128]{3,2,1,0:T(8,128)} %get-tuple-element.94), channel_id=1, source_target_pairs={{1,0},{2,1},{3,2},{4,3},{5,4},{6,5},{7,6},{8,7},{9,8},{10,9},{11,1... | collective-permute-start | bytes 580616 | tf_op jit(solution)/shard_map/ppermute | solution.py:70
  148.5 14.0 %copy-start.64 = (pred[12,18]{1,0:T(8,128)(4,1)S(1)}, pred[12,18]{1,0:T(8,128)(4,1)}, u32[]{:S(2)}) copy-start(pred[12,18]{1,0:T(8,128)(4,1)} %slice_bitcast_fusion.21) | copy-start | bytes 652
  148.7 23.1 %copy-start.96 = (pred[18]{0:T(512)(128)(4,1)S(1)}, pred[18]{0:T(512)(128)(4,1)}, u32[]{:S(2)}) copy-start(pred[18]{0:T(512)(128)(4,1)} %copy-done.95) | copy-start | bytes 58
  149.6 6.9 %collective-permute-start.19 = (f32[3,2,8,64]{3,2,1,0:T(8,128)S(1)}, f32[3,2,8,64]{3,2,1,0:T(8,128)S(1)}, u32[]{:S(2)}, u32[]{:S(2)}) collective-permute-start(f32[3,2,8,64]{3,2,1,0:T(8,128)S(1)} %pad_maximum_fusion.4), channel_id=1, source_target_pairs={{0,16},{16,32},{32,48},{48,64},{64,80},{80,96},{96,112},{112,128},... | collective-permute-start | bytes 36872 | tf_op jit(solution)/shard_map/ppermute | solution.py:69
  151.6 5.1 %collective-permute-start.20 = (f32[3,2,8,64]{3,2,1,0:T(8,128)S(1)}, f32[3,2,8,64]{3,2,1,0:T(8,128)S(1)}, u32[]{:S(2)}, u32[]{:S(2)}) collective-permute-start(f32[3,2,8,64]{3,2,1,0:T(8,128)S(1)} %pad_maximum_fusion.4), channel_id=1, source_target_pairs={{0,496},{16,0},{32,16},{48,32},{64,48},{80,64},{96,80},{112,96},{1... | collective-permute-start | bytes 36872 | tf_op jit(solution)/shard_map/ppermute | solution.py:70
  156.7 10.5 %collective-permute-start.21 = (f32[3,6,8,64]{3,2,1,0:T(8,128)S(1)}, f32[3,6,8,64]{3,2,1,0:T(8,128)S(1)}, u32[]{:S(2)}, u32[]{:S(2)}) collective-permute-start(f32[3,6,8,64]{3,2,1,0:T(8,128)S(1)} %pad_maximum_fusion.3), channel_id=1, source_target_pairs={{0,48},{16,64},{32,80},{48,96},{64,112},{80,128},{96,144},{112,160... | collective-permute-start | bytes 110600 | tf_op jit(solution)/shard_map/ppermute | solution.py:69
  163.2 8.5 %collective-permute-start.22 = (f32[3,6,8,64]{3,2,1,0:T(8,128)S(1)}, f32[3,6,8,64]{3,2,1,0:T(8,128)S(1)}, u32[]{:S(2)}, u32[]{:S(2)}) collective-permute-start(f32[3,6,8,64]{3,2,1,0:T(8,128)S(1)} %pad_maximum_fusion.3), channel_id=1, source_target_pairs={{0,464},{16,480},{32,496},{48,0},{64,16},{80,32},{96,48},{112,64},... | collective-permute-start | bytes 110600 | tf_op jit(solution)/shard_map/ppermute | solution.py:70
  171.8 8.4 %collective-permute-start.23 = (f32[3,18,8,64]{3,2,1,0:T(8,128)S(1)}, f32[3,18,8,64]{3,2,1,0:T(8,128)}, u32[]{:S(2)}, u32[]{:S(2)}) collective-permute-start(f32[3,18,8,64]{3,2,1,0:T(8,128)S(1)} %broadcast_select_fusion), channel_id=1, source_target_pairs={{0,1},{1,2},{2,3},{3,4},{4,5},{5,6},{6,7},{7,8},{8,9},{9,10},{10,1... | collective-permute-start | bytes 331784 | tf_op jit(solution)/shard_map/ppermute | solution.py:69
  174.5 9.4 %collective-permute-start.24 = (f32[3,18,8,64]{3,2,1,0:T(8,128)S(1)}, f32[3,18,8,64]{3,2,1,0:T(8,128)}, u32[]{:S(2)}, u32[]{:S(2)}) collective-permute-start(f32[3,18,8,64]{3,2,1,0:T(8,128)S(1)} %broadcast_select_fusion), channel_id=1, source_target_pairs={{1,0},{2,1},{3,2},{4,3},{5,4},{6,5},{7,6},{8,7},{9,8},{10,9},{11,1... | collective-permute-start | bytes 331784 | tf_op jit(solution)/shard_map/ppermute | solution.py:70
  187.2 62.8 %copy-start.98 = (pred[24]{0:T(512)(128)(4,1)S(1)}, pred[24]{0:T(512)(128)(4,1)}, u32[]{:S(2)}) copy-start(pred[24]{0:T(512)(128)(4,1)} %copy-done.97) | copy-start | bytes 76
  214.3 7.6 %collective-permute-start.25 = (f32[3,21,4,32]{3,2,1,0:T(4,128)S(1)}, f32[3,21,4,32]{3,2,1,0:T(4,128)S(1)}, u32[]{:S(2)}, u32[]{:S(2)}) collective-permute-start(f32[3,21,4,32]{3,2,1,0:T(4,128)S(1)} %pad_dynamic-slice_fusion), channel_id=1, source_target_pairs={{0,1},{1,2},{2,3},{3,4},{4,5},{5,6},{6,7},{7,8},{8,9},{9,10},{10,1... | collective-permute-start | bytes 96776 | tf_op jit(solution)/shard_map/ppermute | solution.py:69
  216.6 10.2 %collective-permute-start.26 = (f32[3,21,4,32]{3,2,1,0:T(4,128)S(1)}, f32[3,21,4,32]{3,2,1,0:T(4,128)S(1)}, u32[]{:S(2)}, u32[]{:S(2)}) collective-permute-start(f32[3,21,4,32]{3,2,1,0:T(4,128)S(1)} %pad_dynamic-slice_fusion), channel_id=1, source_target_pairs={{0,15},{1,0},{2,1},{3,2},{4,3},{5,4},{6,5},{7,6},{8,7},{9,8},{10,9... | collective-permute-start | bytes 96776 | tf_op jit(solution)/shard_map/ppermute | solution.py:70
  228.6 15.1 %collective-permute-start.27 = (f32[3,21,6,32]{3,2,1,0:T(8,128)}, f32[3,21,6,32]{3,2,1,0:T(8,128)}, u32[]{:S(2)}, u32[]{:S(2)}) collective-permute-start(f32[3,21,6,32]{3,2,1,0:T(8,128)} %get-tuple-element.89), channel_id=1, source_target_pairs={{0,2},{1,3},{2,4},{3,5},{4,6},{5,7},{6,8},{7,9},{8,10},{9,11},{10,... | collective-permute-start | bytes 145160 | tf_op jit(solution)/shard_map/ppermute | solution.py:69
  233.4 16.6 %collective-permute-start.28 = (f32[3,21,6,32]{3,2,1,0:T(8,128)}, f32[3,21,6,32]{3,2,1,0:T(8,128)}, u32[]{:S(2)}, u32[]{:S(2)}) collective-permute-start(f32[3,21,6,32]{3,2,1,0:T(8,128)} %get-tuple-element.90), channel_id=1, source_target_pairs={{0,14},{1,15},{2,0},{3,1},{4,2},{5,3},{6,4},{7,5},{8,6},{9,7},{10,... | collective-permute-start | bytes 145160 | tf_op jit(solution)/shard_map/ppermute | solution.py:70
  (88 other events, 175.7 us)

commit v5 on v4

--- a/solution.py
+++ b/solution.py
@@ -40,13 +40,13 @@
     )
 
 
-def extend(x, depth):
+def extend(x, depth, gather=False):
     dim0 = x.ndim - 3
     for axis, dim in (("gx", dim0), ("gy", dim0 + 1)):
         peers = lax.axis_size(axis)
         size = x.shape[dim]
         plan = halo_plan(size, depth)
-        if len(plan) > 2:
+        if gather or len(plan) > 2:
             whole = lax.all_gather(x, axis, axis=dim, tiled=True)
             pads = [(0, 0, 0)] * x.ndim
             pads[dim] = (depth, depth, 0)
@@ -133,9 +133,9 @@
 
 
 class Level:
-    def __init__(self, source, alpha, beta, inv_spacing, upper, depth):
+    def __init__(self, source, alpha, beta, inv_spacing, upper, depth, gather=False):
         self.depth = depth
-        stacked = extend(jnp.stack([source, beta, alpha]), self.depth)
+        stacked = extend(jnp.stack([source, beta, alpha]), self.depth, gather)
         self.source = stacked[0]
         beta_ext = stacked[1]
         self.alpha = stacked[2]
@@ -236,7 +236,9 @@
         source = restrict(crop(residual, e - 1))
         fields.append((smoothed, e))
     last = LEVELS - 1
-    level = Level(source, alphas[last], betas[last], 1.0 / 4.0**last, uppers[last], depths[last])
+    level = Level(
+        source, alphas[last], betas[last], 1.0 / 4.0**last, uppers[last], depths[last], True
+    )
     coarse, e = smooth(level, None, 0, COARSE_STEPS, True)
     for level_idx in range(LEVELS - 2, -1, -1):
         smoothed, have = fields[level_idx]

time: 267 us -> 292 us (1.094)
  the two profiles are of different devices: /device:TPU:98 before, /device:TPU:8 now
where the time goes in v5:
time: 292 us; the launch traced here: 290 us
  starting transfers between devices  102 us (35%)
  blocking collectives  73 us (25%)
  local copies, waits for them, and re-layouts  37.4 us (13%)
  other arithmetic  29.5 us (10%)
  waiting for transfers between devices  26.3 us (9%)
  matrix products  12.7 us (4%)
  between operations  8.42 us (3%)
    all_gather x2, blocking collectives, extend(): whole = lax.all_gather(x, axis, axis=dim, tiled=True)  73 us
    ppermute x9, starting transfers between devices, all_max(): values = jnp.maximum(values, lax.ppermute(values, axis, pairs))  49.6 us
    ppermute x8, starting transfers between devices, extend(): after = lax.ppermute(high, axis, down)  32.6 us
    broadcast_in_dim x28, local copies, waits for them, and re-layouts, residual(): r = jnp.where(crop(self.mask, self.depth - out), r, 0.0)  23.3 us
    ppermute x8, starting transfers between devices, extend(): before = lax.ppermute(low, axis, up)  20.3 us
    ppermute x9, waiting for transfers between devices, all_max(): values = jnp.maximum(values, lax.ppermute(values, axis, pairs))  14 us
    ppermute x8, waiting for transfers between devices, extend(): after = lax.ppermute(high, axis, down)  12.1 us
    add x22, other arithmetic, smooth(): field = crop(field, 1) + direction  11 us
  transfers between devices with their start and end apart: 25, of which 12 were waited for; matrix products, arithmetic and copies ran while one was open for 11% of the time, Pallas kernels for 0%

profile of v5, /device:TPU:8, one launch (start us, length us, event | category | flops | bytes accessed | tf_op | source)
XLA Modules:
  0.0 289.8 jit_solution(16561271281909010949)
XLA Ops:
  0.1 1.6 reduce_max.72
  1.7 1.7 reduce_max.73
  10.4 1.4 fusion.525
  13.0 2.4 maximum_bitcast_fusion.2
  15.5 2.6 maximum_bitcast_fusion
  18.1 1.9 collective-permute-start.4
  21.4 2.4 collective-permute-start
  23.8 5.3 %collective-permute-start.1 = (f32[3,5,32,256]{3,2,1,0:T(8,128)S(1)}, f32[3,5,32,256]{3,2,1,0:T(8,128)S(1)}, u32[]{:S(2)}, u32[]{:S(2)}) collective-permute-start(f32[3,5,32,256]{3,2,1,0:T(8,128)S(1)} %get-tuple-element.76), channel_id=1, source_target_pairs={{16,0},{32,16},{48,32},{64,48},{80,64},{96,80},{112,96},{128,112},... | collective-permute-start | bytes 1474568 | tf_op jit(solution)/shard_map/ppermute | solution.py:70
  41.3 1.9 collective-permute-start.5
  43.8 3.8 %collective-permute-start.2 = (f32[3,18,5,256]{3,2,1,0:T(8,128)S(1)}, f32[3,18,5,256]{3,2,1,0:T(8,128)S(1)}, u32[]{:S(2)}, u32[]{:S(2)}) collective-permute-start(f32[3,18,5,256]{3,2,1,0:T(8,128)S(1)} %get-tuple-element.66), channel_id=1, source_target_pairs={{0,1},{1,2},{2,3},{3,4},{4,5},{5,6},{6,7},{7,8},{8,9},{9,10},{10,1... | collective-permute-start | bytes 829448 | tf_op jit(solution)/shard_map/ppermute | solution.py:69
  49.0 4.0 %collective-permute-start.6 = (f32[4,2]{1,0:T(4,128)S(1)}, f32[4,2]{1,0:T(4,128)S(1)}, u32[]{:S(2)}, u32[]{:S(2)}) collective-permute-start(f32[4,2]{1,0:T(4,128)S(1)} %fusion.543), channel_id=1, source_target_pairs={{0,64},{16,80},{32,96},{48,112},{64,0},{80,16},{96,32},{112,48},{1... | collective-permute-start | bytes 104 | tf_op jit(solution)/shard_map/ppermute | solution.py:202
  53.0 3.0 %collective-permute-done.6 = f32[4,2]{1,0:T(4,128)S(1)} collective-permute-done((f32[4,2]{1,0:T(4,128)S(1)}, f32[4,2]{1,0:T(4,128)S(1)}, u32[]{:S(2)}, u32[]{:S(2)}) %collective-permute-start.6) | collective-permute-done | bytes 64 | tf_op jit(solution)/shard_map/ppermute | solution.py:202
  56.0 3.4 %collective-permute-start.7 = (f32[4,2]{1,0:T(4,128)S(1)}, f32[4,2]{1,0:T(4,128)S(1)}, u32[]{:S(2)}, u32[]{:S(2)}) collective-permute-start(f32[4,2]{1,0:T(4,128)S(1)} %max.29), channel_id=1, source_target_pairs={{0,128},{16,144},{32,160},{48,176},{64,192},{80,208},{96,224},{112... | collective-permute-start | bytes 104 | tf_op jit(solution)/shard_map/ppermute | solution.py:202
  59.4 2.0 collective-permute-done.7
  61.5 4.2 %collective-permute-start.8 = (f32[4,2]{1,0:T(4,128)S(1)}, f32[4,2]{1,0:T(4,128)S(1)}, u32[]{:S(2)}, u32[]{:S(2)}) collective-permute-start(f32[4,2]{1,0:T(4,128)S(1)} %max.30), channel_id=1, source_target_pairs={{0,256},{16,272},{32,288},{48,304},{64,320},{80,336},{96,352},{112... | collective-permute-start | bytes 104 | tf_op jit(solution)/shard_map/ppermute | solution.py:202
  65.7 2.8 collective-permute-done.8
  68.4 4.5 %collective-permute-start.9 = (f32[4,2]{1,0:T(4,128)S(1)}, f32[4,2]{1,0:T(4,128)S(1)}, u32[]{:S(2)}, u32[]{:S(2)}) collective-permute-start(f32[4,2]{1,0:T(4,128)S(1)} %max.31), channel_id=1, source_target_pairs={{0,1},{1,0},{2,3},{3,2},{4,5},{5,4},{6,7},{7,6},{8,9},{9,8},{10,11... | collective-permute-start | bytes 104 | tf_op jit(solution)/shard_map/ppermute | solution.py:202
  73.0 1.5 collective-permute-done.9
  74.5 6.3 %collective-permute-start.10 = (f32[4,2]{1,0:T(4,128)S(1)}, f32[4,2]{1,0:T(4,128)S(1)}, u32[]{:S(2)}, u32[]{:S(2)}) collective-permute-start(f32[4,2]{1,0:T(4,128)S(1)} %max.32), channel_id=1, source_target_pairs={{0,2},{1,3},{2,0},{3,1},{4,6},{5,7},{6,4},{7,5},{8,10},{9,11},{10,... | collective-permute-start | bytes 104 | tf_op jit(solution)/shard_map/ppermute | solution.py:202
  80.8 1.5 collective-permute-done.10
  82.4 9.1 %collective-permute-start.11 = (f32[4,2]{1,0:T(4,128)S(1)}, f32[4,2]{1,0:T(4,128)S(1)}, u32[]{:S(2)}, u32[]{:S(2)}) collective-permute-start(f32[4,2]{1,0:T(4,128)S(1)} %max.33), channel_id=1, source_target_pairs={{0,4},{1,5},{2,6},{3,7},{4,0},{5,1},{6,2},{7,3},{8,12},{9,13},{10,... | collective-permute-start | bytes 104 | tf_op jit(solution)/shard_map/ppermute | solution.py:202
  91.5 1.5 collective-permute-done.11
  93.0 14.3 %collective-permute-start.12 = (f32[4,2]{1,0:T(4,128)S(1)}, f32[4,2]{1,0:T(4,128)S(1)}, u32[]{:S(2)}, u32[]{:S(2)}) collective-permute-start(f32[4,2]{1,0:T(4,128)S(1)} %max.34), channel_id=1, source_target_pairs={{0,8},{1,9},{2,10},{3,11},{4,12},{5,13},{6,14},{7,15},{8,0},{9,1},... | collective-permute-start | bytes 104 | tf_op jit(solution)/shard_map/ppermute | solution.py:202
  107.3 1.5 collective-permute-done.12
  112.6 1.5 slice_add_fusion.4
  117.8 1.9 collective-permute-start.13
  119.8 1.3 slice_bitcast_fusion.29
  121.1 5.7 %collective-permute-start.15 = (f32[3,4,16,128]{3,2,1,0:T(8,128)S(1)}, f32[3,4,16,128]{3,2,1,0:T(8,128)S(1)}, u32[]{:S(2)}, u32[]{:S(2)}) collective-permute-start(f32[3,4,16,128]{3,2,1,0:T(8,128)S(1)} %pad_maximum_fusion.2), channel_id=1, source_target_pairs={{16,0},{32,16},{48,32},{64,48},{80,64},{96,80},{112,96},{128,112},... | collective-permute-start | bytes 294920 | tf_op jit(solution)/shard_map/ppermute | solution.py:70
  126.9 1.9 collective-permute-start.14
  128.8 1.3 slice_bitcast_fusion.28
  130.9 5.8 %collective-permute-start.16 = (f32[3,3,16,128]{3,2,1,0:T(8,128)S(1)}, f32[3,3,16,128]{3,2,1,0:T(8,128)S(1)}, u32[]{:S(2)}, u32[]{:S(2)}) collective-permute-start(f32[3,3,16,128]{3,2,1,0:T(8,128)S(1)} %slice.1963), channel_id=1, source_target_pairs={{16,0},{32,16},{48,32},{64,48},{80,64},{96,80},{112,96},{128,112},... | collective-permute-start | bytes 221192 | tf_op jit(solution)/shard_map/ppermute | solution.py:70
  136.7 1.9 collective-permute-done.16
  139.4 2.9 %collective-permute-start.17 = (f32[3,18,7,128]{3,2,1,0:T(8,128)}, f32[3,18,7,128]{3,2,1,0:T(8,128)}, u32[]{:S(2)}, u32[]{:S(2)}) collective-permute-start(f32[3,18,7,128]{3,2,1,0:T(8,128)} %get-tuple-element.92), channel_id=1, source_target_pairs={{0,1},{1,2},{2,3},{3,4},{4,5},{5,6},{6,7},{7,8},{8,9},{9,10},{10,1... | collective-permute-start | bytes 580616 | tf_op jit(solution)/shard_map/ppermute | solution.py:69
  146.6 3.9 %collective-permute-done.18 = f32[3,18,7,128]{3,2,1,0:T(8,128)} collective-permute-done((f32[3,18,7,128]{3,2,1,0:T(8,128)}, f32[3,18,7,128]{3,2,1,0:T(8,128)}, u32[]{:S(2)}, u32[]{:S(2)}) %collective-permute-start.18) | collective-permute-done | bytes 193568 | tf_op jit(solution)/shard_map/ppermute | solution.py:70
  154.7 1.9 collective-permute-start.19
  156.6 5.8 %collective-permute-start.20 = (f32[3,2,8,64]{3,2,1,0:T(8,128)S(1)}, f32[3,2,8,64]{3,2,1,0:T(8,128)}, u32[]{:S(2)}, u32[]{:S(2)}) collective-permute-start(f32[3,2,8,64]{3,2,1,0:T(8,128)S(1)} %pad_maximum_fusion.4), channel_id=1, source_target_pairs={{0,496},{16,0},{32,16},{48,32},{64,48},{80,64},{96,80},{112,96},{1... | collective-permute-start | bytes 36872 | tf_op jit(solution)/shard_map/ppermute | solution.py:70
  163.9 1.4 pad_maximum_fusion.3
  165.3 1.9 collective-permute-start.21
  170.4 1.4 copy.9
  174.4 1.3 copy.12
  175.7 1.4 copy.13
  177.1 6.0 %collective-permute-start.22 = (f32[3,6,8,64]{3,2,1,0:T(8,128)}, f32[3,6,8,64]{3,2,1,0:T(8,128)S(1)}, u32[]{:S(2)}, u32[]{:S(2)}) collective-permute-start(f32[3,6,8,64]{3,2,1,0:T(8,128)} %pad_maximum_fusion.3), channel_id=1, source_target_pairs={{0,464},{16,480},{32,496},{48,0},{64,16},{80,32},{96,48},{112,64},... | collective-permute-start | bytes 110600 | tf_op jit(solution)/shard_map/ppermute | solution.py:70
  185.5 1.4 broadcast_select_fusion
  186.9 3.4 %collective-permute-start.23 = (f32[3,18,8,64]{3,2,1,0:T(8,128)}, f32[3,18,8,64]{3,2,1,0:T(8,128)}, u32[]{:S(2)}, u32[]{:S(2)}) collective-permute-start(f32[3,18,8,64]{3,2,1,0:T(8,128)} %broadcast_select_fusion), channel_id=1, source_target_pairs={{0,1},{1,2},{2,3},{3,4},{4,5},{5,6},{6,7},{7,8},{8,9},{9,10},{10,1... | collective-permute-start | bytes 331784 | tf_op jit(solution)/shard_map/ppermute | solution.py:69
  190.3 1.5 collective-permute-start.24
  195.4 5.3 %collective-permute-done.24 = f32[3,18,8,64]{3,2,1,0:T(8,128)} collective-permute-done((f32[3,18,8,64]{3,2,1,0:T(8,128)}, f32[3,18,8,64]{3,2,1,0:T(8,128)}, u32[]{:S(2)}, u32[]{:S(2)}) %collective-permute-start.24) | collective-permute-done | bytes 110624 | tf_op jit(solution)/shard_map/ppermute | solution.py:70
  204.2 22.8 %all_gather.6 = f32[3,32,4,32]{3,2,1,0:T(4,128)S(1)} all-gather(f32[3,1,4,32]{3,2,1,0:T(4,128)S(1)} %pad_maximum_fusion.5), channel_id=1, replica_groups=mesh['gx'=32,'gy'=16] {'gx'}, dimensions={1}, use_global_device_ids=true | all-gather | bytes 50688 | tf_op jit(solution)/shard_map/all_gather | solution.py:50
  227.1 50.2 %all_gather.7 = f32[3,21,64,32]{3,1,0,2:T(8,128)S(1)} all-gather(f32[3,21,4,32]{3,1,0,2:T(8,128)S(1)} %copy.4), channel_id=1, replica_groups=mesh['gx'=32,'gy'=16] {'gy'}, dimensions={2}, use_global_device_ids=true | all-gather | bytes 548352 | tf_op jit(solution)/shard_map/all_gather | solution.py:50
  (370 shorter events, 62.7 us)
Async XLA Ops:
  0.0 20.0 %copy-start.34 = (s32[256]{0:T(256)}, s32[256]{0:T(256)S(1)}, u32[]{:S(2)}) copy-start(s32[256]{0:T(256)S(1)} %and_select_fusion.7) | copy-start | bytes 3076
  0.0 20.0 %copy-start.69 = (s32[32]{0:T(128)}, s32[32]{0:T(128)S(1)}, u32[]{:S(2)}) copy-start(s32[32]{0:T(128)S(1)} %and_select_fusion.8) | copy-start | bytes 388
  0.0 20.0 %copy-start.84 = (s32[16]{0:T(128)}, s32[16]{0:T(128)S(1)}, u32[]{:S(2)}) copy-start(s32[16]{0:T(128)S(1)} %and_select_fusion.6) | copy-start | bytes 196
  0.1 21.3 %copy-start.53 = (s32[128]{0:T(128)}, s32[128]{0:T(128)S(1)}, u32[]{:S(2)}) copy-start(s32[128]{0:T(128)S(1)} %and_select_fusion.5) | copy-start | bytes 1540
  0.1 21.3 %copy-start.82 = (s32[8]{0:T(128)}, s32[8]{0:T(128)S(1)}, u32[]{:S(2)}) copy-start(s32[8]{0:T(128)S(1)} %and_select_fusion.4) | copy-start | bytes 100
  0.1 21.3 %copy-start.77 = (s32[64]{0:T(128)}, s32[64]{0:T(128)S(1)}, u32[]{:S(2)}) copy-start(s32[64]{0:T(128)S(1)} %and_select_fusion.3) | copy-start | bytes 772
  3.4 40.0 %copy-start.24 = (f32[8,32,256]{2,1,0:T(8,128)S(1)}, f32[8,32,256]{2,1,0:T(8,128)}, u32[]{:S(2)}) copy-start(f32[8,32,256]{2,1,0:T(8,128)} %param.5) | copy-start | bytes 786436
  3.4 40.0 %copy-start.25 = (f32[8,32,256]{2,1,0:T(8,128)S(1)}, f32[8,32,256]{2,1,0:T(8,128)}, u32[]{:S(2)}) copy-start(f32[8,32,256]{2,1,0:T(8,128)} %param.4) | copy-start | bytes 786436
  3.4 40.0 %copy-start.26 = (f32[8,32,256]{2,1,0:T(8,128)S(1)}, f32[8,32,256]{2,1,0:T(8,128)}, u32[]{:S(2)}) copy-start(f32[8,32,256]{2,1,0:T(8,128)} %param.3) | copy-start | bytes 786436
  6.9 13.1 %copy-start.27 = (f32[4,16,128]{2,1,0:T(8,128)}, f32[4,16,128]{2,1,0:T(8,128)S(1)}, u32[]{:S(2)}) copy-start(f32[4,16,128]{2,1,0:T(8,128)S(1)} %get-tuple-element.167) | copy-start | bytes 98308
  7.8 12.2 %copy-start.29 = (f32[4,16,128]{2,1,0:T(8,128)}, f32[4,16,128]{2,1,0:T(8,128)S(1)}, u32[]{:S(2)}) copy-start(f32[4,16,128]{2,1,0:T(8,128)S(1)} %get-tuple-element.165) | copy-start | bytes 98308
  15.5 27.8 %copy-start.58 = (f32[1,2]{1,0:T(1,128)}, f32[1,2]{1,0:T(1,128)S(1)}, u32[]{:S(2)}) copy-start(f32[1,2]{1,0:T(1,128)S(1)} %get-tuple-element.174) | copy-start | bytes 28
  15.5 27.8 %copy-start.60 = (f32[1,2]{1,0:T(1,128)}, f32[1,2]{1,0:T(1,128)S(1)}, u32[]{:S(2)}) copy-start(f32[1,2]{1,0:T(1,128)S(1)} %get-tuple-element.175) | copy-start | bytes 28
  18.0 25.3 %copy-start.62 = (f32[1,2]{1,0:T(1,128)}, f32[1,2]{1,0:T(1,128)S(1)}, u32[]{:S(2)}) copy-start(f32[1,2]{1,0:T(1,128)S(1)} %get-tuple-element.172) | copy-start | bytes 28
  18.0 25.3 %copy-start.64 = (f32[1,2]{1,0:T(1,128)}, f32[1,2]{1,0:T(1,128)S(1)}, u32[]{:S(2)}) copy-start(f32[1,2]{1,0:T(1,128)S(1)} %get-tuple-element.173) | copy-start | bytes 28
  18.1 23.3 %collective-permute-start.4 = (f32[4,2]{1,0:T(4,128)S(1)}, f32[4,2]{1,0:T(4,128)S(1)}, u32[]{:S(2)}, u32[]{:S(2)}) collective-permute-start(f32[4,2]{1,0:T(4,128)S(1)} %pad_maximum_fusion.6), channel_id=1, source_target_pairs={{0,16},{16,0},{32,48},{48,32},{64,80},{80,64},{96,112},{112,96},{1... | collective-permute-start | bytes 104 | tf_op jit(solution)/shard_map/ppermute | solution.py:202
  21.4 21.9 %collective-permute-start = (f32[3,5,32,256]{3,2,1,0:T(8,128)S(1)}, f32[3,5,32,256]{3,2,1,0:T(8,128)S(1)}, u32[]{:S(2)}, u32[]{:S(2)}) collective-permute-start(f32[3,5,32,256]{3,2,1,0:T(8,128)S(1)} %get-tuple-element.75), channel_id=1, source_target_pairs={{0,16},{16,32},{32,48},{48,64},{64,80},{80,96},{96,112},{112,128},... | collective-permute-start | bytes 1474568 | tf_op jit(solution)/shard_map/ppermute | solution.py:69
  23.8 19.6 %collective-permute-start.1 = (f32[3,5,32,256]{3,2,1,0:T(8,128)S(1)}, f32[3,5,32,256]{3,2,1,0:T(8,128)S(1)}, u32[]{:S(2)}, u32[]{:S(2)}) collective-permute-start(f32[3,5,32,256]{3,2,1,0:T(8,128)S(1)} %get-tuple-element.76), channel_id=1, source_target_pairs={{16,0},{32,16},{48,32},{64,48},{80,64},{96,80},{112,96},{128,112},... | collective-permute-start | bytes 1474568 | tf_op jit(solution)/shard_map/ppermute | solution.py:70
  30.5 12.8 %copy-start.36 = (pred[12,36]{1,0:T(8,128)(4,1)}, pred[12,36]{1,0:T(8,128)(4,1)S(1)}, u32[]{:S(2)}) copy-start(pred[12,36]{1,0:T(8,128)(4,1)S(1)} %slice_bitcast_fusion.24) | copy-start | bytes 1300
  30.6 12.7 %copy-start.32 = (pred[18,30,1]{1,0,2:T(8,128)(4,1)}, pred[18,30,1]{1,0,2:T(8,128)(4,1)S(1)}, u32[]{:S(2)}) copy-start(pred[18,30,1]{1,0,2:T(8,128)(4,1)S(1)} %broadcast_and_fusion.2) | copy-start | bytes 1624
  32.6 10.8 %copy-start.76 = (pred[18]{0:T(512)(128)(4,1)}, pred[18]{0:T(512)(128)(4,1)S(1)}, u32[]{:S(2)}) copy-start(pred[18]{0:T(512)(128)(4,1)S(1)} %compare_and_fusion.3) | copy-start | bytes 58
  32.7 10.7 %copy-start.33 = (pred[18,24,1]{1,0,2:T(8,128)(4,1)}, pred[18,24,1]{1,0,2:T(8,128)(4,1)S(1)}, u32[]{:S(2)}) copy-start(pred[18,24,1]{1,0,2:T(8,128)(4,1)S(1)} %broadcast_and_fusion.1) | copy-start | bytes 1300
  34.8 8.6 %copy-start.31 = (pred[21,24,1]{1,0,2:T(8,128)(4,1)}, pred[21,24,1]{1,0,2:T(8,128)(4,1)S(1)}, u32[]{:S(2)}) copy-start(pred[21,24,1]{1,0,2:T(8,128)(4,1)S(1)} %broadcast_and_fusion) | copy-start | bytes 1516
  41.3 7.6 %collective-permute-start.5 = (f32[4,2]{1,0:T(4,128)S(1)}, f32[4,2]{1,0:T(4,128)S(1)}, u32[]{:S(2)}, u32[]{:S(2)}) collective-permute-start(f32[4,2]{1,0:T(4,128)S(1)} %fusion.474), channel_id=1, source_target_pairs={{0,32},{16,48},{32,0},{48,16},{64,96},{80,112},{96,64},{112,80},{1... | collective-permute-start | bytes 104 | tf_op jit(solution)/shard_map/ppermute | solution.py:202
  43.4 5.5 %copy-start.57 = (f32[4,2]{1,0:T(4,128)S(1)}, f32[4,2]{1,0:T(4,128)}, u32[]{:S(2)}) copy-start(f32[4,2]{1,0:T(4,128)} %copy-done.56) | copy-start | bytes 100
  43.8 67.2 %collective-permute-start.2 = (f32[3,18,5,256]{3,2,1,0:T(8,128)S(1)}, f32[3,18,5,256]{3,2,1,0:T(8,128)S(1)}, u32[]{:S(2)}, u32[]{:S(2)}) collective-permute-start(f32[3,18,5,256]{3,2,1,0:T(8,128)S(1)} %get-tuple-element.66), channel_id=1, source_target_pairs={{0,1},{1,2},{2,3},{3,4},{4,5},{5,6},{6,7},{7,8},{8,9},{9,10},{10,1... | collective-permute-start | bytes 829448 | tf_op jit(solution)/shard_map/ppermute | solution.py:69
  47.6 63.4 %collective-permute-start.3 = (f32[3,18,5,256]{3,2,1,0:T(8,128)S(1)}, f32[3,18,5,256]{3,2,1,0:T(8,128)S(1)}, u32[]{:S(2)}, u32[]{:S(2)}) collective-permute-start(f32[3,18,5,256]{3,2,1,0:T(8,128)S(1)} %get-tuple-element.67), channel_id=1, source_target_pairs={{1,0},{2,1},{3,2},{4,3},{5,4},{6,5},{7,6},{8,7},{9,8},{10,9},{11,1... | collective-permute-start | bytes 829448 | tf_op jit(solution)/shard_map/ppermute | solution.py:70
  49.0 7.0 %collective-permute-start.6 = (f32[4,2]{1,0:T(4,128)S(1)}, f32[4,2]{1,0:T(4,128)S(1)}, u32[]{:S(2)}, u32[]{:S(2)}) collective-permute-start(f32[4,2]{1,0:T(4,128)S(1)} %fusion.543), channel_id=1, source_target_pairs={{0,64},{16,80},{32,96},{48,112},{64,0},{80,16},{96,32},{112,48},{1... | collective-permute-start | bytes 104 | tf_op jit(solution)/shard_map/ppermute | solution.py:202
  56.0 5.5 %collective-permute-start.7 = (f32[4,2]{1,0:T(4,128)S(1)}, f32[4,2]{1,0:T(4,128)S(1)}, u32[]{:S(2)}, u32[]{:S(2)}) collective-permute-start(f32[4,2]{1,0:T(4,128)S(1)} %max.29), channel_id=1, source_target_pairs={{0,128},{16,144},{32,160},{48,176},{64,192},{80,208},{96,224},{112... | collective-permute-start | bytes 104 | tf_op jit(solution)/shard_map/ppermute | solution.py:202
  61.5 7.0 %collective-permute-start.8 = (f32[4,2]{1,0:T(4,128)S(1)}, f32[4,2]{1,0:T(4,128)S(1)}, u32[]{:S(2)}, u32[]{:S(2)}) collective-permute-start(f32[4,2]{1,0:T(4,128)S(1)} %max.30), channel_id=1, source_target_pairs={{0,256},{16,272},{32,288},{48,304},{64,320},{80,336},{96,352},{112... | collective-permute-start | bytes 104 | tf_op jit(solution)/shard_map/ppermute | solution.py:202
  68.4 6.1 %collective-permute-start.9 = (f32[4,2]{1,0:T(4,128)S(1)}, f32[4,2]{1,0:T(4,128)S(1)}, u32[]{:S(2)}, u32[]{:S(2)}) collective-permute-start(f32[4,2]{1,0:T(4,128)S(1)} %max.31), channel_id=1, source_target_pairs={{0,1},{1,0},{2,3},{3,2},{4,5},{5,4},{6,7},{7,6},{8,9},{9,8},{10,11... | collective-permute-start | bytes 104 | tf_op jit(solution)/shard_map/ppermute | solution.py:202
  74.5 7.8 %collective-permute-start.10 = (f32[4,2]{1,0:T(4,128)S(1)}, f32[4,2]{1,0:T(4,128)S(1)}, u32[]{:S(2)}, u32[]{:S(2)}) collective-permute-start(f32[4,2]{1,0:T(4,128)S(1)} %max.32), channel_id=1, source_target_pairs={{0,2},{1,3},{2,0},{3,1},{4,6},{5,7},{6,4},{7,5},{8,10},{9,11},{10,... | collective-permute-start | bytes 104 | tf_op jit(solution)/shard_map/ppermute | solution.py:202
  82.4 10.6 %collective-permute-start.11 = (f32[4,2]{1,0:T(4,128)S(1)}, f32[4,2]{1,0:T(4,128)S(1)}, u32[]{:S(2)}, u32[]{:S(2)}) collective-permute-start(f32[4,2]{1,0:T(4,128)S(1)} %max.33), channel_id=1, source_target_pairs={{0,4},{1,5},{2,6},{3,7},{4,0},{5,1},{6,2},{7,3},{8,12},{9,13},{10,... | collective-permute-start | bytes 104 | tf_op jit(solution)/shard_map/ppermute | solution.py:202
  93.0 15.8 %collective-permute-start.12 = (f32[4,2]{1,0:T(4,128)S(1)}, f32[4,2]{1,0:T(4,128)S(1)}, u32[]{:S(2)}, u32[]{:S(2)}) collective-permute-start(f32[4,2]{1,0:T(4,128)S(1)} %max.34), channel_id=1, source_target_pairs={{0,8},{1,9},{2,10},{3,11},{4,12},{5,13},{6,14},{7,15},{8,0},{9,1},... | collective-permute-start | bytes 104 | tf_op jit(solution)/shard_map/ppermute | solution.py:202
  117.8 9.0 %collective-permute-start.13 = (f32[3,4,16,128]{3,2,1,0:T(8,128)S(1)}, f32[3,4,16,128]{3,2,1,0:T(8,128)S(1)}, u32[]{:S(2)}, u32[]{:S(2)}) collective-permute-start(f32[3,4,16,128]{3,2,1,0:T(8,128)S(1)} %pad_maximum_fusion.2), channel_id=1, source_target_pairs={{0,16},{16,32},{32,48},{48,64},{64,80},{80,96},{96,112},{112,128},... | collective-permute-start | bytes 294920 | tf_op jit(solution)/shard_map/ppermute | solution.py:69
  121.1 9.8 %collective-permute-start.15 = (f32[3,4,16,128]{3,2,1,0:T(8,128)S(1)}, f32[3,4,16,128]{3,2,1,0:T(8,128)S(1)}, u32[]{:S(2)}, u32[]{:S(2)}) collective-permute-start(f32[3,4,16,128]{3,2,1,0:T(8,128)S(1)} %pad_maximum_fusion.2), channel_id=1, source_target_pairs={{16,0},{32,16},{48,32},{64,48},{80,64},{96,80},{112,96},{128,112},... | collective-permute-start | bytes 294920 | tf_op jit(solution)/shard_map/ppermute | solution.py:70
  126.9 9.8 %collective-permute-start.14 = (f32[3,3,16,128]{3,2,1,0:T(8,128)S(1)}, f32[3,3,16,128]{3,2,1,0:T(8,128)S(1)}, u32[]{:S(2)}, u32[]{:S(2)}) collective-permute-start(f32[3,3,16,128]{3,2,1,0:T(8,128)S(1)} %slice.1962), channel_id=1, source_target_pairs={{0,16},{16,32},{32,48},{48,64},{64,80},{80,96},{96,112},{112,128},... | collective-permute-start | bytes 221192 | tf_op jit(solution)/shard_map/ppermute | solution.py:69
  130.9 7.7 %collective-permute-start.16 = (f32[3,3,16,128]{3,2,1,0:T(8,128)S(1)}, f32[3,3,16,128]{3,2,1,0:T(8,128)S(1)}, u32[]{:S(2)}, u32[]{:S(2)}) collective-permute-start(f32[3,3,16,128]{3,2,1,0:T(8,128)S(1)} %slice.1963), channel_id=1, source_target_pairs={{16,0},{32,16},{48,32},{64,48},{80,64},{96,80},{112,96},{128,112},... | collective-permute-start | bytes 221192 | tf_op jit(solution)/shard_map/ppermute | solution.py:70
  139.4 7.1 %collective-permute-start.17 = (f32[3,18,7,128]{3,2,1,0:T(8,128)}, f32[3,18,7,128]{3,2,1,0:T(8,128)}, u32[]{:S(2)}, u32[]{:S(2)}) collective-permute-start(f32[3,18,7,128]{3,2,1,0:T(8,128)} %get-tuple-element.92), channel_id=1, source_target_pairs={{0,1},{1,2},{2,3},{3,4},{4,5},{5,6},{6,7},{7,8},{8,9},{9,10},{10,1... | collective-permute-start | bytes 580616 | tf_op jit(solution)/shard_map/ppermute | solution.py:69
  142.4 8.1 %collective-permute-start.18 = (f32[3,18,7,128]{3,2,1,0:T(8,128)}, f32[3,18,7,128]{3,2,1,0:T(8,128)}, u32[]{:S(2)}, u32[]{:S(2)}) collective-permute-start(f32[3,18,7,128]{3,2,1,0:T(8,128)} %get-tuple-element.93), channel_id=1, source_target_pairs={{1,0},{2,1},{3,2},{4,3},{5,4},{6,5},{7,6},{8,7},{9,8},{10,9},{11,1... | collective-permute-start | bytes 580616 | tf_op jit(solution)/shard_map/ppermute | solution.py:70
  153.6 15.3 %copy-start.39 = (pred[19,22]{1,0:T(8,128)(4,1)S(1)}, pred[19,22]{1,0:T(8,128)(4,1)}, u32[]{:S(2)}) copy-start(pred[19,22]{1,0:T(8,128)(4,1)} %slice_bitcast_fusion.10) | copy-start | bytes 1258
  154.7 8.3 %collective-permute-start.19 = (f32[3,2,8,64]{3,2,1,0:T(8,128)S(1)}, f32[3,2,8,64]{3,2,1,0:T(8,128)}, u32[]{:S(2)}, u32[]{:S(2)}) collective-permute-start(f32[3,2,8,64]{3,2,1,0:T(8,128)S(1)} %pad_maximum_fusion.4), channel_id=1, source_target_pairs={{0,16},{16,32},{32,48},{48,64},{64,80},{80,96},{96,112},{112,128},... | collective-permute-start | bytes 36872 | tf_op jit(solution)/shard_map/ppermute | solution.py:69
  156.6 7.3 %collective-permute-start.20 = (f32[3,2,8,64]{3,2,1,0:T(8,128)S(1)}, f32[3,2,8,64]{3,2,1,0:T(8,128)}, u32[]{:S(2)}, u32[]{:S(2)}) collective-permute-start(f32[3,2,8,64]{3,2,1,0:T(8,128)S(1)} %pad_maximum_fusion.4), channel_id=1, source_target_pairs={{0,496},{16,0},{32,16},{48,32},{64,48},{80,64},{96,80},{112,96},{1... | collective-permute-start | bytes 36872 | tf_op jit(solution)/shard_map/ppermute | solution.py:70
  165.3 17.9 %collective-permute-start.21 = (f32[3,6,8,64]{3,2,1,0:T(8,128)}, f32[3,6,8,64]{3,2,1,0:T(8,128)}, u32[]{:S(2)}, u32[]{:S(2)}) collective-permute-start(f32[3,6,8,64]{3,2,1,0:T(8,128)} %pad_maximum_fusion.3), channel_id=1, source_target_pairs={{0,48},{16,64},{32,80},{48,96},{64,112},{80,128},{96,144},{112,160... | collective-permute-start | bytes 110600 | tf_op jit(solution)/shard_map/ppermute | solution.py:69
  177.1 8.4 %collective-permute-start.22 = (f32[3,6,8,64]{3,2,1,0:T(8,128)}, f32[3,6,8,64]{3,2,1,0:T(8,128)S(1)}, u32[]{:S(2)}, u32[]{:S(2)}) collective-permute-start(f32[3,6,8,64]{3,2,1,0:T(8,128)} %pad_maximum_fusion.3), channel_id=1, source_target_pairs={{0,464},{16,480},{32,496},{48,0},{64,16},{80,32},{96,48},{112,64},... | collective-permute-start | bytes 110600 | tf_op jit(solution)/shard_map/ppermute | solution.py:70
  186.9 8.5 %collective-permute-start.23 = (f32[3,18,8,64]{3,2,1,0:T(8,128)}, f32[3,18,8,64]{3,2,1,0:T(8,128)}, u32[]{:S(2)}, u32[]{:S(2)}) collective-permute-start(f32[3,18,8,64]{3,2,1,0:T(8,128)} %broadcast_select_fusion), channel_id=1, source_target_pairs={{0,1},{1,2},{2,3},{3,4},{4,5},{5,6},{6,7},{7,8},{8,9},{9,10},{10,1... | collective-permute-start | bytes 331784 | tf_op jit(solution)/shard_map/ppermute | solution.py:69
  190.3 10.4 %collective-permute-start.24 = (f32[3,18,8,64]{3,2,1,0:T(8,128)}, f32[3,18,8,64]{3,2,1,0:T(8,128)}, u32[]{:S(2)}, u32[]{:S(2)}) collective-permute-start(f32[3,18,8,64]{3,2,1,0:T(8,128)} %broadcast_select_fusion), channel_id=1, source_target_pairs={{1,0},{2,1},{3,2},{4,3},{5,4},{6,5},{7,6},{8,7},{9,8},{10,9},{11,1... | collective-permute-start | bytes 331784 | tf_op jit(solution)/shard_map/ppermute | solution.py:70
  195.2 7.1 %copy-start.48 = (pred[16,22]{1,0:T(8,128)(4,1)S(1)}, pred[16,22]{1,0:T(8,128)(4,1)}, u32[]{:S(2)}) copy-start(pred[16,22]{1,0:T(8,128)(4,1)} %slice_bitcast_fusion.20) | copy-start | bytes 1060
  (63 other events, 89.1 us)

commit v6 on v4

--- a/solution.py
+++ b/solution.py
@@ -193,6 +193,9 @@
 def all_max(values):
     for axis in ("gx", "gy"):
         peers = lax.axis_size(axis)
+        if axis == "gy":
+            values = jnp.max(lax.all_gather(values, axis), axis=0)
+            continue
         if peers & (peers - 1):
             values = lax.pmax(values, axis)
             continue

time: 267 us -> 265 us (level)
  blocking collectives: 26.4 us -> 59 us
  starting transfers between devices: 107 us -> 83.1 us
  waiting for transfers between devices: 55.2 us -> 39.7 us
    all_gather x0 -> x1, blocking collectives: none -> 32.6 us  [all_max(): values = jnp.max(lax.all_gather(values, axis), axis=0)]
    ppermute x9 -> x5, starting transfers between devices: 43.9 us -> 20.3 us  [all_max(): values = jnp.maximum(values, lax.ppermute(values, axis, pairs))]
    ppermute x9 -> x5, waiting for transfers between devices: 18.3 us -> 5.23 us  [all_max(): values = jnp.maximum(values, lax.ppermute(values, axis, pairs))]
    ppermute x10, waiting for transfers between devices: 26.4 us -> 22.8 us  [extend(): after = lax.ppermute(high, axis, down)]
  transfers between devices with their start and end apart: 29 -> 25, of which waited for: 19 -> 15; matrix products, arithmetic and copies ran while one was open for 7% -> 8% of each run, Pallas kernels for 0% -> 0%
where the time goes in v6:
time: 265 us; the launch traced here: 263 us
  starting transfers between devices  83.1 us (31%)
  blocking collectives  59 us (22%)
  waiting for transfers between devices  39.7 us (15%)
  local copies, waits for them, and re-layouts  30.6 us (12%)
  other arithmetic  29.1 us (11%)
  matrix products  12.8 us (5%)
  between operations  8.57 us (3%)
    all_gather x1, blocking collectives, all_max(): values = jnp.max(lax.all_gather(values, axis), axis=0)  32.6 us
    ppermute x10, starting transfers between devices, extend(): after = lax.ppermute(high, axis, down)  32.1 us
    ppermute x10, starting transfers between devices, extend(): before = lax.ppermute(low, axis, up)  30.6 us
    all_gather x1, blocking collectives, extend(): whole = lax.all_gather(x, axis, axis=dim, tiled=True)  26.4 us
    ppermute x10, waiting for transfers between devices, extend(): after = lax.ppermute(high, axis, down)  22.8 us
    ppermute x5, starting transfers between devices, all_max(): values = jnp.maximum(values, lax.ppermute(values, axis, pairs))  20.3 us
    broadcast_in_dim x21, local copies, waits for them, and re-layouts, residual(): r = jnp.where(crop(self.mask, self.depth - out), r, 0.0)  13.3 us
    ppermute x10, waiting for transfers between devices, extend(): before = lax.ppermute(low, axis, up)  11.7 us
  transfers between devices with their start and end apart: 25, of which 15 were waited for; matrix products, arithmetic and copies ran while one was open for 8% of the time, Pallas kernels for 0%

profile of v6, /device:TPU:98, one launch (start us, length us, event | category | flops | bytes accessed | tf_op | source)
XLA Modules:
  0.0 263.0 jit_solution(8284257780651552463)
XLA Ops:
  0.1 1.7 reduce_max.81
  1.8 1.7 reduce_max.82
  10.4 1.4 fusion.522
  11.7 1.4 fusion.521
  13.1 2.6 maximum_bitcast_fusion.2
  15.7 2.6 maximum_bitcast_fusion
  18.4 1.9 collective-permute-start.4
  21.8 2.4 collective-permute-start
  24.2 3.2 %collective-permute-start.1 = (f32[3,5,32,256]{3,2,1,0:T(8,128)S(1)}, f32[3,5,32,256]{3,2,1,0:T(8,128)S(1)}, u32[]{:S(2)}, u32[]{:S(2)}) collective-permute-start(f32[3,5,32,256]{3,2,1,0:T(8,128)S(1)} %get-tuple-element.72), channel_id=1, source_target_pairs={{16,0},{32,16},{48,32},{64,48},{80,64},{96,80},{112,96},{128,112},... | collective-permute-start | bytes 1474568 | tf_op jit(solution)/shard_map/ppermute | solution.py:70
  38.4 1.9 collective-permute-start.5
  40.8 5.0 %collective-permute-start.2 = (f32[3,18,5,256]{3,2,1,0:T(8,128)S(1)}, f32[3,18,5,256]{3,2,1,0:T(8,128)S(1)}, u32[]{:S(2)}, u32[]{:S(2)}) collective-permute-start(f32[3,18,5,256]{3,2,1,0:T(8,128)S(1)} %get-tuple-element.62), channel_id=1, source_target_pairs={{0,1},{1,2},{2,3},{3,4},{4,5},{5,6},{6,7},{7,8},{8,9},{9,10},{10,1... | collective-permute-start | bytes 829448 | tf_op jit(solution)/shard_map/ppermute | solution.py:69
  45.8 1.9 collective-permute-start.3
  47.8 4.8 %collective-permute-start.6 = (f32[4,2]{1,0:T(4,128)S(1)}, f32[4,2]{1,0:T(4,128)S(1)}, u32[]{:S(2)}, u32[]{:S(2)}) collective-permute-start(f32[4,2]{1,0:T(4,128)S(1)} %fusion.540), channel_id=1, source_target_pairs={{0,64},{16,80},{32,96},{48,112},{64,0},{80,16},{96,32},{112,48},{1... | collective-permute-start | bytes 104 | tf_op jit(solution)/shard_map/ppermute | solution.py:205
  52.7 2.1 collective-permute-done.6
  54.8 6.1 %collective-permute-start.7 = (f32[4,2]{1,0:T(4,128)S(1)}, f32[4,2]{1,0:T(4,128)S(1)}, u32[]{:S(2)}, u32[]{:S(2)}) collective-permute-start(f32[4,2]{1,0:T(4,128)S(1)} %max.17), channel_id=1, source_target_pairs={{0,128},{16,144},{32,160},{48,176},{64,192},{80,208},{96,224},{112... | collective-permute-start | bytes 104 | tf_op jit(solution)/shard_map/ppermute | solution.py:205
  60.9 1.5 collective-permute-done.7
  62.5 5.5 %collective-permute-start.8 = (f32[4,2]{1,0:T(4,128)S(1)}, f32[4,2]{1,0:T(4,128)S(1)}, u32[]{:S(2)}, u32[]{:S(2)}) collective-permute-start(f32[4,2]{1,0:T(4,128)S(1)} %max.18), channel_id=1, source_target_pairs={{0,256},{16,272},{32,288},{48,304},{64,320},{80,336},{96,352},{112... | collective-permute-start | bytes 104 | tf_op jit(solution)/shard_map/ppermute | solution.py:205
  68.0 1.5 collective-permute-done.8
  71.5 32.6 %all-gather.1 = f32[16,4,2]{1,2,0:T(2,128)} all-gather(f32[1,4,2]{1,2,0:T(2,128)} %bitcast.248), channel_id=2, replica_groups=mesh['gx'=32,'gy'=16] {'gy'}, dimensions={0}, use_global_device_ids=true | all-gather | bytes 544 | tf_op jit(solution)/shard_map/all_gather | solution.py:197
  105.5 1.6 fusion.520
  110.3 1.5 slice_add_fusion.4
  115.8 1.9 collective-permute-start.9
  117.8 3.6 %collective-permute-start.11 = (f32[3,4,16,128]{3,2,1,0:T(8,128)S(1)}, f32[3,4,16,128]{3,2,1,0:T(8,128)S(1)}, u32[]{:S(2)}, u32[]{:S(2)}) collective-permute-start(f32[3,4,16,128]{3,2,1,0:T(8,128)S(1)} %pad_maximum_fusion.2), channel_id=1, source_target_pairs={{16,0},{32,16},{48,32},{64,48},{80,64},{96,80},{112,96},{128,112},... | collective-permute-start | bytes 294920 | tf_op jit(solution)/shard_map/ppermute | solution.py:70
  121.7 1.9 collective-permute-start.10
  124.3 3.6 %collective-permute-start.12 = (f32[3,3,16,128]{3,2,1,0:T(8,128)S(1)}, f32[3,3,16,128]{3,2,1,0:T(8,128)S(1)}, u32[]{:S(2)}, u32[]{:S(2)}) collective-permute-start(f32[3,3,16,128]{3,2,1,0:T(8,128)S(1)} %slice.1971), channel_id=1, source_target_pairs={{16,0},{32,16},{48,32},{64,48},{80,64},{96,80},{112,96},{128,112},... | collective-permute-start | bytes 221192 | tf_op jit(solution)/shard_map/ppermute | solution.py:70
  128.1 1.9 collective-permute-done.12
  130.7 3.5 %collective-permute-start.13 = (f32[3,18,7,128]{3,2,1,0:T(8,128)}, f32[3,18,7,128]{3,2,1,0:T(8,128)}, u32[]{:S(2)}, u32[]{:S(2)}) collective-permute-start(f32[3,18,7,128]{3,2,1,0:T(8,128)} %get-tuple-element.93), channel_id=1, source_target_pairs={{0,1},{1,2},{2,3},{3,4},{4,5},{5,6},{6,7},{7,8},{8,9},{9,10},{10,1... | collective-permute-start | bytes 580616 | tf_op jit(solution)/shard_map/ppermute | solution.py:69
  134.2 2.3 collective-permute-start.14
  139.3 1.5 collective-permute-done.13
  140.8 4.4 %collective-permute-done.14 = f32[3,18,7,128]{3,2,1,0:T(8,128)} collective-permute-done((f32[3,18,7,128]{3,2,1,0:T(8,128)}, f32[3,18,7,128]{3,2,1,0:T(8,128)}, u32[]{:S(2)}, u32[]{:S(2)}) %collective-permute-start.14) | collective-permute-done | bytes 193568 | tf_op jit(solution)/shard_map/ppermute | solution.py:70
  149.6 1.9 collective-permute-start.15
  151.5 3.6 %collective-permute-start.16 = (f32[3,2,8,64]{3,2,1,0:T(8,128)S(1)}, f32[3,2,8,64]{3,2,1,0:T(8,128)S(1)}, u32[]{:S(2)}, u32[]{:S(2)}) collective-permute-start(f32[3,2,8,64]{3,2,1,0:T(8,128)S(1)} %pad_maximum_fusion.4), channel_id=1, source_target_pairs={{0,496},{16,0},{32,16},{48,32},{64,48},{80,64},{96,80},{112,96},{1... | collective-permute-start | bytes 36872 | tf_op jit(solution)/shard_map/ppermute | solution.py:70
  156.7 5.2 %collective-permute-start.17 = (f32[3,6,8,64]{3,2,1,0:T(8,128)S(1)}, f32[3,6,8,64]{3,2,1,0:T(8,128)S(1)}, u32[]{:S(2)}, u32[]{:S(2)}) collective-permute-start(f32[3,6,8,64]{3,2,1,0:T(8,128)S(1)} %pad_maximum_fusion.3), channel_id=1, source_target_pairs={{0,48},{16,64},{32,80},{48,96},{64,112},{80,128},{96,144},{112,160... | collective-permute-start | bytes 110600 | tf_op jit(solution)/shard_map/ppermute | solution.py:69
  163.1 4.0 %collective-permute-start.18 = (f32[3,6,8,64]{3,2,1,0:T(8,128)S(1)}, f32[3,6,8,64]{3,2,1,0:T(8,128)S(1)}, u32[]{:S(2)}, u32[]{:S(2)}) collective-permute-start(f32[3,6,8,64]{3,2,1,0:T(8,128)S(1)} %pad_maximum_fusion.3), channel_id=1, source_target_pairs={{0,464},{16,480},{32,496},{48,0},{64,16},{80,32},{96,48},{112,64},... | collective-permute-start | bytes 110600 | tf_op jit(solution)/shard_map/ppermute | solution.py:70
  167.2 4.4 %collective-permute-done.18 = f32[3,6,8,64]{3,2,1,0:T(8,128)S(1)} collective-permute-done((f32[3,6,8,64]{3,2,1,0:T(8,128)S(1)}, f32[3,6,8,64]{3,2,1,0:T(8,128)S(1)}, u32[]{:S(2)}, u32[]{:S(2)}) %collective-permute-start.18) | collective-permute-done | bytes 36896 | tf_op jit(solution)/shard_map/ppermute | solution.py:70
  171.7 2.6 %collective-permute-start.19 = (f32[3,18,8,64]{3,2,1,0:T(8,128)S(1)}, f32[3,18,8,64]{3,2,1,0:T(8,128)}, u32[]{:S(2)}, u32[]{:S(2)}) collective-permute-start(f32[3,18,8,64]{3,2,1,0:T(8,128)S(1)} %broadcast_select_fusion), channel_id=1, source_target_pairs={{0,1},{1,2},{2,3},{3,4},{4,5},{5,6},{6,7},{7,8},{8,9},{9,10},{10,1... | collective-permute-start | bytes 331784 | tf_op jit(solution)/shard_map/ppermute | solution.py:69
  174.4 3.4 %collective-permute-start.20 = (f32[3,18,8,64]{3,2,1,0:T(8,128)S(1)}, f32[3,18,8,64]{3,2,1,0:T(8,128)}, u32[]{:S(2)}, u32[]{:S(2)}) collective-permute-start(f32[3,18,8,64]{3,2,1,0:T(8,128)S(1)} %broadcast_select_fusion), channel_id=1, source_target_pairs={{1,0},{2,1},{3,2},{4,3},{5,4},{6,5},{7,6},{8,7},{9,8},{10,9},{11,1... | collective-permute-start | bytes 331784 | tf_op jit(solution)/shard_map/ppermute | solution.py:70
  180.2 3.6 %collective-permute-done.20 = f32[3,18,8,64]{3,2,1,0:T(8,128)} collective-permute-done((f32[3,18,8,64]{3,2,1,0:T(8,128)S(1)}, f32[3,18,8,64]{3,2,1,0:T(8,128)}, u32[]{:S(2)}, u32[]{:S(2)}) %collective-permute-start.20) | collective-permute-done | bytes 110624 | tf_op jit(solution)/shard_map/ppermute | solution.py:70
  187.8 26.4 %all_gather.11 = f32[3,32,4,32]{3,2,1,0:T(4,128)S(1)} all-gather(f32[3,1,4,32]{3,2,1,0:T(4,128)S(1)} %pad_maximum_fusion.5), channel_id=1, replica_groups=mesh['gx'=32,'gy'=16] {'gx'}, dimensions={1}, use_global_device_ids=true | all-gather | bytes 50688 | tf_op jit(solution)/shard_map/all_gather | solution.py:50
  214.2 1.9 collective-permute-start.21
  216.1 3.9 %collective-permute-start.22 = (f32[3,21,4,32]{3,2,1,0:T(4,128)S(1)}, f32[3,21,4,32]{3,2,1,0:T(4,128)S(1)}, u32[]{:S(2)}, u32[]{:S(2)}) collective-permute-start(f32[3,21,4,32]{3,2,1,0:T(4,128)S(1)} %pad_dynamic-slice_fusion), channel_id=1, source_target_pairs={{0,15},{1,0},{2,1},{3,2},{4,3},{5,4},{6,5},{7,6},{8,7},{9,8},{10,9... | collective-permute-start | bytes 96776 | tf_op jit(solution)/shard_map/ppermute | solution.py:70
  220.1 1.7 collective-permute-done.21
  221.8 3.1 %collective-permute-done.22 = f32[3,21,4,32]{3,2,1,0:T(4,128)S(1)} collective-permute-done((f32[3,21,4,32]{3,2,1,0:T(4,128)S(1)}, f32[3,21,4,32]{3,2,1,0:T(4,128)S(1)}, u32[]{:S(2)}, u32[]{:S(2)}) %collective-permute-start.22) | collective-permute-done | bytes 32288 | tf_op jit(solution)/shard_map/ppermute | solution.py:70
  226.8 4.2 %collective-permute-start.23 = (f32[3,21,6,32]{3,2,1,0:T(8,128)}, f32[3,21,6,32]{3,2,1,0:T(8,128)}, u32[]{:S(2)}, u32[]{:S(2)}) collective-permute-start(f32[3,21,6,32]{3,2,1,0:T(8,128)} %get-tuple-element.89), channel_id=1, source_target_pairs={{0,2},{1,3},{2,4},{3,5},{4,6},{5,7},{6,8},{7,9},{8,10},{9,11},{10,... | collective-permute-start | bytes 145160 | tf_op jit(solution)/shard_map/ppermute | solution.py:69
  231.0 2.5 collective-permute-start.24
  235.5 7.2 %collective-permute-done.23 = f32[3,21,6,32]{3,2,1,0:T(8,128)} collective-permute-done((f32[3,21,6,32]{3,2,1,0:T(8,128)}, f32[3,21,6,32]{3,2,1,0:T(8,128)}, u32[]{:S(2)}, u32[]{:S(2)}) %collective-permute-start.23) | collective-permute-done | bytes 48416 | tf_op jit(solution)/shard_map/ppermute | solution.py:69
  242.7 5.2 %collective-permute-done.24 = f32[3,21,6,32]{3,2,1,0:T(8,128)} collective-permute-done((f32[3,21,6,32]{3,2,1,0:T(8,128)}, f32[3,21,6,32]{3,2,1,0:T(8,128)}, u32[]{:S(2)}, u32[]{:S(2)}) %collective-permute-start.24) | collective-permute-done | bytes 48416 | tf_op jit(solution)/shard_map/ppermute | solution.py:70
  247.9 1.4 add_select_fusion
  (406 shorter events, 58.0 us)
Async XLA Ops:
  0.0 20.3 %copy-start.56 = (s32[256]{0:T(256)}, s32[256]{0:T(256)S(1)}, u32[]{:S(2)}) copy-start(s32[256]{0:T(256)S(1)} %and_select_fusion.7) | copy-start | bytes 3076
  0.0 8.1 %copy-start.87 = (s32[32]{0:T(128)}, s32[32]{0:T(128)S(1)}, u32[]{:S(2)}) copy-start(s32[32]{0:T(128)S(1)} %and_select_fusion.8) | copy-start | bytes 388
  0.0 20.3 %copy-start.105 = (s32[16]{0:T(128)}, s32[16]{0:T(128)S(1)}, u32[]{:S(2)}) copy-start(s32[16]{0:T(128)S(1)} %and_select_fusion.6) | copy-start | bytes 196
  0.1 20.3 %copy-start.72 = (s32[128]{0:T(128)}, s32[128]{0:T(128)S(1)}, u32[]{:S(2)}) copy-start(s32[128]{0:T(128)S(1)} %and_select_fusion.5) | copy-start | bytes 1540
  0.1 20.3 %copy-start.103 = (s32[8]{0:T(128)}, s32[8]{0:T(128)S(1)}, u32[]{:S(2)}) copy-start(s32[8]{0:T(128)S(1)} %and_select_fusion.4) | copy-start | bytes 100
  0.1 20.3 %copy-start.99 = (s32[64]{0:T(128)}, s32[64]{0:T(128)S(1)}, u32[]{:S(2)}) copy-start(s32[64]{0:T(128)S(1)} %and_select_fusion.3) | copy-start | bytes 772
  6.9 13.4 %copy-start.46 = (f32[4,16,128]{2,1,0:T(8,128)}, f32[4,16,128]{2,1,0:T(8,128)S(1)}, u32[]{:S(2)}) copy-start(f32[4,16,128]{2,1,0:T(8,128)S(1)} %get-tuple-element.168) | copy-start | bytes 98308
  7.8 12.5 %copy-start.48 = (f32[4,16,128]{2,1,0:T(8,128)}, f32[4,16,128]{2,1,0:T(8,128)S(1)}, u32[]{:S(2)}) copy-start(f32[4,16,128]{2,1,0:T(8,128)S(1)} %get-tuple-element.166) | copy-start | bytes 98308
  15.7 22.6 %copy-start.76 = (f32[1,2]{1,0:T(1,128)}, f32[1,2]{1,0:T(1,128)S(1)}, u32[]{:S(2)}) copy-start(f32[1,2]{1,0:T(1,128)S(1)} %get-tuple-element.171) | copy-start | bytes 28
  15.7 22.6 %copy-start.78 = (f32[1,2]{1,0:T(1,128)}, f32[1,2]{1,0:T(1,128)S(1)}, u32[]{:S(2)}) copy-start(f32[1,2]{1,0:T(1,128)S(1)} %get-tuple-element.172) | copy-start | bytes 28
  18.3 20.0 %copy-start.80 = (f32[1,2]{1,0:T(1,128)}, f32[1,2]{1,0:T(1,128)S(1)}, u32[]{:S(2)}) copy-start(f32[1,2]{1,0:T(1,128)S(1)} %get-tuple-element.169) | copy-start | bytes 28
  18.3 20.0 %copy-start.82 = (f32[1,2]{1,0:T(1,128)}, f32[1,2]{1,0:T(1,128)S(1)}, u32[]{:S(2)}) copy-start(f32[1,2]{1,0:T(1,128)S(1)} %get-tuple-element.170) | copy-start | bytes 28
  18.4 20.0 %collective-permute-start.4 = (f32[4,2]{1,0:T(4,128)S(1)}, f32[4,2]{1,0:T(4,128)S(1)}, u32[]{:S(2)}, u32[]{:S(2)}) collective-permute-start(f32[4,2]{1,0:T(4,128)S(1)} %pad_maximum_fusion.6), channel_id=1, source_target_pairs={{0,16},{16,0},{32,48},{48,32},{64,80},{80,64},{96,112},{112,96},{1... | collective-permute-start | bytes 104 | tf_op jit(solution)/shard_map/ppermute | solution.py:205
  20.4 20.1 %copy-start.43 = (f32[8,32,256]{2,1,0:T(8,128)S(1)}, f32[8,32,256]{2,1,0:T(8,128)}, u32[]{:S(2)}) copy-start(f32[8,32,256]{2,1,0:T(8,128)} %param.5) | copy-start | bytes 786436
  20.4 20.1 %copy-start.44 = (f32[8,32,256]{2,1,0:T(8,128)S(1)}, f32[8,32,256]{2,1,0:T(8,128)}, u32[]{:S(2)}) copy-start(f32[8,32,256]{2,1,0:T(8,128)} %param.4) | copy-start | bytes 786436
  20.4 20.1 %copy-start.45 = (f32[8,32,256]{2,1,0:T(8,128)S(1)}, f32[8,32,256]{2,1,0:T(8,128)}, u32[]{:S(2)}) copy-start(f32[8,32,256]{2,1,0:T(8,128)} %param.3) | copy-start | bytes 786436
  21.8 18.6 %collective-permute-start = (f32[3,5,32,256]{3,2,1,0:T(8,128)S(1)}, f32[3,5,32,256]{3,2,1,0:T(8,128)S(1)}, u32[]{:S(2)}, u32[]{:S(2)}) collective-permute-start(f32[3,5,32,256]{3,2,1,0:T(8,128)S(1)} %get-tuple-element.71), channel_id=1, source_target_pairs={{0,16},{16,32},{32,48},{48,64},{64,80},{80,96},{96,112},{112,128},... | collective-permute-start | bytes 1474568 | tf_op jit(solution)/shard_map/ppermute | solution.py:69
  24.2 16.2 %collective-permute-start.1 = (f32[3,5,32,256]{3,2,1,0:T(8,128)S(1)}, f32[3,5,32,256]{3,2,1,0:T(8,128)S(1)}, u32[]{:S(2)}, u32[]{:S(2)}) collective-permute-start(f32[3,5,32,256]{3,2,1,0:T(8,128)S(1)} %get-tuple-element.72), channel_id=1, source_target_pairs={{16,0},{32,16},{48,32},{64,48},{80,64},{96,80},{112,96},{128,112},... | collective-permute-start | bytes 1474568 | tf_op jit(solution)/shard_map/ppermute | solution.py:70
  28.8 11.6 %copy-start.58 = (pred[12,36]{1,0:T(8,128)(4,1)}, pred[12,36]{1,0:T(8,128)(4,1)S(1)}, u32[]{:S(2)}) copy-start(pred[12,36]{1,0:T(8,128)(4,1)S(1)} %slice_bitcast_fusion.27) | copy-start | bytes 1300
  30.9 9.5 %copy-start.95 = (pred[18]{0:T(512)(128)(4,1)}, pred[18]{0:T(512)(128)(4,1)S(1)}, u32[]{:S(2)}) copy-start(pred[18]{0:T(512)(128)(4,1)S(1)} %compare_and_fusion.3) | copy-start | bytes 58
  31.0 9.4 %copy-start.53 = (pred[18,24,1]{1,0,2:T(8,128)(4,1)}, pred[18,24,1]{1,0,2:T(8,128)(4,1)S(1)}, u32[]{:S(2)}) copy-start(pred[18,24,1]{1,0,2:T(8,128)(4,1)S(1)} %broadcast_and_fusion.1) | copy-start | bytes 1300
  38.4 9.4 %collective-permute-start.5 = (f32[4,2]{1,0:T(4,128)S(1)}, f32[4,2]{1,0:T(4,128)S(1)}, u32[]{:S(2)}, u32[]{:S(2)}) collective-permute-start(f32[4,2]{1,0:T(4,128)S(1)} %fusion.471), channel_id=1, source_target_pairs={{0,32},{16,48},{32,0},{48,16},{64,96},{80,112},{96,64},{112,80},{1... | collective-permute-start | bytes 104 | tf_op jit(solution)/shard_map/ppermute | solution.py:205
  40.8 67.9 %collective-permute-start.2 = (f32[3,18,5,256]{3,2,1,0:T(8,128)S(1)}, f32[3,18,5,256]{3,2,1,0:T(8,128)S(1)}, u32[]{:S(2)}, u32[]{:S(2)}) collective-permute-start(f32[3,18,5,256]{3,2,1,0:T(8,128)S(1)} %get-tuple-element.62), channel_id=1, source_target_pairs={{0,1},{1,2},{2,3},{3,4},{4,5},{5,6},{6,7},{7,8},{8,9},{9,10},{10,1... | collective-permute-start | bytes 829448 | tf_op jit(solution)/shard_map/ppermute | solution.py:69
  45.8 62.8 %collective-permute-start.3 = (f32[3,18,5,256]{3,2,1,0:T(8,128)S(1)}, f32[3,18,5,256]{3,2,1,0:T(8,128)S(1)}, u32[]{:S(2)}, u32[]{:S(2)}) collective-permute-start(f32[3,18,5,256]{3,2,1,0:T(8,128)S(1)} %get-tuple-element.63), channel_id=1, source_target_pairs={{1,0},{2,1},{3,2},{4,3},{5,4},{6,5},{7,6},{8,7},{9,8},{10,9},{11,1... | collective-permute-start | bytes 829448 | tf_op jit(solution)/shard_map/ppermute | solution.py:70
  47.8 7.0 %collective-permute-start.6 = (f32[4,2]{1,0:T(4,128)S(1)}, f32[4,2]{1,0:T(4,128)S(1)}, u32[]{:S(2)}, u32[]{:S(2)}) collective-permute-start(f32[4,2]{1,0:T(4,128)S(1)} %fusion.540), channel_id=1, source_target_pairs={{0,64},{16,80},{32,96},{48,112},{64,0},{80,16},{96,32},{112,48},{1... | collective-permute-start | bytes 104 | tf_op jit(solution)/shard_map/ppermute | solution.py:205
  54.8 7.7 %collective-permute-start.7 = (f32[4,2]{1,0:T(4,128)S(1)}, f32[4,2]{1,0:T(4,128)S(1)}, u32[]{:S(2)}, u32[]{:S(2)}) collective-permute-start(f32[4,2]{1,0:T(4,128)S(1)} %max.17), channel_id=1, source_target_pairs={{0,128},{16,144},{32,160},{48,176},{64,192},{80,208},{96,224},{112... | collective-permute-start | bytes 104 | tf_op jit(solution)/shard_map/ppermute | solution.py:205
  62.5 7.1 %collective-permute-start.8 = (f32[4,2]{1,0:T(4,128)S(1)}, f32[4,2]{1,0:T(4,128)S(1)}, u32[]{:S(2)}, u32[]{:S(2)}) collective-permute-start(f32[4,2]{1,0:T(4,128)S(1)} %max.18), channel_id=1, source_target_pairs={{0,256},{16,272},{32,288},{48,304},{64,320},{80,336},{96,352},{112... | collective-permute-start | bytes 104 | tf_op jit(solution)/shard_map/ppermute | solution.py:205
  114.6 9.0 %copy-start.55 = (pred[18,42,1]{1,0,2:T(8,128)(4,1)S(1)}, pred[18,42,1]{1,0,2:T(8,128)(4,1)}, u32[]{:S(2)}) copy-start(pred[18,42,1]{1,0,2:T(8,128)(4,1)} %copy-done.54) | copy-start | bytes 2272
  114.6 9.1 %copy-start.63 = (pred[12,24]{1,0:T(8,128)(4,1)S(1)}, pred[12,24]{1,0:T(8,128)(4,1)}, u32[]{:S(2)}) copy-start(pred[12,24]{1,0:T(8,128)(4,1)} %slice_bitcast_fusion.24) | copy-start | bytes 868
  115.8 5.9 %collective-permute-start.9 = (f32[3,4,16,128]{3,2,1,0:T(8,128)S(1)}, f32[3,4,16,128]{3,2,1,0:T(8,128)S(1)}, u32[]{:S(2)}, u32[]{:S(2)}) collective-permute-start(f32[3,4,16,128]{3,2,1,0:T(8,128)S(1)} %pad_maximum_fusion.2), channel_id=1, source_target_pairs={{0,16},{16,32},{32,48},{48,64},{64,80},{80,96},{96,112},{112,128},... | collective-permute-start | bytes 294920 | tf_op jit(solution)/shard_map/ppermute | solution.py:69
  117.8 6.5 %collective-permute-start.11 = (f32[3,4,16,128]{3,2,1,0:T(8,128)S(1)}, f32[3,4,16,128]{3,2,1,0:T(8,128)S(1)}, u32[]{:S(2)}, u32[]{:S(2)}) collective-permute-start(f32[3,4,16,128]{3,2,1,0:T(8,128)S(1)} %pad_maximum_fusion.2), channel_id=1, source_target_pairs={{16,0},{32,16},{48,32},{64,48},{80,64},{96,80},{112,96},{128,112},... | collective-permute-start | bytes 294920 | tf_op jit(solution)/shard_map/ppermute | solution.py:70
  121.7 6.3 %collective-permute-start.10 = (f32[3,3,16,128]{3,2,1,0:T(8,128)S(1)}, f32[3,3,16,128]{3,2,1,0:T(8,128)S(1)}, u32[]{:S(2)}, u32[]{:S(2)}) collective-permute-start(f32[3,3,16,128]{3,2,1,0:T(8,128)S(1)} %slice.1970), channel_id=1, source_target_pairs={{0,16},{16,32},{32,48},{48,64},{64,80},{80,96},{96,112},{112,128},... | collective-permute-start | bytes 221192 | tf_op jit(solution)/shard_map/ppermute | solution.py:69
  124.3 5.6 %collective-permute-start.12 = (f32[3,3,16,128]{3,2,1,0:T(8,128)S(1)}, f32[3,3,16,128]{3,2,1,0:T(8,128)S(1)}, u32[]{:S(2)}, u32[]{:S(2)}) collective-permute-start(f32[3,3,16,128]{3,2,1,0:T(8,128)S(1)} %slice.1971), channel_id=1, source_target_pairs={{16,0},{32,16},{48,32},{64,48},{80,64},{96,80},{112,96},{128,112},... | collective-permute-start | bytes 221192 | tf_op jit(solution)/shard_map/ppermute | solution.py:70
  130.7 10.1 %collective-permute-start.13 = (f32[3,18,7,128]{3,2,1,0:T(8,128)}, f32[3,18,7,128]{3,2,1,0:T(8,128)}, u32[]{:S(2)}, u32[]{:S(2)}) collective-permute-start(f32[3,18,7,128]{3,2,1,0:T(8,128)} %get-tuple-element.93), channel_id=1, source_target_pairs={{0,1},{1,2},{2,3},{3,4},{4,5},{5,6},{6,7},{7,8},{8,9},{9,10},{10,1... | collective-permute-start | bytes 580616 | tf_op jit(solution)/shard_map/ppermute | solution.py:69
  134.2 11.0 %collective-permute-start.14 = (f32[3,18,7,128]{3,2,1,0:T(8,128)}, f32[3,18,7,128]{3,2,1,0:T(8,128)}, u32[]{:S(2)}, u32[]{:S(2)}) collective-permute-start(f32[3,18,7,128]{3,2,1,0:T(8,128)} %get-tuple-element.94), channel_id=1, source_target_pairs={{1,0},{2,1},{3,2},{4,3},{5,4},{6,5},{7,6},{8,7},{9,8},{10,9},{11,1... | collective-permute-start | bytes 580616 | tf_op jit(solution)/shard_map/ppermute | solution.py:70
  148.5 14.0 %copy-start.64 = (pred[12,18]{1,0:T(8,128)(4,1)S(1)}, pred[12,18]{1,0:T(8,128)(4,1)}, u32[]{:S(2)}) copy-start(pred[12,18]{1,0:T(8,128)(4,1)} %slice_bitcast_fusion.21) | copy-start | bytes 652
  148.6 23.0 %copy-start.96 = (pred[18]{0:T(512)(128)(4,1)S(1)}, pred[18]{0:T(512)(128)(4,1)}, u32[]{:S(2)}) copy-start(pred[18]{0:T(512)(128)(4,1)} %copy-done.95) | copy-start | bytes 58
  149.6 6.9 %collective-permute-start.15 = (f32[3,2,8,64]{3,2,1,0:T(8,128)S(1)}, f32[3,2,8,64]{3,2,1,0:T(8,128)S(1)}, u32[]{:S(2)}, u32[]{:S(2)}) collective-permute-start(f32[3,2,8,64]{3,2,1,0:T(8,128)S(1)} %pad_maximum_fusion.4), channel_id=1, source_target_pairs={{0,16},{16,32},{32,48},{48,64},{64,80},{80,96},{96,112},{112,128},... | collective-permute-start | bytes 36872 | tf_op jit(solution)/shard_map/ppermute | solution.py:69
  151.5 5.1 %collective-permute-start.16 = (f32[3,2,8,64]{3,2,1,0:T(8,128)S(1)}, f32[3,2,8,64]{3,2,1,0:T(8,128)S(1)}, u32[]{:S(2)}, u32[]{:S(2)}) collective-permute-start(f32[3,2,8,64]{3,2,1,0:T(8,128)S(1)} %pad_maximum_fusion.4), channel_id=1, source_target_pairs={{0,496},{16,0},{32,16},{48,32},{64,48},{80,64},{96,80},{112,96},{1... | collective-permute-start | bytes 36872 | tf_op jit(solution)/shard_map/ppermute | solution.py:70
  156.7 10.4 %collective-permute-start.17 = (f32[3,6,8,64]{3,2,1,0:T(8,128)S(1)}, f32[3,6,8,64]{3,2,1,0:T(8,128)S(1)}, u32[]{:S(2)}, u32[]{:S(2)}) collective-permute-start(f32[3,6,8,64]{3,2,1,0:T(8,128)S(1)} %pad_maximum_fusion.3), channel_id=1, source_target_pairs={{0,48},{16,64},{32,80},{48,96},{64,112},{80,128},{96,144},{112,160... | collective-permute-start | bytes 110600 | tf_op jit(solution)/shard_map/ppermute | solution.py:69
  163.1 8.5 %collective-permute-start.18 = (f32[3,6,8,64]{3,2,1,0:T(8,128)S(1)}, f32[3,6,8,64]{3,2,1,0:T(8,128)S(1)}, u32[]{:S(2)}, u32[]{:S(2)}) collective-permute-start(f32[3,6,8,64]{3,2,1,0:T(8,128)S(1)} %pad_maximum_fusion.3), channel_id=1, source_target_pairs={{0,464},{16,480},{32,496},{48,0},{64,16},{80,32},{96,48},{112,64},... | collective-permute-start | bytes 110600 | tf_op jit(solution)/shard_map/ppermute | solution.py:70
  171.7 8.4 %collective-permute-start.19 = (f32[3,18,8,64]{3,2,1,0:T(8,128)S(1)}, f32[3,18,8,64]{3,2,1,0:T(8,128)}, u32[]{:S(2)}, u32[]{:S(2)}) collective-permute-start(f32[3,18,8,64]{3,2,1,0:T(8,128)S(1)} %broadcast_select_fusion), channel_id=1, source_target_pairs={{0,1},{1,2},{2,3},{3,4},{4,5},{5,6},{6,7},{7,8},{8,9},{9,10},{10,1... | collective-permute-start | bytes 331784 | tf_op jit(solution)/shard_map/ppermute | solution.py:69
  174.4 9.4 %collective-permute-start.20 = (f32[3,18,8,64]{3,2,1,0:T(8,128)S(1)}, f32[3,18,8,64]{3,2,1,0:T(8,128)}, u32[]{:S(2)}, u32[]{:S(2)}) collective-permute-start(f32[3,18,8,64]{3,2,1,0:T(8,128)S(1)} %broadcast_select_fusion), channel_id=1, source_target_pairs={{1,0},{2,1},{3,2},{4,3},{5,4},{6,5},{7,6},{8,7},{9,8},{10,9},{11,1... | collective-permute-start | bytes 331784 | tf_op jit(solution)/shard_map/ppermute | solution.py:70
  187.1 60.7 %copy-start.98 = (pred[24]{0:T(512)(128)(4,1)S(1)}, pred[24]{0:T(512)(128)(4,1)}, u32[]{:S(2)}) copy-start(pred[24]{0:T(512)(128)(4,1)} %copy-done.97) | copy-start | bytes 76
  214.2 7.6 %collective-permute-start.21 = (f32[3,21,4,32]{3,2,1,0:T(4,128)S(1)}, f32[3,21,4,32]{3,2,1,0:T(4,128)S(1)}, u32[]{:S(2)}, u32[]{:S(2)}) collective-permute-start(f32[3,21,4,32]{3,2,1,0:T(4,128)S(1)} %pad_dynamic-slice_fusion), channel_id=1, source_target_pairs={{0,1},{1,2},{2,3},{3,4},{4,5},{5,6},{6,7},{7,8},{8,9},{9,10},{10,1... | collective-permute-start | bytes 96776 | tf_op jit(solution)/shard_map/ppermute | solution.py:69
  216.1 8.8 %collective-permute-start.22 = (f32[3,21,4,32]{3,2,1,0:T(4,128)S(1)}, f32[3,21,4,32]{3,2,1,0:T(4,128)S(1)}, u32[]{:S(2)}, u32[]{:S(2)}) collective-permute-start(f32[3,21,4,32]{3,2,1,0:T(4,128)S(1)} %pad_dynamic-slice_fusion), channel_id=1, source_target_pairs={{0,15},{1,0},{2,1},{3,2},{4,3},{5,4},{6,5},{7,6},{8,7},{9,8},{10,9... | collective-permute-start | bytes 96776 | tf_op jit(solution)/shard_map/ppermute | solution.py:70
  226.8 15.9 %collective-permute-start.23 = (f32[3,21,6,32]{3,2,1,0:T(8,128)}, f32[3,21,6,32]{3,2,1,0:T(8,128)}, u32[]{:S(2)}, u32[]{:S(2)}) collective-permute-start(f32[3,21,6,32]{3,2,1,0:T(8,128)} %get-tuple-element.89), channel_id=1, source_target_pairs={{0,2},{1,3},{2,4},{3,5},{4,6},{5,7},{6,8},{7,9},{8,10},{9,11},{10,... | collective-permute-start | bytes 145160 | tf_op jit(solution)/shard_map/ppermute | solution.py:69
  231.0 16.9 %collective-permute-start.24 = (f32[3,21,6,32]{3,2,1,0:T(8,128)}, f32[3,21,6,32]{3,2,1,0:T(8,128)}, u32[]{:S(2)}, u32[]{:S(2)}) collective-permute-start(f32[3,21,6,32]{3,2,1,0:T(8,128)} %get-tuple-element.90), channel_id=1, source_target_pairs={{0,14},{1,15},{2,0},{3,1},{4,2},{5,3},{6,4},{7,5},{8,6},{9,7},{10,... | collective-permute-start | bytes 145160 | tf_op jit(solution)/shard_map/ppermute | solution.py:70
  (84 other events, 139.9 us)

commit v7 on v6

--- a/solution.py
+++ b/solution.py
@@ -133,15 +133,19 @@
 
 
 class Level:
-    def __init__(self, source, alpha, beta, inv_spacing, upper, depth):
+    def __init__(self, source, alpha, beta, inv_spacing, upper, depth, extended=False):
         self.depth = depth
-        stacked = extend(jnp.stack([source, beta, alpha]), self.depth)
-        self.source = stacked[0]
-        beta_ext = stacked[1]
-        self.alpha = stacked[2]
-        centre, near = neighbours(beta_ext)
+        if not extended:
+            stacked = extend(jnp.stack([source, beta, alpha]), self.depth)
+            source, beta, alpha = stacked[0], stacked[1], stacked[2]
+        self.source = source
+        self.beta = beta
+        self.alpha = alpha
+        centre, near = neighbours(beta)
         self.sums = [centre + b for b in near]
-        self.mask = inside_mask(source.shape, self.depth)
+        n0 = source.shape[0] - 2 * depth
+        n1 = source.shape[1] - 2 * depth
+        self.mask = inside_mask((n0, n1), self.depth)
         self.inv_spacing = inv_spacing
         self.upper = upper
 
@@ -221,6 +225,8 @@
         out_depth.append(-(-(out_depth[-1] + POST_STEPS) // 2))
     depths = [out_depth[i] + POST_STEPS + PRE_STEPS - 1 for i in range(LEVELS - 1)]
     depths.append(out_depth[LEVELS - 1] + COARSE_STEPS - 1)
+    second = LEVELS - 2
+    depths[second] = max(depths[second], 2 * depths[LEVELS - 1] + PRE_STEPS)
     levels = []
     fields = []
     source = rhs_field
@@ -236,10 +242,24 @@
         levels.append(level)
         smoothed, e = smooth(level, None, 0, PRE_STEPS, True)
         residual = level.residual(smoothed, e)
-        source = restrict(crop(residual, e - 1))
+        if level_idx == second:
+            keep = 2 * depths[LEVELS - 1]
+            source = restrict(crop(residual, e - 1 - keep))
+            coarse_beta = restrict(crop(level.beta, level.depth - keep))
+            coarse_alpha = restrict(crop(level.alpha, level.depth - keep))
+        else:
+            source = restrict(crop(residual, e - 1))
         fields.append((smoothed, e))
     last = LEVELS - 1
-    level = Level(source, alphas[last], betas[last], 1.0 / 4.0**last, uppers[last], depths[last])
+    level = Level(
+        source,
+        coarse_alpha,
+        coarse_beta,
+        1.0 / 4.0**last,
+        uppers[last],
+        depths[last],
+        extended=True,
+    )
     coarse, e = smooth(level, None, 0, COARSE_STEPS, True)
     for level_idx in range(LEVELS - 2, -1, -1):
         smoothed, have = fields[level_idx]

time: 265 us -> 286 us (1.079)
  the two profiles are of different devices: /device:TPU:98 before, /device:TPU:32 now
where the time goes in v7:
time: 286 us; the launch traced here: 284 us
  waiting for transfers between devices  75.8 us (27%)
  blocking collectives  64.1 us (22%)
  starting transfers between devices  56.6 us (20%)
  local copies, waits for them, and re-layouts  33.5 us (12%)
  other arithmetic  32.6 us (11%)
  matrix products  13.4 us (5%)
  between operations  8.21 us (3%)
    ppermute x7, waiting for transfers between devices, extend(): before = lax.ppermute(low, axis, up)  51.9 us
    all_gather x1, blocking collectives, all_max(): values = jnp.max(lax.all_gather(values, axis), axis=0)  34.3 us
    all_gather x1, blocking collectives, extend(): whole = lax.all_gather(x, axis, axis=dim, tiled=True)  29.8 us
    ppermute x7, starting transfers between devices, extend(): before = lax.ppermute(low, axis, up)  23.6 us
    add x22, other arithmetic, smooth(): field = crop(field, 1) + direction  16.8 us
    ppermute x7, starting transfers between devices, extend(): after = lax.ppermute(high, axis, down)  16.5 us
    ppermute x5, starting transfers between devices, all_max(): values = jnp.maximum(values, lax.ppermute(values, axis, pairs))  16.5 us
    ppermute x7, waiting for transfers between devices, extend(): after = lax.ppermute(high, axis, down)  13.9 us
  transfers between devices with their start and end apart: 19, of which 10 were waited for; matrix products, arithmetic and copies ran while one was open for 7% of the time, Pallas kernels for 0%

profile of v7, /device:TPU:32, one launch (start us, length us, event | category | flops | bytes accessed | tf_op | source)
XLA Modules:
  0.0 284.3 jit_solution(15174755773815765241)
XLA Ops:
  0.1 1.8 reduce_max.81
  1.9 1.7 reduce_max.82
  3.6 1.3 convolution_bitcast_fusion.8
  4.8 1.3 convolution_bitcast_fusion.7
  12.0 2.5 maximum_bitcast_fusion.2
  14.5 2.6 maximum_bitcast_fusion
  17.2 1.9 collective-permute-start.4
  19.4 2.4 collective-permute-start
  21.8 1.3 collective-permute-start.1
  35.3 5.2 %collective-permute-start.5 = (f32[4,2]{1,0:T(4,128)S(1)}, f32[4,2]{1,0:T(4,128)S(1)}, u32[]{:S(2)}, u32[]{:S(2)}) collective-permute-start(f32[4,2]{1,0:T(4,128)S(1)} %fusion.493), channel_id=1, source_target_pairs={{0,32},{16,48},{32,0},{48,16},{64,96},{80,112},{96,64},{112,80},{1... | collective-permute-start | bytes 104 | tf_op jit(solution)/shard_map/ppermute | solution.py:209
  40.9 3.8 %collective-permute-start.2 = (f32[3,18,5,256]{3,2,1,0:T(8,128)S(1)}, f32[3,18,5,256]{3,2,1,0:T(8,128)S(1)}, u32[]{:S(2)}, u32[]{:S(2)}) collective-permute-start(f32[3,18,5,256]{3,2,1,0:T(8,128)S(1)} %get-tuple-element.67), channel_id=1, source_target_pairs={{0,1},{1,2},{2,3},{3,4},{4,5},{5,6},{6,7},{7,8},{8,9},{9,10},{10,1... | collective-permute-start | bytes 829448 | tf_op jit(solution)/shard_map/ppermute | solution.py:69
  44.7 3.7 %collective-permute-start.3 = (f32[3,18,5,256]{3,2,1,0:T(8,128)S(1)}, f32[3,18,5,256]{3,2,1,0:T(8,128)S(1)}, u32[]{:S(2)}, u32[]{:S(2)}) collective-permute-start(f32[3,18,5,256]{3,2,1,0:T(8,128)S(1)} %get-tuple-element.68), channel_id=1, source_target_pairs={{1,0},{2,1},{3,2},{4,3},{5,4},{6,5},{7,6},{8,7},{9,8},{10,9},{11,1... | collective-permute-start | bytes 829448 | tf_op jit(solution)/shard_map/ppermute | solution.py:70
  48.5 2.9 %collective-permute-start.6 = (f32[4,2]{1,0:T(4,128)S(1)}, f32[4,2]{1,0:T(4,128)S(1)}, u32[]{:S(2)}, u32[]{:S(2)}) collective-permute-start(f32[4,2]{1,0:T(4,128)S(1)} %fusion.563), channel_id=1, source_target_pairs={{0,64},{16,80},{32,96},{48,112},{64,0},{80,16},{96,32},{112,48},{1... | collective-permute-start | bytes 104 | tf_op jit(solution)/shard_map/ppermute | solution.py:209
  51.5 4.0 %collective-permute-done.6 = f32[4,2]{1,0:T(4,128)S(1)} collective-permute-done((f32[4,2]{1,0:T(4,128)S(1)}, f32[4,2]{1,0:T(4,128)S(1)}, u32[]{:S(2)}, u32[]{:S(2)}) %collective-permute-start.6) | collective-permute-done | bytes 64 | tf_op jit(solution)/shard_map/ppermute | solution.py:209
  55.5 2.4 collective-permute-start.7
  57.9 3.1 %collective-permute-done.7 = f32[4,2]{1,0:T(4,128)S(1)} collective-permute-done((f32[4,2]{1,0:T(4,128)S(1)}, f32[4,2]{1,0:T(4,128)S(1)}, u32[]{:S(2)}, u32[]{:S(2)}) %collective-permute-start.7) | collective-permute-done | bytes 64 | tf_op jit(solution)/shard_map/ppermute | solution.py:209
  61.0 4.0 %collective-permute-start.8 = (f32[4,2]{1,0:T(4,128)S(1)}, f32[4,2]{1,0:T(4,128)S(1)}, u32[]{:S(2)}, u32[]{:S(2)}) collective-permute-start(f32[4,2]{1,0:T(4,128)S(1)} %max.18), channel_id=1, source_target_pairs={{0,256},{16,272},{32,288},{48,304},{64,320},{80,336},{96,352},{112... | collective-permute-start | bytes 104 | tf_op jit(solution)/shard_map/ppermute | solution.py:209
  65.0 2.9 %collective-permute-done.8 = f32[4,2]{1,0:T(4,128)S(1)} collective-permute-done((f32[4,2]{1,0:T(4,128)S(1)}, f32[4,2]{1,0:T(4,128)S(1)}, u32[]{:S(2)}, u32[]{:S(2)}) %collective-permute-start.8) | collective-permute-done | bytes 64 | tf_op jit(solution)/shard_map/ppermute | solution.py:209
  68.6 34.3 %all-gather.1 = f32[16,4,2]{1,2,0:T(2,128)} all-gather(f32[1,4,2]{1,2,0:T(2,128)} %bitcast.264), channel_id=2, replica_groups=mesh['gx'=32,'gy'=16] {'gy'}, dimensions={0}, use_global_device_ids=true | all-gather | bytes 544 | tf_op jit(solution)/shard_map/all_gather | solution.py:201
  107.7 1.5 slice_add_fusion.9
  110.1 1.3 fusion.71
  113.4 1.3 collective-permute-start.9
  114.7 1.3 collective-permute-start.11
  116.1 5.3 %collective-permute-start.10 = (f32[3,3,16,128]{3,2,1,0:T(8,128)S(1)}, f32[3,3,16,128]{3,2,1,0:T(8,128)S(1)}, u32[]{:S(2)}, u32[]{:S(2)}) collective-permute-start(f32[3,3,16,128]{3,2,1,0:T(8,128)S(1)} %slice.2006), channel_id=1, source_target_pairs={{0,16},{16,32},{32,48},{48,64},{64,80},{80,96},{96,112},{112,128},... | collective-permute-start | bytes 221192 | tf_op jit(solution)/shard_map/ppermute | solution.py:69
  122.0 1.3 collective-permute-start.12
  123.3 3.3 %collective-permute-done.12 = f32[3,3,16,128]{3,2,1,0:T(8,128)S(1)} collective-permute-done((f32[3,3,16,128]{3,2,1,0:T(8,128)S(1)}, f32[3,3,16,128]{3,2,1,0:T(8,128)S(1)}, u32[]{:S(2)}, u32[]{:S(2)}) %collective-permute-start.12) | collective-permute-done | bytes 73760 | tf_op jit(solution)/shard_map/ppermute | solution.py:70
  126.7 2.8 collective-permute-start.13
  129.5 3.0 %collective-permute-start.14 = (f32[3,18,7,128]{3,2,1,0:T(8,128)S(1)}, f32[3,18,7,128]{3,2,1,0:T(8,128)S(1)}, u32[]{:S(2)}, u32[]{:S(2)}) collective-permute-start(f32[3,18,7,128]{3,2,1,0:T(8,128)S(1)} %get-tuple-element.101), channel_id=1, source_target_pairs={{1,0},{2,1},{3,2},{4,3},{5,4},{6,5},{7,6},{8,7},{9,8},{10,9},{11,1... | collective-permute-start | bytes 580616 | tf_op jit(solution)/shard_map/ppermute | solution.py:70
  134.9 3.1 %collective-permute-done.14 = f32[3,18,7,128]{3,2,1,0:T(8,128)S(1)} collective-permute-done((f32[3,18,7,128]{3,2,1,0:T(8,128)S(1)}, f32[3,18,7,128]{3,2,1,0:T(8,128)S(1)}, u32[]{:S(2)}, u32[]{:S(2)}) %collective-permute-start.14) | collective-permute-done | bytes 193568 | tf_op jit(solution)/shard_map/ppermute | solution.py:70
  141.5 29.8 %all_gather.11 = f32[3,64,8,64]{3,2,1,0:T(8,128)S(1)} all-gather(f32[3,2,8,64]{3,2,1,0:T(8,128)S(1)} %pad_maximum_fusion.3), channel_id=1, replica_groups=mesh['gx'=32,'gy'=16] {'gx'}, dimensions={1}, use_global_device_ids=true | all-gather | bytes 405504 | tf_op jit(solution)/shard_map/all_gather | solution.py:50
  171.4 2.9 %collective-permute-start.15 = (f32[3,48,8,64]{3,2,1,0:T(8,128)S(1)}, f32[3,48,8,64]{3,2,1,0:T(8,128)S(1)}, u32[]{:S(2)}, u32[]{:S(2)}) collective-permute-start(f32[3,48,8,64]{3,2,1,0:T(8,128)S(1)} %pad_dynamic-slice_fusion), channel_id=1, source_target_pairs={{0,1},{1,2},{2,3},{3,4},{4,5},{5,6},{6,7},{7,8},{8,9},{9,10},{10,1... | collective-permute-start | bytes 884744 | tf_op jit(solution)/shard_map/ppermute | solution.py:69
  174.2 3.0 %collective-permute-start.16 = (f32[3,48,8,64]{3,2,1,0:T(8,128)S(1)}, f32[3,48,8,64]{3,2,1,0:T(8,128)S(1)}, u32[]{:S(2)}, u32[]{:S(2)}) collective-permute-start(f32[3,48,8,64]{3,2,1,0:T(8,128)S(1)} %pad_dynamic-slice_fusion), channel_id=1, source_target_pairs={{0,15},{1,0},{2,1},{3,2},{4,3},{5,4},{6,5},{7,6},{8,7},{9,8},{10,9... | collective-permute-start | bytes 884744 | tf_op jit(solution)/shard_map/ppermute | solution.py:70
  177.3 11.5 %collective-permute-done.15 = f32[3,48,8,64]{3,2,1,0:T(8,128)S(1)} collective-permute-done((f32[3,48,8,64]{3,2,1,0:T(8,128)S(1)}, f32[3,48,8,64]{3,2,1,0:T(8,128)S(1)}, u32[]{:S(2)}, u32[]{:S(2)}) %collective-permute-start.15) | collective-permute-done | bytes 294944 | tf_op jit(solution)/shard_map/ppermute | solution.py:69
  188.9 3.7 %collective-permute-done.16 = f32[3,48,8,64]{3,2,1,0:T(8,128)S(1)} collective-permute-done((f32[3,48,8,64]{3,2,1,0:T(8,128)S(1)}, f32[3,48,8,64]{3,2,1,0:T(8,128)S(1)}, u32[]{:S(2)}, u32[]{:S(2)}) %collective-permute-start.16) | collective-permute-done | bytes 294944 | tf_op jit(solution)/shard_map/ppermute | solution.py:70
  192.8 1.4 copy.6
  194.2 5.0 %collective-permute-start.17 = (f32[3,48,15,64]{3,1,2,0:T(8,128)}, f32[3,48,15,64]{3,1,2,0:T(8,128)}, u32[]{:S(2)}, u32[]{:S(2)}) collective-permute-start(f32[3,48,15,64]{3,1,2,0:T(8,128)} %copy.6), channel_id=1, source_target_pairs={{0,2},{1,3},{2,4},{3,5},{4,6},{5,7},{6,8},{7,9},{8,10},{9,11},{10,... | collective-permute-start | bytes 1658888 | tf_op jit(solution)/shard_map/ppermute | solution.py:69
  199.2 1.3 copy.8
  200.6 2.9 %collective-permute-start.18 = (f32[3,48,15,64]{3,1,2,0:T(8,128)}, f32[3,48,15,64]{3,1,2,0:T(8,128)}, u32[]{:S(2)}, u32[]{:S(2)}) collective-permute-start(f32[3,48,15,64]{3,1,2,0:T(8,128)} %copy.8), channel_id=1, source_target_pairs={{0,14},{1,15},{2,0},{3,1},{4,2},{5,3},{6,4},{7,5},{8,6},{9,7},{10,... | collective-permute-start | bytes 1658888 | tf_op jit(solution)/shard_map/ppermute | solution.py:70
  207.0 40.2 %collective-permute-done.17 = f32[3,48,15,64]{3,1,2,0:T(8,128)} collective-permute-done((f32[3,48,15,64]{3,1,2,0:T(8,128)}, f32[3,48,15,64]{3,1,2,0:T(8,128)}, u32[]{:S(2)}, u32[]{:S(2)}) %collective-permute-start.17) | collective-permute-done | bytes 552992 | tf_op jit(solution)/shard_map/ppermute | solution.py:69
  247.2 1.6 copy.7
  248.8 3.8 %collective-permute-done.18 = f32[3,48,15,64]{3,1,2,0:T(8,128)} collective-permute-done((f32[3,48,15,64]{3,1,2,0:T(8,128)}, f32[3,48,15,64]{3,1,2,0:T(8,128)}, u32[]{:S(2)}, u32[]{:S(2)}) %collective-permute-start.18) | collective-permute-done | bytes 552992 | tf_op jit(solution)/shard_map/ppermute | solution.py:70
  252.6 1.6 copy.9
  255.8 1.1 slice.2137
  257.3 3.6 %slice_add_fusion.4 = (f32[46,52,64]{2,1,0:T(8,128)S(1)}, f32[46,52,64]{2,1,0:T(8,128)S(1)}, f32[46,52,64]{2,1,0:T(8,128)S(1)}, f32[46,52,64]{2,1,0:T(8,128)S(1)...) fusion(f32[48,54,64]{2,1,0:T(8,128)S(1)} %broadcast_divide_fusi, ...), kind=kLoop, calls=%fused_computation.61 | loop fusion | flops 5051904 | bytes 14660576 | tf_op jit(solution)/shard_map/add | solution.py:192
  261.3 3.0 %fusion.23 = f32[44,50,64]{2,1,0:T(8,128)S(1)} fusion(f32[46,52,64]{2,1,0:T(8,128)S(1)} %get-tuple-element.42, f32[46,52,64]{2,1,0:T(8,128)S(1)} %get-tuple-element.41, f32[46,52,64]{2,1,0:T(8,128)S(1)} %get-tuple-element.35, f32[46,52,64]{2,1,0:T(8,128)S(1)} %get-tuple-element.40, f32[46,52,64]{2,1,0:T(8,128)S(1)} %get-tuple-element.39, ...), kind=kLoop, calls=%fused_computation.43 | loop fusion | flops 3801600 | bytes 9559008 | tf_op jit(solution)/shard_map/add | solution.py:192
  264.7 2.4 fusion.511
  280.5 1.0 slice_add_fusion.13
  283.1 1.2 fusion.136
  (347 shorter events, 47.7 us)
Async XLA Ops:
  0.0 19.2 %copy-start.31 = (f32[8,32,256]{2,1,0:T(8,128)S(1)}, f32[8,32,256]{2,1,0:T(8,128)}, u32[]{:S(2)}) copy-start(f32[8,32,256]{2,1,0:T(8,128)} %param.4) | copy-start | bytes 786436
  0.0 19.2 %copy-start.30 = (f32[8,32,256]{2,1,0:T(8,128)S(1)}, f32[8,32,256]{2,1,0:T(8,128)}, u32[]{:S(2)}) copy-start(f32[8,32,256]{2,1,0:T(8,128)} %param.5) | copy-start | bytes 786436
  0.0 19.2 %copy-start.33 = (f32[8,32,256]{2,1,0:T(8,128)S(1)}, f32[8,32,256]{2,1,0:T(8,128)}, u32[]{:S(2)}) copy-start(f32[8,32,256]{2,1,0:T(8,128)} %param.3) | copy-start | bytes 786436
  0.0 19.1 %copy-start.42 = (s32[256]{0:T(256)}, s32[256]{0:T(256)S(1)}, u32[]{:S(2)}) copy-start(s32[256]{0:T(256)S(1)} %and_select_fusion.8) | copy-start | bytes 3076
  0.0 8.1 %copy-start.74 = (s32[32]{0:T(128)}, s32[32]{0:T(128)S(1)}, u32[]{:S(2)}) copy-start(s32[32]{0:T(128)S(1)} %and_select_fusion.9) | copy-start | bytes 388
  0.1 19.1 %copy-start.84 = (s32[16]{0:T(128)}, s32[16]{0:T(128)S(1)}, u32[]{:S(2)}) copy-start(s32[16]{0:T(128)S(1)} %and_select_fusion.7) | copy-start | bytes 196
  0.1 19.1 %copy-start.59 = (s32[128]{0:T(128)}, s32[128]{0:T(128)S(1)}, u32[]{:S(2)}) copy-start(s32[128]{0:T(128)S(1)} %and_select_fusion.6) | copy-start | bytes 1540
  0.1 19.0 %copy-start.72 = (s32[64]{0:T(128)}, s32[64]{0:T(128)S(1)}, u32[]{:S(2)}) copy-start(s32[64]{0:T(128)S(1)} %and_select_fusion.4) | copy-start | bytes 772
  6.9 12.2 %copy-start.34 = (f32[4,16,128]{2,1,0:T(8,128)}, f32[4,16,128]{2,1,0:T(8,128)S(1)}, u32[]{:S(2)}) copy-start(f32[4,16,128]{2,1,0:T(8,128)S(1)} %get-tuple-element.159) | copy-start | bytes 98308
  7.9 11.2 %copy-start.36 = (f32[4,16,128]{2,1,0:T(8,128)}, f32[4,16,128]{2,1,0:T(8,128)S(1)}, u32[]{:S(2)}) copy-start(f32[4,16,128]{2,1,0:T(8,128)S(1)} %get-tuple-element.157) | copy-start | bytes 98308
  9.2 9.9 %copy-start.38 = (f32[2,8,64]{2,1,0:T(8,128)}, f32[2,8,64]{2,1,0:T(8,128)S(1)}, u32[]{:S(2)}) copy-start(f32[2,8,64]{2,1,0:T(8,128)S(1)} %get-tuple-element.155) | copy-start | bytes 12292
  10.0 9.2 %copy-start.40 = (f32[2,8,64]{2,1,0:T(8,128)}, f32[2,8,64]{2,1,0:T(8,128)S(1)}, u32[]{:S(2)}) copy-start(f32[2,8,64]{2,1,0:T(8,128)S(1)} %get-tuple-element.153) | copy-start | bytes 12292
  14.5 20.7 %copy-start.61 = (f32[1,2]{1,0:T(1,128)}, f32[1,2]{1,0:T(1,128)S(1)}, u32[]{:S(2)}) copy-start(f32[1,2]{1,0:T(1,128)S(1)} %get-tuple-element.164) | copy-start | bytes 28
  14.5 20.7 %copy-start.63 = (f32[1,2]{1,0:T(1,128)}, f32[1,2]{1,0:T(1,128)S(1)}, u32[]{:S(2)}) copy-start(f32[1,2]{1,0:T(1,128)S(1)} %get-tuple-element.165) | copy-start | bytes 28
  17.1 18.1 %copy-start.65 = (f32[1,2]{1,0:T(1,128)}, f32[1,2]{1,0:T(1,128)S(1)}, u32[]{:S(2)}) copy-start(f32[1,2]{1,0:T(1,128)S(1)} %get-tuple-element.162) | copy-start | bytes 28
  17.1 18.1 %copy-start.67 = (f32[1,2]{1,0:T(1,128)}, f32[1,2]{1,0:T(1,128)S(1)}, u32[]{:S(2)}) copy-start(f32[1,2]{1,0:T(1,128)S(1)} %get-tuple-element.163) | copy-start | bytes 28
  17.2 18.1 %collective-permute-start.4 = (f32[4,2]{1,0:T(4,128)S(1)}, f32[4,2]{1,0:T(4,128)S(1)}, u32[]{:S(2)}, u32[]{:S(2)}) collective-permute-start(f32[4,2]{1,0:T(4,128)S(1)} %pad_maximum_fusion.4), channel_id=1, source_target_pairs={{0,16},{16,0},{32,48},{48,32},{64,80},{80,64},{96,112},{112,96},{1... | collective-permute-start | bytes 104 | tf_op jit(solution)/shard_map/ppermute | solution.py:209
  19.4 21.1 %collective-permute-start = (f32[3,5,32,256]{3,2,1,0:T(8,128)S(1)}, f32[3,5,32,256]{3,2,1,0:T(8,128)S(1)}, u32[]{:S(2)}, u32[]{:S(2)}) collective-permute-start(f32[3,5,32,256]{3,2,1,0:T(8,128)S(1)} %get-tuple-element.86), channel_id=1, source_target_pairs={{0,16},{16,32},{32,48},{48,64},{64,80},{80,96},{96,112},{112,128},... | collective-permute-start | bytes 1474568 | tf_op jit(solution)/shard_map/ppermute | solution.py:69
  21.8 18.7 %collective-permute-start.1 = (f32[3,5,32,256]{3,2,1,0:T(8,128)S(1)}, f32[3,5,32,256]{3,2,1,0:T(8,128)S(1)}, u32[]{:S(2)}, u32[]{:S(2)}) collective-permute-start(f32[3,5,32,256]{3,2,1,0:T(8,128)S(1)} %get-tuple-element.87), channel_id=1, source_target_pairs={{16,0},{32,16},{48,32},{64,48},{80,64},{96,80},{112,96},{128,112},... | collective-permute-start | bytes 1474568 | tf_op jit(solution)/shard_map/ppermute | solution.py:70
  24.6 15.9 %copy-start.44 = (pred[12,36]{1,0:T(8,128)(4,1)}, pred[12,36]{1,0:T(8,128)(4,1)S(1)}, u32[]{:S(2)}) copy-start(pred[12,36]{1,0:T(8,128)(4,1)S(1)} %slice_bitcast_fusion.25) | copy-start | bytes 1300
  26.1 14.4 %copy-start.50 = (pred[12,24]{1,0:T(8,128)(4,1)}, pred[12,24]{1,0:T(8,128)(4,1)S(1)}, u32[]{:S(2)}) copy-start(pred[12,24]{1,0:T(8,128)(4,1)S(1)} %slice_bitcast_fusion.22) | copy-start | bytes 868
  30.0 10.5 %copy-start.80 = (pred[54]{0:T(512)(128)(4,1)}, pred[54]{0:T(512)(128)(4,1)S(1)}, u32[]{:S(2)}) copy-start(pred[54]{0:T(512)(128)(4,1)S(1)} %compare_and_fusion.3) | copy-start | bytes 166
  35.3 13.2 %collective-permute-start.5 = (f32[4,2]{1,0:T(4,128)S(1)}, f32[4,2]{1,0:T(4,128)S(1)}, u32[]{:S(2)}, u32[]{:S(2)}) collective-permute-start(f32[4,2]{1,0:T(4,128)S(1)} %fusion.493), channel_id=1, source_target_pairs={{0,32},{16,48},{32,0},{48,16},{64,96},{80,112},{96,64},{112,80},{1... | collective-permute-start | bytes 104 | tf_op jit(solution)/shard_map/ppermute | solution.py:209
  40.8 7.7 %copy-start.62 = (f32[1,2]{1,0:T(1,128)S(1)}, f32[1,2]{1,0:T(1,128)}, u32[]{:S(2)}) copy-start(f32[1,2]{1,0:T(1,128)} %copy-done.61) | copy-start | bytes 28
  40.8 7.7 %copy-start.64 = (f32[1,2]{1,0:T(1,128)S(1)}, f32[1,2]{1,0:T(1,128)}, u32[]{:S(2)}) copy-start(f32[1,2]{1,0:T(1,128)} %copy-done.63) | copy-start | bytes 28
  40.8 7.7 %copy-start.66 = (f32[1,2]{1,0:T(1,128)S(1)}, f32[1,2]{1,0:T(1,128)}, u32[]{:S(2)}) copy-start(f32[1,2]{1,0:T(1,128)} %copy-done.65) | copy-start | bytes 28
  40.8 7.7 %copy-start.68 = (f32[1,2]{1,0:T(1,128)S(1)}, f32[1,2]{1,0:T(1,128)}, u32[]{:S(2)}) copy-start(f32[1,2]{1,0:T(1,128)} %copy-done.67) | copy-start | bytes 28
  40.9 65.0 %collective-permute-start.2 = (f32[3,18,5,256]{3,2,1,0:T(8,128)S(1)}, f32[3,18,5,256]{3,2,1,0:T(8,128)S(1)}, u32[]{:S(2)}, u32[]{:S(2)}) collective-permute-start(f32[3,18,5,256]{3,2,1,0:T(8,128)S(1)} %get-tuple-element.67), channel_id=1, source_target_pairs={{0,1},{1,2},{2,3},{3,4},{4,5},{5,6},{6,7},{7,8},{8,9},{9,10},{10,1... | collective-permute-start | bytes 829448 | tf_op jit(solution)/shard_map/ppermute | solution.py:69
  44.7 61.2 %collective-permute-start.3 = (f32[3,18,5,256]{3,2,1,0:T(8,128)S(1)}, f32[3,18,5,256]{3,2,1,0:T(8,128)S(1)}, u32[]{:S(2)}, u32[]{:S(2)}) collective-permute-start(f32[3,18,5,256]{3,2,1,0:T(8,128)S(1)} %get-tuple-element.68), channel_id=1, source_target_pairs={{1,0},{2,1},{3,2},{4,3},{5,4},{6,5},{7,6},{8,7},{9,8},{10,9},{11,1... | collective-permute-start | bytes 829448 | tf_op jit(solution)/shard_map/ppermute | solution.py:70
  48.5 7.0 %collective-permute-start.6 = (f32[4,2]{1,0:T(4,128)S(1)}, f32[4,2]{1,0:T(4,128)S(1)}, u32[]{:S(2)}, u32[]{:S(2)}) collective-permute-start(f32[4,2]{1,0:T(4,128)S(1)} %fusion.563), channel_id=1, source_target_pairs={{0,64},{16,80},{32,96},{48,112},{64,0},{80,16},{96,32},{112,48},{1... | collective-permute-start | bytes 104 | tf_op jit(solution)/shard_map/ppermute | solution.py:209
  55.5 5.5 %collective-permute-start.7 = (f32[4,2]{1,0:T(4,128)S(1)}, f32[4,2]{1,0:T(4,128)S(1)}, u32[]{:S(2)}, u32[]{:S(2)}) collective-permute-start(f32[4,2]{1,0:T(4,128)S(1)} %max.17), channel_id=1, source_target_pairs={{0,128},{16,144},{32,160},{48,176},{64,192},{80,208},{96,224},{112... | collective-permute-start | bytes 104 | tf_op jit(solution)/shard_map/ppermute | solution.py:209
  61.0 7.0 %collective-permute-start.8 = (f32[4,2]{1,0:T(4,128)S(1)}, f32[4,2]{1,0:T(4,128)S(1)}, u32[]{:S(2)}, u32[]{:S(2)}) collective-permute-start(f32[4,2]{1,0:T(4,128)S(1)} %max.18), channel_id=1, source_target_pairs={{0,256},{16,272},{32,288},{48,304},{64,320},{80,336},{96,352},{112... | collective-permute-start | bytes 104 | tf_op jit(solution)/shard_map/ppermute | solution.py:209
  106.6 3.0 %copy-start = (f32[18,42,256]{2,1,0:T(8,128)}, f32[18,42,256]{2,1,0:T(8,128)S(1)}, u32[]{:S(2)}) copy-start(f32[18,42,256]{2,1,0:T(8,128)S(1)} %get-tuple-element.64) | copy-start | bytes 2322436
  109.2 2.3 copy-start.4
  109.2 2.3 copy-start.6
  109.2 2.3 copy-start.8
  113.4 2.6 collective-permute-start.9
  114.7 7.2 %collective-permute-start.11 = (f32[3,4,16,128]{3,2,1,0:T(8,128)S(1)}, f32[3,4,16,128]{3,2,1,0:T(8,128)S(1)}, u32[]{:S(2)}, u32[]{:S(2)}) collective-permute-start(f32[3,4,16,128]{3,2,1,0:T(8,128)S(1)} %pad_maximum_fusion.2), channel_id=1, source_target_pairs={{16,0},{32,16},{48,32},{64,48},{80,64},{96,80},{112,96},{128,112},... | collective-permute-start | bytes 294920 | tf_op jit(solution)/shard_map/ppermute | solution.py:70
  116.1 7.2 %collective-permute-start.10 = (f32[3,3,16,128]{3,2,1,0:T(8,128)S(1)}, f32[3,3,16,128]{3,2,1,0:T(8,128)S(1)}, u32[]{:S(2)}, u32[]{:S(2)}) collective-permute-start(f32[3,3,16,128]{3,2,1,0:T(8,128)S(1)} %slice.2006), channel_id=1, source_target_pairs={{0,16},{16,32},{32,48},{48,64},{64,80},{80,96},{96,112},{112,128},... | collective-permute-start | bytes 221192 | tf_op jit(solution)/shard_map/ppermute | solution.py:69
  122.0 4.7 %collective-permute-start.12 = (f32[3,3,16,128]{3,2,1,0:T(8,128)S(1)}, f32[3,3,16,128]{3,2,1,0:T(8,128)S(1)}, u32[]{:S(2)}, u32[]{:S(2)}) collective-permute-start(f32[3,3,16,128]{3,2,1,0:T(8,128)S(1)} %slice.2007), channel_id=1, source_target_pairs={{16,0},{32,16},{48,32},{64,48},{80,64},{96,80},{112,96},{128,112},... | collective-permute-start | bytes 221192 | tf_op jit(solution)/shard_map/ppermute | solution.py:70
  126.7 8.2 %collective-permute-start.13 = (f32[3,18,7,128]{3,2,1,0:T(8,128)S(1)}, f32[3,18,7,128]{3,2,1,0:T(8,128)S(1)}, u32[]{:S(2)}, u32[]{:S(2)}) collective-permute-start(f32[3,18,7,128]{3,2,1,0:T(8,128)S(1)} %get-tuple-element.100), channel_id=1, source_target_pairs={{0,1},{1,2},{2,3},{3,4},{4,5},{5,6},{6,7},{7,8},{8,9},{9,10},{10,1... | collective-permute-start | bytes 580616 | tf_op jit(solution)/shard_map/ppermute | solution.py:69
  129.5 8.4 %collective-permute-start.14 = (f32[3,18,7,128]{3,2,1,0:T(8,128)S(1)}, f32[3,18,7,128]{3,2,1,0:T(8,128)S(1)}, u32[]{:S(2)}, u32[]{:S(2)}) collective-permute-start(f32[3,18,7,128]{3,2,1,0:T(8,128)S(1)} %get-tuple-element.101), channel_id=1, source_target_pairs={{1,0},{2,1},{3,2},{4,3},{5,4},{6,5},{7,6},{8,7},{9,8},{10,9},{11,1... | collective-permute-start | bytes 580616 | tf_op jit(solution)/shard_map/ppermute | solution.py:70
  171.4 17.5 %collective-permute-start.15 = (f32[3,48,8,64]{3,2,1,0:T(8,128)S(1)}, f32[3,48,8,64]{3,2,1,0:T(8,128)S(1)}, u32[]{:S(2)}, u32[]{:S(2)}) collective-permute-start(f32[3,48,8,64]{3,2,1,0:T(8,128)S(1)} %pad_dynamic-slice_fusion), channel_id=1, source_target_pairs={{0,1},{1,2},{2,3},{3,4},{4,5},{5,6},{6,7},{7,8},{8,9},{9,10},{10,1... | collective-permute-start | bytes 884744 | tf_op jit(solution)/shard_map/ppermute | solution.py:69
  174.2 18.3 %collective-permute-start.16 = (f32[3,48,8,64]{3,2,1,0:T(8,128)S(1)}, f32[3,48,8,64]{3,2,1,0:T(8,128)S(1)}, u32[]{:S(2)}, u32[]{:S(2)}) collective-permute-start(f32[3,48,8,64]{3,2,1,0:T(8,128)S(1)} %pad_dynamic-slice_fusion), channel_id=1, source_target_pairs={{0,15},{1,0},{2,1},{3,2},{4,3},{5,4},{6,5},{7,6},{8,7},{9,8},{10,9... | collective-permute-start | bytes 884744 | tf_op jit(solution)/shard_map/ppermute | solution.py:70
  194.2 53.0 %collective-permute-start.17 = (f32[3,48,15,64]{3,1,2,0:T(8,128)}, f32[3,48,15,64]{3,1,2,0:T(8,128)}, u32[]{:S(2)}, u32[]{:S(2)}) collective-permute-start(f32[3,48,15,64]{3,1,2,0:T(8,128)} %copy.6), channel_id=1, source_target_pairs={{0,2},{1,3},{2,4},{3,5},{4,6},{5,7},{6,8},{7,9},{8,10},{9,11},{10,... | collective-permute-start | bytes 1658888 | tf_op jit(solution)/shard_map/ppermute | solution.py:69
  200.6 52.0 %collective-permute-start.18 = (f32[3,48,15,64]{3,1,2,0:T(8,128)}, f32[3,48,15,64]{3,1,2,0:T(8,128)}, u32[]{:S(2)}, u32[]{:S(2)}) collective-permute-start(f32[3,48,15,64]{3,1,2,0:T(8,128)} %copy.8), channel_id=1, source_target_pairs={{0,14},{1,15},{2,0},{3,1},{4,2},{5,3},{6,4},{7,5},{8,6},{9,7},{10,... | collective-permute-start | bytes 1658888 | tf_op jit(solution)/shard_map/ppermute | solution.py:70
  248.8 5.4 %copy-start.81 = (pred[54]{0:T(512)(128)(4,1)S(1)}, pred[54]{0:T(512)(128)(4,1)}, u32[]{:S(2)}) copy-start(pred[54]{0:T(512)(128)(4,1)} %copy-done.80) | copy-start | bytes 166
  264.7 2.8 %copy-start.73 = (s32[64]{0:T(128)S(1)}, s32[64]{0:T(128)}, u32[]{:S(2)}) copy-start(s32[64]{0:T(128)} %copy-done.72) | copy-start | bytes 772
  (57 other events, 59.8 us)

commit v8 on v6

--- a/solution.py
+++ b/solution.py
@@ -191,7 +191,7 @@
 
 
 def all_max(values):
-    for axis in ("gx", "gy"):
+    for axis in ("gy", "gx"):
         peers = lax.axis_size(axis)
         if axis == "gy":
             values = jnp.max(lax.all_gather(values, axis), axis=0)

time: 265 us -> 263 us (level)
  the two profiles are of different devices: /device:TPU:98 before, /device:TPU:64 now
where the time goes in v8:
time: 263 us; the launch traced here: 261 us
  starting transfers between devices  84.8 us (32%)
  blocking collectives  61.6 us (23%)
  waiting for transfers between devices  36.5 us (14%)
  local copies, waits for them, and re-layouts  28.6 us (11%)
  other arithmetic  28.2 us (11%)
  matrix products  12.7 us (5%)
  between operations  8.57 us (3%)
    all_gather x1, blocking collectives, all_max(): values = jnp.max(lax.all_gather(values, axis), axis=0)  32.4 us
    ppermute x10, starting transfers between devices, extend(): before = lax.ppermute(low, axis, up)  31.6 us
    all_gather x1, blocking collectives, extend(): whole = lax.all_gather(x, axis, axis=dim, tiled=True)  29.1 us
    ppermute x10, starting transfers between devices, extend(): after = lax.ppermute(high, axis, down)  29 us
    ppermute x5, starting transfers between devices, all_max(): values = jnp.maximum(values, lax.ppermute(values, axis, pairs))  24.2 us
    ppermute x10, waiting for transfers between devices, extend(): after = lax.ppermute(high, axis, down)  21.5 us
    broadcast_in_dim x21, local copies, waits for them, and re-layouts, residual(): r = jnp.where(crop(self.mask, self.depth - out), r, 0.0)  13.1 us
    add x22, other arithmetic, smooth(): field = crop(field, 1) + direction  10.9 us
  transfers between devices with their start and end apart: 25, of which 13 were waited for; matrix products, arithmetic and copies ran while one was open for 7% of the time, Pallas kernels for 0%

profile of v8, /device:TPU:64, one launch (start us, length us, event | category | flops | bytes accessed | tf_op | source)
XLA Modules:
  0.0 261.0 jit_solution(11385890614831208322)
XLA Ops:
  0.1 1.6 reduce_max.81
  1.7 1.6 reduce_max.82
  10.6 1.3 fusion.521
  11.9 1.3 fusion.520
  13.3 2.6 maximum_bitcast_fusion.2
  15.9 2.5 maximum_bitcast_fusion
  18.4 32.4 %all-gather.1 = f32[16,4,2]{1,2,0:T(2,128)S(1)} all-gather(f32[1,4,2]{1,2,0:T(2,128)S(1)} %bitcast.248), channel_id=2, replica_groups=mesh['gx'=32,'gy'=16] {'gy'}, dimensions={0}, use_global_device_ids=true | all-gather | bytes 544 | tf_op jit(solution)/shard_map/all_gather | solution.py:197
  51.5 1.9 collective-permute-start.4
  54.8 2.4 collective-permute-start
  57.3 1.3 collective-permute-start.1
  69.2 1.9 collective-permute-start.2
  71.2 3.9 %collective-permute-start.3 = (f32[3,18,5,256]{3,2,1,0:T(8,128)S(1)}, f32[3,18,5,256]{3,2,1,0:T(8,128)S(1)}, u32[]{:S(2)}, u32[]{:S(2)}) collective-permute-start(f32[3,18,5,256]{3,2,1,0:T(8,128)S(1)} %get-tuple-element.63), channel_id=1, source_target_pairs={{1,0},{2,1},{3,2},{4,3},{5,4},{6,5},{7,6},{8,7},{9,8},{10,9},{11,1... | collective-permute-start | bytes 829448 | tf_op jit(solution)/shard_map/ppermute | solution.py:70
  76.4 5.2 %collective-permute-start.5 = (f32[4,2]{0,1:T(2,128)S(1)}, f32[4,2]{0,1:T(2,128)S(1)}, u32[]{:S(2)}, u32[]{:S(2)}) collective-permute-start(f32[4,2]{0,1:T(2,128)S(1)} %max.15), channel_id=1, source_target_pairs={{0,32},{16,48},{32,0},{48,16},{64,96},{80,112},{96,64},{112,80},{1... | collective-permute-start | bytes 104 | tf_op jit(solution)/shard_map/ppermute | solution.py:205
  81.6 1.5 collective-permute-done.5
  83.2 5.4 %collective-permute-start.6 = (f32[4,2]{0,1:T(2,128)S(1)}, f32[4,2]{0,1:T(2,128)S(1)}, u32[]{:S(2)}, u32[]{:S(2)}) collective-permute-start(f32[4,2]{0,1:T(2,128)S(1)} %max.16), channel_id=1, source_target_pairs={{0,64},{16,80},{32,96},{48,112},{64,0},{80,16},{96,32},{112,48},{1... | collective-permute-start | bytes 104 | tf_op jit(solution)/shard_map/ppermute | solution.py:205
  88.6 1.5 collective-permute-done.6
  90.2 6.1 %collective-permute-start.7 = (f32[4,2]{0,1:T(2,128)S(1)}, f32[4,2]{0,1:T(2,128)S(1)}, u32[]{:S(2)}, u32[]{:S(2)}) collective-permute-start(f32[4,2]{0,1:T(2,128)S(1)} %max.17), channel_id=1, source_target_pairs={{0,128},{16,144},{32,160},{48,176},{64,192},{80,208},{96,224},{112... | collective-permute-start | bytes 104 | tf_op jit(solution)/shard_map/ppermute | solution.py:205
  96.3 1.5 collective-permute-done.7
  97.8 5.5 %collective-permute-start.8 = (f32[4,2]{0,1:T(2,128)S(1)}, f32[4,2]{0,1:T(2,128)S(1)}, u32[]{:S(2)}, u32[]{:S(2)}) collective-permute-start(f32[4,2]{0,1:T(2,128)S(1)} %max.18), channel_id=1, source_target_pairs={{0,256},{16,272},{32,288},{48,304},{64,320},{80,336},{96,352},{112... | collective-permute-start | bytes 104 | tf_op jit(solution)/shard_map/ppermute | solution.py:205
  103.3 1.5 collective-permute-done.8
  108.7 1.5 slice_add_fusion.4
  114.3 1.3 collective-permute-start.9
  115.7 1.3 collective-permute-start.11
  117.0 3.3 %collective-permute-start.10 = (f32[3,3,16,128]{3,2,1,0:T(8,128)S(1)}, f32[3,3,16,128]{3,2,1,0:T(8,128)S(1)}, u32[]{:S(2)}, u32[]{:S(2)}) collective-permute-start(f32[3,3,16,128]{3,2,1,0:T(8,128)S(1)} %slice.1970), channel_id=1, source_target_pairs={{0,16},{16,32},{32,48},{48,64},{64,80},{80,96},{96,112},{112,128},... | collective-permute-start | bytes 221192 | tf_op jit(solution)/shard_map/ppermute | solution.py:69
  121.0 1.3 collective-permute-start.12
  122.4 3.3 %collective-permute-done.12 = f32[3,3,16,128]{3,2,1,0:T(8,128)S(1)} collective-permute-done((f32[3,3,16,128]{3,2,1,0:T(8,128)S(1)}, f32[3,3,16,128]{3,2,1,0:T(8,128)S(1)}, u32[]{:S(2)}, u32[]{:S(2)}) %collective-permute-start.12) | collective-permute-done | bytes 73760 | tf_op jit(solution)/shard_map/ppermute | solution.py:70
  126.5 1.9 collective-permute-start.13
  128.4 3.9 %collective-permute-start.14 = (f32[3,18,7,128]{3,2,1,0:T(8,128)}, f32[3,18,7,128]{3,2,1,0:T(8,128)}, u32[]{:S(2)}, u32[]{:S(2)}) collective-permute-start(f32[3,18,7,128]{3,2,1,0:T(8,128)} %get-tuple-element.94), channel_id=1, source_target_pairs={{1,0},{2,1},{3,2},{4,3},{5,4},{6,5},{7,6},{8,7},{9,8},{10,9},{11,1... | collective-permute-start | bytes 580616 | tf_op jit(solution)/shard_map/ppermute | solution.py:70
  132.3 1.3 slice_bitcast_fusion.32
  135.2 2.9 %collective-permute-done.14 = f32[3,18,7,128]{3,2,1,0:T(8,128)} collective-permute-done((f32[3,18,7,128]{3,2,1,0:T(8,128)}, f32[3,18,7,128]{3,2,1,0:T(8,128)}, u32[]{:S(2)}, u32[]{:S(2)}) %collective-permute-start.14) | collective-permute-done | bytes 193568 | tf_op jit(solution)/shard_map/ppermute | solution.py:70
  142.5 3.8 %collective-permute-start.15 = (f32[3,2,8,64]{3,2,1,0:T(8,128)S(1)}, f32[3,2,8,64]{3,2,1,0:T(8,128)S(1)}, u32[]{:S(2)}, u32[]{:S(2)}) collective-permute-start(f32[3,2,8,64]{3,2,1,0:T(8,128)S(1)} %pad_maximum_fusion.4), channel_id=1, source_target_pairs={{0,16},{16,32},{32,48},{48,64},{64,80},{80,96},{96,112},{112,128},... | collective-permute-start | bytes 36872 | tf_op jit(solution)/shard_map/ppermute | solution.py:69
  146.2 5.1 %collective-permute-start.16 = (f32[3,2,8,64]{3,2,1,0:T(8,128)S(1)}, f32[3,2,8,64]{3,2,1,0:T(8,128)S(1)}, u32[]{:S(2)}, u32[]{:S(2)}) collective-permute-start(f32[3,2,8,64]{3,2,1,0:T(8,128)S(1)} %pad_maximum_fusion.4), channel_id=1, source_target_pairs={{0,496},{16,0},{32,16},{48,32},{64,48},{80,64},{96,80},{112,96},{1... | collective-permute-start | bytes 36872 | tf_op jit(solution)/shard_map/ppermute | solution.py:70
  152.9 4.0 %collective-permute-start.17 = (f32[3,6,8,64]{3,2,1,0:T(8,128)S(1)}, f32[3,6,8,64]{3,2,1,0:T(8,128)S(1)}, u32[]{:S(2)}, u32[]{:S(2)}) collective-permute-start(f32[3,6,8,64]{3,2,1,0:T(8,128)S(1)} %pad_maximum_fusion.3), channel_id=1, source_target_pairs={{0,48},{16,64},{32,80},{48,96},{64,112},{80,128},{96,144},{112,160... | collective-permute-start | bytes 110600 | tf_op jit(solution)/shard_map/ppermute | solution.py:69
  158.0 5.2 %collective-permute-start.18 = (f32[3,6,8,64]{3,2,1,0:T(8,128)S(1)}, f32[3,6,8,64]{3,2,1,0:T(8,128)S(1)}, u32[]{:S(2)}, u32[]{:S(2)}) collective-permute-start(f32[3,6,8,64]{3,2,1,0:T(8,128)S(1)} %pad_maximum_fusion.3), channel_id=1, source_target_pairs={{0,464},{16,480},{32,496},{48,0},{64,16},{80,32},{96,48},{112,64},... | collective-permute-start | bytes 110600 | tf_op jit(solution)/shard_map/ppermute | solution.py:70
  163.3 2.8 %collective-permute-done.18 = f32[3,6,8,64]{3,2,1,0:T(8,128)S(1)} collective-permute-done((f32[3,6,8,64]{3,2,1,0:T(8,128)S(1)}, f32[3,6,8,64]{3,2,1,0:T(8,128)S(1)}, u32[]{:S(2)}, u32[]{:S(2)}) %collective-permute-start.18) | collective-permute-done | bytes 36896 | tf_op jit(solution)/shard_map/ppermute | solution.py:70
  166.2 5.1 %collective-permute-start.19 = (f32[3,18,8,64]{3,2,1,0:T(8,128)S(1)}, f32[3,18,8,64]{3,2,1,0:T(8,128)}, u32[]{:S(2)}, u32[]{:S(2)}) collective-permute-start(f32[3,18,8,64]{3,2,1,0:T(8,128)S(1)} %broadcast_select_fusion), channel_id=1, source_target_pairs={{0,1},{1,2},{2,3},{3,4},{4,5},{5,6},{6,7},{7,8},{8,9},{9,10},{10,1... | collective-permute-start | bytes 331784 | tf_op jit(solution)/shard_map/ppermute | solution.py:69
  171.3 2.1 collective-permute-start.20
  175.0 4.2 %collective-permute-done.20 = f32[3,18,8,64]{3,2,1,0:T(8,128)} collective-permute-done((f32[3,18,8,64]{3,2,1,0:T(8,128)S(1)}, f32[3,18,8,64]{3,2,1,0:T(8,128)}, u32[]{:S(2)}, u32[]{:S(2)}) %collective-permute-start.20) | collective-permute-done | bytes 110624 | tf_op jit(solution)/shard_map/ppermute | solution.py:70
  183.2 29.1 %all_gather.11 = f32[3,32,4,32]{3,2,1,0:T(4,128)S(1)} all-gather(f32[3,1,4,32]{3,2,1,0:T(4,128)S(1)} %pad_maximum_fusion.5), channel_id=1, replica_groups=mesh['gx'=32,'gy'=16] {'gx'}, dimensions={1}, use_global_device_ids=true | all-gather | bytes 50688 | tf_op jit(solution)/shard_map/all_gather | solution.py:50
  212.4 2.9 %collective-permute-start.21 = (f32[3,21,4,32]{3,2,1,0:T(4,128)S(1)}, f32[3,21,4,32]{3,2,1,0:T(4,128)S(1)}, u32[]{:S(2)}, u32[]{:S(2)}) collective-permute-start(f32[3,21,4,32]{3,2,1,0:T(4,128)S(1)} %pad_dynamic-slice_fusion), channel_id=1, source_target_pairs={{0,1},{1,2},{2,3},{3,4},{4,5},{5,6},{6,7},{7,8},{8,9},{9,10},{10,1... | collective-permute-start | bytes 96776 | tf_op jit(solution)/shard_map/ppermute | solution.py:69
  215.2 3.0 %collective-permute-start.22 = (f32[3,21,4,32]{3,2,1,0:T(4,128)S(1)}, f32[3,21,4,32]{3,2,1,0:T(4,128)S(1)}, u32[]{:S(2)}, u32[]{:S(2)}) collective-permute-start(f32[3,21,4,32]{3,2,1,0:T(4,128)S(1)} %pad_dynamic-slice_fusion), channel_id=1, source_target_pairs={{0,15},{1,0},{2,1},{3,2},{4,3},{5,4},{6,5},{7,6},{8,7},{9,8},{10,9... | collective-permute-start | bytes 96776 | tf_op jit(solution)/shard_map/ppermute | solution.py:70
  218.2 1.7 collective-permute-done.21
  220.0 2.6 collective-permute-done.22
  224.3 5.1 %collective-permute-start.23 = (f32[3,21,6,32]{3,2,1,0:T(8,128)}, f32[3,21,6,32]{3,2,1,0:T(8,128)}, u32[]{:S(2)}, u32[]{:S(2)}) collective-permute-start(f32[3,21,6,32]{3,2,1,0:T(8,128)} %get-tuple-element.89), channel_id=1, source_target_pairs={{0,2},{1,3},{2,4},{3,5},{4,6},{5,7},{6,8},{7,9},{8,10},{9,11},{10,... | collective-permute-start | bytes 145160 | tf_op jit(solution)/shard_map/ppermute | solution.py:69
  229.5 1.9 collective-permute-start.24
  233.3 7.0 %collective-permute-done.23 = f32[3,21,6,32]{3,2,1,0:T(8,128)} collective-permute-done((f32[3,21,6,32]{3,2,1,0:T(8,128)}, f32[3,21,6,32]{3,2,1,0:T(8,128)}, u32[]{:S(2)}, u32[]{:S(2)}) %collective-permute-start.23) | collective-permute-done | bytes 48416 | tf_op jit(solution)/shard_map/ppermute | solution.py:69
  240.4 5.6 %collective-permute-done.24 = f32[3,21,6,32]{3,2,1,0:T(8,128)} collective-permute-done((f32[3,21,6,32]{3,2,1,0:T(8,128)}, f32[3,21,6,32]{3,2,1,0:T(8,128)}, u32[]{:S(2)}, u32[]{:S(2)}) %collective-permute-start.24) | collective-permute-done | bytes 48416 | tf_op jit(solution)/shard_map/ppermute | solution.py:70
  246.0 1.4 add_select_fusion
  (388 shorter events, 54.6 us)
Async XLA Ops:
  0.0 18.4 %copy-start.57 = (s32[256]{0:T(256)}, s32[256]{0:T(256)S(1)}, u32[]{:S(2)}) copy-start(s32[256]{0:T(256)S(1)} %and_select_fusion.7) | copy-start | bytes 3076
  0.0 7.6 %copy-start.78 = (s32[32]{0:T(128)}, s32[32]{0:T(128)S(1)}, u32[]{:S(2)}) copy-start(s32[32]{0:T(128)S(1)} %and_select_fusion.8) | copy-start | bytes 388
  0.0 15.8 %copy-start.96 = (s32[16]{0:T(128)}, s32[16]{0:T(128)S(1)}, u32[]{:S(2)}) copy-start(s32[16]{0:T(128)S(1)} %and_select_fusion.6) | copy-start | bytes 196
  0.1 18.4 %copy-start.73 = (s32[128]{0:T(128)}, s32[128]{0:T(128)S(1)}, u32[]{:S(2)}) copy-start(s32[128]{0:T(128)S(1)} %and_select_fusion.5) | copy-start | bytes 1540
  0.1 15.8 %copy-start.94 = (s32[8]{0:T(128)}, s32[8]{0:T(128)S(1)}, u32[]{:S(2)}) copy-start(s32[8]{0:T(128)S(1)} %and_select_fusion.4) | copy-start | bytes 100
  0.1 13.2 %copy-start.90 = (s32[64]{0:T(128)}, s32[64]{0:T(128)S(1)}, u32[]{:S(2)}) copy-start(s32[64]{0:T(128)S(1)} %and_select_fusion.3) | copy-start | bytes 772
  51.5 24.2 %collective-permute-start.4 = (f32[4,2]{0,1:T(2,128)}, f32[4,2]{0,1:T(2,128)}, u32[]{:S(2)}, u32[]{:S(2)}) collective-permute-start(f32[4,2]{0,1:T(2,128)} %reduce_max.89), channel_id=1, source_target_pairs={{0,16},{16,0},{32,48},{48,32},{64,80},{80,64},{96,112},{112,96},{1... | collective-permute-start | bytes 104 | tf_op jit(solution)/shard_map/ppermute | solution.py:205
  53.4 15.5 %copy-start.43 = (f32[8,32,256]{2,1,0:T(8,128)S(1)}, f32[8,32,256]{2,1,0:T(8,128)}, u32[]{:S(2)}) copy-start(f32[8,32,256]{2,1,0:T(8,128)} %param.5) | copy-start | bytes 786436
  53.4 15.5 %copy-start.44 = (f32[8,32,256]{2,1,0:T(8,128)S(1)}, f32[8,32,256]{2,1,0:T(8,128)}, u32[]{:S(2)}) copy-start(f32[8,32,256]{2,1,0:T(8,128)} %param.4) | copy-start | bytes 786436
  53.4 15.5 %copy-start.45 = (f32[8,32,256]{2,1,0:T(8,128)S(1)}, f32[8,32,256]{2,1,0:T(8,128)}, u32[]{:S(2)}) copy-start(f32[8,32,256]{2,1,0:T(8,128)} %param.3) | copy-start | bytes 786436
  54.8 14.0 %collective-permute-start = (f32[3,5,32,256]{3,2,1,0:T(8,128)S(1)}, f32[3,5,32,256]{3,2,1,0:T(8,128)S(1)}, u32[]{:S(2)}, u32[]{:S(2)}) collective-permute-start(f32[3,5,32,256]{3,2,1,0:T(8,128)S(1)} %get-tuple-element.71), channel_id=1, source_target_pairs={{0,16},{16,32},{32,48},{48,64},{64,80},{80,96},{96,112},{112,128},... | collective-permute-start | bytes 1474568 | tf_op jit(solution)/shard_map/ppermute | solution.py:69
  57.3 11.6 %collective-permute-start.1 = (f32[3,5,32,256]{3,2,1,0:T(8,128)S(1)}, f32[3,5,32,256]{3,2,1,0:T(8,128)S(1)}, u32[]{:S(2)}, u32[]{:S(2)}) collective-permute-start(f32[3,5,32,256]{3,2,1,0:T(8,128)S(1)} %get-tuple-element.72), channel_id=1, source_target_pairs={{16,0},{32,16},{48,32},{64,48},{80,64},{96,80},{112,96},{128,112},... | collective-permute-start | bytes 1474568 | tf_op jit(solution)/shard_map/ppermute | solution.py:70
  60.1 8.8 %copy-start.59 = (pred[12,36]{1,0:T(8,128)(4,1)}, pred[12,36]{1,0:T(8,128)(4,1)S(1)}, u32[]{:S(2)}) copy-start(pred[12,36]{1,0:T(8,128)(4,1)S(1)} %slice_bitcast_fusion.27) | copy-start | bytes 1300
  60.2 4.0 %copy-start.51 = (pred[18,30,1]{1,0,2:T(8,128)(4,1)}, pred[18,30,1]{1,0,2:T(8,128)(4,1)S(1)}, u32[]{:S(2)}) copy-start(pred[18,30,1]{1,0,2:T(8,128)(4,1)S(1)} %broadcast_and_fusion.2) | copy-start | bytes 1624
  62.1 6.7 %copy-start.86 = (pred[18]{0:T(512)(128)(4,1)}, pred[18]{0:T(512)(128)(4,1)S(1)}, u32[]{:S(2)}) copy-start(pred[18]{0:T(512)(128)(4,1)S(1)} %compare_and_fusion.3) | copy-start | bytes 58
  62.2 6.6 %copy-start.53 = (pred[18,24,1]{1,0,2:T(8,128)(4,1)}, pred[18,24,1]{1,0,2:T(8,128)(4,1)S(1)}, u32[]{:S(2)}) copy-start(pred[18,24,1]{1,0,2:T(8,128)(4,1)S(1)} %broadcast_and_fusion.1) | copy-start | bytes 1300
  64.2 4.6 %copy-start.88 = (pred[24]{0:T(512)(128)(4,1)}, pred[24]{0:T(512)(128)(4,1)S(1)}, u32[]{:S(2)}) copy-start(pred[24]{0:T(512)(128)(4,1)S(1)} %compare_and_fusion.1) | copy-start | bytes 76
  64.3 4.6 %copy-start.50 = (pred[21,24,1]{1,0,2:T(8,128)(4,1)}, pred[21,24,1]{1,0,2:T(8,128)(4,1)S(1)}, u32[]{:S(2)}) copy-start(pred[21,24,1]{1,0,2:T(8,128)(4,1)S(1)} %broadcast_and_fusion) | copy-start | bytes 1516
  69.1 6.0 %copy-start.54 = (pred[18,24,1]{1,0,2:T(8,128)(4,1)S(1)}, pred[18,24,1]{1,0,2:T(8,128)(4,1)}, u32[]{:S(2)}) copy-start(pred[18,24,1]{1,0,2:T(8,128)(4,1)} %copy-done.53) | copy-start | bytes 1300
  69.2 37.9 %collective-permute-start.2 = (f32[3,18,5,256]{3,2,1,0:T(8,128)S(1)}, f32[3,18,5,256]{3,2,1,0:T(8,128)S(1)}, u32[]{:S(2)}, u32[]{:S(2)}) collective-permute-start(f32[3,18,5,256]{3,2,1,0:T(8,128)S(1)} %get-tuple-element.62), channel_id=1, source_target_pairs={{0,1},{1,2},{2,3},{3,4},{4,5},{5,6},{6,7},{7,8},{8,9},{9,10},{10,1... | collective-permute-start | bytes 829448 | tf_op jit(solution)/shard_map/ppermute | solution.py:69
  71.2 35.9 %collective-permute-start.3 = (f32[3,18,5,256]{3,2,1,0:T(8,128)S(1)}, f32[3,18,5,256]{3,2,1,0:T(8,128)S(1)}, u32[]{:S(2)}, u32[]{:S(2)}) collective-permute-start(f32[3,18,5,256]{3,2,1,0:T(8,128)S(1)} %get-tuple-element.63), channel_id=1, source_target_pairs={{1,0},{2,1},{3,2},{4,3},{5,4},{6,5},{7,6},{8,7},{9,8},{10,9},{11,1... | collective-permute-start | bytes 829448 | tf_op jit(solution)/shard_map/ppermute | solution.py:70
  76.4 6.8 %collective-permute-start.5 = (f32[4,2]{0,1:T(2,128)S(1)}, f32[4,2]{0,1:T(2,128)S(1)}, u32[]{:S(2)}, u32[]{:S(2)}) collective-permute-start(f32[4,2]{0,1:T(2,128)S(1)} %max.15), channel_id=1, source_target_pairs={{0,32},{16,48},{32,0},{48,16},{64,96},{80,112},{96,64},{112,80},{1... | collective-permute-start | bytes 104 | tf_op jit(solution)/shard_map/ppermute | solution.py:205
  83.2 7.0 %collective-permute-start.6 = (f32[4,2]{0,1:T(2,128)S(1)}, f32[4,2]{0,1:T(2,128)S(1)}, u32[]{:S(2)}, u32[]{:S(2)}) collective-permute-start(f32[4,2]{0,1:T(2,128)S(1)} %max.16), channel_id=1, source_target_pairs={{0,64},{16,80},{32,96},{48,112},{64,0},{80,16},{96,32},{112,48},{1... | collective-permute-start | bytes 104 | tf_op jit(solution)/shard_map/ppermute | solution.py:205
  90.2 7.6 %collective-permute-start.7 = (f32[4,2]{0,1:T(2,128)S(1)}, f32[4,2]{0,1:T(2,128)S(1)}, u32[]{:S(2)}, u32[]{:S(2)}) collective-permute-start(f32[4,2]{0,1:T(2,128)S(1)} %max.17), channel_id=1, source_target_pairs={{0,128},{16,144},{32,160},{48,176},{64,192},{80,208},{96,224},{112... | collective-permute-start | bytes 104 | tf_op jit(solution)/shard_map/ppermute | solution.py:205
  97.8 7.1 %collective-permute-start.8 = (f32[4,2]{0,1:T(2,128)S(1)}, f32[4,2]{0,1:T(2,128)S(1)}, u32[]{:S(2)}, u32[]{:S(2)}) collective-permute-start(f32[4,2]{0,1:T(2,128)S(1)} %max.18), channel_id=1, source_target_pairs={{0,256},{16,272},{32,288},{48,304},{64,320},{80,336},{96,352},{112... | collective-permute-start | bytes 104 | tf_op jit(solution)/shard_map/ppermute | solution.py:205
  110.2 2.2 copy-start
  113.1 2.5 copy-start.52
  113.1 7.2 %copy-start.56 = (pred[18,42,1]{1,0,2:T(8,128)(4,1)S(1)}, pred[18,42,1]{1,0,2:T(8,128)(4,1)}, u32[]{:S(2)}) copy-start(pred[18,42,1]{1,0,2:T(8,128)(4,1)} %copy-done.55) | copy-start | bytes 2272
  113.1 7.3 %copy-start.64 = (pred[12,24]{1,0:T(8,128)(4,1)S(1)}, pred[12,24]{1,0:T(8,128)(4,1)}, u32[]{:S(2)}) copy-start(pred[12,24]{1,0:T(8,128)(4,1)} %slice_bitcast_fusion.24) | copy-start | bytes 868
  114.3 2.7 %collective-permute-start.9 = (f32[3,4,16,128]{3,2,1,0:T(8,128)S(1)}, f32[3,4,16,128]{3,2,1,0:T(8,128)S(1)}, u32[]{:S(2)}, u32[]{:S(2)}) collective-permute-start(f32[3,4,16,128]{3,2,1,0:T(8,128)S(1)} %pad_maximum_fusion.2), channel_id=1, source_target_pairs={{0,16},{16,32},{32,48},{48,64},{64,80},{80,96},{96,112},{112,128},... | collective-permute-start | bytes 294920 | tf_op jit(solution)/shard_map/ppermute | solution.py:69
  115.7 5.3 %collective-permute-start.11 = (f32[3,4,16,128]{3,2,1,0:T(8,128)S(1)}, f32[3,4,16,128]{3,2,1,0:T(8,128)S(1)}, u32[]{:S(2)}, u32[]{:S(2)}) collective-permute-start(f32[3,4,16,128]{3,2,1,0:T(8,128)S(1)} %pad_maximum_fusion.2), channel_id=1, source_target_pairs={{16,0},{32,16},{48,32},{64,48},{80,64},{96,80},{112,96},{128,112},... | collective-permute-start | bytes 294920 | tf_op jit(solution)/shard_map/ppermute | solution.py:70
  117.0 5.3 %collective-permute-start.10 = (f32[3,3,16,128]{3,2,1,0:T(8,128)S(1)}, f32[3,3,16,128]{3,2,1,0:T(8,128)S(1)}, u32[]{:S(2)}, u32[]{:S(2)}) collective-permute-start(f32[3,3,16,128]{3,2,1,0:T(8,128)S(1)} %slice.1970), channel_id=1, source_target_pairs={{0,16},{16,32},{32,48},{48,64},{64,80},{80,96},{96,112},{112,128},... | collective-permute-start | bytes 221192 | tf_op jit(solution)/shard_map/ppermute | solution.py:69
  121.0 4.6 %collective-permute-start.12 = (f32[3,3,16,128]{3,2,1,0:T(8,128)S(1)}, f32[3,3,16,128]{3,2,1,0:T(8,128)S(1)}, u32[]{:S(2)}, u32[]{:S(2)}) collective-permute-start(f32[3,3,16,128]{3,2,1,0:T(8,128)S(1)} %slice.1971), channel_id=1, source_target_pairs={{16,0},{32,16},{48,32},{64,48},{80,64},{96,80},{112,96},{128,112},... | collective-permute-start | bytes 221192 | tf_op jit(solution)/shard_map/ppermute | solution.py:70
  126.5 8.7 %collective-permute-start.13 = (f32[3,18,7,128]{3,2,1,0:T(8,128)}, f32[3,18,7,128]{3,2,1,0:T(8,128)}, u32[]{:S(2)}, u32[]{:S(2)}) collective-permute-start(f32[3,18,7,128]{3,2,1,0:T(8,128)} %get-tuple-element.93), channel_id=1, source_target_pairs={{0,1},{1,2},{2,3},{3,4},{4,5},{5,6},{6,7},{7,8},{8,9},{9,10},{10,1... | collective-permute-start | bytes 580616 | tf_op jit(solution)/shard_map/ppermute | solution.py:69
  128.4 9.7 %collective-permute-start.14 = (f32[3,18,7,128]{3,2,1,0:T(8,128)}, f32[3,18,7,128]{3,2,1,0:T(8,128)}, u32[]{:S(2)}, u32[]{:S(2)}) collective-permute-start(f32[3,18,7,128]{3,2,1,0:T(8,128)} %get-tuple-element.94), channel_id=1, source_target_pairs={{1,0},{2,1},{3,2},{4,3},{5,4},{6,5},{7,6},{8,7},{9,8},{10,9},{11,1... | collective-permute-start | bytes 580616 | tf_op jit(solution)/shard_map/ppermute | solution.py:70
  141.3 16.1 %copy-start.65 = (pred[12,18]{1,0:T(8,128)(4,1)S(1)}, pred[12,18]{1,0:T(8,128)(4,1)}, u32[]{:S(2)}) copy-start(pred[12,18]{1,0:T(8,128)(4,1)} %slice_bitcast_fusion.21) | copy-start | bytes 652
  141.5 24.6 %copy-start.87 = (pred[18]{0:T(512)(128)(4,1)S(1)}, pred[18]{0:T(512)(128)(4,1)}, u32[]{:S(2)}) copy-start(pred[18]{0:T(512)(128)(4,1)} %copy-done.86) | copy-start | bytes 58
  142.5 10.2 %collective-permute-start.15 = (f32[3,2,8,64]{3,2,1,0:T(8,128)S(1)}, f32[3,2,8,64]{3,2,1,0:T(8,128)S(1)}, u32[]{:S(2)}, u32[]{:S(2)}) collective-permute-start(f32[3,2,8,64]{3,2,1,0:T(8,128)S(1)} %pad_maximum_fusion.4), channel_id=1, source_target_pairs={{0,16},{16,32},{32,48},{48,64},{64,80},{80,96},{96,112},{112,128},... | collective-permute-start | bytes 36872 | tf_op jit(solution)/shard_map/ppermute | solution.py:69
  146.2 6.6 %collective-permute-start.16 = (f32[3,2,8,64]{3,2,1,0:T(8,128)S(1)}, f32[3,2,8,64]{3,2,1,0:T(8,128)S(1)}, u32[]{:S(2)}, u32[]{:S(2)}) collective-permute-start(f32[3,2,8,64]{3,2,1,0:T(8,128)S(1)} %pad_maximum_fusion.4), channel_id=1, source_target_pairs={{0,496},{16,0},{32,16},{48,32},{64,48},{80,64},{96,80},{112,96},{1... | collective-permute-start | bytes 36872 | tf_op jit(solution)/shard_map/ppermute | solution.py:70
  152.9 10.4 %collective-permute-start.17 = (f32[3,6,8,64]{3,2,1,0:T(8,128)S(1)}, f32[3,6,8,64]{3,2,1,0:T(8,128)S(1)}, u32[]{:S(2)}, u32[]{:S(2)}) collective-permute-start(f32[3,6,8,64]{3,2,1,0:T(8,128)S(1)} %pad_maximum_fusion.3), channel_id=1, source_target_pairs={{0,48},{16,64},{32,80},{48,96},{64,112},{80,128},{96,144},{112,160... | collective-permute-start | bytes 110600 | tf_op jit(solution)/shard_map/ppermute | solution.py:69
  158.0 8.0 %collective-permute-start.18 = (f32[3,6,8,64]{3,2,1,0:T(8,128)S(1)}, f32[3,6,8,64]{3,2,1,0:T(8,128)S(1)}, u32[]{:S(2)}, u32[]{:S(2)}) collective-permute-start(f32[3,6,8,64]{3,2,1,0:T(8,128)S(1)} %pad_maximum_fusion.3), channel_id=1, source_target_pairs={{0,464},{16,480},{32,496},{48,0},{64,16},{80,32},{96,48},{112,64},... | collective-permute-start | bytes 110600 | tf_op jit(solution)/shard_map/ppermute | solution.py:70
  166.2 8.8 %collective-permute-start.19 = (f32[3,18,8,64]{3,2,1,0:T(8,128)S(1)}, f32[3,18,8,64]{3,2,1,0:T(8,128)}, u32[]{:S(2)}, u32[]{:S(2)}) collective-permute-start(f32[3,18,8,64]{3,2,1,0:T(8,128)S(1)} %broadcast_select_fusion), channel_id=1, source_target_pairs={{0,1},{1,2},{2,3},{3,4},{4,5},{5,6},{6,7},{7,8},{8,9},{9,10},{10,1... | collective-permute-start | bytes 331784 | tf_op jit(solution)/shard_map/ppermute | solution.py:69
  171.3 7.9 %collective-permute-start.20 = (f32[3,18,8,64]{3,2,1,0:T(8,128)S(1)}, f32[3,18,8,64]{3,2,1,0:T(8,128)}, u32[]{:S(2)}, u32[]{:S(2)}) collective-permute-start(f32[3,18,8,64]{3,2,1,0:T(8,128)S(1)} %broadcast_select_fusion), channel_id=1, source_target_pairs={{1,0},{2,1},{3,2},{4,3},{5,4},{6,5},{7,6},{8,7},{9,8},{10,9},{11,1... | collective-permute-start | bytes 331784 | tf_op jit(solution)/shard_map/ppermute | solution.py:70
  182.6 63.4 %copy-start.89 = (pred[24]{0:T(512)(128)(4,1)S(1)}, pred[24]{0:T(512)(128)(4,1)}, u32[]{:S(2)}) copy-start(pred[24]{0:T(512)(128)(4,1)} %copy-done.88) | copy-start | bytes 76
  212.4 7.6 %collective-permute-start.21 = (f32[3,21,4,32]{3,2,1,0:T(4,128)S(1)}, f32[3,21,4,32]{3,2,1,0:T(4,128)S(1)}, u32[]{:S(2)}, u32[]{:S(2)}) collective-permute-start(f32[3,21,4,32]{3,2,1,0:T(4,128)S(1)} %pad_dynamic-slice_fusion), channel_id=1, source_target_pairs={{0,1},{1,2},{2,3},{3,4},{4,5},{5,6},{6,7},{7,8},{8,9},{9,10},{10,1... | collective-permute-start | bytes 96776 | tf_op jit(solution)/shard_map/ppermute | solution.py:69
  215.2 7.3 %collective-permute-start.22 = (f32[3,21,4,32]{3,2,1,0:T(4,128)S(1)}, f32[3,21,4,32]{3,2,1,0:T(4,128)S(1)}, u32[]{:S(2)}, u32[]{:S(2)}) collective-permute-start(f32[3,21,4,32]{3,2,1,0:T(4,128)S(1)} %pad_dynamic-slice_fusion), channel_id=1, source_target_pairs={{0,15},{1,0},{2,1},{3,2},{4,3},{5,4},{6,5},{7,6},{8,7},{9,8},{10,9... | collective-permute-start | bytes 96776 | tf_op jit(solution)/shard_map/ppermute | solution.py:70
  224.3 16.0 %collective-permute-start.23 = (f32[3,21,6,32]{3,2,1,0:T(8,128)}, f32[3,21,6,32]{3,2,1,0:T(8,128)}, u32[]{:S(2)}, u32[]{:S(2)}) collective-permute-start(f32[3,21,6,32]{3,2,1,0:T(8,128)} %get-tuple-element.89), channel_id=1, source_target_pairs={{0,2},{1,3},{2,4},{3,5},{4,6},{5,7},{6,8},{7,9},{8,10},{9,11},{10,... | collective-permute-start | bytes 145160 | tf_op jit(solution)/shard_map/ppermute | solution.py:69
  229.5 16.5 %collective-permute-start.24 = (f32[3,21,6,32]{3,2,1,0:T(8,128)}, f32[3,21,6,32]{3,2,1,0:T(8,128)}, u32[]{:S(2)}, u32[]{:S(2)}) collective-permute-start(f32[3,21,6,32]{3,2,1,0:T(8,128)} %get-tuple-element.90), channel_id=1, source_target_pairs={{0,14},{1,15},{2,0},{3,1},{4,2},{5,3},{6,4},{7,5},{8,6},{9,7},{10,... | collective-permute-start | bytes 145160 | tf_op jit(solution)/shard_map/ppermute | solution.py:70
  (75 other events, 80.1 us)

commit v9 on v8

--- a/solution.py
+++ b/solution.py
@@ -2,6 +2,7 @@
 import jax.numpy as jnp
 from jax import lax
 from jax.sharding import PartitionSpec as P
+
 
 LEVELS = 4
 PRE_STEPS = 3
@@ -178,7 +179,7 @@
         e -= 1
         direction = residual / middle
         field = crop(field, 1) + direction
-    for k in range(1, sweeps):
+    for _ in range(1, sweeps):
         residual = level.residual(field, e)
         e -= 1
         factor_new = 1.0 / (2.0 * scaled - factor)
@@ -210,14 +211,14 @@
 def local(rhs_field, alpha_coef, beta_coef):
     alphas = [alpha_coef]
     betas = [beta_coef]
-    for level_idx in range(1, LEVELS):
+    for _ in range(1, LEVELS):
         alphas.append(restrict(alphas[-1]))
         betas.append(restrict(betas[-1]))
     maxima = jnp.stack([jnp.stack([jnp.max(alphas[i]), jnp.max(betas[i])]) for i in range(LEVELS)])
     maxima = all_max(maxima)
     uppers = [HELM_SHIFT * maxima[i, 0] + 12.0 * maxima[i, 1] / 4.0**i for i in range(LEVELS)]
     out_depth = [0]
-    for level_idx in range(1, LEVELS):
+    for _ in range(1, LEVELS):
         out_depth.append(-(-(out_depth[-1] + POST_STEPS) // 2))
     depths = [out_depth[i] + POST_STEPS + PRE_STEPS - 1 for i in range(LEVELS - 1)]
     depths.append(out_depth[LEVELS - 1] + COARSE_STEPS - 1)

time: 263 us -> 263 us (level)
  no operation moved by 1% of the time
where the time goes in v9:
time: 263 us; the launch traced here: 261 us
  starting transfers between devices  84.8 us (32%)
  blocking collectives  61.6 us (23%)
  waiting for transfers between devices  36.5 us (14%)
  local copies, waits for them, and re-layouts  28.6 us (11%)
  other arithmetic  28.2 us (11%)
  matrix products  12.7 us (5%)
  between operations  8.57 us (3%)
    all_gather x1, blocking collectives, all_max(): values = jnp.max(lax.all_gather(values, axis), axis=0)  32.4 us
    ppermute x10, starting transfers between devices, extend(): before = lax.ppermute(low, axis, up)  31.6 us
    all_gather x1, blocking collectives, extend(): whole = lax.all_gather(x, axis, axis=dim, tiled=True)  29.1 us
    ppermute x10, starting transfers between devices, extend(): after = lax.ppermute(high, axis, down)  29 us
    ppermute x5, starting transfers between devices, all_max(): values = jnp.maximum(values, lax.ppermute(values, axis, pairs))  24.2 us
    ppermute x10, waiting for transfers between devices, extend(): after = lax.ppermute(high, axis, down)  21.5 us
    broadcast_in_dim x21, local copies, waits for them, and re-layouts, residual(): r = jnp.where(crop(self.mask, self.depth - out), r, 0.0)  13.1 us
    add x22, other arithmetic, smooth(): field = crop(field, 1) + direction  10.9 us
  transfers between devices with their start and end apart: 25, of which 13 were waited for; matrix products, arithmetic and copies ran while one was open for 7% of the time, Pallas kernels for 0%

profile of v9, /device:TPU:64, one launch (start us, length us, event | category | flops | bytes accessed | tf_op | source)
XLA Modules:
  0.0 261.0 jit_solution(11385890614831208322)
XLA Ops:
  0.1 1.6 reduce_max.81
  1.7 1.6 reduce_max.82
  10.6 1.3 fusion.521
  11.9 1.3 fusion.520
  13.3 2.6 maximum_bitcast_fusion.2
  15.9 2.5 maximum_bitcast_fusion
  18.4 32.4 %all-gather.1 = f32[16,4,2]{1,2,0:T(2,128)S(1)} all-gather(f32[1,4,2]{1,2,0:T(2,128)S(1)} %bitcast.248), channel_id=2, replica_groups=mesh['gx'=32,'gy'=16] {'gy'}, dimensions={0}, use_global_device_ids=true | all-gather | bytes 544 | tf_op jit(solution)/shard_map/all_gather | solution.py:198
  51.5 1.9 collective-permute-start.4
  54.8 2.4 collective-permute-start
  57.3 1.3 collective-permute-start.1
  69.2 1.9 collective-permute-start.2
  71.2 3.9 %collective-permute-start.3 = (f32[3,18,5,256]{3,2,1,0:T(8,128)S(1)}, f32[3,18,5,256]{3,2,1,0:T(8,128)S(1)}, u32[]{:S(2)}, u32[]{:S(2)}) collective-permute-start(f32[3,18,5,256]{3,2,1,0:T(8,128)S(1)} %get-tuple-element.63), channel_id=1, source_target_pairs={{1,0},{2,1},{3,2},{4,3},{5,4},{6,5},{7,6},{8,7},{9,8},{10,9},{11,1... | collective-permute-start | bytes 829448 | tf_op jit(solution)/shard_map/ppermute | solution.py:71
  76.4 5.2 %collective-permute-start.5 = (f32[4,2]{0,1:T(2,128)S(1)}, f32[4,2]{0,1:T(2,128)S(1)}, u32[]{:S(2)}, u32[]{:S(2)}) collective-permute-start(f32[4,2]{0,1:T(2,128)S(1)} %max.15), channel_id=1, source_target_pairs={{0,32},{16,48},{32,0},{48,16},{64,96},{80,112},{96,64},{112,80},{1... | collective-permute-start | bytes 104 | tf_op jit(solution)/shard_map/ppermute | solution.py:206
  81.6 1.5 collective-permute-done.5
  83.2 5.4 %collective-permute-start.6 = (f32[4,2]{0,1:T(2,128)S(1)}, f32[4,2]{0,1:T(2,128)S(1)}, u32[]{:S(2)}, u32[]{:S(2)}) collective-permute-start(f32[4,2]{0,1:T(2,128)S(1)} %max.16), channel_id=1, source_target_pairs={{0,64},{16,80},{32,96},{48,112},{64,0},{80,16},{96,32},{112,48},{1... | collective-permute-start | bytes 104 | tf_op jit(solution)/shard_map/ppermute | solution.py:206
  88.6 1.5 collective-permute-done.6
  90.2 6.1 %collective-permute-start.7 = (f32[4,2]{0,1:T(2,128)S(1)}, f32[4,2]{0,1:T(2,128)S(1)}, u32[]{:S(2)}, u32[]{:S(2)}) collective-permute-start(f32[4,2]{0,1:T(2,128)S(1)} %max.17), channel_id=1, source_target_pairs={{0,128},{16,144},{32,160},{48,176},{64,192},{80,208},{96,224},{112... | collective-permute-start | bytes 104 | tf_op jit(solution)/shard_map/ppermute | solution.py:206
  96.3 1.5 collective-permute-done.7
  97.8 5.5 %collective-permute-start.8 = (f32[4,2]{0,1:T(2,128)S(1)}, f32[4,2]{0,1:T(2,128)S(1)}, u32[]{:S(2)}, u32[]{:S(2)}) collective-permute-start(f32[4,2]{0,1:T(2,128)S(1)} %max.18), channel_id=1, source_target_pairs={{0,256},{16,272},{32,288},{48,304},{64,320},{80,336},{96,352},{112... | collective-permute-start | bytes 104 | tf_op jit(solution)/shard_map/ppermute | solution.py:206
  103.3 1.5 collective-permute-done.8
  108.7 1.5 slice_add_fusion.4
  114.3 1.3 collective-permute-start.9
  115.7 1.3 collective-permute-start.11
  117.0 3.3 %collective-permute-start.10 = (f32[3,3,16,128]{3,2,1,0:T(8,128)S(1)}, f32[3,3,16,128]{3,2,1,0:T(8,128)S(1)}, u32[]{:S(2)}, u32[]{:S(2)}) collective-permute-start(f32[3,3,16,128]{3,2,1,0:T(8,128)S(1)} %slice.1970), channel_id=1, source_target_pairs={{0,16},{16,32},{32,48},{48,64},{64,80},{80,96},{96,112},{112,128},... | collective-permute-start | bytes 221192 | tf_op jit(solution)/shard_map/ppermute | solution.py:70
  121.0 1.3 collective-permute-start.12
  122.4 3.3 %collective-permute-done.12 = f32[3,3,16,128]{3,2,1,0:T(8,128)S(1)} collective-permute-done((f32[3,3,16,128]{3,2,1,0:T(8,128)S(1)}, f32[3,3,16,128]{3,2,1,0:T(8,128)S(1)}, u32[]{:S(2)}, u32[]{:S(2)}) %collective-permute-start.12) | collective-permute-done | bytes 73760 | tf_op jit(solution)/shard_map/ppermute | solution.py:71
  126.5 1.9 collective-permute-start.13
  128.4 3.9 %collective-permute-start.14 = (f32[3,18,7,128]{3,2,1,0:T(8,128)}, f32[3,18,7,128]{3,2,1,0:T(8,128)}, u32[]{:S(2)}, u32[]{:S(2)}) collective-permute-start(f32[3,18,7,128]{3,2,1,0:T(8,128)} %get-tuple-element.94), channel_id=1, source_target_pairs={{1,0},{2,1},{3,2},{4,3},{5,4},{6,5},{7,6},{8,7},{9,8},{10,9},{11,1... | collective-permute-start | bytes 580616 | tf_op jit(solution)/shard_map/ppermute | solution.py:71
  132.3 1.3 slice_bitcast_fusion.32
  135.2 2.9 %collective-permute-done.14 = f32[3,18,7,128]{3,2,1,0:T(8,128)} collective-permute-done((f32[3,18,7,128]{3,2,1,0:T(8,128)}, f32[3,18,7,128]{3,2,1,0:T(8,128)}, u32[]{:S(2)}, u32[]{:S(2)}) %collective-permute-start.14) | collective-permute-done | bytes 193568 | tf_op jit(solution)/shard_map/ppermute | solution.py:71
  142.5 3.8 %collective-permute-start.15 = (f32[3,2,8,64]{3,2,1,0:T(8,128)S(1)}, f32[3,2,8,64]{3,2,1,0:T(8,128)S(1)}, u32[]{:S(2)}, u32[]{:S(2)}) collective-permute-start(f32[3,2,8,64]{3,2,1,0:T(8,128)S(1)} %pad_maximum_fusion.4), channel_id=1, source_target_pairs={{0,16},{16,32},{32,48},{48,64},{64,80},{80,96},{96,112},{112,128},... | collective-permute-start | bytes 36872 | tf_op jit(solution)/shard_map/ppermute | solution.py:70
  146.2 5.1 %collective-permute-start.16 = (f32[3,2,8,64]{3,2,1,0:T(8,128)S(1)}, f32[3,2,8,64]{3,2,1,0:T(8,128)S(1)}, u32[]{:S(2)}, u32[]{:S(2)}) collective-permute-start(f32[3,2,8,64]{3,2,1,0:T(8,128)S(1)} %pad_maximum_fusion.4), channel_id=1, source_target_pairs={{0,496},{16,0},{32,16},{48,32},{64,48},{80,64},{96,80},{112,96},{1... | collective-permute-start | bytes 36872 | tf_op jit(solution)/shard_map/ppermute | solution.py:71
  152.9 4.0 %collective-permute-start.17 = (f32[3,6,8,64]{3,2,1,0:T(8,128)S(1)}, f32[3,6,8,64]{3,2,1,0:T(8,128)S(1)}, u32[]{:S(2)}, u32[]{:S(2)}) collective-permute-start(f32[3,6,8,64]{3,2,1,0:T(8,128)S(1)} %pad_maximum_fusion.3), channel_id=1, source_target_pairs={{0,48},{16,64},{32,80},{48,96},{64,112},{80,128},{96,144},{112,160... | collective-permute-start | bytes 110600 | tf_op jit(solution)/shard_map/ppermute | solution.py:70
  158.0 5.2 %collective-permute-start.18 = (f32[3,6,8,64]{3,2,1,0:T(8,128)S(1)}, f32[3,6,8,64]{3,2,1,0:T(8,128)S(1)}, u32[]{:S(2)}, u32[]{:S(2)}) collective-permute-start(f32[3,6,8,64]{3,2,1,0:T(8,128)S(1)} %pad_maximum_fusion.3), channel_id=1, source_target_pairs={{0,464},{16,480},{32,496},{48,0},{64,16},{80,32},{96,48},{112,64},... | collective-permute-start | bytes 110600 | tf_op jit(solution)/shard_map/ppermute | solution.py:71
  163.3 2.8 %collective-permute-done.18 = f32[3,6,8,64]{3,2,1,0:T(8,128)S(1)} collective-permute-done((f32[3,6,8,64]{3,2,1,0:T(8,128)S(1)}, f32[3,6,8,64]{3,2,1,0:T(8,128)S(1)}, u32[]{:S(2)}, u32[]{:S(2)}) %collective-permute-start.18) | collective-permute-done | bytes 36896 | tf_op jit(solution)/shard_map/ppermute | solution.py:71
  166.2 5.1 %collective-permute-start.19 = (f32[3,18,8,64]{3,2,1,0:T(8,128)S(1)}, f32[3,18,8,64]{3,2,1,0:T(8,128)}, u32[]{:S(2)}, u32[]{:S(2)}) collective-permute-start(f32[3,18,8,64]{3,2,1,0:T(8,128)S(1)} %broadcast_select_fusion), channel_id=1, source_target_pairs={{0,1},{1,2},{2,3},{3,4},{4,5},{5,6},{6,7},{7,8},{8,9},{9,10},{10,1... | collective-permute-start | bytes 331784 | tf_op jit(solution)/shard_map/ppermute | solution.py:70
  171.3 2.1 collective-permute-start.20
  175.0 4.2 %collective-permute-done.20 = f32[3,18,8,64]{3,2,1,0:T(8,128)} collective-permute-done((f32[3,18,8,64]{3,2,1,0:T(8,128)S(1)}, f32[3,18,8,64]{3,2,1,0:T(8,128)}, u32[]{:S(2)}, u32[]{:S(2)}) %collective-permute-start.20) | collective-permute-done | bytes 110624 | tf_op jit(solution)/shard_map/ppermute | solution.py:71
  183.2 29.1 %all_gather.11 = f32[3,32,4,32]{3,2,1,0:T(4,128)S(1)} all-gather(f32[3,1,4,32]{3,2,1,0:T(4,128)S(1)} %pad_maximum_fusion.5), channel_id=1, replica_groups=mesh['gx'=32,'gy'=16] {'gx'}, dimensions={1}, use_global_device_ids=true | all-gather | bytes 50688 | tf_op jit(solution)/shard_map/all_gather | solution.py:51
  212.4 2.9 %collective-permute-start.21 = (f32[3,21,4,32]{3,2,1,0:T(4,128)S(1)}, f32[3,21,4,32]{3,2,1,0:T(4,128)S(1)}, u32[]{:S(2)}, u32[]{:S(2)}) collective-permute-start(f32[3,21,4,32]{3,2,1,0:T(4,128)S(1)} %pad_dynamic-slice_fusion), channel_id=1, source_target_pairs={{0,1},{1,2},{2,3},{3,4},{4,5},{5,6},{6,7},{7,8},{8,9},{9,10},{10,1... | collective-permute-start | bytes 96776 | tf_op jit(solution)/shard_map/ppermute | solution.py:70
  215.2 3.0 %collective-permute-start.22 = (f32[3,21,4,32]{3,2,1,0:T(4,128)S(1)}, f32[3,21,4,32]{3,2,1,0:T(4,128)S(1)}, u32[]{:S(2)}, u32[]{:S(2)}) collective-permute-start(f32[3,21,4,32]{3,2,1,0:T(4,128)S(1)} %pad_dynamic-slice_fusion), channel_id=1, source_target_pairs={{0,15},{1,0},{2,1},{3,2},{4,3},{5,4},{6,5},{7,6},{8,7},{9,8},{10,9... | collective-permute-start | bytes 96776 | tf_op jit(solution)/shard_map/ppermute | solution.py:71
  218.2 1.7 collective-permute-done.21
  220.0 2.6 collective-permute-done.22
  224.3 5.1 %collective-permute-start.23 = (f32[3,21,6,32]{3,2,1,0:T(8,128)}, f32[3,21,6,32]{3,2,1,0:T(8,128)}, u32[]{:S(2)}, u32[]{:S(2)}) collective-permute-start(f32[3,21,6,32]{3,2,1,0:T(8,128)} %get-tuple-element.89), channel_id=1, source_target_pairs={{0,2},{1,3},{2,4},{3,5},{4,6},{5,7},{6,8},{7,9},{8,10},{9,11},{10,... | collective-permute-start | bytes 145160 | tf_op jit(solution)/shard_map/ppermute | solution.py:70
  229.5 1.9 collective-permute-start.24
  233.3 7.0 %collective-permute-done.23 = f32[3,21,6,32]{3,2,1,0:T(8,128)} collective-permute-done((f32[3,21,6,32]{3,2,1,0:T(8,128)}, f32[3,21,6,32]{3,2,1,0:T(8,128)}, u32[]{:S(2)}, u32[]{:S(2)}) %collective-permute-start.23) | collective-permute-done | bytes 48416 | tf_op jit(solution)/shard_map/ppermute | solution.py:70
  240.4 5.6 %collective-permute-done.24 = f32[3,21,6,32]{3,2,1,0:T(8,128)} collective-permute-done((f32[3,21,6,32]{3,2,1,0:T(8,128)}, f32[3,21,6,32]{3,2,1,0:T(8,128)}, u32[]{:S(2)}, u32[]{:S(2)}) %collective-permute-start.24) | collective-permute-done | bytes 48416 | tf_op jit(solution)/shard_map/ppermute | solution.py:71
  246.0 1.4 add_select_fusion
  (388 shorter events, 54.6 us)
Async XLA Ops:
  0.0 18.4 %copy-start.57 = (s32[256]{0:T(256)}, s32[256]{0:T(256)S(1)}, u32[]{:S(2)}) copy-start(s32[256]{0:T(256)S(1)} %and_select_fusion.7) | copy-start | bytes 3076
  0.0 7.6 %copy-start.78 = (s32[32]{0:T(128)}, s32[32]{0:T(128)S(1)}, u32[]{:S(2)}) copy-start(s32[32]{0:T(128)S(1)} %and_select_fusion.8) | copy-start | bytes 388
  0.0 15.8 %copy-start.96 = (s32[16]{0:T(128)}, s32[16]{0:T(128)S(1)}, u32[]{:S(2)}) copy-start(s32[16]{0:T(128)S(1)} %and_select_fusion.6) | copy-start | bytes 196
  0.1 18.4 %copy-start.73 = (s32[128]{0:T(128)}, s32[128]{0:T(128)S(1)}, u32[]{:S(2)}) copy-start(s32[128]{0:T(128)S(1)} %and_select_fusion.5) | copy-start | bytes 1540
  0.1 15.8 %copy-start.94 = (s32[8]{0:T(128)}, s32[8]{0:T(128)S(1)}, u32[]{:S(2)}) copy-start(s32[8]{0:T(128)S(1)} %and_select_fusion.4) | copy-start | bytes 100
  0.1 13.2 %copy-start.90 = (s32[64]{0:T(128)}, s32[64]{0:T(128)S(1)}, u32[]{:S(2)}) copy-start(s32[64]{0:T(128)S(1)} %and_select_fusion.3) | copy-start | bytes 772
  51.5 24.2 %collective-permute-start.4 = (f32[4,2]{0,1:T(2,128)}, f32[4,2]{0,1:T(2,128)}, u32[]{:S(2)}, u32[]{:S(2)}) collective-permute-start(f32[4,2]{0,1:T(2,128)} %reduce_max.89), channel_id=1, source_target_pairs={{0,16},{16,0},{32,48},{48,32},{64,80},{80,64},{96,112},{112,96},{1... | collective-permute-start | bytes 104 | tf_op jit(solution)/shard_map/ppermute | solution.py:206
  53.4 15.5 %copy-start.43 = (f32[8,32,256]{2,1,0:T(8,128)S(1)}, f32[8,32,256]{2,1,0:T(8,128)}, u32[]{:S(2)}) copy-start(f32[8,32,256]{2,1,0:T(8,128)} %param.5) | copy-start | bytes 786436
  53.4 15.5 %copy-start.44 = (f32[8,32,256]{2,1,0:T(8,128)S(1)}, f32[8,32,256]{2,1,0:T(8,128)}, u32[]{:S(2)}) copy-start(f32[8,32,256]{2,1,0:T(8,128)} %param.4) | copy-start | bytes 786436
  53.4 15.5 %copy-start.45 = (f32[8,32,256]{2,1,0:T(8,128)S(1)}, f32[8,32,256]{2,1,0:T(8,128)}, u32[]{:S(2)}) copy-start(f32[8,32,256]{2,1,0:T(8,128)} %param.3) | copy-start | bytes 786436
  54.8 14.0 %collective-permute-start = (f32[3,5,32,256]{3,2,1,0:T(8,128)S(1)}, f32[3,5,32,256]{3,2,1,0:T(8,128)S(1)}, u32[]{:S(2)}, u32[]{:S(2)}) collective-permute-start(f32[3,5,32,256]{3,2,1,0:T(8,128)S(1)} %get-tuple-element.71), channel_id=1, source_target_pairs={{0,16},{16,32},{32,48},{48,64},{64,80},{80,96},{96,112},{112,128},... | collective-permute-start | bytes 1474568 | tf_op jit(solution)/shard_map/ppermute | solution.py:70
  57.3 11.6 %collective-permute-start.1 = (f32[3,5,32,256]{3,2,1,0:T(8,128)S(1)}, f32[3,5,32,256]{3,2,1,0:T(8,128)S(1)}, u32[]{:S(2)}, u32[]{:S(2)}) collective-permute-start(f32[3,5,32,256]{3,2,1,0:T(8,128)S(1)} %get-tuple-element.72), channel_id=1, source_target_pairs={{16,0},{32,16},{48,32},{64,48},{80,64},{96,80},{112,96},{128,112},... | collective-permute-start | bytes 1474568 | tf_op jit(solution)/shard_map/ppermute | solution.py:71
  60.1 8.8 %copy-start.59 = (pred[12,36]{1,0:T(8,128)(4,1)}, pred[12,36]{1,0:T(8,128)(4,1)S(1)}, u32[]{:S(2)}) copy-start(pred[12,36]{1,0:T(8,128)(4,1)S(1)} %slice_bitcast_fusion.27) | copy-start | bytes 1300
  60.2 4.0 %copy-start.51 = (pred[18,30,1]{1,0,2:T(8,128)(4,1)}, pred[18,30,1]{1,0,2:T(8,128)(4,1)S(1)}, u32[]{:S(2)}) copy-start(pred[18,30,1]{1,0,2:T(8,128)(4,1)S(1)} %broadcast_and_fusion.2) | copy-start | bytes 1624
  62.1 6.7 %copy-start.86 = (pred[18]{0:T(512)(128)(4,1)}, pred[18]{0:T(512)(128)(4,1)S(1)}, u32[]{:S(2)}) copy-start(pred[18]{0:T(512)(128)(4,1)S(1)} %compare_and_fusion.3) | copy-start | bytes 58
  62.2 6.6 %copy-start.53 = (pred[18,24,1]{1,0,2:T(8,128)(4,1)}, pred[18,24,1]{1,0,2:T(8,128)(4,1)S(1)}, u32[]{:S(2)}) copy-start(pred[18,24,1]{1,0,2:T(8,128)(4,1)S(1)} %broadcast_and_fusion.1) | copy-start | bytes 1300
  64.2 4.6 %copy-start.88 = (pred[24]{0:T(512)(128)(4,1)}, pred[24]{0:T(512)(128)(4,1)S(1)}, u32[]{:S(2)}) copy-start(pred[24]{0:T(512)(128)(4,1)S(1)} %compare_and_fusion.1) | copy-start | bytes 76
  64.3 4.6 %copy-start.50 = (pred[21,24,1]{1,0,2:T(8,128)(4,1)}, pred[21,24,1]{1,0,2:T(8,128)(4,1)S(1)}, u32[]{:S(2)}) copy-start(pred[21,24,1]{1,0,2:T(8,128)(4,1)S(1)} %broadcast_and_fusion) | copy-start | bytes 1516
  69.1 6.0 %copy-start.54 = (pred[18,24,1]{1,0,2:T(8,128)(4,1)S(1)}, pred[18,24,1]{1,0,2:T(8,128)(4,1)}, u32[]{:S(2)}) copy-start(pred[18,24,1]{1,0,2:T(8,128)(4,1)} %copy-done.53) | copy-start | bytes 1300
  69.2 37.9 %collective-permute-start.2 = (f32[3,18,5,256]{3,2,1,0:T(8,128)S(1)}, f32[3,18,5,256]{3,2,1,0:T(8,128)S(1)}, u32[]{:S(2)}, u32[]{:S(2)}) collective-permute-start(f32[3,18,5,256]{3,2,1,0:T(8,128)S(1)} %get-tuple-element.62), channel_id=1, source_target_pairs={{0,1},{1,2},{2,3},{3,4},{4,5},{5,6},{6,7},{7,8},{8,9},{9,10},{10,1... | collective-permute-start | bytes 829448 | tf_op jit(solution)/shard_map/ppermute | solution.py:70
  71.2 35.9 %collective-permute-start.3 = (f32[3,18,5,256]{3,2,1,0:T(8,128)S(1)}, f32[3,18,5,256]{3,2,1,0:T(8,128)S(1)}, u32[]{:S(2)}, u32[]{:S(2)}) collective-permute-start(f32[3,18,5,256]{3,2,1,0:T(8,128)S(1)} %get-tuple-element.63), channel_id=1, source_target_pairs={{1,0},{2,1},{3,2},{4,3},{5,4},{6,5},{7,6},{8,7},{9,8},{10,9},{11,1... | collective-permute-start | bytes 829448 | tf_op jit(solution)/shard_map/ppermute | solution.py:71
  76.4 6.8 %collective-permute-start.5 = (f32[4,2]{0,1:T(2,128)S(1)}, f32[4,2]{0,1:T(2,128)S(1)}, u32[]{:S(2)}, u32[]{:S(2)}) collective-permute-start(f32[4,2]{0,1:T(2,128)S(1)} %max.15), channel_id=1, source_target_pairs={{0,32},{16,48},{32,0},{48,16},{64,96},{80,112},{96,64},{112,80},{1... | collective-permute-start | bytes 104 | tf_op jit(solution)/shard_map/ppermute | solution.py:206
  83.2 7.0 %collective-permute-start.6 = (f32[4,2]{0,1:T(2,128)S(1)}, f32[4,2]{0,1:T(2,128)S(1)}, u32[]{:S(2)}, u32[]{:S(2)}) collective-permute-start(f32[4,2]{0,1:T(2,128)S(1)} %max.16), channel_id=1, source_target_pairs={{0,64},{16,80},{32,96},{48,112},{64,0},{80,16},{96,32},{112,48},{1... | collective-permute-start | bytes 104 | tf_op jit(solution)/shard_map/ppermute | solution.py:206
  90.2 7.6 %collective-permute-start.7 = (f32[4,2]{0,1:T(2,128)S(1)}, f32[4,2]{0,1:T(2,128)S(1)}, u32[]{:S(2)}, u32[]{:S(2)}) collective-permute-start(f32[4,2]{0,1:T(2,128)S(1)} %max.17), channel_id=1, source_target_pairs={{0,128},{16,144},{32,160},{48,176},{64,192},{80,208},{96,224},{112... | collective-permute-start | bytes 104 | tf_op jit(solution)/shard_map/ppermute | solution.py:206
  97.8 7.1 %collective-permute-start.8 = (f32[4,2]{0,1:T(2,128)S(1)}, f32[4,2]{0,1:T(2,128)S(1)}, u32[]{:S(2)}, u32[]{:S(2)}) collective-permute-start(f32[4,2]{0,1:T(2,128)S(1)} %max.18), channel_id=1, source_target_pairs={{0,256},{16,272},{32,288},{48,304},{64,320},{80,336},{96,352},{112... | collective-permute-start | bytes 104 | tf_op jit(solution)/shard_map/ppermute | solution.py:206
  110.2 2.2 copy-start
  113.1 2.5 copy-start.52
  113.1 7.2 %copy-start.56 = (pred[18,42,1]{1,0,2:T(8,128)(4,1)S(1)}, pred[18,42,1]{1,0,2:T(8,128)(4,1)}, u32[]{:S(2)}) copy-start(pred[18,42,1]{1,0,2:T(8,128)(4,1)} %copy-done.55) | copy-start | bytes 2272
  113.1 7.3 %copy-start.64 = (pred[12,24]{1,0:T(8,128)(4,1)S(1)}, pred[12,24]{1,0:T(8,128)(4,1)}, u32[]{:S(2)}) copy-start(pred[12,24]{1,0:T(8,128)(4,1)} %slice_bitcast_fusion.24) | copy-start | bytes 868
  114.3 2.7 %collective-permute-start.9 = (f32[3,4,16,128]{3,2,1,0:T(8,128)S(1)}, f32[3,4,16,128]{3,2,1,0:T(8,128)S(1)}, u32[]{:S(2)}, u32[]{:S(2)}) collective-permute-start(f32[3,4,16,128]{3,2,1,0:T(8,128)S(1)} %pad_maximum_fusion.2), channel_id=1, source_target_pairs={{0,16},{16,32},{32,48},{48,64},{64,80},{80,96},{96,112},{112,128},... | collective-permute-start | bytes 294920 | tf_op jit(solution)/shard_map/ppermute | solution.py:70
  115.7 5.3 %collective-permute-start.11 = (f32[3,4,16,128]{3,2,1,0:T(8,128)S(1)}, f32[3,4,16,128]{3,2,1,0:T(8,128)S(1)}, u32[]{:S(2)}, u32[]{:S(2)}) collective-permute-start(f32[3,4,16,128]{3,2,1,0:T(8,128)S(1)} %pad_maximum_fusion.2), channel_id=1, source_target_pairs={{16,0},{32,16},{48,32},{64,48},{80,64},{96,80},{112,96},{128,112},... | collective-permute-start | bytes 294920 | tf_op jit(solution)/shard_map/ppermute | solution.py:71
  117.0 5.3 %collective-permute-start.10 = (f32[3,3,16,128]{3,2,1,0:T(8,128)S(1)}, f32[3,3,16,128]{3,2,1,0:T(8,128)S(1)}, u32[]{:S(2)}, u32[]{:S(2)}) collective-permute-start(f32[3,3,16,128]{3,2,1,0:T(8,128)S(1)} %slice.1970), channel_id=1, source_target_pairs={{0,16},{16,32},{32,48},{48,64},{64,80},{80,96},{96,112},{112,128},... | collective-permute-start | bytes 221192 | tf_op jit(solution)/shard_map/ppermute | solution.py:70
  121.0 4.6 %collective-permute-start.12 = (f32[3,3,16,128]{3,2,1,0:T(8,128)S(1)}, f32[3,3,16,128]{3,2,1,0:T(8,128)S(1)}, u32[]{:S(2)}, u32[]{:S(2)}) collective-permute-start(f32[3,3,16,128]{3,2,1,0:T(8,128)S(1)} %slice.1971), channel_id=1, source_target_pairs={{16,0},{32,16},{48,32},{64,48},{80,64},{96,80},{112,96},{128,112},... | collective-permute-start | bytes 221192 | tf_op jit(solution)/shard_map/ppermute | solution.py:71
  126.5 8.7 %collective-permute-start.13 = (f32[3,18,7,128]{3,2,1,0:T(8,128)}, f32[3,18,7,128]{3,2,1,0:T(8,128)}, u32[]{:S(2)}, u32[]{:S(2)}) collective-permute-start(f32[3,18,7,128]{3,2,1,0:T(8,128)} %get-tuple-element.93), channel_id=1, source_target_pairs={{0,1},{1,2},{2,3},{3,4},{4,5},{5,6},{6,7},{7,8},{8,9},{9,10},{10,1... | collective-permute-start | bytes 580616 | tf_op jit(solution)/shard_map/ppermute | solution.py:70
  128.4 9.7 %collective-permute-start.14 = (f32[3,18,7,128]{3,2,1,0:T(8,128)}, f32[3,18,7,128]{3,2,1,0:T(8,128)}, u32[]{:S(2)}, u32[]{:S(2)}) collective-permute-start(f32[3,18,7,128]{3,2,1,0:T(8,128)} %get-tuple-element.94), channel_id=1, source_target_pairs={{1,0},{2,1},{3,2},{4,3},{5,4},{6,5},{7,6},{8,7},{9,8},{10,9},{11,1... | collective-permute-start | bytes 580616 | tf_op jit(solution)/shard_map/ppermute | solution.py:71
  141.3 16.1 %copy-start.65 = (pred[12,18]{1,0:T(8,128)(4,1)S(1)}, pred[12,18]{1,0:T(8,128)(4,1)}, u32[]{:S(2)}) copy-start(pred[12,18]{1,0:T(8,128)(4,1)} %slice_bitcast_fusion.21) | copy-start | bytes 652
  141.5 24.6 %copy-start.87 = (pred[18]{0:T(512)(128)(4,1)S(1)}, pred[18]{0:T(512)(128)(4,1)}, u32[]{:S(2)}) copy-start(pred[18]{0:T(512)(128)(4,1)} %copy-done.86) | copy-start | bytes 58
  142.5 10.2 %collective-permute-start.15 = (f32[3,2,8,64]{3,2,1,0:T(8,128)S(1)}, f32[3,2,8,64]{3,2,1,0:T(8,128)S(1)}, u32[]{:S(2)}, u32[]{:S(2)}) collective-permute-start(f32[3,2,8,64]{3,2,1,0:T(8,128)S(1)} %pad_maximum_fusion.4), channel_id=1, source_target_pairs={{0,16},{16,32},{32,48},{48,64},{64,80},{80,96},{96,112},{112,128},... | collective-permute-start | bytes 36872 | tf_op jit(solution)/shard_map/ppermute | solution.py:70
  146.2 6.6 %collective-permute-start.16 = (f32[3,2,8,64]{3,2,1,0:T(8,128)S(1)}, f32[3,2,8,64]{3,2,1,0:T(8,128)S(1)}, u32[]{:S(2)}, u32[]{:S(2)}) collective-permute-start(f32[3,2,8,64]{3,2,1,0:T(8,128)S(1)} %pad_maximum_fusion.4), channel_id=1, source_target_pairs={{0,496},{16,0},{32,16},{48,32},{64,48},{80,64},{96,80},{112,96},{1... | collective-permute-start | bytes 36872 | tf_op jit(solution)/shard_map/ppermute | solution.py:71
  152.9 10.4 %collective-permute-start.17 = (f32[3,6,8,64]{3,2,1,0:T(8,128)S(1)}, f32[3,6,8,64]{3,2,1,0:T(8,128)S(1)}, u32[]{:S(2)}, u32[]{:S(2)}) collective-permute-start(f32[3,6,8,64]{3,2,1,0:T(8,128)S(1)} %pad_maximum_fusion.3), channel_id=1, source_target_pairs={{0,48},{16,64},{32,80},{48,96},{64,112},{80,128},{96,144},{112,160... | collective-permute-start | bytes 110600 | tf_op jit(solution)/shard_map/ppermute | solution.py:70
  158.0 8.0 %collective-permute-start.18 = (f32[3,6,8,64]{3,2,1,0:T(8,128)S(1)}, f32[3,6,8,64]{3,2,1,0:T(8,128)S(1)}, u32[]{:S(2)}, u32[]{:S(2)}) collective-permute-start(f32[3,6,8,64]{3,2,1,0:T(8,128)S(1)} %pad_maximum_fusion.3), channel_id=1, source_target_pairs={{0,464},{16,480},{32,496},{48,0},{64,16},{80,32},{96,48},{112,64},... | collective-permute-start | bytes 110600 | tf_op jit(solution)/shard_map/ppermute | solution.py:71
  166.2 8.8 %collective-permute-start.19 = (f32[3,18,8,64]{3,2,1,0:T(8,128)S(1)}, f32[3,18,8,64]{3,2,1,0:T(8,128)}, u32[]{:S(2)}, u32[]{:S(2)}) collective-permute-start(f32[3,18,8,64]{3,2,1,0:T(8,128)S(1)} %broadcast_select_fusion), channel_id=1, source_target_pairs={{0,1},{1,2},{2,3},{3,4},{4,5},{5,6},{6,7},{7,8},{8,9},{9,10},{10,1... | collective-permute-start | bytes 331784 | tf_op jit(solution)/shard_map/ppermute | solution.py:70
  171.3 7.9 %collective-permute-start.20 = (f32[3,18,8,64]{3,2,1,0:T(8,128)S(1)}, f32[3,18,8,64]{3,2,1,0:T(8,128)}, u32[]{:S(2)}, u32[]{:S(2)}) collective-permute-start(f32[3,18,8,64]{3,2,1,0:T(8,128)S(1)} %broadcast_select_fusion), channel_id=1, source_target_pairs={{1,0},{2,1},{3,2},{4,3},{5,4},{6,5},{7,6},{8,7},{9,8},{10,9},{11,1... | collective-permute-start | bytes 331784 | tf_op jit(solution)/shard_map/ppermute | solution.py:71
  182.6 63.4 %copy-start.89 = (pred[24]{0:T(512)(128)(4,1)S(1)}, pred[24]{0:T(512)(128)(4,1)}, u32[]{:S(2)}) copy-start(pred[24]{0:T(512)(128)(4,1)} %copy-done.88) | copy-start | bytes 76
  212.4 7.6 %collective-permute-start.21 = (f32[3,21,4,32]{3,2,1,0:T(4,128)S(1)}, f32[3,21,4,32]{3,2,1,0:T(4,128)S(1)}, u32[]{:S(2)}, u32[]{:S(2)}) collective-permute-start(f32[3,21,4,32]{3,2,1,0:T(4,128)S(1)} %pad_dynamic-slice_fusion), channel_id=1, source_target_pairs={{0,1},{1,2},{2,3},{3,4},{4,5},{5,6},{6,7},{7,8},{8,9},{9,10},{10,1... | collective-permute-start | bytes 96776 | tf_op jit(solution)/shard_map/ppermute | solution.py:70
  215.2 7.3 %collective-permute-start.22 = (f32[3,21,4,32]{3,2,1,0:T(4,128)S(1)}, f32[3,21,4,32]{3,2,1,0:T(4,128)S(1)}, u32[]{:S(2)}, u32[]{:S(2)}) collective-permute-start(f32[3,21,4,32]{3,2,1,0:T(4,128)S(1)} %pad_dynamic-slice_fusion), channel_id=1, source_target_pairs={{0,15},{1,0},{2,1},{3,2},{4,3},{5,4},{6,5},{7,6},{8,7},{9,8},{10,9... | collective-permute-start | bytes 96776 | tf_op jit(solution)/shard_map/ppermute | solution.py:71
  224.3 16.0 %collective-permute-start.23 = (f32[3,21,6,32]{3,2,1,0:T(8,128)}, f32[3,21,6,32]{3,2,1,0:T(8,128)}, u32[]{:S(2)}, u32[]{:S(2)}) collective-permute-start(f32[3,21,6,32]{3,2,1,0:T(8,128)} %get-tuple-element.89), channel_id=1, source_target_pairs={{0,2},{1,3},{2,4},{3,5},{4,6},{5,7},{6,8},{7,9},{8,10},{9,11},{10,... | collective-permute-start | bytes 145160 | tf_op jit(solution)/shard_map/ppermute | solution.py:70
  229.5 16.5 %collective-permute-start.24 = (f32[3,21,6,32]{3,2,1,0:T(8,128)}, f32[3,21,6,32]{3,2,1,0:T(8,128)}, u32[]{:S(2)}, u32[]{:S(2)}) collective-permute-start(f32[3,21,6,32]{3,2,1,0:T(8,128)} %get-tuple-element.90), channel_id=1, source_target_pairs={{0,14},{1,15},{2,0},{3,1},{4,2},{5,3},{6,4},{7,5},{8,6},{9,7},{10,... | collective-permute-start | bytes 145160 | tf_op jit(solution)/shard_map/ppermute | solution.py:71
  (75 other events, 80.1 us)

commit v10 on v8

--- a/solution.py
+++ b/solution.py
@@ -199,11 +199,11 @@
         if peers & (peers - 1):
             values = lax.pmax(values, axis)
             continue
-        step = 1
-        while step < peers:
+        step = peers // 2
+        while step >= 1:
             pairs = [(i, i ^ step) for i in range(peers)]
             values = jnp.maximum(values, lax.ppermute(values, axis, pairs))
-            step *= 2
+            step //= 2
     return values
 
 

time: 263 us -> 261 us (level)
  the two profiles are of different devices: /device:TPU:64 before, /device:TPU:66 now
where the time goes in v10:
time: 261 us; the launch traced here: 259 us
  starting transfers between devices  80 us (31%)
  blocking collectives  57.8 us (22%)
  waiting for transfers between devices  43.1 us (17%)
  local copies, waits for them, and re-layouts  28.6 us (11%)
  other arithmetic  28.2 us (11%)
  matrix products  12.7 us (5%)
  between operations  8.54 us (3%)
    all_gather x1, blocking collectives, all_max(): values = jnp.max(lax.all_gather(values, axis), axis=0)  32.4 us
    ppermute x10, starting transfers between devices, extend(): before = lax.ppermute(low, axis, up)  32.1 us
    ppermute x10, starting transfers between devices, extend(): after = lax.ppermute(high, axis, down)  31.1 us
    all_gather x1, blocking collectives, extend(): whole = lax.all_gather(x, axis, axis=dim, tiled=True)  25.4 us
    ppermute x10, waiting for transfers between devices, extend(): after = lax.ppermute(high, axis, down)  23.5 us
    ppermute x5, starting transfers between devices, all_max(): values = jnp.maximum(values, lax.ppermute(values, axis, pairs))  16.8 us
    broadcast_in_dim x21, local copies, waits for them, and re-layouts, residual(): r = jnp.where(crop(self.mask, self.depth - out), r, 0.0)  13.1 us
    add x22, other arithmetic, smooth(): field = crop(field, 1) + direction  10.9 us
  transfers between devices with their start and end apart: 25, of which 16 were waited for; matrix products, arithmetic and copies ran while one was open for 7% of the time, Pallas kernels for 0%

profile of v10, /device:TPU:66, one launch (start us, length us, event | category | flops | bytes accessed | tf_op | source)
XLA Modules:
  0.0 258.9 jit_solution(16699828370727491526)
XLA Ops:
  0.1 1.6 reduce_max.81
  1.7 1.6 reduce_max.82
  10.6 1.3 fusion.521
  11.9 1.3 fusion.520
  13.3 2.6 maximum_bitcast_fusion.2
  15.9 2.5 maximum_bitcast_fusion
  18.4 32.4 %all-gather.1 = f32[16,4,2]{1,2,0:T(2,128)S(1)} all-gather(f32[1,4,2]{1,2,0:T(2,128)S(1)} %bitcast.248), channel_id=2, replica_groups=mesh['gx'=32,'gy'=16] {'gy'}, dimensions={0}, use_global_device_ids=true | all-gather | bytes 544 | tf_op jit(solution)/shard_map/all_gather | solution.py:197
  51.5 5.1 %collective-permute-start.4 = (f32[4,2]{0,1:T(2,128)}, f32[4,2]{0,1:T(2,128)}, u32[]{:S(2)}, u32[]{:S(2)}) collective-permute-start(f32[4,2]{0,1:T(2,128)} %reduce_max.89), channel_id=1, source_target_pairs={{0,256},{16,272},{32,288},{48,304},{64,320},{80,336},{96,352},{112... | collective-permute-start | bytes 104 | tf_op jit(solution)/shard_map/ppermute | solution.py:205
  58.0 1.9 collective-permute-start
  59.9 3.6 %collective-permute-start.1 = (f32[3,5,32,256]{3,2,1,0:T(8,128)S(1)}, f32[3,5,32,256]{3,2,1,0:T(8,128)S(1)}, u32[]{:S(2)}, u32[]{:S(2)}) collective-permute-start(f32[3,5,32,256]{3,2,1,0:T(8,128)S(1)} %get-tuple-element.72), channel_id=1, source_target_pairs={{16,0},{32,16},{48,32},{64,48},{80,64},{96,80},{112,96},{128,112},... | collective-permute-start | bytes 1474568 | tf_op jit(solution)/shard_map/ppermute | solution.py:70
  74.3 1.9 collective-permute-start.2
  76.2 3.9 %collective-permute-start.3 = (f32[3,18,5,256]{3,2,1,0:T(8,128)S(1)}, f32[3,18,5,256]{3,2,1,0:T(8,128)S(1)}, u32[]{:S(2)}, u32[]{:S(2)}) collective-permute-start(f32[3,18,5,256]{3,2,1,0:T(8,128)S(1)} %get-tuple-element.63), channel_id=1, source_target_pairs={{1,0},{2,1},{3,2},{4,3},{5,4},{6,5},{7,6},{8,7},{9,8},{10,9},{11,1... | collective-permute-start | bytes 829448 | tf_op jit(solution)/shard_map/ppermute | solution.py:70
  81.4 2.6 collective-permute-start.5
  84.0 2.9 %collective-permute-done.5 = f32[4,2]{0,1:T(2,128)S(1)} collective-permute-done((f32[4,2]{0,1:T(2,128)S(1)}, f32[4,2]{0,1:T(2,128)S(1)}, u32[]{:S(2)}, u32[]{:S(2)}) %collective-permute-start.5) | collective-permute-done | bytes 64 | tf_op jit(solution)/shard_map/ppermute | solution.py:205
  86.9 4.0 %collective-permute-start.6 = (f32[4,2]{0,1:T(2,128)S(1)}, f32[4,2]{0,1:T(2,128)S(1)}, u32[]{:S(2)}, u32[]{:S(2)}) collective-permute-start(f32[4,2]{0,1:T(2,128)S(1)} %max.16), channel_id=1, source_target_pairs={{0,64},{16,80},{32,96},{48,112},{64,0},{80,16},{96,32},{112,48},{1... | collective-permute-start | bytes 104 | tf_op jit(solution)/shard_map/ppermute | solution.py:205
  90.9 2.9 %collective-permute-done.6 = f32[4,2]{0,1:T(2,128)S(1)} collective-permute-done((f32[4,2]{0,1:T(2,128)S(1)}, f32[4,2]{0,1:T(2,128)S(1)}, u32[]{:S(2)}, u32[]{:S(2)}) %collective-permute-start.6) | collective-permute-done | bytes 64 | tf_op jit(solution)/shard_map/ppermute | solution.py:205
  93.8 3.2 %collective-permute-start.7 = (f32[4,2]{0,1:T(2,128)S(1)}, f32[4,2]{0,1:T(2,128)S(1)}, u32[]{:S(2)}, u32[]{:S(2)}) collective-permute-start(f32[4,2]{0,1:T(2,128)S(1)} %max.17), channel_id=1, source_target_pairs={{0,32},{16,48},{32,0},{48,16},{64,96},{80,112},{96,64},{112,80},{1... | collective-permute-start | bytes 104 | tf_op jit(solution)/shard_map/ppermute | solution.py:205
  97.1 2.2 collective-permute-done.7
  99.3 1.9 collective-permute-start.8
  106.2 1.5 slice_add_fusion.4
  111.8 2.1 collective-permute-start.9
  114.0 3.5 %collective-permute-start.11 = (f32[3,4,16,128]{3,2,1,0:T(8,128)S(1)}, f32[3,4,16,128]{3,2,1,0:T(8,128)S(1)}, u32[]{:S(2)}, u32[]{:S(2)}) collective-permute-start(f32[3,4,16,128]{3,2,1,0:T(8,128)S(1)} %pad_maximum_fusion.2), channel_id=1, source_target_pairs={{16,0},{32,16},{48,32},{64,48},{80,64},{96,80},{112,96},{128,112},... | collective-permute-start | bytes 294920 | tf_op jit(solution)/shard_map/ppermute | solution.py:70
  117.7 1.9 collective-permute-start.10
  120.4 3.6 %collective-permute-start.12 = (f32[3,3,16,128]{3,2,1,0:T(8,128)S(1)}, f32[3,3,16,128]{3,2,1,0:T(8,128)S(1)}, u32[]{:S(2)}, u32[]{:S(2)}) collective-permute-start(f32[3,3,16,128]{3,2,1,0:T(8,128)S(1)} %slice.1971), channel_id=1, source_target_pairs={{16,0},{32,16},{48,32},{64,48},{80,64},{96,80},{112,96},{128,112},... | collective-permute-start | bytes 221192 | tf_op jit(solution)/shard_map/ppermute | solution.py:70
  124.1 1.9 collective-permute-done.12
  126.8 1.9 collective-permute-start.13
  128.7 3.9 %collective-permute-start.14 = (f32[3,18,7,128]{3,2,1,0:T(8,128)}, f32[3,18,7,128]{3,2,1,0:T(8,128)}, u32[]{:S(2)}, u32[]{:S(2)}) collective-permute-start(f32[3,18,7,128]{3,2,1,0:T(8,128)} %get-tuple-element.94), channel_id=1, source_target_pairs={{1,0},{2,1},{3,2},{4,3},{5,4},{6,5},{7,6},{8,7},{9,8},{10,9},{11,1... | collective-permute-start | bytes 580616 | tf_op jit(solution)/shard_map/ppermute | solution.py:70
  132.6 1.3 slice_bitcast_fusion.32
  136.6 3.1 %collective-permute-done.14 = f32[3,18,7,128]{3,2,1,0:T(8,128)} collective-permute-done((f32[3,18,7,128]{3,2,1,0:T(8,128)}, f32[3,18,7,128]{3,2,1,0:T(8,128)}, u32[]{:S(2)}, u32[]{:S(2)}) %collective-permute-start.14) | collective-permute-done | bytes 193568 | tf_op jit(solution)/shard_map/ppermute | solution.py:70
  144.1 2.4 collective-permute-start.15
  146.5 3.1 %collective-permute-start.16 = (f32[3,2,8,64]{3,2,1,0:T(8,128)S(1)}, f32[3,2,8,64]{3,2,1,0:T(8,128)S(1)}, u32[]{:S(2)}, u32[]{:S(2)}) collective-permute-start(f32[3,2,8,64]{3,2,1,0:T(8,128)S(1)} %pad_maximum_fusion.4), channel_id=1, source_target_pairs={{0,496},{16,0},{32,16},{48,32},{64,48},{80,64},{96,80},{112,96},{1... | collective-permute-start | bytes 36872 | tf_op jit(solution)/shard_map/ppermute | solution.py:70
  149.7 1.3 slice_bitcast_fusion.31
  151.2 6.8 %collective-permute-start.17 = (f32[3,6,8,64]{3,2,1,0:T(8,128)S(1)}, f32[3,6,8,64]{3,2,1,0:T(8,128)S(1)}, u32[]{:S(2)}, u32[]{:S(2)}) collective-permute-start(f32[3,6,8,64]{3,2,1,0:T(8,128)S(1)} %pad_maximum_fusion.3), channel_id=1, source_target_pairs={{0,48},{16,64},{32,80},{48,96},{64,112},{80,128},{96,144},{112,160... | collective-permute-start | bytes 110600 | tf_op jit(solution)/shard_map/ppermute | solution.py:69
  159.3 2.3 collective-permute-start.18
  161.7 5.8 %collective-permute-done.18 = f32[3,6,8,64]{3,2,1,0:T(8,128)S(1)} collective-permute-done((f32[3,6,8,64]{3,2,1,0:T(8,128)S(1)}, f32[3,6,8,64]{3,2,1,0:T(8,128)S(1)}, u32[]{:S(2)}, u32[]{:S(2)}) %collective-permute-start.18) | collective-permute-done | bytes 36896 | tf_op jit(solution)/shard_map/ppermute | solution.py:70
  167.6 5.1 %collective-permute-start.19 = (f32[3,18,8,64]{3,2,1,0:T(8,128)S(1)}, f32[3,18,8,64]{3,2,1,0:T(8,128)}, u32[]{:S(2)}, u32[]{:S(2)}) collective-permute-start(f32[3,18,8,64]{3,2,1,0:T(8,128)S(1)} %broadcast_select_fusion), channel_id=1, source_target_pairs={{0,1},{1,2},{2,3},{3,4},{4,5},{5,6},{6,7},{7,8},{8,9},{9,10},{10,1... | collective-permute-start | bytes 331784 | tf_op jit(solution)/shard_map/ppermute | solution.py:69
  172.7 2.1 collective-permute-start.20
  176.7 4.2 %collective-permute-done.20 = f32[3,18,8,64]{3,2,1,0:T(8,128)} collective-permute-done((f32[3,18,8,64]{3,2,1,0:T(8,128)S(1)}, f32[3,18,8,64]{3,2,1,0:T(8,128)}, u32[]{:S(2)}, u32[]{:S(2)}) %collective-permute-start.20) | collective-permute-done | bytes 110624 | tf_op jit(solution)/shard_map/ppermute | solution.py:70
  184.9 25.4 %all_gather.11 = f32[3,32,4,32]{3,2,1,0:T(4,128)S(1)} all-gather(f32[3,1,4,32]{3,2,1,0:T(4,128)S(1)} %pad_maximum_fusion.5), channel_id=1, replica_groups=mesh['gx'=32,'gy'=16] {'gx'}, dimensions={1}, use_global_device_ids=true | all-gather | bytes 50688 | tf_op jit(solution)/shard_map/all_gather | solution.py:50
  210.3 2.9 %collective-permute-start.21 = (f32[3,21,4,32]{3,2,1,0:T(4,128)S(1)}, f32[3,21,4,32]{3,2,1,0:T(4,128)S(1)}, u32[]{:S(2)}, u32[]{:S(2)}) collective-permute-start(f32[3,21,4,32]{3,2,1,0:T(4,128)S(1)} %pad_dynamic-slice_fusion), channel_id=1, source_target_pairs={{0,1},{1,2},{2,3},{3,4},{4,5},{5,6},{6,7},{7,8},{8,9},{9,10},{10,1... | collective-permute-start | bytes 96776 | tf_op jit(solution)/shard_map/ppermute | solution.py:69
  213.2 3.0 %collective-permute-start.22 = (f32[3,21,4,32]{3,2,1,0:T(4,128)S(1)}, f32[3,21,4,32]{3,2,1,0:T(4,128)S(1)}, u32[]{:S(2)}, u32[]{:S(2)}) collective-permute-start(f32[3,21,4,32]{3,2,1,0:T(4,128)S(1)} %pad_dynamic-slice_fusion), channel_id=1, source_target_pairs={{0,15},{1,0},{2,1},{3,2},{4,3},{5,4},{6,5},{7,6},{8,7},{9,8},{10,9... | collective-permute-start | bytes 96776 | tf_op jit(solution)/shard_map/ppermute | solution.py:70
  216.2 1.7 collective-permute-done.21
  217.9 2.6 collective-permute-done.22
  222.3 5.1 %collective-permute-start.23 = (f32[3,21,6,32]{3,2,1,0:T(8,128)}, f32[3,21,6,32]{3,2,1,0:T(8,128)}, u32[]{:S(2)}, u32[]{:S(2)}) collective-permute-start(f32[3,21,6,32]{3,2,1,0:T(8,128)} %get-tuple-element.89), channel_id=1, source_target_pairs={{0,2},{1,3},{2,4},{3,5},{4,6},{5,7},{6,8},{7,9},{8,10},{9,11},{10,... | collective-permute-start | bytes 145160 | tf_op jit(solution)/shard_map/ppermute | solution.py:69
  227.4 1.9 collective-permute-start.24
  231.2 7.0 %collective-permute-done.23 = f32[3,21,6,32]{3,2,1,0:T(8,128)} collective-permute-done((f32[3,21,6,32]{3,2,1,0:T(8,128)}, f32[3,21,6,32]{3,2,1,0:T(8,128)}, u32[]{:S(2)}, u32[]{:S(2)}) %collective-permute-start.23) | collective-permute-done | bytes 48416 | tf_op jit(solution)/shard_map/ppermute | solution.py:69
  238.3 5.6 %collective-permute-done.24 = f32[3,21,6,32]{3,2,1,0:T(8,128)} collective-permute-done((f32[3,21,6,32]{3,2,1,0:T(8,128)}, f32[3,21,6,32]{3,2,1,0:T(8,128)}, u32[]{:S(2)}, u32[]{:S(2)}) %collective-permute-start.24) | collective-permute-done | bytes 48416 | tf_op jit(solution)/shard_map/ppermute | solution.py:70
  243.9 1.4 add_select_fusion
  (388 shorter events, 56.1 us)
Async XLA Ops:
  0.0 18.4 %copy-start.57 = (s32[256]{0:T(256)}, s32[256]{0:T(256)S(1)}, u32[]{:S(2)}) copy-start(s32[256]{0:T(256)S(1)} %and_select_fusion.7) | copy-start | bytes 3076
  0.0 7.6 %copy-start.78 = (s32[32]{0:T(128)}, s32[32]{0:T(128)S(1)}, u32[]{:S(2)}) copy-start(s32[32]{0:T(128)S(1)} %and_select_fusion.8) | copy-start | bytes 388
  0.0 15.8 %copy-start.96 = (s32[16]{0:T(128)}, s32[16]{0:T(128)S(1)}, u32[]{:S(2)}) copy-start(s32[16]{0:T(128)S(1)} %and_select_fusion.6) | copy-start | bytes 196
  0.1 18.4 %copy-start.73 = (s32[128]{0:T(128)}, s32[128]{0:T(128)S(1)}, u32[]{:S(2)}) copy-start(s32[128]{0:T(128)S(1)} %and_select_fusion.5) | copy-start | bytes 1540
  0.1 15.8 %copy-start.94 = (s32[8]{0:T(128)}, s32[8]{0:T(128)S(1)}, u32[]{:S(2)}) copy-start(s32[8]{0:T(128)S(1)} %and_select_fusion.4) | copy-start | bytes 100
  0.1 13.2 %copy-start.90 = (s32[64]{0:T(128)}, s32[64]{0:T(128)S(1)}, u32[]{:S(2)}) copy-start(s32[64]{0:T(128)S(1)} %and_select_fusion.3) | copy-start | bytes 772
  51.5 29.2 %collective-permute-start.4 = (f32[4,2]{0,1:T(2,128)}, f32[4,2]{0,1:T(2,128)}, u32[]{:S(2)}, u32[]{:S(2)}) collective-permute-start(f32[4,2]{0,1:T(2,128)} %reduce_max.89), channel_id=1, source_target_pairs={{0,256},{16,272},{32,288},{48,304},{64,320},{80,336},{96,352},{112... | collective-permute-start | bytes 104 | tf_op jit(solution)/shard_map/ppermute | solution.py:205
  56.6 17.3 %copy-start.43 = (f32[8,32,256]{2,1,0:T(8,128)S(1)}, f32[8,32,256]{2,1,0:T(8,128)}, u32[]{:S(2)}) copy-start(f32[8,32,256]{2,1,0:T(8,128)} %param.5) | copy-start | bytes 786436
  56.6 17.3 %copy-start.44 = (f32[8,32,256]{2,1,0:T(8,128)S(1)}, f32[8,32,256]{2,1,0:T(8,128)}, u32[]{:S(2)}) copy-start(f32[8,32,256]{2,1,0:T(8,128)} %param.4) | copy-start | bytes 786436
  56.6 17.3 %copy-start.45 = (f32[8,32,256]{2,1,0:T(8,128)S(1)}, f32[8,32,256]{2,1,0:T(8,128)}, u32[]{:S(2)}) copy-start(f32[8,32,256]{2,1,0:T(8,128)} %param.3) | copy-start | bytes 786436
  58.0 15.9 %collective-permute-start = (f32[3,5,32,256]{3,2,1,0:T(8,128)S(1)}, f32[3,5,32,256]{3,2,1,0:T(8,128)S(1)}, u32[]{:S(2)}, u32[]{:S(2)}) collective-permute-start(f32[3,5,32,256]{3,2,1,0:T(8,128)S(1)} %get-tuple-element.71), channel_id=1, source_target_pairs={{0,16},{16,32},{32,48},{48,64},{64,80},{80,96},{96,112},{112,128},... | collective-permute-start | bytes 1474568 | tf_op jit(solution)/shard_map/ppermute | solution.py:69
  59.9 14.0 %collective-permute-start.1 = (f32[3,5,32,256]{3,2,1,0:T(8,128)S(1)}, f32[3,5,32,256]{3,2,1,0:T(8,128)S(1)}, u32[]{:S(2)}, u32[]{:S(2)}) collective-permute-start(f32[3,5,32,256]{3,2,1,0:T(8,128)S(1)} %get-tuple-element.72), channel_id=1, source_target_pairs={{16,0},{32,16},{48,32},{64,48},{80,64},{96,80},{112,96},{128,112},... | collective-permute-start | bytes 1474568 | tf_op jit(solution)/shard_map/ppermute | solution.py:70
  65.1 8.8 %copy-start.59 = (pred[12,36]{1,0:T(8,128)(4,1)}, pred[12,36]{1,0:T(8,128)(4,1)S(1)}, u32[]{:S(2)}) copy-start(pred[12,36]{1,0:T(8,128)(4,1)S(1)} %slice_bitcast_fusion.27) | copy-start | bytes 1300
  65.2 4.0 %copy-start.51 = (pred[18,30,1]{1,0,2:T(8,128)(4,1)}, pred[18,30,1]{1,0,2:T(8,128)(4,1)S(1)}, u32[]{:S(2)}) copy-start(pred[18,30,1]{1,0,2:T(8,128)(4,1)S(1)} %broadcast_and_fusion.2) | copy-start | bytes 1624
  67.2 6.7 %copy-start.86 = (pred[18]{0:T(512)(128)(4,1)}, pred[18]{0:T(512)(128)(4,1)S(1)}, u32[]{:S(2)}) copy-start(pred[18]{0:T(512)(128)(4,1)S(1)} %compare_and_fusion.3) | copy-start | bytes 58
  67.3 6.6 %copy-start.53 = (pred[18,24,1]{1,0,2:T(8,128)(4,1)}, pred[18,24,1]{1,0,2:T(8,128)(4,1)S(1)}, u32[]{:S(2)}) copy-start(pred[18,24,1]{1,0,2:T(8,128)(4,1)S(1)} %broadcast_and_fusion.1) | copy-start | bytes 1300
  69.3 4.6 %copy-start.88 = (pred[24]{0:T(512)(128)(4,1)}, pred[24]{0:T(512)(128)(4,1)S(1)}, u32[]{:S(2)}) copy-start(pred[24]{0:T(512)(128)(4,1)S(1)} %compare_and_fusion.1) | copy-start | bytes 76
  69.3 4.6 %copy-start.50 = (pred[21,24,1]{1,0,2:T(8,128)(4,1)}, pred[21,24,1]{1,0,2:T(8,128)(4,1)S(1)}, u32[]{:S(2)}) copy-start(pred[21,24,1]{1,0,2:T(8,128)(4,1)S(1)} %broadcast_and_fusion) | copy-start | bytes 1516
  74.2 6.0 %copy-start.54 = (pred[18,24,1]{1,0,2:T(8,128)(4,1)S(1)}, pred[18,24,1]{1,0,2:T(8,128)(4,1)}, u32[]{:S(2)}) copy-start(pred[18,24,1]{1,0,2:T(8,128)(4,1)} %copy-done.53) | copy-start | bytes 1300
  74.3 30.3 %collective-permute-start.2 = (f32[3,18,5,256]{3,2,1,0:T(8,128)S(1)}, f32[3,18,5,256]{3,2,1,0:T(8,128)S(1)}, u32[]{:S(2)}, u32[]{:S(2)}) collective-permute-start(f32[3,18,5,256]{3,2,1,0:T(8,128)S(1)} %get-tuple-element.62), channel_id=1, source_target_pairs={{0,1},{1,2},{2,3},{3,4},{4,5},{5,6},{6,7},{7,8},{8,9},{9,10},{10,1... | collective-permute-start | bytes 829448 | tf_op jit(solution)/shard_map/ppermute | solution.py:69
  76.2 28.4 %collective-permute-start.3 = (f32[3,18,5,256]{3,2,1,0:T(8,128)S(1)}, f32[3,18,5,256]{3,2,1,0:T(8,128)S(1)}, u32[]{:S(2)}, u32[]{:S(2)}) collective-permute-start(f32[3,18,5,256]{3,2,1,0:T(8,128)S(1)} %get-tuple-element.63), channel_id=1, source_target_pairs={{1,0},{2,1},{3,2},{4,3},{5,4},{6,5},{7,6},{8,7},{9,8},{10,9},{11,1... | collective-permute-start | bytes 829448 | tf_op jit(solution)/shard_map/ppermute | solution.py:70
  81.4 5.5 %collective-permute-start.5 = (f32[4,2]{0,1:T(2,128)S(1)}, f32[4,2]{0,1:T(2,128)S(1)}, u32[]{:S(2)}, u32[]{:S(2)}) collective-permute-start(f32[4,2]{0,1:T(2,128)S(1)} %max.15), channel_id=1, source_target_pairs={{0,128},{16,144},{32,160},{48,176},{64,192},{80,208},{96,224},{112... | collective-permute-start | bytes 104 | tf_op jit(solution)/shard_map/ppermute | solution.py:205
  86.9 7.0 %collective-permute-start.6 = (f32[4,2]{0,1:T(2,128)S(1)}, f32[4,2]{0,1:T(2,128)S(1)}, u32[]{:S(2)}, u32[]{:S(2)}) collective-permute-start(f32[4,2]{0,1:T(2,128)S(1)} %max.16), channel_id=1, source_target_pairs={{0,64},{16,80},{32,96},{48,112},{64,0},{80,16},{96,32},{112,48},{1... | collective-permute-start | bytes 104 | tf_op jit(solution)/shard_map/ppermute | solution.py:205
  93.8 5.5 %collective-permute-start.7 = (f32[4,2]{0,1:T(2,128)S(1)}, f32[4,2]{0,1:T(2,128)S(1)}, u32[]{:S(2)}, u32[]{:S(2)}) collective-permute-start(f32[4,2]{0,1:T(2,128)S(1)} %max.17), channel_id=1, source_target_pairs={{0,32},{16,48},{32,0},{48,16},{64,96},{80,112},{96,64},{112,80},{1... | collective-permute-start | bytes 104 | tf_op jit(solution)/shard_map/ppermute | solution.py:205
  99.3 3.0 %collective-permute-start.8 = (f32[4,2]{0,1:T(2,128)S(1)}, f32[4,2]{0,1:T(2,128)S(1)}, u32[]{:S(2)}, u32[]{:S(2)}) collective-permute-start(f32[4,2]{0,1:T(2,128)S(1)} %max.18), channel_id=1, source_target_pairs={{0,16},{16,0},{32,48},{48,32},{64,80},{80,64},{96,112},{112,96},{1... | collective-permute-start | bytes 104 | tf_op jit(solution)/shard_map/ppermute | solution.py:205
  107.7 2.2 copy-start
  110.6 3.3 %copy-start.52 = (pred[18,30,1]{1,0,2:T(8,128)(4,1)S(1)}, pred[18,30,1]{1,0,2:T(8,128)(4,1)}, u32[]{:S(2)}) copy-start(pred[18,30,1]{1,0,2:T(8,128)(4,1)} %copy-done.51) | copy-start | bytes 1624
  110.6 9.1 %copy-start.56 = (pred[18,42,1]{1,0,2:T(8,128)(4,1)S(1)}, pred[18,42,1]{1,0,2:T(8,128)(4,1)}, u32[]{:S(2)}) copy-start(pred[18,42,1]{1,0,2:T(8,128)(4,1)} %copy-done.55) | copy-start | bytes 2272
  110.6 9.1 %copy-start.64 = (pred[12,24]{1,0:T(8,128)(4,1)S(1)}, pred[12,24]{1,0:T(8,128)(4,1)}, u32[]{:S(2)}) copy-start(pred[12,24]{1,0:T(8,128)(4,1)} %slice_bitcast_fusion.24) | copy-start | bytes 868
  111.8 5.9 %collective-permute-start.9 = (f32[3,4,16,128]{3,2,1,0:T(8,128)S(1)}, f32[3,4,16,128]{3,2,1,0:T(8,128)S(1)}, u32[]{:S(2)}, u32[]{:S(2)}) collective-permute-start(f32[3,4,16,128]{3,2,1,0:T(8,128)S(1)} %pad_maximum_fusion.2), channel_id=1, source_target_pairs={{0,16},{16,32},{32,48},{48,64},{64,80},{80,96},{96,112},{112,128},... | collective-permute-start | bytes 294920 | tf_op jit(solution)/shard_map/ppermute | solution.py:69
  114.0 6.4 %collective-permute-start.11 = (f32[3,4,16,128]{3,2,1,0:T(8,128)S(1)}, f32[3,4,16,128]{3,2,1,0:T(8,128)S(1)}, u32[]{:S(2)}, u32[]{:S(2)}) collective-permute-start(f32[3,4,16,128]{3,2,1,0:T(8,128)S(1)} %pad_maximum_fusion.2), channel_id=1, source_target_pairs={{16,0},{32,16},{48,32},{64,48},{80,64},{96,80},{112,96},{128,112},... | collective-permute-start | bytes 294920 | tf_op jit(solution)/shard_map/ppermute | solution.py:70
  117.7 6.3 %collective-permute-start.10 = (f32[3,3,16,128]{3,2,1,0:T(8,128)S(1)}, f32[3,3,16,128]{3,2,1,0:T(8,128)S(1)}, u32[]{:S(2)}, u32[]{:S(2)}) collective-permute-start(f32[3,3,16,128]{3,2,1,0:T(8,128)S(1)} %slice.1970), channel_id=1, source_target_pairs={{0,16},{16,32},{32,48},{48,64},{64,80},{80,96},{96,112},{112,128},... | collective-permute-start | bytes 221192 | tf_op jit(solution)/shard_map/ppermute | solution.py:69
  120.4 5.6 %collective-permute-start.12 = (f32[3,3,16,128]{3,2,1,0:T(8,128)S(1)}, f32[3,3,16,128]{3,2,1,0:T(8,128)S(1)}, u32[]{:S(2)}, u32[]{:S(2)}) collective-permute-start(f32[3,3,16,128]{3,2,1,0:T(8,128)S(1)} %slice.1971), channel_id=1, source_target_pairs={{16,0},{32,16},{48,32},{64,48},{80,64},{96,80},{112,96},{128,112},... | collective-permute-start | bytes 221192 | tf_op jit(solution)/shard_map/ppermute | solution.py:70
  126.8 9.8 %collective-permute-start.13 = (f32[3,18,7,128]{3,2,1,0:T(8,128)}, f32[3,18,7,128]{3,2,1,0:T(8,128)}, u32[]{:S(2)}, u32[]{:S(2)}) collective-permute-start(f32[3,18,7,128]{3,2,1,0:T(8,128)} %get-tuple-element.93), channel_id=1, source_target_pairs={{0,1},{1,2},{2,3},{3,4},{4,5},{5,6},{6,7},{7,8},{8,9},{9,10},{10,1... | collective-permute-start | bytes 580616 | tf_op jit(solution)/shard_map/ppermute | solution.py:69
  128.7 11.0 %collective-permute-start.14 = (f32[3,18,7,128]{3,2,1,0:T(8,128)}, f32[3,18,7,128]{3,2,1,0:T(8,128)}, u32[]{:S(2)}, u32[]{:S(2)}) collective-permute-start(f32[3,18,7,128]{3,2,1,0:T(8,128)} %get-tuple-element.94), channel_id=1, source_target_pairs={{1,0},{2,1},{3,2},{4,3},{5,4},{6,5},{7,6},{8,7},{9,8},{10,9},{11,1... | collective-permute-start | bytes 580616 | tf_op jit(solution)/shard_map/ppermute | solution.py:70
  143.0 15.7 %copy-start.65 = (pred[12,18]{1,0:T(8,128)(4,1)S(1)}, pred[12,18]{1,0:T(8,128)(4,1)}, u32[]{:S(2)}) copy-start(pred[12,18]{1,0:T(8,128)(4,1)} %slice_bitcast_fusion.21) | copy-start | bytes 652
  143.1 24.4 %copy-start.87 = (pred[18]{0:T(512)(128)(4,1)S(1)}, pred[18]{0:T(512)(128)(4,1)}, u32[]{:S(2)}) copy-start(pred[18]{0:T(512)(128)(4,1)} %copy-done.86) | copy-start | bytes 58
  144.1 6.9 %collective-permute-start.15 = (f32[3,2,8,64]{3,2,1,0:T(8,128)S(1)}, f32[3,2,8,64]{3,2,1,0:T(8,128)S(1)}, u32[]{:S(2)}, u32[]{:S(2)}) collective-permute-start(f32[3,2,8,64]{3,2,1,0:T(8,128)S(1)} %pad_maximum_fusion.4), channel_id=1, source_target_pairs={{0,16},{16,32},{32,48},{48,64},{64,80},{80,96},{96,112},{112,128},... | collective-permute-start | bytes 36872 | tf_op jit(solution)/shard_map/ppermute | solution.py:69
  146.5 4.6 %collective-permute-start.16 = (f32[3,2,8,64]{3,2,1,0:T(8,128)S(1)}, f32[3,2,8,64]{3,2,1,0:T(8,128)S(1)}, u32[]{:S(2)}, u32[]{:S(2)}) collective-permute-start(f32[3,2,8,64]{3,2,1,0:T(8,128)S(1)} %pad_maximum_fusion.4), channel_id=1, source_target_pairs={{0,496},{16,0},{32,16},{48,32},{64,48},{80,64},{96,80},{112,96},{1... | collective-permute-start | bytes 36872 | tf_op jit(solution)/shard_map/ppermute | solution.py:70
  151.2 10.4 %collective-permute-start.17 = (f32[3,6,8,64]{3,2,1,0:T(8,128)S(1)}, f32[3,6,8,64]{3,2,1,0:T(8,128)S(1)}, u32[]{:S(2)}, u32[]{:S(2)}) collective-permute-start(f32[3,6,8,64]{3,2,1,0:T(8,128)S(1)} %pad_maximum_fusion.3), channel_id=1, source_target_pairs={{0,48},{16,64},{32,80},{48,96},{64,112},{80,128},{96,144},{112,160... | collective-permute-start | bytes 110600 | tf_op jit(solution)/shard_map/ppermute | solution.py:69
  159.3 8.2 %collective-permute-start.18 = (f32[3,6,8,64]{3,2,1,0:T(8,128)S(1)}, f32[3,6,8,64]{3,2,1,0:T(8,128)S(1)}, u32[]{:S(2)}, u32[]{:S(2)}) collective-permute-start(f32[3,6,8,64]{3,2,1,0:T(8,128)S(1)} %pad_maximum_fusion.3), channel_id=1, source_target_pairs={{0,464},{16,480},{32,496},{48,0},{64,16},{80,32},{96,48},{112,64},... | collective-permute-start | bytes 110600 | tf_op jit(solution)/shard_map/ppermute | solution.py:70
  167.6 9.1 %collective-permute-start.19 = (f32[3,18,8,64]{3,2,1,0:T(8,128)S(1)}, f32[3,18,8,64]{3,2,1,0:T(8,128)}, u32[]{:S(2)}, u32[]{:S(2)}) collective-permute-start(f32[3,18,8,64]{3,2,1,0:T(8,128)S(1)} %broadcast_select_fusion), channel_id=1, source_target_pairs={{0,1},{1,2},{2,3},{3,4},{4,5},{5,6},{6,7},{7,8},{8,9},{9,10},{10,1... | collective-permute-start | bytes 331784 | tf_op jit(solution)/shard_map/ppermute | solution.py:69
  172.7 8.2 %collective-permute-start.20 = (f32[3,18,8,64]{3,2,1,0:T(8,128)S(1)}, f32[3,18,8,64]{3,2,1,0:T(8,128)}, u32[]{:S(2)}, u32[]{:S(2)}) collective-permute-start(f32[3,18,8,64]{3,2,1,0:T(8,128)S(1)} %broadcast_select_fusion), channel_id=1, source_target_pairs={{1,0},{2,1},{3,2},{4,3},{5,4},{6,5},{7,6},{8,7},{9,8},{10,9},{11,1... | collective-permute-start | bytes 331784 | tf_op jit(solution)/shard_map/ppermute | solution.py:70
  184.3 59.6 %copy-start.89 = (pred[24]{0:T(512)(128)(4,1)S(1)}, pred[24]{0:T(512)(128)(4,1)}, u32[]{:S(2)}) copy-start(pred[24]{0:T(512)(128)(4,1)} %copy-done.88) | copy-start | bytes 76
  210.3 7.6 %collective-permute-start.21 = (f32[3,21,4,32]{3,2,1,0:T(4,128)S(1)}, f32[3,21,4,32]{3,2,1,0:T(4,128)S(1)}, u32[]{:S(2)}, u32[]{:S(2)}) collective-permute-start(f32[3,21,4,32]{3,2,1,0:T(4,128)S(1)} %pad_dynamic-slice_fusion), channel_id=1, source_target_pairs={{0,1},{1,2},{2,3},{3,4},{4,5},{5,6},{6,7},{7,8},{8,9},{9,10},{10,1... | collective-permute-start | bytes 96776 | tf_op jit(solution)/shard_map/ppermute | solution.py:69
  213.2 7.3 %collective-permute-start.22 = (f32[3,21,4,32]{3,2,1,0:T(4,128)S(1)}, f32[3,21,4,32]{3,2,1,0:T(4,128)S(1)}, u32[]{:S(2)}, u32[]{:S(2)}) collective-permute-start(f32[3,21,4,32]{3,2,1,0:T(4,128)S(1)} %pad_dynamic-slice_fusion), channel_id=1, source_target_pairs={{0,15},{1,0},{2,1},{3,2},{4,3},{5,4},{6,5},{7,6},{8,7},{9,8},{10,9... | collective-permute-start | bytes 96776 | tf_op jit(solution)/shard_map/ppermute | solution.py:70
  222.3 16.0 %collective-permute-start.23 = (f32[3,21,6,32]{3,2,1,0:T(8,128)}, f32[3,21,6,32]{3,2,1,0:T(8,128)}, u32[]{:S(2)}, u32[]{:S(2)}) collective-permute-start(f32[3,21,6,32]{3,2,1,0:T(8,128)} %get-tuple-element.89), channel_id=1, source_target_pairs={{0,2},{1,3},{2,4},{3,5},{4,6},{5,7},{6,8},{7,9},{8,10},{9,11},{10,... | collective-permute-start | bytes 145160 | tf_op jit(solution)/shard_map/ppermute | solution.py:69
  227.4 16.5 %collective-permute-start.24 = (f32[3,21,6,32]{3,2,1,0:T(8,128)}, f32[3,21,6,32]{3,2,1,0:T(8,128)}, u32[]{:S(2)}, u32[]{:S(2)}) collective-permute-start(f32[3,21,6,32]{3,2,1,0:T(8,128)} %get-tuple-element.90), channel_id=1, source_target_pairs={{0,14},{1,15},{2,0},{3,1},{4,2},{5,3},{6,4},{7,5},{8,6},{9,7},{10,... | collective-permute-start | bytes 145160 | tf_op jit(solution)/shard_map/ppermute | solution.py:70
  (75 other events, 80.1 us)

commit v11 on v10

--- a/solution.py
+++ b/solution.py
@@ -193,9 +193,6 @@
 def all_max(values):
     for axis in ("gy", "gx"):
         peers = lax.axis_size(axis)
-        if axis == "gy":
-            values = jnp.max(lax.all_gather(values, axis), axis=0)
-            continue
         if peers & (peers - 1):
             values = lax.pmax(values, axis)
             continue

time: 261 us -> 261 us (level)
  the two profiles are of different devices: /device:TPU:66 before, /device:TPU:40 now
where the time goes in v11:
time: 261 us; the launch traced here: 260 us
  starting transfers between devices  113 us (43%)
  waiting for transfers between devices  46.7 us (18%)
  local copies, waits for them, and re-layouts  28.6 us (11%)
  other arithmetic  26.9 us (10%)
  blocking collectives  23.2 us (9%)
  matrix products  12.7 us (5%)
  between operations  8.59 us (3%)
    ppermute x10, starting transfers between devices, extend(): after = lax.ppermute(high, axis, down)  45.5 us
    ppermute x9, starting transfers between devices, all_max(): values = jnp.maximum(values, lax.ppermute(values, axis, pairs))  41.2 us
    ppermute x10, starting transfers between devices, extend(): before = lax.ppermute(low, axis, up)  26 us
    all_gather x1, blocking collectives, extend(): whole = lax.all_gather(x, axis, axis=dim, tiled=True)  23.2 us
    ppermute x9, waiting for transfers between devices, all_max(): values = jnp.maximum(values, lax.ppermute(values, axis, pairs))  20.4 us
    ppermute x10, waiting for transfers between devices, extend(): after = lax.ppermute(high, axis, down)  16.7 us
    broadcast_in_dim x21, local copies, waits for them, and re-layouts, residual(): r = jnp.where(crop(self.mask, self.depth - out), r, 0.0)  13.4 us
    add x22, other arithmetic, smooth(): field = crop(field, 1) + direction  10.9 us
  transfers between devices with their start and end apart: 29, of which 18 were waited for; matrix products, arithmetic and copies ran while one was open for 7% of the time, Pallas kernels for 0%

profile of v11, /device:TPU:40, one launch (start us, length us, event | category | flops | bytes accessed | tf_op | source)
XLA Modules:
  0.0 259.6 jit_solution(17654442195764531288)
XLA Ops:
  0.1 1.6 reduce_max.72
  1.7 1.6 reduce_max.73
  13.0 2.6 maximum_bitcast_fusion.2
  15.5 2.5 maximum_bitcast_fusion
  18.0 14.8 %collective-permute-start.4 = (f32[4,2]{1,0:T(4,128)S(1)}, f32[4,2]{1,0:T(4,128)S(1)}, u32[]{:S(2)}, u32[]{:S(2)}) collective-permute-start(f32[4,2]{1,0:T(4,128)S(1)} %pad_maximum_fusion.6), channel_id=1, source_target_pairs={{0,8},{1,9},{2,10},{3,11},{4,12},{5,13},{6,14},{7,15},{8,0},{9,1},... | collective-permute-start | bytes 104 | tf_op jit(solution)/shard_map/ppermute | solution.py:202
  34.3 1.9 collective-permute-start
  36.3 5.8 %collective-permute-start.1 = (f32[3,5,32,256]{3,2,1,0:T(8,128)S(1)}, f32[3,5,32,256]{3,2,1,0:T(8,128)S(1)}, u32[]{:S(2)}, u32[]{:S(2)}) collective-permute-start(f32[3,5,32,256]{3,2,1,0:T(8,128)S(1)} %get-tuple-element.72), channel_id=1, source_target_pairs={{16,0},{32,16},{48,32},{64,48},{80,64},{96,80},{112,96},{128,112},... | collective-permute-start | bytes 1474568 | tf_op jit(solution)/shard_map/ppermute | solution.py:70
  53.2 4.3 %collective-permute-start.5 = (f32[4,2]{1,0:T(4,128)S(1)}, f32[4,2]{1,0:T(4,128)S(1)}, u32[]{:S(2)}, u32[]{:S(2)}) collective-permute-start(f32[4,2]{1,0:T(4,128)S(1)} %fusion.471), channel_id=1, source_target_pairs={{0,4},{1,5},{2,6},{3,7},{4,0},{5,1},{6,2},{7,3},{8,12},{9,13},{10,... | collective-permute-start | bytes 104 | tf_op jit(solution)/shard_map/ppermute | solution.py:202
  57.9 2.9 %collective-permute-start.2 = (f32[3,18,5,256]{3,2,1,0:T(8,128)S(1)}, f32[3,18,5,256]{3,2,1,0:T(8,128)S(1)}, u32[]{:S(2)}, u32[]{:S(2)}) collective-permute-start(f32[3,18,5,256]{3,2,1,0:T(8,128)S(1)} %get-tuple-element.62), channel_id=1, source_target_pairs={{0,1},{1,2},{2,3},{3,4},{4,5},{5,6},{6,7},{7,8},{8,9},{9,10},{10,1... | collective-permute-start | bytes 829448 | tf_op jit(solution)/shard_map/ppermute | solution.py:69
  60.8 2.9 %collective-permute-start.3 = (f32[3,18,5,256]{3,2,1,0:T(8,128)S(1)}, f32[3,18,5,256]{3,2,1,0:T(8,128)S(1)}, u32[]{:S(2)}, u32[]{:S(2)}) collective-permute-start(f32[3,18,5,256]{3,2,1,0:T(8,128)S(1)} %get-tuple-element.63), channel_id=1, source_target_pairs={{1,0},{2,1},{3,2},{4,3},{5,4},{6,5},{7,6},{8,7},{9,8},{10,9},{11,1... | collective-permute-start | bytes 829448 | tf_op jit(solution)/shard_map/ppermute | solution.py:70
  63.9 3.5 %collective-permute-start.6 = (f32[4,2]{1,0:T(4,128)S(1)}, f32[4,2]{1,0:T(4,128)S(1)}, u32[]{:S(2)}, u32[]{:S(2)}) collective-permute-start(f32[4,2]{1,0:T(4,128)S(1)} %fusion.540), channel_id=1, source_target_pairs={{0,2},{1,3},{2,0},{3,1},{4,6},{5,7},{6,4},{7,5},{8,10},{9,11},{10,... | collective-permute-start | bytes 104 | tf_op jit(solution)/shard_map/ppermute | solution.py:202
  67.4 5.6 %collective-permute-done.6 = f32[4,2]{1,0:T(4,128)S(1)} collective-permute-done((f32[4,2]{1,0:T(4,128)S(1)}, f32[4,2]{1,0:T(4,128)S(1)}, u32[]{:S(2)}, u32[]{:S(2)}) %collective-permute-start.6) | collective-permute-done | bytes 64 | tf_op jit(solution)/shard_map/ppermute | solution.py:202
  73.0 2.5 collective-permute-start.7
  75.5 3.0 %collective-permute-done.7 = f32[4,2]{1,0:T(4,128)S(1)} collective-permute-done((f32[4,2]{1,0:T(4,128)S(1)}, f32[4,2]{1,0:T(4,128)S(1)}, u32[]{:S(2)}, u32[]{:S(2)}) %collective-permute-start.7) | collective-permute-done | bytes 64 | tf_op jit(solution)/shard_map/ppermute | solution.py:202
  78.5 4.2 %collective-permute-start.8 = (f32[4,2]{1,0:T(4,128)S(1)}, f32[4,2]{1,0:T(4,128)S(1)}, u32[]{:S(2)}, u32[]{:S(2)}) collective-permute-start(f32[4,2]{1,0:T(4,128)S(1)} %max.30), channel_id=1, source_target_pairs={{0,256},{16,272},{32,288},{48,304},{64,320},{80,336},{96,352},{112... | collective-permute-start | bytes 104 | tf_op jit(solution)/shard_map/ppermute | solution.py:202
  82.7 2.8 %collective-permute-done.8 = f32[4,2]{1,0:T(4,128)S(1)} collective-permute-done((f32[4,2]{1,0:T(4,128)S(1)}, f32[4,2]{1,0:T(4,128)S(1)}, u32[]{:S(2)}, u32[]{:S(2)}) %collective-permute-start.8) | collective-permute-done | bytes 64 | tf_op jit(solution)/shard_map/ppermute | solution.py:202
  85.4 2.0 collective-permute-start.9
  87.5 3.4 %collective-permute-done.9 = f32[4,2]{1,0:T(4,128)S(1)} collective-permute-done((f32[4,2]{1,0:T(4,128)S(1)}, f32[4,2]{1,0:T(4,128)S(1)}, u32[]{:S(2)}, u32[]{:S(2)}) %collective-permute-start.9) | collective-permute-done | bytes 64 | tf_op jit(solution)/shard_map/ppermute | solution.py:202
  90.9 4.6 %collective-permute-start.10 = (f32[4,2]{1,0:T(4,128)S(1)}, f32[4,2]{1,0:T(4,128)S(1)}, u32[]{:S(2)}, u32[]{:S(2)}) collective-permute-start(f32[4,2]{1,0:T(4,128)S(1)} %max.32), channel_id=1, source_target_pairs={{0,64},{16,80},{32,96},{48,112},{64,0},{80,16},{96,32},{112,48},{1... | collective-permute-start | bytes 104 | tf_op jit(solution)/shard_map/ppermute | solution.py:202
  95.5 2.4 collective-permute-done.10
  97.9 3.4 %collective-permute-start.11 = (f32[4,2]{1,0:T(4,128)S(1)}, f32[4,2]{1,0:T(4,128)S(1)}, u32[]{:S(2)}, u32[]{:S(2)}) collective-permute-start(f32[4,2]{1,0:T(4,128)S(1)} %max.33), channel_id=1, source_target_pairs={{0,32},{16,48},{32,0},{48,16},{64,96},{80,112},{96,64},{112,80},{1... | collective-permute-start | bytes 104 | tf_op jit(solution)/shard_map/ppermute | solution.py:202
  101.3 2.1 collective-permute-done.11
  103.4 1.9 collective-permute-start.12
  115.7 2.1 collective-permute-start.13
  117.8 5.6 %collective-permute-start.15 = (f32[3,4,16,128]{3,2,1,0:T(8,128)S(1)}, f32[3,4,16,128]{3,2,1,0:T(8,128)S(1)}, u32[]{:S(2)}, u32[]{:S(2)}) collective-permute-start(f32[3,4,16,128]{3,2,1,0:T(8,128)S(1)} %pad_maximum_fusion.2), channel_id=1, source_target_pairs={{16,0},{32,16},{48,32},{64,48},{80,64},{96,80},{112,96},{128,112},... | collective-permute-start | bytes 294920 | tf_op jit(solution)/shard_map/ppermute | solution.py:70
  123.7 1.9 collective-permute-start.14
  126.3 5.8 %collective-permute-start.16 = (f32[3,3,16,128]{3,2,1,0:T(8,128)S(1)}, f32[3,3,16,128]{3,2,1,0:T(8,128)S(1)}, u32[]{:S(2)}, u32[]{:S(2)}) collective-permute-start(f32[3,3,16,128]{3,2,1,0:T(8,128)S(1)} %slice.1971), channel_id=1, source_target_pairs={{16,0},{32,16},{48,32},{64,48},{80,64},{96,80},{112,96},{128,112},... | collective-permute-start | bytes 221192 | tf_op jit(solution)/shard_map/ppermute | solution.py:70
  132.2 1.9 collective-permute-done.16
  134.8 1.9 collective-permute-start.17
  136.8 4.6 %collective-permute-start.18 = (f32[3,18,7,128]{3,2,1,0:T(8,128)}, f32[3,18,7,128]{3,2,1,0:T(8,128)}, u32[]{:S(2)}, u32[]{:S(2)}) collective-permute-start(f32[3,18,7,128]{3,2,1,0:T(8,128)} %get-tuple-element.94), channel_id=1, source_target_pairs={{1,0},{2,1},{3,2},{4,3},{5,4},{6,5},{7,6},{8,7},{9,8},{10,9},{11,1... | collective-permute-start | bytes 580616 | tf_op jit(solution)/shard_map/ppermute | solution.py:70
  149.5 1.9 collective-permute-start.19
  151.4 5.8 %collective-permute-start.20 = (f32[3,2,8,64]{3,2,1,0:T(8,128)S(1)}, f32[3,2,8,64]{3,2,1,0:T(8,128)S(1)}, u32[]{:S(2)}, u32[]{:S(2)}) collective-permute-start(f32[3,2,8,64]{3,2,1,0:T(8,128)S(1)} %pad_maximum_fusion.4), channel_id=1, source_target_pairs={{0,496},{16,0},{32,16},{48,32},{64,48},{80,64},{96,80},{112,96},{1... | collective-permute-start | bytes 36872 | tf_op jit(solution)/shard_map/ppermute | solution.py:70
  158.7 1.9 collective-permute-start.21
  161.9 6.0 %collective-permute-start.22 = (f32[3,6,8,64]{3,2,1,0:T(8,128)S(1)}, f32[3,6,8,64]{3,2,1,0:T(8,128)S(1)}, u32[]{:S(2)}, u32[]{:S(2)}) collective-permute-start(f32[3,6,8,64]{3,2,1,0:T(8,128)S(1)} %pad_maximum_fusion.3), channel_id=1, source_target_pairs={{0,464},{16,480},{32,496},{48,0},{64,16},{80,32},{96,48},{112,64},... | collective-permute-start | bytes 110600 | tf_op jit(solution)/shard_map/ppermute | solution.py:70
  168.0 1.9 collective-permute-done.22
  170.0 3.5 %collective-permute-start.23 = (f32[3,18,8,64]{3,2,1,0:T(8,128)S(1)}, f32[3,18,8,64]{3,2,1,0:T(8,128)}, u32[]{:S(2)}, u32[]{:S(2)}) collective-permute-start(f32[3,18,8,64]{3,2,1,0:T(8,128)S(1)} %broadcast_select_fusion), channel_id=1, source_target_pairs={{0,1},{1,2},{2,3},{3,4},{4,5},{5,6},{6,7},{7,8},{8,9},{9,10},{10,1... | collective-permute-start | bytes 331784 | tf_op jit(solution)/shard_map/ppermute | solution.py:69
  173.5 3.2 %collective-permute-start.24 = (f32[3,18,8,64]{3,2,1,0:T(8,128)S(1)}, f32[3,18,8,64]{3,2,1,0:T(8,128)}, u32[]{:S(2)}, u32[]{:S(2)}) collective-permute-start(f32[3,18,8,64]{3,2,1,0:T(8,128)S(1)} %broadcast_select_fusion), channel_id=1, source_target_pairs={{1,0},{2,1},{3,2},{4,3},{5,4},{6,5},{7,6},{8,7},{9,8},{10,9},{11,1... | collective-permute-start | bytes 331784 | tf_op jit(solution)/shard_map/ppermute | solution.py:70
  178.2 1.5 collective-permute-done.23
  179.7 4.8 %collective-permute-done.24 = f32[3,18,8,64]{3,2,1,0:T(8,128)} collective-permute-done((f32[3,18,8,64]{3,2,1,0:T(8,128)S(1)}, f32[3,18,8,64]{3,2,1,0:T(8,128)}, u32[]{:S(2)}, u32[]{:S(2)}) %collective-permute-start.24) | collective-permute-done | bytes 110624 | tf_op jit(solution)/shard_map/ppermute | solution.py:70
  188.5 23.2 %all_gather.3 = f32[3,32,4,32]{3,2,1,0:T(4,128)S(1)} all-gather(f32[3,1,4,32]{3,2,1,0:T(4,128)S(1)} %pad_maximum_fusion.5), channel_id=1, replica_groups=mesh['gx'=32,'gy'=16] {'gx'}, dimensions={1}, use_global_device_ids=true | all-gather | bytes 50688 | tf_op jit(solution)/shard_map/all_gather | solution.py:50
  211.8 4.0 %collective-permute-start.25 = (f32[3,21,4,32]{3,2,1,0:T(4,128)S(1)}, f32[3,21,4,32]{3,2,1,0:T(4,128)S(1)}, u32[]{:S(2)}, u32[]{:S(2)}) collective-permute-start(f32[3,21,4,32]{3,2,1,0:T(4,128)S(1)} %pad_dynamic-slice_fusion), channel_id=1, source_target_pairs={{0,1},{1,2},{2,3},{3,4},{4,5},{5,6},{6,7},{7,8},{8,9},{9,10},{10,1... | collective-permute-start | bytes 96776 | tf_op jit(solution)/shard_map/ppermute | solution.py:69
  215.8 1.9 collective-permute-start.26
  217.8 1.6 collective-permute-done.25
  219.4 3.7 %collective-permute-done.26 = f32[3,21,4,32]{3,2,1,0:T(4,128)S(1)} collective-permute-done((f32[3,21,4,32]{3,2,1,0:T(4,128)S(1)}, f32[3,21,4,32]{3,2,1,0:T(4,128)S(1)}, u32[]{:S(2)}, u32[]{:S(2)}) %collective-permute-start.26) | collective-permute-done | bytes 32288 | tf_op jit(solution)/shard_map/ppermute | solution.py:70
  224.9 4.0 %collective-permute-start.27 = (f32[3,21,6,32]{3,2,1,0:T(8,128)}, f32[3,21,6,32]{3,2,1,0:T(8,128)}, u32[]{:S(2)}, u32[]{:S(2)}) collective-permute-start(f32[3,21,6,32]{3,2,1,0:T(8,128)} %get-tuple-element.89), channel_id=1, source_target_pairs={{0,2},{1,3},{2,4},{3,5},{4,6},{5,7},{6,8},{7,9},{8,10},{9,11},{10,... | collective-permute-start | bytes 145160 | tf_op jit(solution)/shard_map/ppermute | solution.py:69
  228.9 4.0 %collective-permute-start.28 = (f32[3,21,6,32]{3,2,1,0:T(8,128)}, f32[3,21,6,32]{3,2,1,0:T(8,128)}, u32[]{:S(2)}, u32[]{:S(2)}) collective-permute-start(f32[3,21,6,32]{3,2,1,0:T(8,128)} %get-tuple-element.90), channel_id=1, source_target_pairs={{0,14},{1,15},{2,0},{3,1},{4,2},{5,3},{6,4},{7,5},{8,6},{9,7},{10,... | collective-permute-start | bytes 145160 | tf_op jit(solution)/shard_map/ppermute | solution.py:70
  234.9 6.2 %collective-permute-done.27 = f32[3,21,6,32]{3,2,1,0:T(8,128)} collective-permute-done((f32[3,21,6,32]{3,2,1,0:T(8,128)}, f32[3,21,6,32]{3,2,1,0:T(8,128)}, u32[]{:S(2)}, u32[]{:S(2)}) %collective-permute-start.27) | collective-permute-done | bytes 48416 | tf_op jit(solution)/shard_map/ppermute | solution.py:69
  241.1 3.3 %collective-permute-done.28 = f32[3,21,6,32]{3,2,1,0:T(8,128)} collective-permute-done((f32[3,21,6,32]{3,2,1,0:T(8,128)}, f32[3,21,6,32]{3,2,1,0:T(8,128)}, u32[]{:S(2)}, u32[]{:S(2)}) %collective-permute-start.28) | collective-permute-done | bytes 48416 | tf_op jit(solution)/shard_map/ppermute | solution.py:70
  (415 shorter events, 62.4 us)
Async XLA Ops:
  0.0 32.9 %copy-start.56 = (s32[256]{0:T(256)}, s32[256]{0:T(256)S(1)}, u32[]{:S(2)}) copy-start(s32[256]{0:T(256)S(1)} %and_select_fusion.7) | copy-start | bytes 3076
  0.0 32.9 %copy-start.105 = (s32[16]{0:T(128)}, s32[16]{0:T(128)S(1)}, u32[]{:S(2)}) copy-start(s32[16]{0:T(128)S(1)} %and_select_fusion.6) | copy-start | bytes 196
  0.1 32.9 %copy-start.72 = (s32[128]{0:T(128)}, s32[128]{0:T(128)S(1)}, u32[]{:S(2)}) copy-start(s32[128]{0:T(128)S(1)} %and_select_fusion.5) | copy-start | bytes 1540
  0.1 32.9 %copy-start.103 = (s32[8]{0:T(128)}, s32[8]{0:T(128)S(1)}, u32[]{:S(2)}) copy-start(s32[8]{0:T(128)S(1)} %and_select_fusion.4) | copy-start | bytes 100
  0.1 32.8 %copy-start.99 = (s32[64]{0:T(128)}, s32[64]{0:T(128)S(1)}, u32[]{:S(2)}) copy-start(s32[64]{0:T(128)S(1)} %and_select_fusion.3) | copy-start | bytes 772
  6.7 26.1 %copy-start.46 = (f32[4,16,128]{2,1,0:T(8,128)}, f32[4,16,128]{2,1,0:T(8,128)S(1)}, u32[]{:S(2)}) copy-start(f32[4,16,128]{2,1,0:T(8,128)S(1)} %get-tuple-element.168) | copy-start | bytes 98308
  7.6 25.2 %copy-start.48 = (f32[4,16,128]{2,1,0:T(8,128)}, f32[4,16,128]{2,1,0:T(8,128)S(1)}, u32[]{:S(2)}) copy-start(f32[4,16,128]{2,1,0:T(8,128)S(1)} %get-tuple-element.166) | copy-start | bytes 98308
  15.5 37.6 %copy-start.76 = (f32[1,2]{1,0:T(1,128)}, f32[1,2]{1,0:T(1,128)S(1)}, u32[]{:S(2)}) copy-start(f32[1,2]{1,0:T(1,128)S(1)} %get-tuple-element.171) | copy-start | bytes 28
  15.5 37.6 %copy-start.78 = (f32[1,2]{1,0:T(1,128)}, f32[1,2]{1,0:T(1,128)S(1)}, u32[]{:S(2)}) copy-start(f32[1,2]{1,0:T(1,128)S(1)} %get-tuple-element.172) | copy-start | bytes 28
  18.0 35.1 %copy-start.80 = (f32[1,2]{1,0:T(1,128)}, f32[1,2]{1,0:T(1,128)S(1)}, u32[]{:S(2)}) copy-start(f32[1,2]{1,0:T(1,128)S(1)} %get-tuple-element.169) | copy-start | bytes 28
  18.0 35.1 %copy-start.82 = (f32[1,2]{1,0:T(1,128)}, f32[1,2]{1,0:T(1,128)S(1)}, u32[]{:S(2)}) copy-start(f32[1,2]{1,0:T(1,128)S(1)} %get-tuple-element.170) | copy-start | bytes 28
  18.0 35.1 %collective-permute-start.4 = (f32[4,2]{1,0:T(4,128)S(1)}, f32[4,2]{1,0:T(4,128)S(1)}, u32[]{:S(2)}, u32[]{:S(2)}) collective-permute-start(f32[4,2]{1,0:T(4,128)S(1)} %pad_maximum_fusion.6), channel_id=1, source_target_pairs={{0,8},{1,9},{2,10},{3,11},{4,12},{5,13},{6,14},{7,15},{8,0},{9,1},... | collective-permute-start | bytes 104 | tf_op jit(solution)/shard_map/ppermute | solution.py:202
  32.9 24.6 %copy-start.43 = (f32[8,32,256]{2,1,0:T(8,128)S(1)}, f32[8,32,256]{2,1,0:T(8,128)}, u32[]{:S(2)}) copy-start(f32[8,32,256]{2,1,0:T(8,128)} %param.5) | copy-start | bytes 786436
  33.0 24.6 %copy-start.44 = (f32[8,32,256]{2,1,0:T(8,128)S(1)}, f32[8,32,256]{2,1,0:T(8,128)}, u32[]{:S(2)}) copy-start(f32[8,32,256]{2,1,0:T(8,128)} %param.4) | copy-start | bytes 786436
  33.0 24.6 %copy-start.45 = (f32[8,32,256]{2,1,0:T(8,128)S(1)}, f32[8,32,256]{2,1,0:T(8,128)}, u32[]{:S(2)}) copy-start(f32[8,32,256]{2,1,0:T(8,128)} %param.3) | copy-start | bytes 786436
  34.3 23.1 %collective-permute-start = (f32[3,5,32,256]{3,2,1,0:T(8,128)S(1)}, f32[3,5,32,256]{3,2,1,0:T(8,128)S(1)}, u32[]{:S(2)}, u32[]{:S(2)}) collective-permute-start(f32[3,5,32,256]{3,2,1,0:T(8,128)S(1)} %get-tuple-element.71), channel_id=1, source_target_pairs={{0,16},{16,32},{32,48},{48,64},{64,80},{80,96},{96,112},{112,128},... | collective-permute-start | bytes 1474568 | tf_op jit(solution)/shard_map/ppermute | solution.py:69
  36.3 21.3 %collective-permute-start.1 = (f32[3,5,32,256]{3,2,1,0:T(8,128)S(1)}, f32[3,5,32,256]{3,2,1,0:T(8,128)S(1)}, u32[]{:S(2)}, u32[]{:S(2)}) collective-permute-start(f32[3,5,32,256]{3,2,1,0:T(8,128)S(1)} %get-tuple-element.72), channel_id=1, source_target_pairs={{16,0},{32,16},{48,32},{64,48},{80,64},{96,80},{112,96},{128,112},... | collective-permute-start | bytes 1474568 | tf_op jit(solution)/shard_map/ppermute | solution.py:70
  43.5 13.9 %copy-start.58 = (pred[12,36]{1,0:T(8,128)(4,1)}, pred[12,36]{1,0:T(8,128)(4,1)S(1)}, u32[]{:S(2)}) copy-start(pred[12,36]{1,0:T(8,128)(4,1)S(1)} %slice_bitcast_fusion.27) | copy-start | bytes 1300
  45.6 11.9 %copy-start.95 = (pred[18]{0:T(512)(128)(4,1)}, pred[18]{0:T(512)(128)(4,1)S(1)}, u32[]{:S(2)}) copy-start(pred[18]{0:T(512)(128)(4,1)S(1)} %compare_and_fusion.3) | copy-start | bytes 58
  53.2 10.6 %collective-permute-start.5 = (f32[4,2]{1,0:T(4,128)S(1)}, f32[4,2]{1,0:T(4,128)S(1)}, u32[]{:S(2)}, u32[]{:S(2)}) collective-permute-start(f32[4,2]{1,0:T(4,128)S(1)} %fusion.471), channel_id=1, source_target_pairs={{0,4},{1,5},{2,6},{3,7},{4,0},{5,1},{6,2},{7,3},{8,12},{9,13},{10,... | collective-permute-start | bytes 104 | tf_op jit(solution)/shard_map/ppermute | solution.py:202
  57.9 50.6 %collective-permute-start.2 = (f32[3,18,5,256]{3,2,1,0:T(8,128)S(1)}, f32[3,18,5,256]{3,2,1,0:T(8,128)S(1)}, u32[]{:S(2)}, u32[]{:S(2)}) collective-permute-start(f32[3,18,5,256]{3,2,1,0:T(8,128)S(1)} %get-tuple-element.62), channel_id=1, source_target_pairs={{0,1},{1,2},{2,3},{3,4},{4,5},{5,6},{6,7},{7,8},{8,9},{9,10},{10,1... | collective-permute-start | bytes 829448 | tf_op jit(solution)/shard_map/ppermute | solution.py:69
  60.8 47.7 %collective-permute-start.3 = (f32[3,18,5,256]{3,2,1,0:T(8,128)S(1)}, f32[3,18,5,256]{3,2,1,0:T(8,128)S(1)}, u32[]{:S(2)}, u32[]{:S(2)}) collective-permute-start(f32[3,18,5,256]{3,2,1,0:T(8,128)S(1)} %get-tuple-element.63), channel_id=1, source_target_pairs={{1,0},{2,1},{3,2},{4,3},{5,4},{6,5},{7,6},{8,7},{9,8},{10,9},{11,1... | collective-permute-start | bytes 829448 | tf_op jit(solution)/shard_map/ppermute | solution.py:70
  63.9 9.1 %collective-permute-start.6 = (f32[4,2]{1,0:T(4,128)S(1)}, f32[4,2]{1,0:T(4,128)S(1)}, u32[]{:S(2)}, u32[]{:S(2)}) collective-permute-start(f32[4,2]{1,0:T(4,128)S(1)} %fusion.540), channel_id=1, source_target_pairs={{0,2},{1,3},{2,0},{3,1},{4,6},{5,7},{6,4},{7,5},{8,10},{9,11},{10,... | collective-permute-start | bytes 104 | tf_op jit(solution)/shard_map/ppermute | solution.py:202
  73.0 5.5 %collective-permute-start.7 = (f32[4,2]{1,0:T(4,128)S(1)}, f32[4,2]{1,0:T(4,128)S(1)}, u32[]{:S(2)}, u32[]{:S(2)}) collective-permute-start(f32[4,2]{1,0:T(4,128)S(1)} %max.29), channel_id=1, source_target_pairs={{0,1},{1,0},{2,3},{3,2},{4,5},{5,4},{6,7},{7,6},{8,9},{9,8},{10,11... | collective-permute-start | bytes 104 | tf_op jit(solution)/shard_map/ppermute | solution.py:202
  78.5 7.0 %collective-permute-start.8 = (f32[4,2]{1,0:T(4,128)S(1)}, f32[4,2]{1,0:T(4,128)S(1)}, u32[]{:S(2)}, u32[]{:S(2)}) collective-permute-start(f32[4,2]{1,0:T(4,128)S(1)} %max.30), channel_id=1, source_target_pairs={{0,256},{16,272},{32,288},{48,304},{64,320},{80,336},{96,352},{112... | collective-permute-start | bytes 104 | tf_op jit(solution)/shard_map/ppermute | solution.py:202
  85.4 5.5 %collective-permute-start.9 = (f32[4,2]{1,0:T(4,128)S(1)}, f32[4,2]{1,0:T(4,128)S(1)}, u32[]{:S(2)}, u32[]{:S(2)}) collective-permute-start(f32[4,2]{1,0:T(4,128)S(1)} %max.31), channel_id=1, source_target_pairs={{0,128},{16,144},{32,160},{48,176},{64,192},{80,208},{96,224},{112... | collective-permute-start | bytes 104 | tf_op jit(solution)/shard_map/ppermute | solution.py:202
  90.9 7.0 %collective-permute-start.10 = (f32[4,2]{1,0:T(4,128)S(1)}, f32[4,2]{1,0:T(4,128)S(1)}, u32[]{:S(2)}, u32[]{:S(2)}) collective-permute-start(f32[4,2]{1,0:T(4,128)S(1)} %max.32), channel_id=1, source_target_pairs={{0,64},{16,80},{32,96},{48,112},{64,0},{80,16},{96,32},{112,48},{1... | collective-permute-start | bytes 104 | tf_op jit(solution)/shard_map/ppermute | solution.py:202
  97.9 5.5 %collective-permute-start.11 = (f32[4,2]{1,0:T(4,128)S(1)}, f32[4,2]{1,0:T(4,128)S(1)}, u32[]{:S(2)}, u32[]{:S(2)}) collective-permute-start(f32[4,2]{1,0:T(4,128)S(1)} %max.33), channel_id=1, source_target_pairs={{0,32},{16,48},{32,0},{48,16},{64,96},{80,112},{96,64},{112,80},{1... | collective-permute-start | bytes 104 | tf_op jit(solution)/shard_map/ppermute | solution.py:202
  103.4 3.0 %collective-permute-start.12 = (f32[4,2]{1,0:T(4,128)S(1)}, f32[4,2]{1,0:T(4,128)S(1)}, u32[]{:S(2)}, u32[]{:S(2)}) collective-permute-start(f32[4,2]{1,0:T(4,128)S(1)} %max.34), channel_id=1, source_target_pairs={{0,16},{16,0},{32,48},{48,32},{64,80},{80,64},{96,112},{112,96},{1... | collective-permute-start | bytes 104 | tf_op jit(solution)/shard_map/ppermute | solution.py:202
  115.7 8.0 %collective-permute-start.13 = (f32[3,4,16,128]{3,2,1,0:T(8,128)S(1)}, f32[3,4,16,128]{3,2,1,0:T(8,128)S(1)}, u32[]{:S(2)}, u32[]{:S(2)}) collective-permute-start(f32[3,4,16,128]{3,2,1,0:T(8,128)S(1)} %pad_maximum_fusion.2), channel_id=1, source_target_pairs={{0,16},{16,32},{32,48},{48,64},{64,80},{80,96},{96,112},{112,128},... | collective-permute-start | bytes 294920 | tf_op jit(solution)/shard_map/ppermute | solution.py:69
  117.8 8.5 %collective-permute-start.15 = (f32[3,4,16,128]{3,2,1,0:T(8,128)S(1)}, f32[3,4,16,128]{3,2,1,0:T(8,128)S(1)}, u32[]{:S(2)}, u32[]{:S(2)}) collective-permute-start(f32[3,4,16,128]{3,2,1,0:T(8,128)S(1)} %pad_maximum_fusion.2), channel_id=1, source_target_pairs={{16,0},{32,16},{48,32},{64,48},{80,64},{96,80},{112,96},{128,112},... | collective-permute-start | bytes 294920 | tf_op jit(solution)/shard_map/ppermute | solution.py:70
  123.7 8.4 %collective-permute-start.14 = (f32[3,3,16,128]{3,2,1,0:T(8,128)S(1)}, f32[3,3,16,128]{3,2,1,0:T(8,128)S(1)}, u32[]{:S(2)}, u32[]{:S(2)}) collective-permute-start(f32[3,3,16,128]{3,2,1,0:T(8,128)S(1)} %slice.1970), channel_id=1, source_target_pairs={{0,16},{16,32},{32,48},{48,64},{64,80},{80,96},{96,112},{112,128},... | collective-permute-start | bytes 221192 | tf_op jit(solution)/shard_map/ppermute | solution.py:69
  126.3 7.7 %collective-permute-start.16 = (f32[3,3,16,128]{3,2,1,0:T(8,128)S(1)}, f32[3,3,16,128]{3,2,1,0:T(8,128)S(1)}, u32[]{:S(2)}, u32[]{:S(2)}) collective-permute-start(f32[3,3,16,128]{3,2,1,0:T(8,128)S(1)} %slice.1971), channel_id=1, source_target_pairs={{16,0},{32,16},{48,32},{64,48},{80,64},{96,80},{112,96},{128,112},... | collective-permute-start | bytes 221192 | tf_op jit(solution)/shard_map/ppermute | solution.py:70
  134.8 9.4 %collective-permute-start.17 = (f32[3,18,7,128]{3,2,1,0:T(8,128)}, f32[3,18,7,128]{3,2,1,0:T(8,128)}, u32[]{:S(2)}, u32[]{:S(2)}) collective-permute-start(f32[3,18,7,128]{3,2,1,0:T(8,128)} %get-tuple-element.93), channel_id=1, source_target_pairs={{0,1},{1,2},{2,3},{3,4},{4,5},{5,6},{6,7},{7,8},{8,9},{9,10},{10,1... | collective-permute-start | bytes 580616 | tf_op jit(solution)/shard_map/ppermute | solution.py:69
  136.8 8.3 %collective-permute-start.18 = (f32[3,18,7,128]{3,2,1,0:T(8,128)}, f32[3,18,7,128]{3,2,1,0:T(8,128)}, u32[]{:S(2)}, u32[]{:S(2)}) collective-permute-start(f32[3,18,7,128]{3,2,1,0:T(8,128)} %get-tuple-element.94), channel_id=1, source_target_pairs={{1,0},{2,1},{3,2},{4,3},{5,4},{6,5},{7,6},{8,7},{9,8},{10,9},{11,1... | collective-permute-start | bytes 580616 | tf_op jit(solution)/shard_map/ppermute | solution.py:70
  148.4 12.9 %copy-start.64 = (pred[12,18]{1,0:T(8,128)(4,1)S(1)}, pred[12,18]{1,0:T(8,128)(4,1)}, u32[]{:S(2)}) copy-start(pred[12,18]{1,0:T(8,128)(4,1)} %slice_bitcast_fusion.21) | copy-start | bytes 652
  148.5 21.4 %copy-start.96 = (pred[18]{0:T(512)(128)(4,1)S(1)}, pred[18]{0:T(512)(128)(4,1)}, u32[]{:S(2)}) copy-start(pred[18]{0:T(512)(128)(4,1)} %copy-done.95) | copy-start | bytes 58
  149.5 9.0 %collective-permute-start.19 = (f32[3,2,8,64]{3,2,1,0:T(8,128)S(1)}, f32[3,2,8,64]{3,2,1,0:T(8,128)S(1)}, u32[]{:S(2)}, u32[]{:S(2)}) collective-permute-start(f32[3,2,8,64]{3,2,1,0:T(8,128)S(1)} %pad_maximum_fusion.4), channel_id=1, source_target_pairs={{0,16},{16,32},{32,48},{48,64},{64,80},{80,96},{96,112},{112,128},... | collective-permute-start | bytes 36872 | tf_op jit(solution)/shard_map/ppermute | solution.py:69
  151.4 7.3 %collective-permute-start.20 = (f32[3,2,8,64]{3,2,1,0:T(8,128)S(1)}, f32[3,2,8,64]{3,2,1,0:T(8,128)S(1)}, u32[]{:S(2)}, u32[]{:S(2)}) collective-permute-start(f32[3,2,8,64]{3,2,1,0:T(8,128)S(1)} %pad_maximum_fusion.4), channel_id=1, source_target_pairs={{0,496},{16,0},{32,16},{48,32},{64,48},{80,64},{96,80},{112,96},{1... | collective-permute-start | bytes 36872 | tf_op jit(solution)/shard_map/ppermute | solution.py:70
  158.7 9.3 %collective-permute-start.21 = (f32[3,6,8,64]{3,2,1,0:T(8,128)S(1)}, f32[3,6,8,64]{3,2,1,0:T(8,128)S(1)}, u32[]{:S(2)}, u32[]{:S(2)}) collective-permute-start(f32[3,6,8,64]{3,2,1,0:T(8,128)S(1)} %pad_maximum_fusion.3), channel_id=1, source_target_pairs={{0,48},{16,64},{32,80},{48,96},{64,112},{80,128},{96,144},{112,160... | collective-permute-start | bytes 110600 | tf_op jit(solution)/shard_map/ppermute | solution.py:69
  161.9 8.0 %collective-permute-start.22 = (f32[3,6,8,64]{3,2,1,0:T(8,128)S(1)}, f32[3,6,8,64]{3,2,1,0:T(8,128)S(1)}, u32[]{:S(2)}, u32[]{:S(2)}) collective-permute-start(f32[3,6,8,64]{3,2,1,0:T(8,128)S(1)} %pad_maximum_fusion.3), channel_id=1, source_target_pairs={{0,464},{16,480},{32,496},{48,0},{64,16},{80,32},{96,48},{112,64},... | collective-permute-start | bytes 110600 | tf_op jit(solution)/shard_map/ppermute | solution.py:70
  170.0 9.7 %collective-permute-start.23 = (f32[3,18,8,64]{3,2,1,0:T(8,128)S(1)}, f32[3,18,8,64]{3,2,1,0:T(8,128)}, u32[]{:S(2)}, u32[]{:S(2)}) collective-permute-start(f32[3,18,8,64]{3,2,1,0:T(8,128)S(1)} %broadcast_select_fusion), channel_id=1, source_target_pairs={{0,1},{1,2},{2,3},{3,4},{4,5},{5,6},{6,7},{7,8},{8,9},{9,10},{10,1... | collective-permute-start | bytes 331784 | tf_op jit(solution)/shard_map/ppermute | solution.py:69
  173.5 11.0 %collective-permute-start.24 = (f32[3,18,8,64]{3,2,1,0:T(8,128)S(1)}, f32[3,18,8,64]{3,2,1,0:T(8,128)}, u32[]{:S(2)}, u32[]{:S(2)}) collective-permute-start(f32[3,18,8,64]{3,2,1,0:T(8,128)S(1)} %broadcast_select_fusion), channel_id=1, source_target_pairs={{1,0},{2,1},{3,2},{4,3},{5,4},{6,5},{7,6},{8,7},{9,8},{10,9},{11,1... | collective-permute-start | bytes 331784 | tf_op jit(solution)/shard_map/ppermute | solution.py:70
  187.9 56.6 %copy-start.98 = (pred[24]{0:T(512)(128)(4,1)S(1)}, pred[24]{0:T(512)(128)(4,1)}, u32[]{:S(2)}) copy-start(pred[24]{0:T(512)(128)(4,1)} %copy-done.97) | copy-start | bytes 76
  211.8 7.6 %collective-permute-start.25 = (f32[3,21,4,32]{3,2,1,0:T(4,128)S(1)}, f32[3,21,4,32]{3,2,1,0:T(4,128)S(1)}, u32[]{:S(2)}, u32[]{:S(2)}) collective-permute-start(f32[3,21,4,32]{3,2,1,0:T(4,128)S(1)} %pad_dynamic-slice_fusion), channel_id=1, source_target_pairs={{0,1},{1,2},{2,3},{3,4},{4,5},{5,6},{6,7},{7,8},{8,9},{9,10},{10,1... | collective-permute-start | bytes 96776 | tf_op jit(solution)/shard_map/ppermute | solution.py:69
  215.8 7.3 %collective-permute-start.26 = (f32[3,21,4,32]{3,2,1,0:T(4,128)S(1)}, f32[3,21,4,32]{3,2,1,0:T(4,128)S(1)}, u32[]{:S(2)}, u32[]{:S(2)}) collective-permute-start(f32[3,21,4,32]{3,2,1,0:T(4,128)S(1)} %pad_dynamic-slice_fusion), channel_id=1, source_target_pairs={{0,15},{1,0},{2,1},{3,2},{4,3},{5,4},{6,5},{7,6},{8,7},{9,8},{10,9... | collective-permute-start | bytes 96776 | tf_op jit(solution)/shard_map/ppermute | solution.py:70
  224.9 16.2 %collective-permute-start.27 = (f32[3,21,6,32]{3,2,1,0:T(8,128)}, f32[3,21,6,32]{3,2,1,0:T(8,128)}, u32[]{:S(2)}, u32[]{:S(2)}) collective-permute-start(f32[3,21,6,32]{3,2,1,0:T(8,128)} %get-tuple-element.89), channel_id=1, source_target_pairs={{0,2},{1,3},{2,4},{3,5},{4,6},{5,7},{6,8},{7,9},{8,10},{9,11},{10,... | collective-permute-start | bytes 145160 | tf_op jit(solution)/shard_map/ppermute | solution.py:69
  228.9 15.5 %collective-permute-start.28 = (f32[3,21,6,32]{3,2,1,0:T(8,128)}, f32[3,21,6,32]{3,2,1,0:T(8,128)}, u32[]{:S(2)}, u32[]{:S(2)}) collective-permute-start(f32[3,21,6,32]{3,2,1,0:T(8,128)} %get-tuple-element.90), channel_id=1, source_target_pairs={{0,14},{1,15},{2,0},{3,1},{4,2},{5,3},{6,4},{7,5},{8,6},{9,7},{10,... | collective-permute-start | bytes 145160 | tf_op jit(solution)/shard_map/ppermute | solution.py:70
  (88 other events, 184.1 us)
